TPU v7x, 128 devices: a whole 4x4x4 slice. The times are simulated.
128 devices in a mesh: dp: 8 (over x, core), sector: 16 (over y, z).
Axes of the slice: x: 4, y: 4, z: 4, core: 2. Of those that a mesh axis runs over, the one named last changes fastest.
Arguments:
- hits: bfloat16 [8, 32768, 256], P('dp', 'sector'), may hold values from -6 to 6
- tiles: bfloat16 [8, 256, 8, 128, 128], P('dp', 'sector'), may hold values from -0.1875 to 0.1875
- sources: int32 [8, 256, 8], P('dp', 'sector'), may hold values from 0 to 23
- send_list: int32 [8, 16, 2, 4], P('dp'), may hold values from 0 to 15, as said below
- w_message: bfloat16 [2, 256, 256], replicated, may hold values from -0.375 to 0.375
- w_self: bfloat16 [2, 256, 256], replicated, may hold values from -0.375 to 0.375
- cotangent: float32 [8, 32768, 256], P('dp', 'sector'), may hold values from -6 to 6
Outputs:
- hit_output: bfloat16 [8, 32768, 256], P('dp', 'sector')
- hit_grad: float32 [8, 32768, 256], P('dp', 'sector')
- message_grad: float32 [2, 256, 256], replicated
- self_grad: float32 [2, 256, 256], replicated
Inputs may be any that keep to these rules, and one draw needn't show every extreme that they name: `send_list`: each list holds 4 distinct local block numbers of its sector.
All inputs are finite; a program needn't handle non-finite values.
Results may differ from a plain program's by a relative error of at most 0.007.
Values may be sent and summed in bfloat16 or wider, within the bound.
No kernel may reach another device: no remote copies, remote signals or barrier semaphores. Data moves between devices by JAX's collectives and lax.ppermute only.
A program may use at most 128 MiB of HBM per device.

v0:
```python
import jax
import jax.numpy as jnp
from jax import lax
from jax.experimental import pallas as pl
from jax.experimental.pallas import tpu as pltpu
from jax.sharding import PartitionSpec as P

LAYERS = 2
GROUP = 4


def aggregate_kernel(src_ref, tiles_ref, table_ref, out_ref):
    step = pl.program_id(0)
    for i in range(GROUP):
        block = step * GROUP + i
        acc = None
        for k in range(tiles_ref.shape[1]):
            slot = src_ref[block, k]
            part = jnp.dot(tiles_ref[i, k], table_ref[slot], preferred_element_type=jnp.float32)
            acc = part if acc is None else acc + part
        out_ref[i] = acc


def block_aggregate(slot_ids, tile_data, table):
    blocks, listed, rows, _ = tile_data.shape
    width = table.shape[-1]
    return pl.pallas_call(
        aggregate_kernel,
        grid_spec=pltpu.PrefetchScalarGridSpec(
            num_scalar_prefetch=1,
            grid=(blocks // GROUP,),
            in_specs=[
                pl.BlockSpec((GROUP, listed, rows, rows), lambda g, src: (g, 0, 0, 0)),
                pl.BlockSpec(table.shape, lambda g, src: (0, 0, 0)),
            ],
            out_specs=pl.BlockSpec((GROUP, rows, width), lambda g, src: (g, 0, 0)),
        ),
        out_shape=jax.ShapeDtypeStruct((blocks, rows, width), jnp.float32),
    )(slot_ids, tile_data, table)


def slot_grad_kernel(src_ref, tiles_ref, dpre_ref, out_ref):
    step = pl.program_id(0)

    @pl.when(step == 0)
    def _():
        out_ref[...] = jnp.zeros(out_ref.shape, out_ref.dtype)

    for i in range(GROUP):
        block = step * GROUP + i
        grad = dpre_ref[i]
        for k in range(tiles_ref.shape[1]):
            slot = src_ref[block, k]
            part = lax.dot_general(
                tiles_ref[i, k], grad, (((0,), (0,)), ((), ())),
                preferred_element_type=jnp.float32,
            )
            out_ref[slot] += part


def block_slot_grad(slot_ids, tile_data, dpre_blocks, slot_count):
    blocks, listed, rows, _ = tile_data.shape
    width = dpre_blocks.shape[-1]
    return pl.pallas_call(
        slot_grad_kernel,
        grid_spec=pltpu.PrefetchScalarGridSpec(
            num_scalar_prefetch=1,
            grid=(blocks // GROUP,),
            in_specs=[
                pl.BlockSpec((GROUP, listed, rows, rows), lambda g, src: (g, 0, 0, 0)),
                pl.BlockSpec((GROUP, rows, width), lambda g, src: (g, 0, 0)),
            ],
            out_specs=pl.BlockSpec((slot_count, rows, width), lambda g, src: (0, 0, 0)),
        ),
        out_shape=jax.ShapeDtypeStruct((slot_count, rows, width), jnp.float32),
        compiler_params=pltpu.CompilerParams(dimension_semantics=("arbitrary",)),
    )(slot_ids, tile_data, dpre_blocks)


def extended_2(cells, sides, width):
    for axis, dim in sides:
        count = lax.axis_size(axis)
        head = lax.slice_in_dim(cells, 0, width, axis=dim)
        tail = lax.slice_in_dim(cells, cells.shape[dim] - width, cells.shape[dim], axis=dim)
        cells = jnp.concatenate(
            [
                lax.ppermute(tail, axis, [(i, (i + 1) % count) for i in range(count)]),
                cells,
                lax.ppermute(head, axis, [((i + 1) % count, i) for i in range(count)]),
            ],
            axis=dim,
        )
    return cells


def all_reduce(x, axes):
    count = lax.axis_size(axes)
    pieces = x.reshape(count, -1)
    mine = lax.all_to_all(pieces, axes, 0, 0, tiled=True).sum(0)
    spread = jnp.broadcast_to(mine[None], (count,) + mine.shape)
    return lax.all_to_all(spread, axes, 0, 0, tiled=True).reshape(x.shape)


def silu_grad(pre):
    sig = jax.nn.sigmoid(pre)
    return sig * (1.0 + pre * (1.0 - sig))


def per_device(hits, tiles, sources, send_list, w_message, w_self, cotangent):
    blocks_here = tiles.shape[1]
    tile_rows = tiles.shape[3]
    width = hits.shape[2]
    lent = send_list.shape[3]
    listed = tiles.shape[2]
    sector_here = lax.axis_index("sector")
    lists = send_list[0]
    own_lists = lax.dynamic_index_in_dim(lists, sector_here, 0, keepdims=False)
    tile_data = tiles[0]
    slot_ids = sources[0]
    slot_count = blocks_here + 2 * lent
    current = hits[0]
    saved = []
    for layer_index in range(LAYERS):
        message = jnp.dot(
            current, w_message[layer_index], preferred_element_type=jnp.float32
        ).astype(jnp.bfloat16)
        message_blocks = message.reshape(blocks_here, tile_rows, width)
        packet = jnp.concatenate(
            [message_blocks[own_lists[1]], message_blocks[own_lists[0]]]
        ).reshape(2 * lent * tile_rows, width)
        extended = extended_2(packet, (("sector", 0),), lent * tile_rows)
        table = jnp.concatenate(
            [
                message_blocks,
                extended[: lent * tile_rows].reshape(lent, tile_rows, width),
                extended[-lent * tile_rows :].reshape(lent, tile_rows, width),
            ]
        )
        aggregate = block_aggregate(slot_ids, tile_data, table)
        pre = aggregate.reshape(-1, width) + jnp.dot(
            current, w_self[layer_index], preferred_element_type=jnp.float32
        )
        saved.append((current, pre))
        current = (current.astype(jnp.float32) + jax.nn.silu(pre)).astype(jnp.bfloat16)
    grad = cotangent[0]
    message_steps = [None] * LAYERS
    self_steps = [None] * LAYERS
    for layer_index in reversed(range(LAYERS)):
        layer_in, pre = saved[layer_index]
        dpre = (grad * silu_grad(pre)).astype(jnp.bfloat16)
        slot_grad = block_slot_grad(
            slot_ids, tile_data, dpre.reshape(blocks_here, tile_rows, width), slot_count
        )
        packet = slot_grad[blocks_here:].reshape(2 * lent * tile_rows, width)
        extended = extended_2(packet, (("sector", 0),), lent * tile_rows)
        dblocks = slot_grad[:blocks_here].reshape(blocks_here, tile_rows, width)
        dblocks = dblocks.at[own_lists[1]].add(
            extended[: lent * tile_rows].reshape(lent, tile_rows, width)
        )
        dblocks = dblocks.at[own_lists[0]].add(
            extended[-lent * tile_rows :].reshape(lent, tile_rows, width)
        )
        dmessage = dblocks.reshape(-1, width).astype(jnp.bfloat16)
        self_part = jnp.dot(layer_in.T, dpre, preferred_element_type=jnp.float32)
        message_part = jnp.dot(layer_in.T, dmessage, preferred_element_type=jnp.float32)
        message_steps[layer_index] = message_part
        self_steps[layer_index] = self_part
        grad = grad + jnp.dot(dpre, w_self[layer_index].T, preferred_element_type=jnp.float32)
        grad = grad + jnp.dot(
            dmessage, w_message[layer_index].T, preferred_element_type=jnp.float32
        )
    message_total = jnp.stack(message_steps)
    self_total = jnp.stack(self_steps)
    both = all_reduce(jnp.stack([message_total, self_total]), ("dp", "sector"))
    message_total, self_total = both[0], both[1]
    total_rows = blocks_here * tile_rows * lax.axis_size(("dp", "sector"))
    scale = 1.0 / jnp.sqrt(jnp.float32(total_rows))
    return (current[None], grad[None], message_total * scale, self_total * scale)


def solution(mesh):
    in_specs = (
        P("dp", "sector", None),
        P("dp", "sector", None, None, None),
        P("dp", "sector", None),
        P("dp", None, None, None),
        P(),
        P(),
        P("dp", "sector", None),
    )
    out_specs = (P("dp", "sector", None), P("dp", "sector", None), P(), P())
    return jax.shard_map(
        per_device, mesh=mesh, in_specs=in_specs, out_specs=out_specs, check_vma=False
    )
```

profile of v0, /device:TPU:1, one launch (start us, length us, event | category | flops | bytes accessed | tf_op | source)
XLA Modules:
  0.0 181.4 jit_solution(11176525875039284105)
XLA Ops:
  0.6 0.9 dynamic-slice_reduce_fusion.1
  1.6 1.7 convolution_convert_fusion.1
  3.3 0.6 gather_fusion
  3.8 2.5 %collective-permute-start = (bf16[512,256]{1,0:T(8,128)(2,1)S(1)}, bf16[512,256]{1,0:T(8,128)(2,1)S(1)}, u32[]{:S(2)}, u32[]{:S(2)}) collective-permute-start(bf16[512,256]{1,0:T(8,128)(2,1)S(1)} %bitcast.144), channel_id=1, source_target_pairs={{0,1},{1,2},{2,3},{3,4},{4,5},{5,6},{6,7},{7,8},{8,9},{9,10},{10,1... | collective-permute-start | bytes 786440 | tf_op jit(solution)/shard_map/ppermute | solution.py:87
  6.9 4.7 %collective-permute-start.1 = (bf16[512,256]{1,0:T(8,128)(2,1)S(1)}, bf16[512,256]{1,0:T(8,128)(2,1)S(1)}, u32[]{:S(2)}, u32[]{:S(2)}) collective-permute-start(bf16[512,256]{1,0:T(8,128)(2,1)S(1)} %bitcast.145), channel_id=1, source_target_pairs={{1,0},{2,1},{3,2},{4,3},{5,4},{6,5},{7,6},{8,7},{9,8},{10,9},{11,1... | collective-permute-start | bytes 786440 | tf_op jit(solution)/shard_map/ppermute | solution.py:89
  11.6 0.7 copy.24.src_ref
  12.2 4.7 %collective-permute-done = bf16[512,256]{1,0:T(8,128)(2,1)S(1)} collective-permute-done((bf16[512,256]{1,0:T(8,128)(2,1)S(1)}, bf16[512,256]{1,0:T(8,128)(2,1)S(1)}, u32[]{:S(2)}, u32[]{:S(2)}) %collective-permute-start) | collective-permute-done | bytes 262176 | tf_op jit(solution)/shard_map/ppermute | solution.py:87
  16.9 1.4 pad_maximum_fusion.table_ref
  18.3 7.1 %shard_map.102 = f32[16,128,256]{2,1,0:T(8,128)} custom-call(s32[16,8]{1,0:T(8,128)} %copy.24.src_ref, bf16[16,8,128,128]{3,2,1,0:T(8,128)(2,1)} %bitcast.119, bf16[24,128,256]{2,1,0:T(8,128)(2,1)} %pad_maximum_fusion.table_ref), custom_call_target="tpu_custom_call" | custom-call | tf_op jit(solution)/shard_map/pallas_call | solution.py:27
  25.4 3.8 %add_convert_fusion.1 = (bf16[2048,256]{1,0:T(8,128)(2,1)S(1)}, f32[2048,256]{1,0:T(8,128)}) fusion(bf16[1,2048,256]{2,1,0:T(8,128)(2,1)S(1)} %copy-done, bf16[2,256,256]{2,1,0:T(8,128)(2,1)S(1)} %copy-done.20, f32[16,128,256]{2,1,0:T(8,128)} %shard_map.102), kind=kOutput, calls=%fused_computation.22 | convolution fusion | flops 272629760 | bytes 7471104 | tf_op jit(solution)/shard_map/dot_general | solution.py:140
  29.6 1.3 gather_fusion.3
  30.8 1.3 gather_fusion.2
  32.1 5.2 %collective-permute-start.3 = (bf16[512,256]{1,0:T(8,128)(2,1)}, bf16[512,256]{1,0:T(8,128)(2,1)S(1)}, u32[]{:S(2)}, u32[]{:S(2)}) collective-permute-start(bf16[512,256]{1,0:T(8,128)(2,1)} %bitcast.143), channel_id=1, source_target_pairs={{1,0},{2,1},{3,2},{4,3},{5,4},{6,5},{7,6},{8,7},{9,8},{10,9},{11,1... | collective-permute-start | bytes 786440 | tf_op jit(solution)/shard_map/ppermute | solution.py:89
  37.3 5.4 %collective-permute-done.2 = bf16[512,256]{1,0:T(8,128)(2,1)S(1)} collective-permute-done((bf16[512,256]{1,0:T(8,128)(2,1)}, bf16[512,256]{1,0:T(8,128)(2,1)S(1)}, u32[]{:S(2)}, u32[]{:S(2)}) %collective-permute-start.2) | collective-permute-done | bytes 262176 | tf_op jit(solution)/shard_map/ppermute | solution.py:87
  42.6 1.4 pad_maximum_fusion.1.table_ref
  44.0 7.1 %shard_map.103 = f32[16,128,256]{2,1,0:T(8,128)} custom-call(s32[16,8]{1,0:T(8,128)} %copy.24.src_ref, bf16[16,8,128,128]{3,2,1,0:T(8,128)(2,1)} %bitcast.120, bf16[24,128,256]{2,1,0:T(8,128)(2,1)} %pad_maximum_fusion.1.table_ref), custom_call_target="tpu_custom_call" | custom-call | tf_op jit(solution)/shard_map/pallas_call | solution.py:27
  51.1 4.9 %fusion.1 = (bf16[2048,256]{1,0:T(8,128)(2,1)}, bf16[1,2048,256]{2,1,0:T(8,128)(2,1)}) fusion(f32[1,2048,256]{2,1,0:T(8,128)S(1)} %copy-done.7, f32[16,128,256]{2,1,0:T(8,128)} %shard_map.103, bf16[2048,256]{1,0:T(8,128)(2,1)} %copy-done.12, bf16[2,256,256]{2,1,0:T(8,128)(2,1)} %param.12), kind=kOutput, calls=%fused_computation.16 | convolution fusion | flops 275775488 | bytes 8519680 | tf_op jit(solution)/shard_map/dot_general | solution.py:140
  56.0 7.6 %shard_map.104 = f32[24,128,256]{2,1,0:T(8,128)} custom-call(s32[16,8]{1,0:T(8,128)} %copy.24.src_ref, bf16[16,8,128,128]{3,2,1,0:T(8,128)(2,1)} %bitcast.121, bf16[16,128,256]{2,1,0:T(8,128)(2,1)} %bitcast.132), custom_call_target="tpu_custom_call" | custom-call | tf_op jit(solution)/shard_map/pallas_call | solution.py:64
  63.5 2.1 %fusion.32 = (f32[4,128,256]{2,1,0:T(8,128)}, f32[4,128,256]{2,1,0:T(8,128)S(1)}) fusion(f32[24,128,256]{2,1,0:T(8,128)} %shard_map.104), kind=kLoop, calls=%fused_computation.69 | loop fusion | bytes 2097152 | tf_op jit(solution)/shard_map/slice | solution.py:83
  65.7 4.8 %collective-permute-start.5 = (f32[512,256]{1,0:T(8,128)}, f32[512,256]{1,0:T(8,128)}, u32[]{:S(2)}, u32[]{:S(2)}) collective-permute-start(f32[512,256]{1,0:T(8,128)} %bitcast.26), channel_id=1, source_target_pairs={{1,0},{2,1},{3,2},{4,3},{5,4},{6,5},{7,6},{8,7},{9,8},{10,9},{11,1... | collective-permute-start | bytes 1572872 | tf_op jit(solution)/shard_map/ppermute | solution.py:89
  70.5 1.2 convolution_bitcast_fusion
  71.7 1.8 convolution_add_fusion.3
  73.5 6.8 %collective-permute-done.4 = f32[512,256]{1,0:T(8,128)S(1)} collective-permute-done((f32[512,256]{1,0:T(8,128)S(1)}, f32[512,256]{1,0:T(8,128)S(1)}, u32[]{:S(2)}, u32[]{:S(2)}) %collective-permute-start.4) | collective-permute-done | bytes 524320 | tf_op jit(solution)/shard_map/ppermute | solution.py:87
  80.4 0.8 copy-done.17
  81.2 1.9 %scatter_fusion = f32[16,128,256]{2,1,0:T(8,128)S(1)} fusion(f32[16,128,256]{2,1,0:T(8,128)S(1)} %slice-done.1, s32[4]{0:T(128)S(1)} %get-tuple-element.19, f32[4,128,256]{2,1,0:T(8,128)} %bitcast.136), kind=kCustom, calls=%fused_computation.4 | custom fusion | flops 131072 | bytes 1572880 | tf_op jit(solution)/shard_map/scatter-add | solution.py:157
  83.1 1.9 %scatter_fusion.1 = f32[16,128,256]{2,1,0:T(8,128)S(1)} fusion(f32[16,128,256]{2,1,0:T(8,128)S(1)} %scatter_fusion, s32[4]{0:T(128)S(1)} %get-tuple-element.18, f32[4,128,256]{2,1,0:T(8,128)} %bitcast.27), kind=kCustom, calls=%fused_computation.5 | custom fusion | flops 131072 | bytes 1572880 | tf_op jit(solution)/shard_map/scatter-add | solution.py:160
  85.1 1.8 copy-done.9
  86.9 4.2 %multiply_convert_fusion = (bf16[2048,256]{1,0:T(8,128)(2,1)}, f32[2048,256]{1,0:T(8,128)}) fusion(f32[2048,256]{1,0:T(8,128)} %get-tuple-element.15, f32[2048,256]{1,0:T(8,128)S(1)} %copy-done.9, bf16[2048,256]{1,0:T(8,128)(2,1)S(1)} %bitcast.133, bf16[2,256,256]{2,1,0:T(8,128)(2,1)S(1)} %copy-done.15), kind=kOutput, calls=%fused_computation.19 | convolution fusion | flops 273678336 | bytes 8519680 | tf_op jit(solution)/shard_map/dot_general | solution.py:169
  91.1 7.6 %shard_map.105 = f32[24,128,256]{2,1,0:T(8,128)} custom-call(s32[16,8]{1,0:T(8,128)} %copy.24.src_ref, bf16[16,8,128,128]{3,2,1,0:T(8,128)(2,1)} %bitcast.122, bf16[16,128,256]{2,1,0:T(8,128)(2,1)} %bitcast.123), custom_call_target="tpu_custom_call" | custom-call | tf_op jit(solution)/shard_map/pallas_call | solution.py:64
  98.7 2.1 %fusion.31 = (f32[4,128,256]{2,1,0:T(8,128)}, f32[4,128,256]{2,1,0:T(8,128)S(1)}) fusion(f32[24,128,256]{2,1,0:T(8,128)} %shard_map.105), kind=kLoop, calls=%fused_computation.68 | loop fusion | bytes 2097152 | tf_op jit(solution)/shard_map/slice | solution.py:83
  100.8 4.8 %collective-permute-start.7 = (f32[512,256]{1,0:T(8,128)}, f32[512,256]{1,0:T(8,128)}, u32[]{:S(2)}, u32[]{:S(2)}) collective-permute-start(f32[512,256]{1,0:T(8,128)} %bitcast.32), channel_id=1, source_target_pairs={{1,0},{2,1},{3,2},{4,3},{5,4},{6,5},{7,6},{8,7},{9,8},{10,9},{11,1... | collective-permute-start | bytes 1572872 | tf_op jit(solution)/shard_map/ppermute | solution.py:89
  106.1 0.8 maximum_bitcast_fusion.1
  107.0 1.2 convolution_bitcast_fusion.2
  108.2 6.5 %collective-permute-done.6 = f32[512,256]{1,0:T(8,128)S(1)} collective-permute-done((f32[512,256]{1,0:T(8,128)S(1)}, f32[512,256]{1,0:T(8,128)S(1)}, u32[]{:S(2)}, u32[]{:S(2)}) %collective-permute-start.6) | collective-permute-done | bytes 524320 | tf_op jit(solution)/shard_map/ppermute | solution.py:87
  114.7 0.8 copy-done.16
  115.5 1.9 %scatter_fusion.2 = f32[16,128,256]{2,1,0:T(8,128)S(1)} fusion(f32[16,128,256]{2,1,0:T(8,128)S(1)} %slice-done, s32[4]{0:T(128)S(1)} %get-tuple-element.19, f32[4,128,256]{2,1,0:T(8,128)} %bitcast.135), kind=kCustom, calls=%fused_computation.6 | custom fusion | flops 131072 | bytes 1572880 | tf_op jit(solution)/shard_map/scatter-add | solution.py:157
  117.4 1.9 %scatter_fusion.3 = f32[16,128,256]{2,1,0:T(8,128)S(1)} fusion(f32[16,128,256]{2,1,0:T(8,128)S(1)} %scatter_fusion.2, s32[4]{0:T(128)S(1)} %get-tuple-element.18, f32[4,128,256]{2,1,0:T(8,128)} %bitcast.33), kind=kCustom, calls=%fused_computation.7 | custom fusion | flops 131072 | bytes 1572880 | tf_op jit(solution)/shard_map/scatter-add | solution.py:160
  121.3 1.1 all_to_all.13
  122.3 28.6 %all_to_all.16 = f32[128,1,2048]{2,1,0:T(1,128)S(1)} all-to-all(f32[128,1,2048]{2,1,0:T(1,128)S(1)} %all_to_all.13), channel_id=1, replica_groups=mesh['dp'=8,'sector'=16] {'dp','sector'}, dimensions={0} | all-to-all | bytes 2097152 | tf_op jit(solution)/shard_map/all_to_all | solution.py:99
  151.0 0.6 reduce_sum.9
  151.6 1.5 broadcast_in_dim.8
  153.1 4.5 %all-to-all-start.1 = ((f32[128,1,2048]{2,1,0:T(1,128)}), f32[128,1,2048]{2,1,0:T(1,128)S(1)}, u32[]{:S(2)}, u32[]{:S(2)}) async-start(f32[128,1,2048]{2,1,0:T(1,128)} %broadcast_in_dim.8), calls=%async_computation.1 | async-start | bytes 2097152 | tf_op jit(solution)/shard_map/all_to_all | solution.py:101
  157.7 2.1 %convolution_add_fusion.1 = f32[2048,256]{1,0:T(8,128)S(1)} fusion(f32[2048,256]{1,0:T(8,128)} %get-tuple-element.17, bf16[2048,256]{1,0:T(8,128)(2,1)S(1)} %copy-done.2, bf16[2,256,256]{2,1,0:T(8,128)(2,1)S(1)} %copy-done.22), kind=kOutput, calls=%fused_computation.10 | convolution fusion | flops 268959744 | bytes 5373952 | tf_op jit(solution)/shard_map/dot_general | solution.py:168
  159.9 1.8 fusion
  161.6 15.1 %all-to-all-done.1 = f32[128,1,2048]{2,1,0:T(1,128)S(1)} async-done(((f32[128,1,2048]{2,1,0:T(1,128)}), f32[128,1,2048]{2,1,0:T(1,128)S(1)}, u32[]{:S(2)}, u32[]{:S(2)}) %all-to-all-start.1) | async-done | bytes 1048608 | tf_op jit(solution)/shard_map/all_to_all | solution.py:101
  176.8 2.9 %fusion.10 = (f32[64,2048]{1,0:T(8,128)S(1)}, f32[64,2048]{1,0:T(8,128)S(1)}) fusion(f32[128,1,2048]{2,1,0:T(1,128)S(1)} %all-to-all-done.1), kind=kLoop, calls=%fused_computation.38 | loop fusion | flops 262144 | bytes 2097152 | tf_op jit(solution)/shard_map/mul | solution.py:178
  179.6 0.9 mul.48
  180.5 0.9 mul.46
  (68 shorter events, 3.8 us)
Async XLA Ops:
  0.6 10.9 %copy-start.23 = (s32[1,16,8]{1,2,0:T(8,128)S(1)}, s32[1,16,8]{1,2,0:T(8,128)}, u32[]{:S(2)}) copy-start(s32[1,16,8]{1,2,0:T(8,128)} %param.9) | copy-start | bytes 1540
  3.8 13.1 %collective-permute-start = (bf16[512,256]{1,0:T(8,128)(2,1)S(1)}, bf16[512,256]{1,0:T(8,128)(2,1)S(1)}, u32[]{:S(2)}, u32[]{:S(2)}) collective-permute-start(bf16[512,256]{1,0:T(8,128)(2,1)S(1)} %bitcast.144), channel_id=1, source_target_pairs={{0,1},{1,2},{2,3},{3,4},{4,5},{5,6},{6,7},{7,8},{8,9},{9,10},{10,1... | collective-permute-start | bytes 786440 | tf_op jit(solution)/shard_map/ppermute | solution.py:87
  6.9 10.0 %collective-permute-start.1 = (bf16[512,256]{1,0:T(8,128)(2,1)S(1)}, bf16[512,256]{1,0:T(8,128)(2,1)S(1)}, u32[]{:S(2)}, u32[]{:S(2)}) collective-permute-start(bf16[512,256]{1,0:T(8,128)(2,1)S(1)} %bitcast.145), channel_id=1, source_target_pairs={{1,0},{2,1},{3,2},{4,3},{5,4},{6,5},{7,6},{8,7},{9,8},{10,9},{11,1... | collective-permute-start | bytes 786440 | tf_op jit(solution)/shard_map/ppermute | solution.py:89
  18.3 7.1 %copy-start = (bf16[1,2048,256]{2,1,0:T(8,128)(2,1)S(1)}, bf16[1,2048,256]{2,1,0:T(8,128)(2,1)}, u32[]{:S(2)}) copy-start(bf16[1,2048,256]{2,1,0:T(8,128)(2,1)} %param.7) | copy-start | bytes 3145732
  18.3 7.1 %copy-start.20 = (bf16[2,256,256]{2,1,0:T(8,128)(2,1)S(1)}, bf16[2,256,256]{2,1,0:T(8,128)(2,1)}, u32[]{:S(2)}) copy-start(bf16[2,256,256]{2,1,0:T(8,128)(2,1)} %param.12) | copy-start | bytes 786436
  25.4 3.8 %copy-start.15 = (bf16[2,256,256]{2,1,0:T(8,128)(2,1)S(1)}, bf16[2,256,256]{2,1,0:T(8,128)(2,1)}, u32[]{:S(2)}) copy-start(bf16[2,256,256]{2,1,0:T(8,128)(2,1)} %param.11) | copy-start | bytes 786436
  29.1 13.5 %copy-start.12 = (bf16[2048,256]{1,0:T(8,128)(2,1)}, bf16[2048,256]{1,0:T(8,128)(2,1)S(1)}, u32[]{:S(2)}) copy-start(bf16[2048,256]{1,0:T(8,128)(2,1)S(1)} %get-tuple-element.14) | copy-start | bytes 3145732
  32.1 10.5 %collective-permute-start.2 = (bf16[512,256]{1,0:T(8,128)(2,1)}, bf16[512,256]{1,0:T(8,128)(2,1)S(1)}, u32[]{:S(2)}, u32[]{:S(2)}) collective-permute-start(bf16[512,256]{1,0:T(8,128)(2,1)} %bitcast.146), channel_id=1, source_target_pairs={{0,1},{1,2},{2,3},{3,4},{4,5},{5,6},{6,7},{7,8},{8,9},{9,10},{10,1... | collective-permute-start | bytes 786440 | tf_op jit(solution)/shard_map/ppermute | solution.py:87
  32.1 10.5 %collective-permute-start.3 = (bf16[512,256]{1,0:T(8,128)(2,1)}, bf16[512,256]{1,0:T(8,128)(2,1)S(1)}, u32[]{:S(2)}, u32[]{:S(2)}) collective-permute-start(bf16[512,256]{1,0:T(8,128)(2,1)} %bitcast.143), channel_id=1, source_target_pairs={{1,0},{2,1},{3,2},{4,3},{5,4},{6,5},{7,6},{8,7},{9,8},{10,9},{11,1... | collective-permute-start | bytes 786440 | tf_op jit(solution)/shard_map/ppermute | solution.py:89
  44.0 7.1 %copy-start.7 = (f32[1,2048,256]{2,1,0:T(8,128)S(1)}, f32[1,2048,256]{2,1,0:T(8,128)}, u32[]{:S(2)}) copy-start(f32[1,2048,256]{2,1,0:T(8,128)} %param.13) | copy-start | bytes 6291460
  65.6 4.9 %copy-start.5 = (bf16[2048,256]{1,0:T(8,128)(2,1)S(1)}, bf16[2048,256]{1,0:T(8,128)(2,1)}, u32[]{:S(2)}) copy-start(bf16[2048,256]{1,0:T(8,128)(2,1)} %get-tuple-element.8) | copy-start | bytes 3145732
  65.6 4.9 %copy-start.13 = (bf16[2048,256]{1,0:T(8,128)(2,1)S(1)}, bf16[2048,256]{1,0:T(8,128)(2,1)}, u32[]{:S(2)}) copy-start(bf16[2048,256]{1,0:T(8,128)(2,1)} %copy-done.12) | copy-start | bytes 3145732
  65.6 6.1 %copy-start.8 = (f32[1,2048,256]{2,1,0:T(8,128)S(1)}, f32[1,2048,256]{2,1,0:T(8,128)}, u32[]{:S(2)}) copy-start(f32[1,2048,256]{2,1,0:T(8,128)} %param.13) | copy-start | bytes 6291460
  65.6 6.1 %copy-start.21 = (bf16[2,256,256]{2,1,0:T(8,128)(2,1)S(1)}, bf16[2,256,256]{2,1,0:T(8,128)(2,1)}, u32[]{:S(2)}) copy-start(bf16[2,256,256]{2,1,0:T(8,128)(2,1)} %param.12) | copy-start | bytes 786436
  65.6 14.8 %collective-permute-start.4 = (f32[512,256]{1,0:T(8,128)S(1)}, f32[512,256]{1,0:T(8,128)S(1)}, u32[]{:S(2)}, u32[]{:S(2)}) collective-permute-start(f32[512,256]{1,0:T(8,128)S(1)} %bitcast.138), channel_id=1, source_target_pairs={{0,1},{1,2},{2,3},{3,4},{4,5},{5,6},{6,7},{7,8},{8,9},{9,10},{10,1... | collective-permute-start | bytes 1572872 | tf_op jit(solution)/shard_map/ppermute | solution.py:87
  65.7 17.4 %collective-permute-start.5 = (f32[512,256]{1,0:T(8,128)}, f32[512,256]{1,0:T(8,128)}, u32[]{:S(2)}, u32[]{:S(2)}) collective-permute-start(f32[512,256]{1,0:T(8,128)} %bitcast.26), channel_id=1, source_target_pairs={{1,0},{2,1},{3,2},{4,3},{5,4},{6,5},{7,6},{8,7},{9,8},{10,9},{11,1... | collective-permute-start | bytes 1572872 | tf_op jit(solution)/shard_map/ppermute | solution.py:89
  71.7 9.5 %slice-start.1 = ((f32[24,128,256]{2,1,0:T(8,128)}), f32[16,128,256]{2,1,0:T(8,128)S(1)}, s32[]{:S(2)}) async-start(f32[24,128,256]{2,1,0:T(8,128)} %shard_map.104), calls=%async_computation.3 | async-start | bytes 4194304 | tf_op jit(solution)/shard_map/slice | solution.py:156
  80.4 0.8 copy-start.17
  84.9 2.0 %copy-start.9 = (f32[2048,256]{1,0:T(8,128)S(1)}, f32[2048,256]{1,0:T(8,128)}, u32[]{:S(2)}) copy-start(f32[2048,256]{1,0:T(8,128)} %convolution_add_fusion.3) | copy-start | bytes 6291460
  85.1 6.1 %copy-start.10 = (bf16[16,128,256]{2,1,0:T(8,128)(2,1)}, bf16[16,128,256]{2,1,0:T(8,128)(2,1)S(1)}, u32[]{:S(2)}) copy-start(bf16[16,128,256]{2,1,0:T(8,128)(2,1)S(1)} %convert_element_type.45) | copy-start | bytes 3145732
  100.8 4.9 %copy-start.1 = (bf16[2048,256]{1,0:T(8,128)(2,1)S(1)}, bf16[2048,256]{1,0:T(8,128)(2,1)}, u32[]{:S(2)}) copy-start(bf16[2048,256]{1,0:T(8,128)(2,1)} %get-tuple-element.16) | copy-start | bytes 3145732
  100.8 5.4 %copy-start.18 = (f32[1,256,256]{1,2,0:T(8,128)S(1)}, f32[1,256,256]{1,2,0:T(8,128)}, u32[]{:S(2)}) copy-start(f32[1,256,256]{1,2,0:T(8,128)} %convolution_bitcast_fusion) | copy-start | bytes 786436
  100.8 6.2 %copy-start.11 = (bf16[16,128,256]{2,1,0:T(8,128)(2,1)S(1)}, bf16[16,128,256]{2,1,0:T(8,128)(2,1)}, u32[]{:S(2)}) copy-start(bf16[16,128,256]{2,1,0:T(8,128)(2,1)} %copy-done.10) | copy-start | bytes 3145732
  100.8 6.2 %copy-start.14 = (bf16[2048,256]{1,0:T(8,128)(2,1)S(1)}, bf16[2048,256]{1,0:T(8,128)(2,1)}, u32[]{:S(2)}) copy-start(bf16[2048,256]{1,0:T(8,128)(2,1)} %copy-done.12) | copy-start | bytes 3145732
  100.8 13.9 %collective-permute-start.6 = (f32[512,256]{1,0:T(8,128)S(1)}, f32[512,256]{1,0:T(8,128)S(1)}, u32[]{:S(2)}, u32[]{:S(2)}) collective-permute-start(f32[512,256]{1,0:T(8,128)S(1)} %bitcast.137), channel_id=1, source_target_pairs={{0,1},{1,2},{2,3},{3,4},{4,5},{5,6},{6,7},{7,8},{8,9},{9,10},{10,1... | collective-permute-start | bytes 1572872 | tf_op jit(solution)/shard_map/ppermute | solution.py:87
  100.8 16.5 %collective-permute-start.7 = (f32[512,256]{1,0:T(8,128)}, f32[512,256]{1,0:T(8,128)}, u32[]{:S(2)}, u32[]{:S(2)}) collective-permute-start(f32[512,256]{1,0:T(8,128)} %bitcast.32), channel_id=1, source_target_pairs={{1,0},{2,1},{3,2},{4,3},{5,4},{6,5},{7,6},{8,7},{9,8},{10,9},{11,1... | collective-permute-start | bytes 1572872 | tf_op jit(solution)/shard_map/ppermute | solution.py:89
  106.1 9.3 %slice-start = ((f32[24,128,256]{2,1,0:T(8,128)}), f32[16,128,256]{2,1,0:T(8,128)S(1)}, s32[]{:S(2)}) async-start(f32[24,128,256]{2,1,0:T(8,128)} %shard_map.105), calls=%async_computation.2 | async-start | bytes 4194304 | tf_op jit(solution)/shard_map/slice | solution.py:156
  114.7 0.8 copy-start.16
  119.2 1.1 copy-start.19
  119.4 1.0 copy-start.3
  119.4 1.4 copy-start.6
  151.0 6.7 %copy-start.2 = (bf16[2048,256]{1,0:T(8,128)(2,1)S(1)}, bf16[2048,256]{1,0:T(8,128)(2,1)}, u32[]{:S(2)}) copy-start(bf16[2048,256]{1,0:T(8,128)(2,1)} %get-tuple-element.16) | copy-start | bytes 3145732
  151.0 6.7 %copy-start.22 = (bf16[2,256,256]{2,1,0:T(8,128)(2,1)S(1)}, bf16[2,256,256]{2,1,0:T(8,128)(2,1)}, u32[]{:S(2)}) copy-start(bf16[2,256,256]{2,1,0:T(8,128)(2,1)} %param.12) | copy-start | bytes 786436
  153.1 23.7 %all-to-all-start.1 = ((f32[128,1,2048]{2,1,0:T(1,128)}), f32[128,1,2048]{2,1,0:T(1,128)S(1)}, u32[]{:S(2)}, u32[]{:S(2)}) async-start(f32[128,1,2048]{2,1,0:T(1,128)} %broadcast_in_dim.8), calls=%async_computation.1 | async-start | bytes 2097152 | tf_op jit(solution)/shard_map/all_to_all | solution.py:101
  157.7 2.2 %copy-start.4 = (bf16[16,128,256]{2,1,0:T(8,128)(2,1)S(1)}, bf16[16,128,256]{2,1,0:T(8,128)(2,1)}, u32[]{:S(2)}) copy-start(bf16[16,128,256]{2,1,0:T(8,128)(2,1)} %copy-done.3) | copy-start | bytes 3145732
where the time goes:
time: 182 us; the launch traced here: 181 us
  waiting for transfers between devices  38.5 us (21%)
  Pallas kernels  29.2 us (16%)
  blocking collectives  28.6 us (16%)
  starting transfers between devices  26.6 us (15%)
  matrix products  24.1 us (13%)
  local copies, waits for them, and re-layouts  18.4 us (10%)
  other arithmetic  14.9 us (8%)
    all_to_all x1, blocking collectives, all_reduce(): mine = lax.all_to_all(pieces, axes, 0, 0, tiled=True).sum(0)  28.6 us
    ppermute x4, waiting for transfers between devices, extended_2(): lax.ppermute(tail, axis, [(i, (i + 1) % count) for i in range(count)])  23.4 us
    ppermute x4, starting transfers between devices, extended_2(): lax.ppermute(head, axis, [((i + 1) % count, i) for i in range(count)])  19.4 us
    all_to_all x1, waiting for transfers between devices, all_reduce(): return lax.all_to_all(spread, axes, 0, 0, tiled=True).reshape(x.shape)  15.1 us
    pallas_call x2, Pallas kernels, block_slot_grad(): pl.pallas_call(slot_grad_kernel, grid_spec=pltpu.PrefetchScalarGridSpec(n...  15.1 us
    pallas_call x2, Pallas kernels, block_aggregate(): pl.pallas_call(aggregate_kernel, grid_spec=pltpu.PrefetchScalarGridSpec(n...  14.1 us
    dot_general x2, matrix products, per_device(): jnp.dot(current, w_self[layer_index], preferred_element_type=jnp.float32)  8.65 us
    dot_general x2, matrix products, per_device(): jnp.dot(dmessage, w_message[layer_index].T, preferred_element_type=jnp.fl...  6.01 us
  transfers between devices with their start and end apart: 9, of which 5 were waited for; matrix products, arithmetic and copies ran while one was open for 8% of the time, Pallas kernels for 0%

commit v1 on v0

--- a/solution.py
+++ b/solution.py
@@ -6,7 +6,7 @@
 from jax.sharding import PartitionSpec as P
 
 LAYERS = 2
-GROUP = 4
+GROUP = 8
 
 
 def aggregate_kernel(src_ref, tiles_ref, table_ref, out_ref):
@@ -77,20 +77,45 @@
     )(slot_ids, tile_data, dpre_blocks)
 
 
-def extended_2(cells, sides, width):
-    for axis, dim in sides:
-        count = lax.axis_size(axis)
-        head = lax.slice_in_dim(cells, 0, width, axis=dim)
-        tail = lax.slice_in_dim(cells, cells.shape[dim] - width, cells.shape[dim], axis=dim)
-        cells = jnp.concatenate(
-            [
-                lax.ppermute(tail, axis, [(i, (i + 1) % count) for i in range(count)]),
-                cells,
-                lax.ppermute(head, axis, [((i + 1) % count, i) for i in range(count)]),
+def fold_kernel(lists_ref, slot_ref, lower_ref, upper_ref, out_ref, acc_ref):
+    acc_ref[...] = slot_ref[...]
+    for i in range(lower_ref.shape[0]):
+        block = lists_ref[1, i]
+        acc_ref[block] += lower_ref[i]
+    for i in range(upper_ref.shape[0]):
+        block = lists_ref[0, i]
+        acc_ref[block] += upper_ref[i]
+    out_ref[...] = acc_ref[...].astype(out_ref.dtype)
+
+
+def fold_lent(own_lists, slot_grad, from_lower, from_upper, blocks):
+    _, rows, width = slot_grad.shape
+    lent = from_lower.shape[0]
+    return pl.pallas_call(
+        fold_kernel,
+        grid_spec=pltpu.PrefetchScalarGridSpec(
+            num_scalar_prefetch=1,
+            grid=(1,),
+            in_specs=[
+                pl.BlockSpec((blocks, rows, width), lambda g, lists: (0, 0, 0)),
+                pl.BlockSpec((lent, rows, width), lambda g, lists: (0, 0, 0)),
+                pl.BlockSpec((lent, rows, width), lambda g, lists: (0, 0, 0)),
             ],
-            axis=dim,
-        )
-    return cells
+            out_specs=pl.BlockSpec((blocks, rows, width), lambda g, lists: (0, 0, 0)),
+            scratch_shapes=[pltpu.VMEM((blocks, rows, width), jnp.float32)],
+        ),
+        out_shape=jax.ShapeDtypeStruct((blocks, rows, width), jnp.bfloat16),
+    )(own_lists, slot_grad, from_lower, from_upper)
+
+
+def to_upper(x, axis):
+    count = lax.axis_size(axis)
+    return lax.ppermute(x, axis, [(i, (i + 1) % count) for i in range(count)])
+
+
+def to_lower(x, axis):
+    count = lax.axis_size(axis)
+    return lax.ppermute(x, axis, [((i + 1) % count, i) for i in range(count)])
 
 
 def all_reduce(x, axes):
@@ -125,17 +150,9 @@
             current, w_message[layer_index], preferred_element_type=jnp.float32
         ).astype(jnp.bfloat16)
         message_blocks = message.reshape(blocks_here, tile_rows, width)
-        packet = jnp.concatenate(
-            [message_blocks[own_lists[1]], message_blocks[own_lists[0]]]
-        ).reshape(2 * lent * tile_rows, width)
-        extended = extended_2(packet, (("sector", 0),), lent * tile_rows)
-        table = jnp.concatenate(
-            [
-                message_blocks,
-                extended[: lent * tile_rows].reshape(lent, tile_rows, width),
-                extended[-lent * tile_rows :].reshape(lent, tile_rows, width),
-            ]
-        )
+        from_lower = to_upper(message_blocks[own_lists[0]], "sector")
+        from_upper = to_lower(message_blocks[own_lists[1]], "sector")
+        table = jnp.concatenate([message_blocks, from_lower, from_upper])
         aggregate = block_aggregate(slot_ids, tile_data, table)
         pre = aggregate.reshape(-1, width) + jnp.dot(
             current, w_self[layer_index], preferred_element_type=jnp.float32
@@ -151,16 +168,11 @@
         slot_grad = block_slot_grad(
             slot_ids, tile_data, dpre.reshape(blocks_here, tile_rows, width), slot_count
         )
-        packet = slot_grad[blocks_here:].reshape(2 * lent * tile_rows, width)
-        extended = extended_2(packet, (("sector", 0),), lent * tile_rows)
-        dblocks = slot_grad[:blocks_here].reshape(blocks_here, tile_rows, width)
-        dblocks = dblocks.at[own_lists[1]].add(
-            extended[: lent * tile_rows].reshape(lent, tile_rows, width)
-        )
-        dblocks = dblocks.at[own_lists[0]].add(
-            extended[-lent * tile_rows :].reshape(lent, tile_rows, width)
-        )
-        dmessage = dblocks.reshape(-1, width).astype(jnp.bfloat16)
+        lent_down_grad = to_upper(slot_grad[blocks_here + lent :], "sector")
+        lent_up_grad = to_lower(slot_grad[blocks_here : blocks_here + lent], "sector")
+        dmessage = fold_lent(
+            own_lists, slot_grad, lent_down_grad, lent_up_grad, blocks_here
+        ).reshape(-1, width)
         self_part = jnp.dot(layer_in.T, dpre, preferred_element_type=jnp.float32)
         message_part = jnp.dot(layer_in.T, dmessage, preferred_element_type=jnp.float32)
         message_steps[layer_index] = message_part

time: 182 us -> 179 us (0.984)
  other arithmetic: 14.9 us -> 6.38 us
  waiting for transfers between devices: 38.5 us -> 44.8 us
  Pallas kernels: 29.2 us -> 34.5 us
  starting transfers between devices: 26.6 us -> 23.2 us
  local copies, waits for them, and re-layouts: 18.4 us -> 15.8 us
    pallas_call x0 -> x2, Pallas kernels: none -> 7.7 us  [fold_lent(): pl.pallas_call(fold_kernel, grid_spec=pltpu.PrefetchScalarGridSpec(num_sc...]
    scatter-add x4 -> x0, other arithmetic: 7.5 us -> none  [the longest x2 3.75 us: per_device(): dblocks.at[own_lists[0]]]
    ppermute x8, waiting for transfers between devices: 23.4 us -> 29.6 us  [the longest x4 17.1 us: to_upper(): return lax.ppermute(x, axis, [(i, (i + 1) % count) for i in range(count)])]
    ppermute x8, starting transfers between devices: 22 us -> 18.7 us  [the longest x4 15.6 us: to_lower(): return lax.ppermute(x, axis, [((i + 1) % count, i) for i in range(count)])]
    unnamed x48 -> x40, local copies, waits for them, and re-layouts: 4.38 us -> 2.65 us
    slice x7 -> x3, local copies, waits for them, and re-layouts: 5.04 us -> 3.76 us  [the longest x2 2.85 us: per_device(): lent_up_grad = to_lower(slot_grad[blocks_here:blocks_here + lent], 'sector')]
  transfers between devices with their start and end apart: 9 -> 9, of which waited for: 5 -> 7; matrix products, arithmetic and copies ran while one was open for 8% -> 6% of each run, Pallas kernels for 0% -> 0%
where the time goes in v1:
time: 179 us
  waiting for transfers between devices  44.8 us (25%)
  Pallas kernels  34.5 us (19%)
  blocking collectives  27.7 us (15%)
  matrix products  25.6 us (14%)
  starting transfers between devices  23.2 us (13%)
  local copies, waits for them, and re-layouts  15.8 us (9%)
  other arithmetic  6.38 us (4%)
    all_to_all x1, blocking collectives, all_reduce(): mine = lax.all_to_all(pieces, axes, 0, 0, tiled=True).sum(0)  27.7 us
    ppermute x4, waiting for transfers between devices, to_upper(): return lax.ppermute(x, axis, [(i, (i + 1) % count) for i in range(count)])  17.1 us
    ppermute x4, starting transfers between devices, to_lower(): return lax.ppermute(x, axis, [((i + 1) % count, i) for i in range(count)])  15.6 us
    all_to_all x1, waiting for transfers between devices, all_reduce(): return lax.all_to_all(spread, axes, 0, 0, tiled=True).reshape(x.shape)  15.1 us
    pallas_call x2, Pallas kernels, block_slot_grad(): pl.pallas_call(slot_grad_kernel, grid_spec=pltpu.PrefetchScalarGridSpec(n...  13.9 us
    pallas_call x2, Pallas kernels, block_aggregate(): pl.pallas_call(aggregate_kernel, grid_spec=pltpu.PrefetchScalarGridSpec(n...  12.9 us
    ppermute x4, waiting for transfers between devices, to_lower(): return lax.ppermute(x, axis, [((i + 1) % count, i) for i in range(count)])  12.5 us
    dot_general x2, matrix products, per_device(): jnp.dot(current, w_self[layer_index], preferred_element_type=jnp.float32)  8.64 us
  transfers between devices with their start and end apart: 9, of which 7 were waited for; matrix products, arithmetic and copies ran while one was open for 6% of the time, Pallas kernels for 0%

profile of v1, /device:TPU:1, one launch (start us, length us, event | category | flops | bytes accessed | tf_op | source)
XLA Modules:
  0.0 178.9 jit_solution(15588744107553080446)
XLA Ops:
  0.6 0.9 dynamic-slice_reduce_fusion.2
  1.6 1.7 convolution_convert_fusion.1
  3.3 0.6 gather_fusion
  3.8 2.5 %collective-permute-start = (bf16[4,128,256]{2,1,0:T(8,128)(2,1)S(1)}, bf16[4,128,256]{2,1,0:T(8,128)(2,1)S(1)}, u32[]{:S(2)}, u32[]{:S(2)}) collective-permute-start(bf16[4,128,256]{2,1,0:T(8,128)(2,1)S(1)} %gather_fusion), channel_id=1, source_target_pairs={{0,1},{1,2},{2,3},{3,4},{4,5},{5,6},{6,7},{7,8},{8,9},{9,10},{10,1... | collective-permute-start | bytes 786440 | tf_op jit(solution)/shard_map/ppermute | solution.py:113
  6.9 4.7 %collective-permute-start.1 = (bf16[4,128,256]{2,1,0:T(8,128)(2,1)S(1)}, bf16[4,128,256]{2,1,0:T(8,128)(2,1)S(1)}, u32[]{:S(2)}, u32[]{:S(2)}) collective-permute-start(bf16[4,128,256]{2,1,0:T(8,128)(2,1)S(1)} %gather_fusion.1), channel_id=1, source_target_pairs={{1,0},{2,1},{3,2},{4,3},{5,4},{6,5},{7,6},{8,7},{9,8},{10,9},{11,1... | collective-permute-start | bytes 786440 | tf_op jit(solution)/shard_map/ppermute | solution.py:118
  11.6 0.7 copy.24.src_ref
  12.2 4.7 %collective-permute-done = bf16[4,128,256]{2,1,0:T(8,128)(2,1)S(1)} collective-permute-done((bf16[4,128,256]{2,1,0:T(8,128)(2,1)S(1)}, bf16[4,128,256]{2,1,0:T(8,128)(2,1)S(1)}, u32[]{:S(2)}, u32[]{:S(2)}) %collective-permute-start) | collective-permute-done | bytes 262176 | tf_op jit(solution)/shard_map/ppermute | solution.py:113
  16.9 1.4 pad_maximum_fusion.table_ref
  18.3 6.4 %shard_map.102 = f32[16,128,256]{2,1,0:T(8,128)} custom-call(s32[16,8]{1,0:T(8,128)} %copy.24.src_ref, bf16[16,8,128,128]{3,2,1,0:T(8,128)(2,1)} %bitcast.103, bf16[24,128,256]{2,1,0:T(8,128)(2,1)} %pad_maximum_fusion.table_ref), custom_call_target="tpu_custom_call" | custom-call | tf_op jit(solution)/shard_map/pallas_call | solution.py:27
  24.7 3.8 %add_convert_fusion.1 = (bf16[2048,256]{1,0:T(8,128)(2,1)S(1)}, f32[2048,256]{1,0:T(8,128)}) fusion(bf16[1,2048,256]{2,1,0:T(8,128)(2,1)S(1)} %copy-done, bf16[2,256,256]{2,1,0:T(8,128)(2,1)S(1)} %copy-done.15, f32[16,128,256]{2,1,0:T(8,128)} %shard_map.102), kind=kOutput, calls=%fused_computation.18 | convolution fusion | flops 272629760 | bytes 7471104 | tf_op jit(solution)/shard_map/dot_general | solution.py:157
  28.5 1.0 copy-done.6
  29.9 0.6 gather_fusion.3
  31.2 5.2 %collective-permute-start.3 = (bf16[4,128,256]{2,1,0:T(8,128)(2,1)S(1)}, bf16[4,128,256]{2,1,0:T(8,128)(2,1)S(1)}, u32[]{:S(2)}, u32[]{:S(2)}) collective-permute-start(bf16[4,128,256]{2,1,0:T(8,128)(2,1)S(1)} %gather_fusion.3), channel_id=1, source_target_pairs={{1,0},{2,1},{3,2},{4,3},{5,4},{6,5},{7,6},{8,7},{9,8},{10,9},{11,1... | collective-permute-start | bytes 786440 | tf_op jit(solution)/shard_map/ppermute | solution.py:118
  36.4 0.8 dynamic-slice_reduce_fusion.lists_ref
  37.2 4.3 %collective-permute-done.2 = bf16[4,128,256]{2,1,0:T(8,128)(2,1)S(1)} collective-permute-done((bf16[4,128,256]{2,1,0:T(8,128)(2,1)S(1)}, bf16[4,128,256]{2,1,0:T(8,128)(2,1)S(1)}, u32[]{:S(2)}, u32[]{:S(2)}) %collective-permute-start.2) | collective-permute-done | bytes 262176 | tf_op jit(solution)/shard_map/ppermute | solution.py:113
  41.5 1.4 pad_maximum_fusion.1.table_ref
  42.8 6.4 %shard_map.103 = f32[16,128,256]{2,1,0:T(8,128)} custom-call(s32[16,8]{1,0:T(8,128)} %copy.24.src_ref, bf16[16,8,128,128]{3,2,1,0:T(8,128)(2,1)} %bitcast.104, bf16[24,128,256]{2,1,0:T(8,128)(2,1)} %pad_maximum_fusion.1.table_ref), custom_call_target="tpu_custom_call" | custom-call | tf_op jit(solution)/shard_map/pallas_call | solution.py:27
  49.3 4.9 %fusion.1 = (bf16[2048,256]{1,0:T(8,128)(2,1)}, bf16[1,2048,256]{2,1,0:T(8,128)(2,1)}) fusion(f32[1,2048,256]{2,1,0:T(8,128)S(1)} %copy-done.4, f32[16,128,256]{2,1,0:T(8,128)} %shard_map.103, bf16[2048,256]{1,0:T(8,128)(2,1)} %copy-done.6, bf16[2,256,256]{2,1,0:T(8,128)(2,1)} %param.12), kind=kOutput, calls=%fused_computation.12 | convolution fusion | flops 275775488 | bytes 8519680 | tf_op jit(solution)/shard_map/dot_general | solution.py:157
  54.2 7.0 %shard_map.104.slot_ref = f32[24,128,256]{2,1,0:T(8,128)} custom-call(s32[16,8]{1,0:T(8,128)} %copy.24.src_ref, bf16[16,8,128,128]{3,2,1,0:T(8,128)(2,1)} %bitcast.105, bf16[16,128,256]{2,1,0:T(8,128)(2,1)} %bitcast.116), custom_call_target="tpu_custom_call" | custom-call | tf_op jit(solution)/shard_map/pallas_call | solution.py:64
  61.1 1.5 fusion.32
  62.6 4.6 %collective-permute-start.5 = (f32[4,128,256]{2,1,0:T(8,128)S(1)}, f32[4,128,256]{2,1,0:T(8,128)S(1)}, u32[]{:S(2)}, u32[]{:S(2)}) collective-permute-start(f32[4,128,256]{2,1,0:T(8,128)S(1)} %get-tuple-element.12), channel_id=1, source_target_pairs={{1,0},{2,1},{3,2},{4,3},{5,4},{6,5},{7,6},{8,7},{9,8},{10,9},{11,1... | collective-permute-start | bytes 1572872 | tf_op jit(solution)/shard_map/ppermute | solution.py:118
  67.2 1.2 convolution_bitcast_fusion
  68.5 1.8 convolution_add_fusion.3
  70.3 5.9 %collective-permute-done.5.upper_ref = f32[4,128,256]{2,1,0:T(8,128)S(1)} collective-permute-done((f32[4,128,256]{2,1,0:T(8,128)S(1)}, f32[4,128,256]{2,1,0:T(8,128)S(1)}, u32[]{:S(2)}, u32[]{:S(2)}) %collective-permute-start.5) | collective-permute-done | bytes 524320 | tf_op jit(solution)/shard_map/ppermute | solution.py:118
  76.1 0.8 copy-done.12
  76.9 4.6 %collective-permute-done.4.lower_ref = f32[4,128,256]{2,1,0:T(8,128)} collective-permute-done((f32[4,128,256]{2,1,0:T(8,128)S(1)}, f32[4,128,256]{2,1,0:T(8,128)}, u32[]{:S(2)}, u32[]{:S(2)}) %collective-permute-start.4) | collective-permute-done | bytes 524320 | tf_op jit(solution)/shard_map/ppermute | solution.py:113
  81.5 3.8 %shard_map.105 = bf16[16,128,256]{2,1,0:T(8,128)(2,1)} custom-call(s32[2,4]{1,0:T(2,128)} %dynamic-slice_reduce_fusion.lists_ref, f32[24,128,256]{2,1,0:T(8,128)} %shard_map.104.slot_ref, f32[4,128,256]{2,1,0:T(8,128)} %collective-permute-done.4.lower_ref, f32[4,128,256]{2,1,0:T(8,128)} %copy-done.12), custom_call_target="tpu_custom_call" | custom-call | tf_op jit(solution)/shard_map/pallas_call | solution.py:94
  85.3 4.5 %multiply_convert_fusion = (bf16[2048,256]{1,0:T(8,128)(2,1)}, f32[2048,256]{1,0:T(8,128)}) fusion(f32[2048,256]{1,0:T(8,128)} %get-tuple-element.15, f32[2048,256]{1,0:T(8,128)S(1)} %copy-done.5, bf16[2048,256]{1,0:T(8,128)(2,1)} %bitcast.117, bf16[2,256,256]{2,1,0:T(8,128)(2,1)S(1)} %copy-done.10), kind=kOutput, calls=%fused_computation.15 | convolution fusion | flops 273678336 | bytes 8519680 | tf_op jit(solution)/shard_map/dot_general | solution.py:181
  89.8 7.0 %shard_map.106.slot_ref = f32[24,128,256]{2,1,0:T(8,128)} custom-call(s32[16,8]{1,0:T(8,128)} %copy.24.src_ref, bf16[16,8,128,128]{3,2,1,0:T(8,128)(2,1)} %bitcast.106, bf16[16,128,256]{2,1,0:T(8,128)(2,1)} %bitcast.107), custom_call_target="tpu_custom_call" | custom-call | tf_op jit(solution)/shard_map/pallas_call | solution.py:64
  96.8 1.4 fusion.31
  98.2 1.0 collective-permute-start.7
  100.3 1.2 convolution_bitcast_fusion.2
  101.5 6.7 %collective-permute-done.7.upper_ref = f32[4,128,256]{2,1,0:T(8,128)S(1)} collective-permute-done((f32[4,128,256]{2,1,0:T(8,128)S(1)}, f32[4,128,256]{2,1,0:T(8,128)S(1)}, u32[]{:S(2)}, u32[]{:S(2)}) %collective-permute-start.7) | collective-permute-done | bytes 524320 | tf_op jit(solution)/shard_map/ppermute | solution.py:118
  108.2 0.8 copy-done.11
  109.0 3.6 %collective-permute-done.6.lower_ref = f32[4,128,256]{2,1,0:T(8,128)} collective-permute-done((f32[4,128,256]{2,1,0:T(8,128)S(1)}, f32[4,128,256]{2,1,0:T(8,128)}, u32[]{:S(2)}, u32[]{:S(2)}) %collective-permute-start.6) | collective-permute-done | bytes 524320 | tf_op jit(solution)/shard_map/ppermute | solution.py:113
  112.6 3.9 %shard_map.107 = bf16[16,128,256]{2,1,0:T(8,128)(2,1)} custom-call(s32[2,4]{1,0:T(2,128)} %dynamic-slice_reduce_fusion.lists_ref, f32[24,128,256]{2,1,0:T(8,128)} %shard_map.106.slot_ref, f32[4,128,256]{2,1,0:T(8,128)} %collective-permute-done.6.lower_ref, f32[4,128,256]{2,1,0:T(8,128)} %copy-done.11), custom_call_target="tpu_custom_call" | custom-call | tf_op jit(solution)/shard_map/pallas_call | solution.py:94
  116.4 1.7 convolution_bitcast_fusion.3
  118.7 2.1 %all_to_all.13 = f32[128,1,2048]{2,1,0:T(1,128)} reshape(f32[2,2,256,256]{3,2,1,0:T(8,128)S(1)} %copy.30) | data formatting | bytes 2097152 | tf_op jit(solution)/shard_map/all_to_all | solution.py:124
  120.7 27.7 %all_to_all.16 = f32[128,1,2048]{2,1,0:T(1,128)S(1)} all-to-all(f32[128,1,2048]{2,1,0:T(1,128)} %all_to_all.13), channel_id=1, replica_groups=mesh['dp'=8,'sector'=16] {'dp','sector'}, dimensions={0} | all-to-all | bytes 2097152 | tf_op jit(solution)/shard_map/all_to_all | solution.py:124
  148.4 0.6 reduce_sum.9
  149.1 1.5 broadcast_in_dim.8
  150.6 4.5 %all-to-all-start.1 = ((f32[128,1,2048]{2,1,0:T(1,128)}), f32[128,1,2048]{2,1,0:T(1,128)S(1)}, u32[]{:S(2)}, u32[]{:S(2)}) async-start(f32[128,1,2048]{2,1,0:T(1,128)} %broadcast_in_dim.8), calls=%async_computation.1 | async-start | bytes 2097152 | tf_op jit(solution)/shard_map/all_to_all | solution.py:126
  155.2 2.1 %convolution_add_fusion.1 = f32[2048,256]{1,0:T(8,128)S(1)} fusion(f32[2048,256]{1,0:T(8,128)} %get-tuple-element.17, bf16[2048,256]{1,0:T(8,128)(2,1)S(1)} %copy-done.1, bf16[2,256,256]{2,1,0:T(8,128)(2,1)S(1)} %copy-done.17), kind=kOutput, calls=%fused_computation.6 | convolution fusion | flops 268959744 | bytes 5373952 | tf_op jit(solution)/shard_map/dot_general | solution.py:180
  157.3 1.8 fusion
  159.1 15.1 %all-to-all-done.1 = f32[128,1,2048]{2,1,0:T(1,128)S(1)} async-done(((f32[128,1,2048]{2,1,0:T(1,128)}), f32[128,1,2048]{2,1,0:T(1,128)S(1)}, u32[]{:S(2)}, u32[]{:S(2)}) %all-to-all-start.1) | async-done | bytes 1048608 | tf_op jit(solution)/shard_map/all_to_all | solution.py:126
  174.3 2.9 %fusion.10 = (f32[64,2048]{1,0:T(8,128)S(1)}, f32[64,2048]{1,0:T(8,128)S(1)}) fusion(f32[128,1,2048]{2,1,0:T(1,128)S(1)} %all-to-all-done.1), kind=kLoop, calls=%fused_computation.34 | loop fusion | flops 262144 | bytes 2097152 | tf_op jit(solution)/shard_map/mul | solution.py:190
  177.1 0.9 mul.48
  178.0 0.9 mul.46
  (53 shorter events, 3.2 us)
Async XLA Ops:
  0.6 11.0 %copy-start.19 = (s32[1,16,8]{1,2,0:T(8,128)S(1)}, s32[1,16,8]{1,2,0:T(8,128)}, u32[]{:S(2)}) copy-start(s32[1,16,8]{1,2,0:T(8,128)} %param.9) | copy-start | bytes 1540
  3.8 13.1 %collective-permute-start = (bf16[4,128,256]{2,1,0:T(8,128)(2,1)S(1)}, bf16[4,128,256]{2,1,0:T(8,128)(2,1)S(1)}, u32[]{:S(2)}, u32[]{:S(2)}) collective-permute-start(bf16[4,128,256]{2,1,0:T(8,128)(2,1)S(1)} %gather_fusion), channel_id=1, source_target_pairs={{0,1},{1,2},{2,3},{3,4},{4,5},{5,6},{6,7},{7,8},{8,9},{9,10},{10,1... | collective-permute-start | bytes 786440 | tf_op jit(solution)/shard_map/ppermute | solution.py:113
  6.9 10.0 %collective-permute-start.1 = (bf16[4,128,256]{2,1,0:T(8,128)(2,1)S(1)}, bf16[4,128,256]{2,1,0:T(8,128)(2,1)S(1)}, u32[]{:S(2)}, u32[]{:S(2)}) collective-permute-start(bf16[4,128,256]{2,1,0:T(8,128)(2,1)S(1)} %gather_fusion.1), channel_id=1, source_target_pairs={{1,0},{2,1},{3,2},{4,3},{5,4},{6,5},{7,6},{8,7},{9,8},{10,9},{11,1... | collective-permute-start | bytes 786440 | tf_op jit(solution)/shard_map/ppermute | solution.py:118
  18.3 6.4 %copy-start = (bf16[1,2048,256]{2,1,0:T(8,128)(2,1)S(1)}, bf16[1,2048,256]{2,1,0:T(8,128)(2,1)}, u32[]{:S(2)}) copy-start(bf16[1,2048,256]{2,1,0:T(8,128)(2,1)} %param.7) | copy-start | bytes 3145732
  18.3 6.4 %copy-start.15 = (bf16[2,256,256]{2,1,0:T(8,128)(2,1)S(1)}, bf16[2,256,256]{2,1,0:T(8,128)(2,1)}, u32[]{:S(2)}) copy-start(bf16[2,256,256]{2,1,0:T(8,128)(2,1)} %param.12) | copy-start | bytes 786436
  24.7 4.8 %copy-start.10 = (bf16[2,256,256]{2,1,0:T(8,128)(2,1)S(1)}, bf16[2,256,256]{2,1,0:T(8,128)(2,1)}, u32[]{:S(2)}) copy-start(bf16[2,256,256]{2,1,0:T(8,128)(2,1)} %param.11) | copy-start | bytes 786436
  28.5 1.0 copy-start.6
  28.5 7.9 %copy-start.18 = (s32[1,16,2,4]{1,3,2,0:T(4,128)S(1)}, s32[1,16,2,4]{1,3,2,0:T(4,128)}, u32[]{:S(2)}) copy-start(s32[1,16,2,4]{1,3,2,0:T(4,128)} %param.10) | copy-start | bytes 1540
  31.1 10.4 %collective-permute-start.2 = (bf16[4,128,256]{2,1,0:T(8,128)(2,1)S(1)}, bf16[4,128,256]{2,1,0:T(8,128)(2,1)S(1)}, u32[]{:S(2)}, u32[]{:S(2)}) collective-permute-start(bf16[4,128,256]{2,1,0:T(8,128)(2,1)S(1)} %gather_fusion.2), channel_id=1, source_target_pairs={{0,1},{1,2},{2,3},{3,4},{4,5},{5,6},{6,7},{7,8},{8,9},{9,10},{10,1... | collective-permute-start | bytes 786440 | tf_op jit(solution)/shard_map/ppermute | solution.py:113
  31.2 10.3 %collective-permute-start.3 = (bf16[4,128,256]{2,1,0:T(8,128)(2,1)S(1)}, bf16[4,128,256]{2,1,0:T(8,128)(2,1)S(1)}, u32[]{:S(2)}, u32[]{:S(2)}) collective-permute-start(bf16[4,128,256]{2,1,0:T(8,128)(2,1)S(1)} %gather_fusion.3), channel_id=1, source_target_pairs={{1,0},{2,1},{3,2},{4,3},{5,4},{6,5},{7,6},{8,7},{9,8},{10,9},{11,1... | collective-permute-start | bytes 786440 | tf_op jit(solution)/shard_map/ppermute | solution.py:118
  42.8 6.4 %copy-start.4 = (f32[1,2048,256]{2,1,0:T(8,128)S(1)}, f32[1,2048,256]{2,1,0:T(8,128)}, u32[]{:S(2)}) copy-start(f32[1,2048,256]{2,1,0:T(8,128)} %param.13) | copy-start | bytes 6291460
  61.1 6.1 %copy-start.3 = (bf16[2048,256]{1,0:T(8,128)(2,1)S(1)}, bf16[2048,256]{1,0:T(8,128)(2,1)}, u32[]{:S(2)}) copy-start(bf16[2048,256]{1,0:T(8,128)(2,1)} %get-tuple-element.8) | copy-start | bytes 3145732
  61.1 6.1 %copy-start.7 = (bf16[2048,256]{1,0:T(8,128)(2,1)S(1)}, bf16[2048,256]{1,0:T(8,128)(2,1)}, u32[]{:S(2)}) copy-start(bf16[2048,256]{1,0:T(8,128)(2,1)} %copy-done.6) | copy-start | bytes 3145732
  61.1 7.3 %copy-start.16 = (bf16[2,256,256]{2,1,0:T(8,128)(2,1)S(1)}, bf16[2,256,256]{2,1,0:T(8,128)(2,1)}, u32[]{:S(2)}) copy-start(bf16[2,256,256]{2,1,0:T(8,128)(2,1)} %param.12) | copy-start | bytes 786436
  62.6 13.5 %collective-permute-start.5 = (f32[4,128,256]{2,1,0:T(8,128)S(1)}, f32[4,128,256]{2,1,0:T(8,128)S(1)}, u32[]{:S(2)}, u32[]{:S(2)}) collective-permute-start(f32[4,128,256]{2,1,0:T(8,128)S(1)} %get-tuple-element.12), channel_id=1, source_target_pairs={{1,0},{2,1},{3,2},{4,3},{5,4},{6,5},{7,6},{8,7},{9,8},{10,9},{11,1... | collective-permute-start | bytes 1572872 | tf_op jit(solution)/shard_map/ppermute | solution.py:118
  67.2 14.2 %collective-permute-start.4 = (f32[4,128,256]{2,1,0:T(8,128)S(1)}, f32[4,128,256]{2,1,0:T(8,128)}, u32[]{:S(2)}, u32[]{:S(2)}) collective-permute-start(f32[4,128,256]{2,1,0:T(8,128)S(1)} %get-tuple-element.13), channel_id=1, source_target_pairs={{0,1},{1,2},{2,3},{3,4},{4,5},{5,6},{6,7},{7,8},{8,9},{9,10},{10,1... | collective-permute-start | bytes 1572872 | tf_op jit(solution)/shard_map/ppermute | solution.py:113
  70.3 15.0 %copy-start.5 = (f32[2048,256]{1,0:T(8,128)S(1)}, f32[2048,256]{1,0:T(8,128)}, u32[]{:S(2)}) copy-start(f32[2048,256]{1,0:T(8,128)} %convolution_add_fusion.3) | copy-start | bytes 6291460
  76.1 0.8 copy-start.12
  96.8 3.0 %copy-start.1 = (bf16[2048,256]{1,0:T(8,128)(2,1)S(1)}, bf16[2048,256]{1,0:T(8,128)(2,1)}, u32[]{:S(2)}) copy-start(bf16[2048,256]{1,0:T(8,128)(2,1)} %get-tuple-element.16) | copy-start | bytes 3145732
  96.8 3.4 %copy-start.13 = (f32[1,256,256]{1,2,0:T(8,128)S(1)}, f32[1,256,256]{1,2,0:T(8,128)}, u32[]{:S(2)}) copy-start(f32[1,256,256]{1,2,0:T(8,128)} %convolution_bitcast_fusion) | copy-start | bytes 786436
  98.2 2.1 %copy-start.8 = (bf16[2048,256]{1,0:T(8,128)(2,1)S(1)}, bf16[2048,256]{1,0:T(8,128)(2,1)}, u32[]{:S(2)}) copy-start(bf16[2048,256]{1,0:T(8,128)(2,1)} %copy-done.6) | copy-start | bytes 3145732
  98.2 2.1 %copy-start.9 = (bf16[16,128,256]{2,1,0:T(8,128)(2,1)S(1)}, bf16[16,128,256]{2,1,0:T(8,128)(2,1)}, u32[]{:S(2)}) copy-start(bf16[16,128,256]{2,1,0:T(8,128)(2,1)} %shard_map.105) | copy-start | bytes 3145732
  98.2 10.0 %collective-permute-start.7 = (f32[4,128,256]{2,1,0:T(8,128)S(1)}, f32[4,128,256]{2,1,0:T(8,128)S(1)}, u32[]{:S(2)}, u32[]{:S(2)}) collective-permute-start(f32[4,128,256]{2,1,0:T(8,128)S(1)} %get-tuple-element.10), channel_id=1, source_target_pairs={{1,0},{2,1},{3,2},{4,3},{5,4},{6,5},{7,6},{8,7},{9,8},{10,9},{11,1... | collective-permute-start | bytes 1572872 | tf_op jit(solution)/shard_map/ppermute | solution.py:118
  99.2 13.3 %collective-permute-start.6 = (f32[4,128,256]{2,1,0:T(8,128)S(1)}, f32[4,128,256]{2,1,0:T(8,128)}, u32[]{:S(2)}, u32[]{:S(2)}) collective-permute-start(f32[4,128,256]{2,1,0:T(8,128)S(1)} %get-tuple-element.11), channel_id=1, source_target_pairs={{0,1},{1,2},{2,3},{3,4},{4,5},{5,6},{6,7},{7,8},{8,9},{9,10},{10,1... | collective-permute-start | bytes 1572872 | tf_op jit(solution)/shard_map/ppermute | solution.py:113
  108.2 0.8 copy-start.11
  116.4 1.7 copy-start.14
  148.4 6.7 %copy-start.17 = (bf16[2,256,256]{2,1,0:T(8,128)(2,1)S(1)}, bf16[2,256,256]{2,1,0:T(8,128)(2,1)}, u32[]{:S(2)}) copy-start(bf16[2,256,256]{2,1,0:T(8,128)(2,1)} %param.12) | copy-start | bytes 786436
  150.6 23.7 %all-to-all-start.1 = ((f32[128,1,2048]{2,1,0:T(1,128)}), f32[128,1,2048]{2,1,0:T(1,128)S(1)}, u32[]{:S(2)}, u32[]{:S(2)}) async-start(f32[128,1,2048]{2,1,0:T(1,128)} %broadcast_in_dim.8), calls=%async_computation.1 | async-start | bytes 2097152 | tf_op jit(solution)/shard_map/all_to_all | solution.py:126
  155.2 2.2 %copy-start.2 = (bf16[16,128,256]{2,1,0:T(8,128)(2,1)S(1)}, bf16[16,128,256]{2,1,0:T(8,128)(2,1)}, u32[]{:S(2)}) copy-start(bf16[16,128,256]{2,1,0:T(8,128)(2,1)} %shard_map.107) | copy-start | bytes 3145732

commit v2 on v1

--- a/solution.py
+++ b/solution.py
@@ -1,3 +1,5 @@
+import functools
+
 import jax
 import jax.numpy as jnp
 from jax import lax
@@ -9,60 +11,87 @@
 GROUP = 8
 
 
-def aggregate_kernel(src_ref, tiles_ref, table_ref, out_ref):
+def aggregate_kernel(lo, src_ref, tiles_ref, table_ref, *rest):
+    out_ref = rest[-1]
+    count = table_ref.shape[0]
     step = pl.program_id(0)
-    for i in range(GROUP):
+
+    def one_block(i, carry):
         block = step * GROUP + i
-        acc = None
+        if len(rest) == 2:
+            out_ref[i] = rest[0][i]
+        else:
+            out_ref[i] = jnp.zeros(out_ref.shape[1:], out_ref.dtype)
         for k in range(tiles_ref.shape[1]):
-            slot = src_ref[block, k]
-            part = jnp.dot(tiles_ref[i, k], table_ref[slot], preferred_element_type=jnp.float32)
-            acc = part if acc is None else acc + part
-        out_ref[i] = acc
-
-
-def block_aggregate(slot_ids, tile_data, table):
+            slot = src_ref[block, k] - lo
+
+            @pl.when((slot >= 0) & (slot < count))
+            def _():
+                out_ref[i] += jnp.dot(
+                    tiles_ref[i, k], table_ref[slot], preferred_element_type=jnp.float32
+                )
+
+        return carry
+
+    lax.fori_loop(0, GROUP, one_block, 0)
+
+
+def block_aggregate(slot_ids, tile_data, table, lo, start=None):
     blocks, listed, rows, _ = tile_data.shape
     width = table.shape[-1]
+    in_specs = [
+        pl.BlockSpec((GROUP, listed, rows, rows), lambda g, src: (g, 0, 0, 0)),
+        pl.BlockSpec(table.shape, lambda g, src: (0, 0, 0)),
+    ]
+    args = [slot_ids, tile_data, table]
+    aliases = {}
+    if start is not None:
+        in_specs.append(pl.BlockSpec((GROUP, rows, width), lambda g, src: (g, 0, 0)))
+        args.append(start)
+        aliases = {3: 0}
     return pl.pallas_call(
-        aggregate_kernel,
+        functools.partial(aggregate_kernel, lo),
         grid_spec=pltpu.PrefetchScalarGridSpec(
             num_scalar_prefetch=1,
             grid=(blocks // GROUP,),
-            in_specs=[
-                pl.BlockSpec((GROUP, listed, rows, rows), lambda g, src: (g, 0, 0, 0)),
-                pl.BlockSpec(table.shape, lambda g, src: (0, 0, 0)),
-            ],
+            in_specs=in_specs,
             out_specs=pl.BlockSpec((GROUP, rows, width), lambda g, src: (g, 0, 0)),
         ),
         out_shape=jax.ShapeDtypeStruct((blocks, rows, width), jnp.float32),
-    )(slot_ids, tile_data, table)
-
-
-def slot_grad_kernel(src_ref, tiles_ref, dpre_ref, out_ref):
+        input_output_aliases=aliases,
+    )(*args)
+
+
+def slot_grad_kernel(lo, src_ref, tiles_ref, dpre_ref, out_ref):
+    count = out_ref.shape[0]
     step = pl.program_id(0)
 
     @pl.when(step == 0)
     def _():
         out_ref[...] = jnp.zeros(out_ref.shape, out_ref.dtype)
 
-    for i in range(GROUP):
+    def one_block(i, carry):
         block = step * GROUP + i
-        grad = dpre_ref[i]
         for k in range(tiles_ref.shape[1]):
-            slot = src_ref[block, k]
-            part = lax.dot_general(
-                tiles_ref[i, k], grad, (((0,), (0,)), ((), ())),
-                preferred_element_type=jnp.float32,
-            )
-            out_ref[slot] += part
-
-
-def block_slot_grad(slot_ids, tile_data, dpre_blocks, slot_count):
+            slot = src_ref[block, k] - lo
+
+            @pl.when((slot >= 0) & (slot < count))
+            def _():
+                out_ref[slot] += lax.dot_general(
+                    tiles_ref[i, k], dpre_ref[i], (((0,), (0,)), ((), ())),
+                    preferred_element_type=jnp.float32,
+                )
+
+        return carry
+
+    lax.fori_loop(0, GROUP, one_block, 0)
+
+
+def block_slot_grad(slot_ids, tile_data, dpre_blocks, lo, count):
     blocks, listed, rows, _ = tile_data.shape
     width = dpre_blocks.shape[-1]
     return pl.pallas_call(
-        slot_grad_kernel,
+        functools.partial(slot_grad_kernel, lo),
         grid_spec=pltpu.PrefetchScalarGridSpec(
             num_scalar_prefetch=1,
             grid=(blocks // GROUP,),
@@ -70,9 +99,9 @@
                 pl.BlockSpec((GROUP, listed, rows, rows), lambda g, src: (g, 0, 0, 0)),
                 pl.BlockSpec((GROUP, rows, width), lambda g, src: (g, 0, 0)),
             ],
-            out_specs=pl.BlockSpec((slot_count, rows, width), lambda g, src: (0, 0, 0)),
+            out_specs=pl.BlockSpec((count, rows, width), lambda g, src: (0, 0, 0)),
         ),
-        out_shape=jax.ShapeDtypeStruct((slot_count, rows, width), jnp.float32),
+        out_shape=jax.ShapeDtypeStruct((count, rows, width), jnp.float32),
         compiler_params=pltpu.CompilerParams(dimension_semantics=("arbitrary",)),
     )(slot_ids, tile_data, dpre_blocks)
 
@@ -152,8 +181,9 @@
         message_blocks = message.reshape(blocks_here, tile_rows, width)
         from_lower = to_upper(message_blocks[own_lists[0]], "sector")
         from_upper = to_lower(message_blocks[own_lists[1]], "sector")
-        table = jnp.concatenate([message_blocks, from_lower, from_upper])
-        aggregate = block_aggregate(slot_ids, tile_data, table)
+        own_part = block_aggregate(slot_ids, tile_data, message_blocks, 0)
+        lent_table = jnp.concatenate([from_lower, from_upper])
+        aggregate = block_aggregate(slot_ids, tile_data, lent_table, blocks_here, own_part)
         pre = aggregate.reshape(-1, width) + jnp.dot(
             current, w_self[layer_index], preferred_element_type=jnp.float32
         )
@@ -165,13 +195,13 @@
     for layer_index in reversed(range(LAYERS)):
         layer_in, pre = saved[layer_index]
         dpre = (grad * silu_grad(pre)).astype(jnp.bfloat16)
-        slot_grad = block_slot_grad(
-            slot_ids, tile_data, dpre.reshape(blocks_here, tile_rows, width), slot_count
-        )
-        lent_down_grad = to_upper(slot_grad[blocks_here + lent :], "sector")
-        lent_up_grad = to_lower(slot_grad[blocks_here : blocks_here + lent], "sector")
+        dpre_blocks = dpre.reshape(blocks_here, tile_rows, width)
+        lent_grad = block_slot_grad(slot_ids, tile_data, dpre_blocks, blocks_here, 2 * lent)
+        lent_down_grad = to_upper(lent_grad[lent:], "sector")
+        lent_up_grad = to_lower(lent_grad[:lent], "sector")
+        own_grad = block_slot_grad(slot_ids, tile_data, dpre_blocks, 0, blocks_here)
         dmessage = fold_lent(
-            own_lists, slot_grad, lent_down_grad, lent_up_grad, blocks_here
+            own_lists, own_grad, lent_down_grad, lent_up_grad, blocks_here
         ).reshape(-1, width)
         self_part = jnp.dot(layer_in.T, dpre, preferred_element_type=jnp.float32)
         message_part = jnp.dot(layer_in.T, dmessage, preferred_element_type=jnp.float32)

time: 179 us -> 260 us (1.45)
  Pallas kernels: 34.5 us -> 133 us
  waiting for transfers between devices: 44.8 us -> 39.3 us
  local copies, waits for them, and re-layouts: 15.8 us -> 11.6 us
  starting transfers between devices: 23.2 us -> 19.6 us
    pallas_call x4 -> x8, Pallas kernels: 26.8 us -> 125 us  [the longest x4 68.5 us: block_slot_grad(): pl.pallas_call(functools.partial(slot_grad_kernel, lo), grid_spec=pltpu.P...]
    ppermute x4, waiting for transfers between devices: 17.1 us -> 6.99 us  [to_upper(): return lax.ppermute(x, axis, [(i, (i + 1) % count) for i in range(count)])]
    ppermute x4, starting transfers between devices: 15.6 us -> 9.76 us  [to_lower(): return lax.ppermute(x, axis, [((i + 1) % count, i) for i in range(count)])]
    ppermute x4, waiting for transfers between devices: 12.5 us -> 17.1 us  [to_lower(): return lax.ppermute(x, axis, [((i + 1) % count, i) for i in range(count)])]
    slice x2, local copies, waits for them, and re-layouts: 2.85 us -> 0.17 us  [per_device(): lent_up_grad = to_lower(lent_grad[:lent], 'sector')]
  transfers between devices with their start and end apart: 9 -> 9, of which waited for: 7 -> 5; matrix products, arithmetic and copies ran while one was open for 6% -> 4% of each run, Pallas kernels for 0% -> 13%
where the time goes in v2:
time: 260 us; the launch traced here: 259 us
  Pallas kernels  133 us (51%)
  waiting for transfers between devices  39.3 us (15%)
  blocking collectives  25.9 us (10%)
  matrix products  24.2 us (9%)
  starting transfers between devices  19.6 us (8%)
  local copies, waits for them, and re-layouts  11.6 us (4%)
  other arithmetic  5.33 us (2%)
    pallas_call x4, Pallas kernels, block_slot_grad(): pl.pallas_call(functools.partial(slot_grad_kernel, lo), grid_spec=pltpu.P...  68.5 us
    pallas_call x4, Pallas kernels, block_aggregate(): pl.pallas_call(functools.partial(aggregate_kernel, lo), grid_spec=pltpu.P...  56.5 us
    all_to_all x1, blocking collectives, all_reduce(): mine = lax.all_to_all(pieces, axes, 0, 0, tiled=True).sum(0)  25.9 us
    ppermute x4, waiting for transfers between devices, to_lower(): return lax.ppermute(x, axis, [((i + 1) % count, i) for i in range(count)])  17.1 us
    all_to_all x1, waiting for transfers between devices, all_reduce(): return lax.all_to_all(spread, axes, 0, 0, tiled=True).reshape(x.shape)  15.2 us
    ppermute x4, starting transfers between devices, to_lower(): return lax.ppermute(x, axis, [((i + 1) % count, i) for i in range(count)])  9.76 us
    dot_general x2, matrix products, per_device(): jnp.dot(current, w_self[layer_index], preferred_element_type=jnp.float32)  8.58 us
    pallas_call x2, Pallas kernels, fold_lent(): pl.pallas_call(fold_kernel, grid_spec=pltpu.PrefetchScalarGridSpec(num_sc...  7.67 us
  transfers between devices with their start and end apart: 9, of which 5 were waited for; matrix products, arithmetic and copies ran while one was open for 4% of the time, Pallas kernels for 13%

profile of v2, /device:TPU:1, one launch (start us, length us, event | category | flops | bytes accessed | tf_op | source)
XLA Modules:
  0.0 259.5 jit_solution(15164616744357980318)
XLA Ops:
  0.6 0.9 dynamic-slice_reduce_fusion.2
  1.6 1.7 convolution_convert_fusion.1
  3.3 0.6 gather_fusion
  3.8 2.5 collective-permute-start
  6.4 0.6 gather_fusion.1
  6.9 4.7 %collective-permute-start.1 = (bf16[4,128,256]{2,1,0:T(8,128)(2,1)S(1)}, bf16[4,128,256]{2,1,0:T(8,128)(2,1)S(1)}, u32[]{:S(2)}, u32[]{:S(2)}) collective-permute-start(bf16[4,128,256]{2,1,0:T(8,128)(2,1)S(1)} %gather_fusion.1), channel_id=1, source_target_pairs={{1,0},{2,1},{3,2},{4,3},{5,4},{6,5},{7,6},{8,7},{9,8},{10,9},{11,1... | collective-permute-start | bytes 786440 | tf_op jit(solution)/shard_map/ppermute | solution.py:147
  11.6 0.7 copy.35.src_ref
  12.3 17.1 %shard_map.102.rest_0_ = f32[16,128,256]{2,1,0:T(8,128)} custom-call(s32[16,8]{1,0:T(8,128)} %copy.35.src_ref, bf16[16,8,128,128]{3,2,1,0:T(8,128)(2,1)} %bitcast.103, bf16[16,128,256]{2,1,0:T(8,128)(2,1)} %bitcast.119), custom_call_target="tpu_custom_call" | custom-call | tf_op jit(solution)/shard_map/pallas_call | solution.py:52
  29.4 0.8 pad_maximum_fusion.1.table_ref
  30.2 11.2 %shard_map.103 = f32[16,128,256]{2,1,0:T(8,128)} custom-call(s32[16,8]{1,0:T(8,128)} %copy.35.src_ref, bf16[16,8,128,128]{3,2,1,0:T(8,128)(2,1)} %bitcast.104, bf16[8,128,256]{2,1,0:T(8,128)(2,1)} %pad_maximum_fusion.1.table_ref, f32[16,128,256]{2,1,0:T(8,128)} %shard_map.102.rest_0_), custom_call_target="tpu_custom_call", output_to_operand_aliasing={{}: (3, {})} | custom-call | tf_op jit(solution)/shard_map/pallas_call | solution.py:52
  41.4 3.7 %add_convert_fusion.1 = (bf16[2048,256]{1,0:T(8,128)(2,1)S(1)}, f32[2048,256]{1,0:T(8,128)}) fusion(bf16[1,2048,256]{2,1,0:T(8,128)(2,1)S(1)} %copy-done.1, bf16[2,256,256]{2,1,0:T(8,128)(2,1)S(1)} %copy-done.18, f32[16,128,256]{2,1,0:T(8,128)} %shard_map.103), kind=kOutput, calls=%fused_computation.18 | convolution fusion | flops 272629760 | bytes 7471104 | tf_op jit(solution)/shard_map/dot_general | solution.py:187
  45.1 1.0 copy-done.11
  46.6 0.6 gather_fusion.3
  47.1 0.6 gather_fusion.2
  47.8 4.8 %collective-permute-start.3 = (bf16[4,128,256]{2,1,0:T(8,128)(2,1)S(1)}, bf16[4,128,256]{2,1,0:T(8,128)(2,1)S(1)}, u32[]{:S(2)}, u32[]{:S(2)}) collective-permute-start(bf16[4,128,256]{2,1,0:T(8,128)(2,1)S(1)} %gather_fusion.3), channel_id=1, source_target_pairs={{1,0},{2,1},{3,2},{4,3},{5,4},{6,5},{7,6},{8,7},{9,8},{10,9},{11,1... | collective-permute-start | bytes 786440 | tf_op jit(solution)/shard_map/ppermute | solution.py:147
  52.6 0.8 dynamic-slice_reduce_fusion.lists_ref
  53.4 17.1 %shard_map.104.rest_0_ = f32[16,128,256]{2,1,0:T(8,128)} custom-call(s32[16,8]{1,0:T(8,128)} %copy.35.src_ref, bf16[16,8,128,128]{3,2,1,0:T(8,128)(2,1)} %bitcast.105, bf16[16,128,256]{2,1,0:T(8,128)(2,1)} %bitcast.122), custom_call_target="tpu_custom_call" | custom-call | tf_op jit(solution)/shard_map/pallas_call | solution.py:52
  70.5 0.8 pad_maximum_fusion.2.table_ref
  71.3 11.2 %shard_map.105 = f32[16,128,256]{2,1,0:T(8,128)} custom-call(s32[16,8]{1,0:T(8,128)} %copy.35.src_ref, bf16[16,8,128,128]{3,2,1,0:T(8,128)(2,1)} %bitcast.106, bf16[8,128,256]{2,1,0:T(8,128)(2,1)} %pad_maximum_fusion.2.table_ref, f32[16,128,256]{2,1,0:T(8,128)} %shard_map.104.rest_0_), custom_call_target="tpu_custom_call", output_to_operand_aliasing={{}: (3, {})} | custom-call | tf_op jit(solution)/shard_map/pallas_call | solution.py:52
  82.5 4.9 %fusion.1 = (bf16[2048,256]{1,0:T(8,128)(2,1)}, bf16[1,2048,256]{2,1,0:T(8,128)(2,1)}) fusion(f32[1,2048,256]{2,1,0:T(8,128)S(1)} %copy-done.8, f32[16,128,256]{2,1,0:T(8,128)} %shard_map.105, bf16[2048,256]{1,0:T(8,128)(2,1)} %copy-done.11, bf16[2,256,256]{2,1,0:T(8,128)(2,1)} %param.12), kind=kOutput, calls=%fused_computation.12 | convolution fusion | flops 275775488 | bytes 8519680 | tf_op jit(solution)/shard_map/dot_general | solution.py:187
  87.4 12.7 %shard_map.107 = f32[8,128,256]{2,1,0:T(8,128)} custom-call(s32[16,8]{1,0:T(8,128)} %copy.35.src_ref, bf16[16,8,128,128]{3,2,1,0:T(8,128)(2,1)} %bitcast.107, bf16[16,128,256]{2,1,0:T(8,128)(2,1)} %bitcast.115), custom_call_target="tpu_custom_call" | custom-call | tf_op jit(solution)/shard_map/pallas_call | solution.py:93
  100.1 21.5 %shard_map.106.slot_ref = f32[16,128,256]{2,1,0:T(8,128)} custom-call(s32[16,8]{1,0:T(8,128)} %copy.35.src_ref, bf16[16,8,128,128]{3,2,1,0:T(8,128)(2,1)} %bitcast.108, bf16[16,128,256]{2,1,0:T(8,128)(2,1)} %bitcast.116), custom_call_target="tpu_custom_call" | custom-call | tf_op jit(solution)/shard_map/pallas_call | solution.py:93
  121.8 1.5 collective-permute-start.4
  123.2 1.2 convolution_bitcast_fusion
  125.0 9.0 %collective-permute-done.5.upper_ref = f32[4,128,256]{2,1,0:T(8,128)} collective-permute-done((f32[4,128,256]{2,1,0:T(8,128)S(1)}, f32[4,128,256]{2,1,0:T(8,128)}, u32[]{:S(2)}, u32[]{:S(2)}) %collective-permute-start.5) | collective-permute-done | bytes 524320 | tf_op jit(solution)/shard_map/ppermute | solution.py:147
  134.0 3.4 %collective-permute-done.4.lower_ref = f32[4,128,256]{2,1,0:T(8,128)} collective-permute-done((f32[4,128,256]{2,1,0:T(8,128)S(1)}, f32[4,128,256]{2,1,0:T(8,128)}, u32[]{:S(2)}, u32[]{:S(2)}) %collective-permute-start.4) | collective-permute-done | bytes 524320 | tf_op jit(solution)/shard_map/ppermute | solution.py:142
  137.4 3.8 %shard_map.108 = bf16[16,128,256]{2,1,0:T(8,128)(2,1)} custom-call(s32[2,4]{1,0:T(2,128)} %dynamic-slice_reduce_fusion.lists_ref, f32[16,128,256]{2,1,0:T(8,128)} %shard_map.106.slot_ref, f32[4,128,256]{2,1,0:T(8,128)} %collective-permute-done.4.lower_ref, f32[4,128,256]{2,1,0:T(8,128)} %collective-permute-done.5.upper_ref), custom_call_target="tpu_custom_call" | custom-call | tf_op jit(solution)/shard_map/pallas_call | solution.py:123
  141.2 4.5 %multiply_convert_fusion = (bf16[2048,256]{1,0:T(8,128)(2,1)}, f32[2048,256]{1,0:T(8,128)}) fusion(f32[2048,256]{1,0:T(8,128)} %get-tuple-element.15, f32[2048,256]{1,0:T(8,128)S(1)} %convolution_add_fusion.3, bf16[2048,256]{1,0:T(8,128)(2,1)} %bitcast.123, bf16[2,256,256]{2,1,0:T(8,128)(2,1)S(1)} %copy-done.14), kind=kOutput, calls=%fused_computation.15 | convolution fusion | flops 273678336 | bytes 8519680 | tf_op jit(solution)/shard_map/dot_general | solution.py:211
  145.7 12.7 %shard_map.110 = f32[8,128,256]{2,1,0:T(8,128)} custom-call(s32[16,8]{1,0:T(8,128)} %copy.35.src_ref, bf16[16,8,128,128]{3,2,1,0:T(8,128)(2,1)} %bitcast.109, bf16[16,128,256]{2,1,0:T(8,128)(2,1)} %bitcast.111), custom_call_target="tpu_custom_call" | custom-call | tf_op jit(solution)/shard_map/pallas_call | solution.py:93
  158.4 21.5 %shard_map.109.slot_ref = f32[16,128,256]{2,1,0:T(8,128)} custom-call(s32[16,8]{1,0:T(8,128)} %copy.35.src_ref, bf16[16,8,128,128]{3,2,1,0:T(8,128)(2,1)} %bitcast.110, bf16[16,128,256]{2,1,0:T(8,128)(2,1)} %bitcast.112), custom_call_target="tpu_custom_call" | custom-call | tf_op jit(solution)/shard_map/pallas_call | solution.py:93
  180.3 1.3 collective-permute-start.6
  181.6 0.5 convolution_bitcast_fusion.1
  182.1 1.2 convolution_bitcast_fusion.2
  183.4 8.1 %collective-permute-done.7.upper_ref = f32[4,128,256]{2,1,0:T(8,128)S(1)} collective-permute-done((f32[4,128,256]{2,1,0:T(8,128)S(1)}, f32[4,128,256]{2,1,0:T(8,128)S(1)}, u32[]{:S(2)}, u32[]{:S(2)}) %collective-permute-start.7) | collective-permute-done | bytes 524320 | tf_op jit(solution)/shard_map/ppermute | solution.py:147
  191.5 3.6 %collective-permute-done.6.lower_ref = f32[4,128,256]{2,1,0:T(8,128)} collective-permute-done((f32[4,128,256]{2,1,0:T(8,128)S(1)}, f32[4,128,256]{2,1,0:T(8,128)}, u32[]{:S(2)}, u32[]{:S(2)}) %collective-permute-start.6) | collective-permute-done | bytes 524320 | tf_op jit(solution)/shard_map/ppermute | solution.py:142
  195.1 3.8 %shard_map.111 = bf16[16,128,256]{2,1,0:T(8,128)(2,1)} custom-call(s32[2,4]{1,0:T(2,128)} %dynamic-slice_reduce_fusion.lists_ref, f32[16,128,256]{2,1,0:T(8,128)} %shard_map.109.slot_ref, f32[4,128,256]{2,1,0:T(8,128)} %collective-permute-done.6.lower_ref, f32[4,128,256]{2,1,0:T(8,128)} %copy-done.15), custom_call_target="tpu_custom_call" | custom-call | tf_op jit(solution)/shard_map/pallas_call | solution.py:123
  198.9 1.7 convolution_bitcast_fusion.3
  201.2 2.1 all_to_all.13
  203.2 25.9 %all_to_all.16 = f32[128,1,2048]{2,1,0:T(1,128)S(1)} all-to-all(f32[128,1,2048]{2,1,0:T(1,128)} %all_to_all.13), channel_id=1, replica_groups=mesh['dp'=8,'sector'=16] {'dp','sector'}, dimensions={0} | all-to-all | bytes 2097152 | tf_op jit(solution)/shard_map/all_to_all | solution.py:153
  229.1 0.6 reduce_sum.9
  229.7 1.5 broadcast_in_dim.8
  231.2 4.5 %all-to-all-start.1 = ((f32[128,1,2048]{2,1,0:T(1,128)}), f32[128,1,2048]{2,1,0:T(1,128)S(1)}, u32[]{:S(2)}, u32[]{:S(2)}) async-start(f32[128,1,2048]{2,1,0:T(1,128)} %broadcast_in_dim.8), calls=%async_computation.1 | async-start | bytes 2097152 | tf_op jit(solution)/shard_map/all_to_all | solution.py:155
  235.8 2.1 convolution_add_fusion.1
  237.9 1.8 fusion
  239.7 15.2 %all-to-all-done.1 = f32[128,1,2048]{2,1,0:T(1,128)S(1)} async-done(((f32[128,1,2048]{2,1,0:T(1,128)}), f32[128,1,2048]{2,1,0:T(1,128)S(1)}, u32[]{:S(2)}, u32[]{:S(2)}) %all-to-all-start.1) | async-done | bytes 1048608 | tf_op jit(solution)/shard_map/all_to_all | solution.py:155
  254.9 2.9 %fusion.10 = (f32[64,2048]{1,0:T(8,128)S(1)}, f32[64,2048]{1,0:T(8,128)S(1)}) fusion(f32[128,1,2048]{2,1,0:T(1,128)S(1)} %all-to-all-done.1), kind=kLoop, calls=%fused_computation.32 | loop fusion | flops 262144 | bytes 2097152 | tf_op jit(solution)/shard_map/mul | solution.py:220
  257.7 0.9 mul.48
  258.6 0.9 mul.46
  (63 shorter events, 2.1 us)
Async XLA Ops:
  0.6 11.0 %copy-start.22 = (s32[1,16,8]{1,2,0:T(8,128)S(1)}, s32[1,16,8]{1,2,0:T(8,128)}, u32[]{:S(2)}) copy-start(s32[1,16,8]{1,2,0:T(8,128)} %param.9) | copy-start | bytes 1540
  3.3 9.0 %copy-start.4 = (bf16[2048,256]{1,0:T(8,128)(2,1)}, bf16[2048,256]{1,0:T(8,128)(2,1)S(1)}, u32[]{:S(2)}) copy-start(bf16[2048,256]{1,0:T(8,128)(2,1)S(1)} %convolution_convert_fusion.1) | copy-start | bytes 3145732
  3.8 25.5 %collective-permute-start = (bf16[4,128,256]{2,1,0:T(8,128)(2,1)S(1)}, bf16[4,128,256]{2,1,0:T(8,128)(2,1)S(1)}, u32[]{:S(2)}, u32[]{:S(2)}) collective-permute-start(bf16[4,128,256]{2,1,0:T(8,128)(2,1)S(1)} %gather_fusion), channel_id=1, source_target_pairs={{0,1},{1,2},{2,3},{3,4},{4,5},{5,6},{6,7},{7,8},{8,9},{9,10},{10,1... | collective-permute-start | bytes 786440 | tf_op jit(solution)/shard_map/ppermute | solution.py:142
  6.9 22.4 %collective-permute-start.1 = (bf16[4,128,256]{2,1,0:T(8,128)(2,1)S(1)}, bf16[4,128,256]{2,1,0:T(8,128)(2,1)S(1)}, u32[]{:S(2)}, u32[]{:S(2)}) collective-permute-start(bf16[4,128,256]{2,1,0:T(8,128)(2,1)S(1)} %gather_fusion.1), channel_id=1, source_target_pairs={{1,0},{2,1},{3,2},{4,3},{5,4},{6,5},{7,6},{8,7},{9,8},{10,9},{11,1... | collective-permute-start | bytes 786440 | tf_op jit(solution)/shard_map/ppermute | solution.py:147
  30.2 11.2 %copy-start.1 = (bf16[1,2048,256]{2,1,0:T(8,128)(2,1)S(1)}, bf16[1,2048,256]{2,1,0:T(8,128)(2,1)}, u32[]{:S(2)}) copy-start(bf16[1,2048,256]{2,1,0:T(8,128)(2,1)} %param.7) | copy-start | bytes 3145732
  30.2 11.2 %copy-start.18 = (bf16[2,256,256]{2,1,0:T(8,128)(2,1)S(1)}, bf16[2,256,256]{2,1,0:T(8,128)(2,1)}, u32[]{:S(2)}) copy-start(bf16[2,256,256]{2,1,0:T(8,128)(2,1)} %param.12) | copy-start | bytes 786436
  41.4 4.7 %copy-start.14 = (bf16[2,256,256]{2,1,0:T(8,128)(2,1)S(1)}, bf16[2,256,256]{2,1,0:T(8,128)(2,1)}, u32[]{:S(2)}) copy-start(bf16[2,256,256]{2,1,0:T(8,128)(2,1)} %param.11) | copy-start | bytes 786436
  45.1 1.0 copy-start.11
  45.1 7.4 %copy-start.21 = (s32[1,16,2,4]{1,3,2,0:T(4,128)S(1)}, s32[1,16,2,4]{1,3,2,0:T(4,128)}, u32[]{:S(2)}) copy-start(s32[1,16,2,4]{1,3,2,0:T(4,128)} %param.10) | copy-start | bytes 1540
  46.5 6.8 %copy-start.5 = (bf16[2048,256]{1,0:T(8,128)(2,1)}, bf16[2048,256]{1,0:T(8,128)(2,1)S(1)}, u32[]{:S(2)}) copy-start(bf16[2048,256]{1,0:T(8,128)(2,1)S(1)} %convolution_convert_fusion) | copy-start | bytes 3145732
  47.7 22.8 %collective-permute-start.2 = (bf16[4,128,256]{2,1,0:T(8,128)(2,1)S(1)}, bf16[4,128,256]{2,1,0:T(8,128)(2,1)S(1)}, u32[]{:S(2)}, u32[]{:S(2)}) collective-permute-start(bf16[4,128,256]{2,1,0:T(8,128)(2,1)S(1)} %gather_fusion.2), channel_id=1, source_target_pairs={{0,1},{1,2},{2,3},{3,4},{4,5},{5,6},{6,7},{7,8},{8,9},{9,10},{10,1... | collective-permute-start | bytes 786440 | tf_op jit(solution)/shard_map/ppermute | solution.py:142
  47.8 22.7 %collective-permute-start.3 = (bf16[4,128,256]{2,1,0:T(8,128)(2,1)S(1)}, bf16[4,128,256]{2,1,0:T(8,128)(2,1)S(1)}, u32[]{:S(2)}, u32[]{:S(2)}) collective-permute-start(bf16[4,128,256]{2,1,0:T(8,128)(2,1)S(1)} %gather_fusion.3), channel_id=1, source_target_pairs={{1,0},{2,1},{3,2},{4,3},{5,4},{6,5},{7,6},{8,7},{9,8},{10,9},{11,1... | collective-permute-start | bytes 786440 | tf_op jit(solution)/shard_map/ppermute | solution.py:147
  71.3 11.2 %copy-start.8 = (f32[1,2048,256]{2,1,0:T(8,128)S(1)}, f32[1,2048,256]{2,1,0:T(8,128)}, u32[]{:S(2)}) copy-start(f32[1,2048,256]{2,1,0:T(8,128)} %param.13) | copy-start | bytes 6291460
  100.1 21.5 %copy-start.7 = (f32[8,128,256]{2,1,0:T(8,128)S(1)}, f32[8,128,256]{2,1,0:T(8,128)}, u32[]{:S(2)}) copy-start(f32[8,128,256]{2,1,0:T(8,128)} %shard_map.107) | copy-start | bytes 3145732
  100.1 23.2 %copy-start.12 = (bf16[2048,256]{1,0:T(8,128)(2,1)S(1)}, bf16[2048,256]{1,0:T(8,128)(2,1)}, u32[]{:S(2)}) copy-start(bf16[2048,256]{1,0:T(8,128)(2,1)} %copy-done.11) | copy-start | bytes 3145732
  121.6 1.6 copy-start.3
  121.6 2.9 %copy-start.9 = (f32[1,2048,256]{2,1,0:T(8,128)S(1)}, f32[1,2048,256]{2,1,0:T(8,128)}, u32[]{:S(2)}) copy-start(f32[1,2048,256]{2,1,0:T(8,128)} %param.13) | copy-start | bytes 6291460
  121.6 2.9 %copy-start.19 = (bf16[2,256,256]{2,1,0:T(8,128)(2,1)S(1)}, bf16[2,256,256]{2,1,0:T(8,128)(2,1)}, u32[]{:S(2)}) copy-start(bf16[2,256,256]{2,1,0:T(8,128)(2,1)} %param.12) | copy-start | bytes 786436
  121.7 12.3 %collective-permute-start.5 = (f32[4,128,256]{2,1,0:T(8,128)S(1)}, f32[4,128,256]{2,1,0:T(8,128)}, u32[]{:S(2)}, u32[]{:S(2)}) collective-permute-start(f32[4,128,256]{2,1,0:T(8,128)S(1)} %get-tuple-element.12), channel_id=1, source_target_pairs={{1,0},{2,1},{3,2},{4,3},{5,4},{6,5},{7,6},{8,7},{9,8},{10,9},{11,1... | collective-permute-start | bytes 1572872 | tf_op jit(solution)/shard_map/ppermute | solution.py:147
  121.8 15.6 %collective-permute-start.4 = (f32[4,128,256]{2,1,0:T(8,128)S(1)}, f32[4,128,256]{2,1,0:T(8,128)}, u32[]{:S(2)}, u32[]{:S(2)}) collective-permute-start(f32[4,128,256]{2,1,0:T(8,128)S(1)} %get-tuple-element.13), channel_id=1, source_target_pairs={{0,1},{1,2},{2,3},{3,4},{4,5},{5,6},{6,7},{7,8},{8,9},{9,10},{10,1... | collective-permute-start | bytes 1572872 | tf_op jit(solution)/shard_map/ppermute | solution.py:142
  158.4 21.5 %copy-start.6 = (f32[8,128,256]{2,1,0:T(8,128)S(1)}, f32[8,128,256]{2,1,0:T(8,128)}, u32[]{:S(2)}) copy-start(f32[8,128,256]{2,1,0:T(8,128)} %shard_map.110) | copy-start | bytes 3145732
  179.9 1.7 copy-start
  179.9 2.2 copy-start.16
  180.0 2.1 copy-start.10
  180.0 2.1 copy-start.13
  180.1 11.4 %collective-permute-start.7 = (f32[4,128,256]{2,1,0:T(8,128)S(1)}, f32[4,128,256]{2,1,0:T(8,128)S(1)}, u32[]{:S(2)}, u32[]{:S(2)}) collective-permute-start(f32[4,128,256]{2,1,0:T(8,128)S(1)} %get-tuple-element.10), channel_id=1, source_target_pairs={{1,0},{2,1},{3,2},{4,3},{5,4},{6,5},{7,6},{8,7},{9,8},{10,9},{11,1... | collective-permute-start | bytes 1572872 | tf_op jit(solution)/shard_map/ppermute | solution.py:147
  180.3 14.8 %collective-permute-start.6 = (f32[4,128,256]{2,1,0:T(8,128)S(1)}, f32[4,128,256]{2,1,0:T(8,128)}, u32[]{:S(2)}, u32[]{:S(2)}) collective-permute-start(f32[4,128,256]{2,1,0:T(8,128)S(1)} %get-tuple-element.11), channel_id=1, source_target_pairs={{0,1},{1,2},{2,3},{3,4},{4,5},{5,6},{6,7},{7,8},{8,9},{9,10},{10,1... | collective-permute-start | bytes 1572872 | tf_op jit(solution)/shard_map/ppermute | solution.py:142
  191.5 3.6 %copy-start.15 = (f32[4,128,256]{2,1,0:T(8,128)}, f32[4,128,256]{2,1,0:T(8,128)S(1)}, u32[]{:S(2)}) copy-start(f32[4,128,256]{2,1,0:T(8,128)S(1)} %collective-permute-done.7.upper_ref) | copy-start | bytes 1572868
  198.9 1.7 copy-start.17
  229.1 6.7 %copy-start.20 = (bf16[2,256,256]{2,1,0:T(8,128)(2,1)S(1)}, bf16[2,256,256]{2,1,0:T(8,128)(2,1)}, u32[]{:S(2)}) copy-start(bf16[2,256,256]{2,1,0:T(8,128)(2,1)} %param.12) | copy-start | bytes 786436
  231.2 23.7 %all-to-all-start.1 = ((f32[128,1,2048]{2,1,0:T(1,128)}), f32[128,1,2048]{2,1,0:T(1,128)S(1)}, u32[]{:S(2)}, u32[]{:S(2)}) async-start(f32[128,1,2048]{2,1,0:T(1,128)} %broadcast_in_dim.8), calls=%async_computation.1 | async-start | bytes 2097152 | tf_op jit(solution)/shard_map/all_to_all | solution.py:155
  235.8 2.2 copy-start.2

commit v3 on v1

--- a/solution.py
+++ b/solution.py
@@ -150,20 +150,31 @@
             current, w_message[layer_index], preferred_element_type=jnp.float32
         ).astype(jnp.bfloat16)
         message_blocks = message.reshape(blocks_here, tile_rows, width)
-        from_lower = to_upper(message_blocks[own_lists[0]], "sector")
-        from_upper = to_lower(message_blocks[own_lists[1]], "sector")
-        table = jnp.concatenate([message_blocks, from_lower, from_upper])
+        current_blocks = current.reshape(blocks_here, tile_rows, width)
+        lent_rows = jnp.concatenate(
+            [
+                to_upper(current_blocks[own_lists[0]], "sector"),
+                to_lower(current_blocks[own_lists[1]], "sector"),
+            ]
+        )
+        lent_message = jnp.dot(
+            lent_rows.reshape(-1, width), w_message[layer_index],
+            preferred_element_type=jnp.float32,
+        ).astype(jnp.bfloat16)
+        table = jnp.concatenate(
+            [message_blocks, lent_message.reshape(2 * lent, tile_rows, width)]
+        )
         aggregate = block_aggregate(slot_ids, tile_data, table)
         pre = aggregate.reshape(-1, width) + jnp.dot(
             current, w_self[layer_index], preferred_element_type=jnp.float32
         )
-        saved.append((current, pre))
+        saved.append((current, lent_rows, pre))
         current = (current.astype(jnp.float32) + jax.nn.silu(pre)).astype(jnp.bfloat16)
     grad = cotangent[0]
     message_steps = [None] * LAYERS
     self_steps = [None] * LAYERS
     for layer_index in reversed(range(LAYERS)):
-        layer_in, pre = saved[layer_index]
+        layer_in, lent_rows, pre = saved[layer_index]
         dpre = (grad * silu_grad(pre)).astype(jnp.bfloat16)
         slot_grad = block_slot_grad(
             slot_ids, tile_data, dpre.reshape(blocks_here, tile_rows, width), slot_count
@@ -174,7 +185,15 @@
             own_lists, slot_grad, lent_down_grad, lent_up_grad, blocks_here
         ).reshape(-1, width)
         self_part = jnp.dot(layer_in.T, dpre, preferred_element_type=jnp.float32)
-        message_part = jnp.dot(layer_in.T, dmessage, preferred_element_type=jnp.float32)
+        slot_rows = jnp.concatenate(
+            [layer_in.reshape(blocks_here, tile_rows, width), lent_rows]
+        ).reshape(-1, width)
+        flat_grad = slot_grad.reshape(-1, width)
+        grad_high = flat_grad.astype(jnp.bfloat16)
+        grad_low = (flat_grad - grad_high.astype(jnp.float32)).astype(jnp.bfloat16)
+        message_part = jnp.dot(
+            slot_rows.T, grad_high, preferred_element_type=jnp.float32
+        ) + jnp.dot(slot_rows.T, grad_low, preferred_element_type=jnp.float32)
         message_steps[layer_index] = message_part
         self_steps[layer_index] = self_part
         grad = grad + jnp.dot(dpre, w_self[layer_index].T, preferred_element_type=jnp.float32)

time: 179 us -> 192 us (1.073)
  waiting for transfers between devices: 44.8 us -> 32.8 us
  local copies, waits for them, and re-layouts: 15.8 us -> 24.6 us
  matrix products: 25.6 us -> 32 us
  starting transfers between devices: 23.2 us -> 28.3 us
  other arithmetic: 6.38 us -> 10.8 us
    all_to_all x1, waiting for transfers between devices: 15.1 us -> 0.01 us  [all_reduce(): return lax.all_to_all(spread, axes, 0, 0, tiled=True).reshape(x.shape)]
    dot_general x2 -> x6, matrix products: 2.96 us -> 11.1 us  [the longest x2 7.68 us: per_device(): jnp.dot(slot_rows.T, grad_low, preferred_element_type=jnp.float32)]
    ppermute x4, waiting for transfers between devices: 12.5 us -> 18.3 us  [to_lower(): return lax.ppermute(x, axis, [((i + 1) % count, i) for i in range(count)])]
    ppermute x4, starting transfers between devices: 15.6 us -> 20.1 us  [to_lower(): return lax.ppermute(x, axis, [((i + 1) % count, i) for i in range(count)])]
    gather x4 -> x8, local copies, waits for them, and re-layouts: 2.25 us -> 5.42 us  [the longest x4 2.74 us: per_device(): current_blocks[own_lists[0]]]
    unnamed x40 -> x62, local copies, waits for them, and re-layouts: 2.65 us -> 5.56 us
    ppermute x4, waiting for transfers between devices: 17.1 us -> 14.4 us  [to_upper(): return lax.ppermute(x, axis, [(i, (i + 1) % count) for i in range(count)])]
  transfers between devices with their start and end apart: 9 -> 9, of which waited for: 7 -> 7; matrix products, arithmetic and copies ran while one was open for 6% -> 9% of each run, Pallas kernels for 0% -> 2%
where the time goes in v3:
time: 192 us; the launch traced here: 191 us
  Pallas kernels  34.6 us (18%)
  waiting for transfers between devices  32.8 us (17%)
  matrix products  32 us (17%)
  starting transfers between devices  28.3 us (15%)
  blocking collectives  27.1 us (14%)
  local copies, waits for them, and re-layouts  24.6 us (13%)
  other arithmetic  10.8 us (6%)
    all_to_all x1, blocking collectives, all_reduce(): mine = lax.all_to_all(pieces, axes, 0, 0, tiled=True).sum(0)  27.1 us
    ppermute x4, starting transfers between devices, to_lower(): return lax.ppermute(x, axis, [((i + 1) % count, i) for i in range(count)])  20.1 us
    ppermute x4, waiting for transfers between devices, to_lower(): return lax.ppermute(x, axis, [((i + 1) % count, i) for i in range(count)])  18.3 us
    ppermute x4, waiting for transfers between devices, to_upper(): return lax.ppermute(x, axis, [(i, (i + 1) % count) for i in range(count)])  14.4 us
    pallas_call x2, Pallas kernels, block_slot_grad(): pl.pallas_call(slot_grad_kernel, grid_spec=pltpu.PrefetchScalarGridSpec(n...  14 us
    pallas_call x2, Pallas kernels, block_aggregate(): pl.pallas_call(aggregate_kernel, grid_spec=pltpu.PrefetchScalarGridSpec(n...  12.9 us
    dot_general x2, matrix products, per_device(): jnp.dot(current, w_self[layer_index], preferred_element_type=jnp.float32)  8.51 us
    pallas_call x2, Pallas kernels, fold_lent(): pl.pallas_call(fold_kernel, grid_spec=pltpu.PrefetchScalarGridSpec(num_sc...  7.76 us
  transfers between devices with their start and end apart: 9, of which 7 were waited for; matrix products, arithmetic and copies ran while one was open for 9% of the time, Pallas kernels for 2%

profile of v3, /device:TPU:1, one launch (start us, length us, event | category | flops | bytes accessed | tf_op | source)
XLA Modules:
  0.0 191.0 jit_solution(16122514971508133120)
XLA Ops:
  0.7 1.0 dynamic-slice_reduce_fusion.2
  1.7 1.8 gather_fusion
  3.7 2.5 %collective-permute-start = (bf16[4,128,256]{1,2,0:T(8,128)(2,1)S(1)}, bf16[4,128,256]{1,2,0:T(8,128)(2,1)S(1)}, u32[]{:S(2)}, u32[]{:S(2)}) collective-permute-start(bf16[4,128,256]{1,2,0:T(8,128)(2,1)S(1)} %copy.41), channel_id=1, source_target_pairs={{0,1},{1,2},{2,3},{3,4},{4,5},{5,6},{6,7},{7,8},{8,9},{9,10},{10,1... | collective-permute-start | bytes 786440 | tf_op jit(solution)/shard_map/ppermute | solution.py:113
  6.3 1.8 gather_fusion.1
  8.2 4.7 %collective-permute-start.1 = (bf16[4,128,256]{1,2,0:T(8,128)(2,1)S(1)}, bf16[4,128,256]{1,2,0:T(8,128)(2,1)}, u32[]{:S(2)}, u32[]{:S(2)}) collective-permute-start(bf16[4,128,256]{1,2,0:T(8,128)(2,1)S(1)} %copy.42), channel_id=1, source_target_pairs={{1,0},{2,1},{3,2},{4,3},{5,4},{6,5},{7,6},{8,7},{9,8},{10,9},{11,1... | collective-permute-start | bytes 786440 | tf_op jit(solution)/shard_map/ppermute | solution.py:118
  12.9 0.8 dynamic-slice_reduce_fusion.lists_ref
  13.7 1.3 copy.51
  16.1 0.7 collective-permute-done
  17.9 1.1 pad_maximum_fusion.9
  19.5 1.3 pad_maximum_fusion.table_ref
  20.8 6.4 %shard_map.102 = f32[16,128,256]{2,1,0:T(8,128)} custom-call(s32[16,8]{1,0:T(8,128)} %copy.44.src_ref, bf16[16,8,128,128]{3,2,1,0:T(8,128)(2,1)} %bitcast.116, bf16[24,128,256]{2,1,0:T(8,128)(2,1)} %pad_maximum_fusion.table_ref), custom_call_target="tpu_custom_call" | custom-call | tf_op jit(solution)/shard_map/pallas_call | solution.py:27
  27.2 3.7 %add_convert_fusion.1 = (bf16[2048,256]{1,0:T(8,128)(2,1)S(1)}, f32[2048,256]{1,0:T(8,128)}) fusion(bf16[1,2048,256]{2,1,0:T(8,128)(2,1)S(1)} %copy-done.5, f32[2048,256]{1,0:T(8,128)} %bitcast.131, bf16[2,256,256]{2,1,0:T(8,128)(2,1)S(1)} %copy-done.25), kind=kOutput, calls=%fused_computation.20 | convolution fusion | flops 272629760 | bytes 7471104 | tf_op jit(solution)/shard_map/dot_general | solution.py:168
  32.1 1.3 copy.52
  33.8 5.7 %collective-permute-start.3 = (bf16[4,128,256]{1,2,0:T(8,128)(2,1)S(1)}, bf16[4,128,256]{1,2,0:T(8,128)(2,1)S(1)}, u32[]{:S(2)}, u32[]{:S(2)}) collective-permute-start(bf16[4,128,256]{1,2,0:T(8,128)(2,1)S(1)} %copy.46), channel_id=1, source_target_pairs={{1,0},{2,1},{3,2},{4,3},{5,4},{6,5},{7,6},{8,7},{9,8},{10,9},{11,1... | collective-permute-start | bytes 786440 | tf_op jit(solution)/shard_map/ppermute | solution.py:118
  40.0 4.6 %collective-permute-done.2 = bf16[4,128,256]{1,2,0:T(8,128)(2,1)S(1)} collective-permute-done((bf16[4,128,256]{1,2,0:T(8,128)(2,1)S(1)}, bf16[4,128,256]{1,2,0:T(8,128)(2,1)S(1)}, u32[]{:S(2)}, u32[]{:S(2)}) %collective-permute-start.2) | collective-permute-done | bytes 262176 | tf_op jit(solution)/shard_map/ppermute | solution.py:113
  46.6 1.3 pad_maximum_fusion.1.table_ref
  47.8 6.4 %shard_map.103 = f32[16,128,256]{2,1,0:T(8,128)} custom-call(s32[16,8]{1,0:T(8,128)} %copy.44.src_ref, bf16[16,8,128,128]{3,2,1,0:T(8,128)(2,1)} %bitcast.117, bf16[24,128,256]{2,1,0:T(8,128)(2,1)} %pad_maximum_fusion.1.table_ref), custom_call_target="tpu_custom_call" | custom-call | tf_op jit(solution)/shard_map/pallas_call | solution.py:27
  54.3 4.8 %fusion.1 = (bf16[2048,256]{1,0:T(8,128)(2,1)}, bf16[1,2048,256]{2,1,0:T(8,128)(2,1)}) fusion(f32[1,2048,256]{2,1,0:T(8,128)} %param.13, bf16[2048,256]{1,0:T(8,128)(2,1)S(1)} %get-tuple-element.14, f32[2048,256]{1,0:T(8,128)} %bitcast.132, bf16[2,256,256]{2,1,0:T(8,128)(2,1)S(1)} %copy-done.26), kind=kOutput, calls=%fused_computation.16 | convolution fusion | flops 275775488 | bytes 8519680 | tf_op jit(solution)/shard_map/dot_general | solution.py:168
  59.1 6.9 %shard_map.104.slot_ref = f32[24,128,256]{2,1,0:T(8,128)} custom-call(s32[16,8]{1,0:T(8,128)} %copy.44.src_ref, bf16[16,8,128,128]{3,2,1,0:T(8,128)(2,1)} %bitcast.118, bf16[16,128,256]{2,1,0:T(8,128)(2,1)} %bitcast.123), custom_call_target="tpu_custom_call" | custom-call | tf_op jit(solution)/shard_map/pallas_call | solution.py:64
  66.0 1.4 fusion.47
  67.5 4.0 %collective-permute-start.5 = (f32[4,128,256]{2,1,0:T(8,128)S(1)}, f32[4,128,256]{2,1,0:T(8,128)S(1)}, u32[]{:S(2)}, u32[]{:S(2)}) collective-permute-start(f32[4,128,256]{2,1,0:T(8,128)S(1)} %get-tuple-element.10), channel_id=1, source_target_pairs={{1,0},{2,1},{3,2},{4,3},{5,4},{6,5},{7,6},{8,7},{9,8},{10,9},{11,1... | collective-permute-start | bytes 1572872 | tf_op jit(solution)/shard_map/ppermute | solution.py:118
  71.5 3.6 %fusion.4 = f32[256,256]{1,0:T(8,128)S(1)} fusion(f32[24,128,256]{2,1,0:T(8,128)} %shard_map.104.slot_ref, bf16[4,128,256]{1,2,0:T(8,128)(2,1)S(1)} %copy-done.23, bf16[4,128,256]{1,2,0:T(8,128)(2,1)S(1)} %copy-done.21, bf16[16,128,256]{1,2,0:T(8,128)(2,1)S(1)} %copy-done.12), kind=kOutput, calls=%fused_computation.32 | convolution fusion | flops 407371776 | bytes 4980736 | tf_op jit(solution)/shard_map/dot_general | solution.py:196
  75.2 1.3 fusion.9
  76.8 1.2 convolution_bitcast_fusion.2
  78.9 1.4 collective-permute-done.5.upper_ref
  80.3 5.2 %collective-permute-done.4.lower_ref = f32[4,128,256]{2,1,0:T(8,128)S(1)} collective-permute-done((f32[4,128,256]{2,1,0:T(8,128)S(1)}, f32[4,128,256]{2,1,0:T(8,128)S(1)}, u32[]{:S(2)}, u32[]{:S(2)}) %collective-permute-start.4) | collective-permute-done | bytes 524320 | tf_op jit(solution)/shard_map/ppermute | solution.py:113
  85.6 0.8 copy-done.15
  86.4 3.9 %shard_map.105 = bf16[16,128,256]{2,1,0:T(8,128)(2,1)} custom-call(s32[2,4]{1,0:T(2,128)} %dynamic-slice_reduce_fusion.lists_ref, f32[24,128,256]{2,1,0:T(8,128)} %shard_map.104.slot_ref, f32[4,128,256]{2,1,0:T(8,128)} %copy-done.15, f32[4,128,256]{2,1,0:T(8,128)} %copy-done.14), custom_call_target="tpu_custom_call" | custom-call | tf_op jit(solution)/shard_map/pallas_call | solution.py:94
  90.2 4.2 %multiply_convert_fusion = (bf16[2048,256]{1,0:T(8,128)(2,1)S(1)}, f32[2048,256]{1,0:T(8,128)}) fusion(f32[2048,256]{1,0:T(8,128)} %get-tuple-element.15, f32[2048,256]{1,0:T(8,128)S(1)} %convolution_add_fusion.3, bf16[2048,256]{1,0:T(8,128)(2,1)} %bitcast.137, bf16[2,256,256]{2,1,0:T(8,128)(2,1)S(1)} %copy-done.10), kind=kOutput, calls=%fused_computation.17 | convolution fusion | flops 273678336 | bytes 8519680 | tf_op jit(solution)/shard_map/dot_general | solution.py:200
  95.4 7.1 %shard_map.106.slot_ref = f32[24,128,256]{2,1,0:T(8,128)} custom-call(s32[16,8]{1,0:T(8,128)} %copy.44.src_ref, bf16[16,8,128,128]{3,2,1,0:T(8,128)(2,1)} %bitcast.119, bf16[16,128,256]{2,1,0:T(8,128)(2,1)} %bitcast.129), custom_call_target="tpu_custom_call" | custom-call | tf_op jit(solution)/shard_map/pallas_call | solution.py:64
  102.6 4.1 %fusion.5 = f32[256,256]{1,0:T(8,128)S(1)} fusion(f32[24,128,256]{2,1,0:T(8,128)} %shard_map.106.slot_ref, bf16[4,128,256]{1,2,0:T(8,128)(2,1)} %collective-permute-done.1, bf16[4,128,256]{1,2,0:T(8,128)(2,1)} %copy-done.18, bf16[16,128,256]{1,2,0:T(8,128)(2,1)} %copy.51), kind=kOutput, calls=%fused_computation.33 | convolution fusion | flops 407371776 | bytes 4980736 | tf_op jit(solution)/shard_map/dot_general | solution.py:196
  107.1 1.6 fusion.7
  108.7 1.1 pad_maximum_fusion.4
  109.8 3.2 %all_to_all.13 = f32[128,1,2048]{2,1,0:T(1,128)} reshape(f32[2,2,256,256]{3,2,1,0:T(8,128)} %pad_maximum_fusion.4) | data formatting | bytes 2097152 | tf_op jit(solution)/shard_map/all_to_all | solution.py:124
  113.1 27.1 %all_to_all.16 = f32[128,1,2048]{2,1,0:T(1,128)} all-to-all(f32[128,1,2048]{2,1,0:T(1,128)} %all_to_all.13), channel_id=1, replica_groups=mesh['dp'=8,'sector'=16] {'dp','sector'}, dimensions={0} | all-to-all | bytes 2097152 | tf_op jit(solution)/shard_map/all_to_all | solution.py:124
  140.1 1.8 reduce_sum.9
  142.0 1.5 broadcast_in_dim.8
  143.5 5.6 %all-to-all-start.1 = ((f32[128,1,2048]{2,1,0:T(1,128)}), f32[128,1,2048]{2,1,0:T(1,128)}, u32[]{:S(2)}, u32[]{:S(2)}) async-start(f32[128,1,2048]{2,1,0:T(1,128)} %broadcast_in_dim.8), calls=%async_computation.1 | async-start | bytes 2097152 | tf_op jit(solution)/shard_map/all_to_all | solution.py:126
  149.2 5.8 %collective-permute-start.7 = (f32[4,128,256]{2,1,0:T(8,128)S(1)}, f32[4,128,256]{2,1,0:T(8,128)S(1)}, u32[]{:S(2)}, u32[]{:S(2)}) collective-permute-start(f32[4,128,256]{2,1,0:T(8,128)S(1)} %get-tuple-element.8), channel_id=1, source_target_pairs={{1,0},{2,1},{3,2},{4,3},{5,4},{6,5},{7,6},{8,7},{9,8},{10,9},{11,1... | collective-permute-start | bytes 1572872 | tf_op jit(solution)/shard_map/ppermute | solution.py:118
  155.0 2.1 %convolution_add_fusion.1 = f32[2048,256]{1,0:T(8,128)S(1)} fusion(f32[2048,256]{1,0:T(8,128)} %get-tuple-element.17, bf16[2048,256]{1,0:T(8,128)(2,1)S(1)} %copy-done.8, bf16[2,256,256]{2,1,0:T(8,128)(2,1)S(1)} %copy-done.28), kind=kOutput, calls=%fused_computation.8 | convolution fusion | flops 268959744 | bytes 5373952 | tf_op jit(solution)/shard_map/dot_general | solution.py:199
  157.0 16.6 %collective-permute-done.7.upper_ref = f32[4,128,256]{2,1,0:T(8,128)S(1)} collective-permute-done((f32[4,128,256]{2,1,0:T(8,128)S(1)}, f32[4,128,256]{2,1,0:T(8,128)S(1)}, u32[]{:S(2)}, u32[]{:S(2)}) %collective-permute-start.7) | collective-permute-done | bytes 524320 | tf_op jit(solution)/shard_map/ppermute | solution.py:118
  173.7 3.9 %collective-permute-done.6.lower_ref = f32[4,128,256]{2,1,0:T(8,128)S(1)} collective-permute-done((f32[4,128,256]{2,1,0:T(8,128)S(1)}, f32[4,128,256]{2,1,0:T(8,128)S(1)}, u32[]{:S(2)}, u32[]{:S(2)}) %collective-permute-start.6) | collective-permute-done | bytes 524320 | tf_op jit(solution)/shard_map/ppermute | solution.py:113
  177.5 0.8 copy-done.17
  178.3 3.9 %shard_map.107 = bf16[16,128,256]{2,1,0:T(8,128)(2,1)} custom-call(s32[2,4]{1,0:T(2,128)} %dynamic-slice_reduce_fusion.lists_ref, f32[24,128,256]{2,1,0:T(8,128)} %shard_map.106.slot_ref, f32[4,128,256]{2,1,0:T(8,128)} %copy-done.17, f32[4,128,256]{2,1,0:T(8,128)} %copy-done.16), custom_call_target="tpu_custom_call" | custom-call | tf_op jit(solution)/shard_map/pallas_call | solution.py:94
  182.2 3.0 %fusion = f32[1,2048,256]{2,1,0:T(8,128)} fusion(f32[2048,256]{1,0:T(8,128)S(1)} %convolution_add_fusion.1, bf16[2048,256]{1,0:T(8,128)(2,1)} %bitcast.130, bf16[2,256,256]{2,1,0:T(8,128)(2,1)S(1)} %copy-done.10), kind=kOutput, calls=%fused_computation.7 | convolution fusion | flops 268959744 | bytes 5373952 | tf_op jit(solution)/shard_map/dot_general | solution.py:200
  185.2 4.1 %fusion.18 = (f32[64,2048]{1,0:T(8,128)S(1)}, f32[64,2048]{1,0:T(8,128)S(1)}) fusion(f32[128,1,2048]{2,1,0:T(1,128)} %all-to-all-done.1), kind=kLoop, calls=%fused_computation.50 | loop fusion | flops 262144 | bytes 2097152 | tf_op jit(solution)/shard_map/mul | solution.py:209
  189.3 0.9 mul.48
  190.2 0.9 mul.46
  (88 shorter events, 10.0 us)
Async XLA Ops:
  0.6 12.3 %copy-start.29 = (s32[1,16,2,4]{1,3,2,0:T(4,128)S(1)}, s32[1,16,2,4]{1,3,2,0:T(4,128)}, u32[]{:S(2)}) copy-start(s32[1,16,2,4]{1,3,2,0:T(4,128)} %param.10) | copy-start | bytes 1540
  0.6 13.0 %copy-start.5 = (bf16[1,2048,256]{2,1,0:T(8,128)(2,1)S(1)}, bf16[1,2048,256]{2,1,0:T(8,128)(2,1)}, u32[]{:S(2)}) copy-start(bf16[1,2048,256]{2,1,0:T(8,128)(2,1)} %param.7) | copy-start | bytes 3145732
  1.7 13.3 %copy-start.30 = (s32[1,16,8]{1,2,0:T(8,128)S(1)}, s32[1,16,8]{1,2,0:T(8,128)}, u32[]{:S(2)}) copy-start(s32[1,16,8]{1,2,0:T(8,128)} %param.9) | copy-start | bytes 1540
  1.7 14.0 %copy-start.10 = (bf16[2,256,256]{2,1,0:T(8,128)(2,1)S(1)}, bf16[2,256,256]{2,1,0:T(8,128)(2,1)}, u32[]{:S(2)}) copy-start(bf16[2,256,256]{2,1,0:T(8,128)(2,1)} %param.11) | copy-start | bytes 786436
  3.7 13.1 %collective-permute-start = (bf16[4,128,256]{1,2,0:T(8,128)(2,1)S(1)}, bf16[4,128,256]{1,2,0:T(8,128)(2,1)S(1)}, u32[]{:S(2)}, u32[]{:S(2)}) collective-permute-start(bf16[4,128,256]{1,2,0:T(8,128)(2,1)S(1)} %copy.41), channel_id=1, source_target_pairs={{0,1},{1,2},{2,3},{3,4},{4,5},{5,6},{6,7},{7,8},{8,9},{9,10},{10,1... | collective-permute-start | bytes 786440 | tf_op jit(solution)/shard_map/ppermute | solution.py:113
  8.2 9.7 %collective-permute-start.1 = (bf16[4,128,256]{1,2,0:T(8,128)(2,1)S(1)}, bf16[4,128,256]{1,2,0:T(8,128)(2,1)}, u32[]{:S(2)}, u32[]{:S(2)}) collective-permute-start(bf16[4,128,256]{1,2,0:T(8,128)(2,1)S(1)} %copy.42), channel_id=1, source_target_pairs={{1,0},{2,1},{3,2},{4,3},{5,4},{6,5},{7,6},{8,7},{9,8},{10,9},{11,1... | collective-permute-start | bytes 786440 | tf_op jit(solution)/shard_map/ppermute | solution.py:118
  16.8 0.7 copy-start.18
  20.8 6.4 %copy-start.25 = (bf16[2,256,256]{2,1,0:T(8,128)(2,1)S(1)}, bf16[2,256,256]{2,1,0:T(8,128)(2,1)}, u32[]{:S(2)}) copy-start(bf16[2,256,256]{2,1,0:T(8,128)(2,1)} %param.12) | copy-start | bytes 786436
  30.9 23.3 %copy-start.2 = (bf16[2048,256]{1,0:T(8,128)(2,1)}, bf16[2048,256]{1,0:T(8,128)(2,1)S(1)}, u32[]{:S(2)}) copy-start(bf16[2048,256]{1,0:T(8,128)(2,1)S(1)} %get-tuple-element.14) | copy-start | bytes 3145732
  33.8 10.8 %collective-permute-start.2 = (bf16[4,128,256]{1,2,0:T(8,128)(2,1)S(1)}, bf16[4,128,256]{1,2,0:T(8,128)(2,1)S(1)}, u32[]{:S(2)}, u32[]{:S(2)}) collective-permute-start(bf16[4,128,256]{1,2,0:T(8,128)(2,1)S(1)} %copy.45), channel_id=1, source_target_pairs={{0,1},{1,2},{2,3},{3,4},{4,5},{5,6},{6,7},{7,8},{8,9},{9,10},{10,1... | collective-permute-start | bytes 786440 | tf_op jit(solution)/shard_map/ppermute | solution.py:113
  33.8 10.8 %collective-permute-start.3 = (bf16[4,128,256]{1,2,0:T(8,128)(2,1)S(1)}, bf16[4,128,256]{1,2,0:T(8,128)(2,1)S(1)}, u32[]{:S(2)}, u32[]{:S(2)}) collective-permute-start(bf16[4,128,256]{1,2,0:T(8,128)(2,1)S(1)} %copy.46), channel_id=1, source_target_pairs={{1,0},{2,1},{3,2},{4,3},{5,4},{6,5},{7,6},{8,7},{9,8},{10,9},{11,1... | collective-permute-start | bytes 786440 | tf_op jit(solution)/shard_map/ppermute | solution.py:118
  44.6 0.7 copy-start.20
  45.3 0.7 copy-start.22
  47.8 6.4 %copy-start.26 = (bf16[2,256,256]{2,1,0:T(8,128)(2,1)S(1)}, bf16[2,256,256]{2,1,0:T(8,128)(2,1)}, u32[]{:S(2)}) copy-start(bf16[2,256,256]{2,1,0:T(8,128)(2,1)} %param.12) | copy-start | bytes 786436
  66.0 5.4 %copy-start.12 = (bf16[16,128,256]{1,2,0:T(8,128)(2,1)S(1)}, bf16[16,128,256]{1,2,0:T(8,128)(2,1)}, u32[]{:S(2)}) copy-start(bf16[16,128,256]{1,2,0:T(8,128)(2,1)} %copy.52) | copy-start | bytes 3145732
  66.0 5.4 %copy-start.21 = (bf16[4,128,256]{1,2,0:T(8,128)(2,1)S(1)}, bf16[4,128,256]{1,2,0:T(8,128)(2,1)}, u32[]{:S(2)}) copy-start(bf16[4,128,256]{1,2,0:T(8,128)(2,1)} %copy-done.20) | copy-start | bytes 786436
  66.0 5.4 %copy-start.23 = (bf16[4,128,256]{1,2,0:T(8,128)(2,1)S(1)}, bf16[4,128,256]{1,2,0:T(8,128)(2,1)}, u32[]{:S(2)}) copy-start(bf16[4,128,256]{1,2,0:T(8,128)(2,1)} %copy-done.22) | copy-start | bytes 786436
  67.5 12.8 %collective-permute-start.5 = (f32[4,128,256]{2,1,0:T(8,128)S(1)}, f32[4,128,256]{2,1,0:T(8,128)S(1)}, u32[]{:S(2)}, u32[]{:S(2)}) collective-permute-start(f32[4,128,256]{2,1,0:T(8,128)S(1)} %get-tuple-element.10), channel_id=1, source_target_pairs={{1,0},{2,1},{3,2},{4,3},{5,4},{6,5},{7,6},{8,7},{9,8},{10,9},{11,1... | collective-permute-start | bytes 1572872 | tf_op jit(solution)/shard_map/ppermute | solution.py:118
  71.4 3.7 %copy-start.1 = (f32[24,128,256]{2,1,0:T(8,128)S(1)}, f32[24,128,256]{2,1,0:T(8,128)}, u32[]{:S(2)}) copy-start(f32[24,128,256]{2,1,0:T(8,128)} %shard_map.104.slot_ref) | copy-start | bytes 9437188
  71.4 14.1 %collective-permute-start.4 = (f32[4,128,256]{2,1,0:T(8,128)S(1)}, f32[4,128,256]{2,1,0:T(8,128)S(1)}, u32[]{:S(2)}, u32[]{:S(2)}) collective-permute-start(f32[4,128,256]{2,1,0:T(8,128)S(1)} %get-tuple-element.11), channel_id=1, source_target_pairs={{0,1},{1,2},{2,3},{3,4},{4,5},{5,6},{6,7},{7,8},{8,9},{9,10},{10,1... | collective-permute-start | bytes 1572872 | tf_op jit(solution)/shard_map/ppermute | solution.py:113
  75.2 1.3 copy-start.3
  75.2 1.6 copy-start.4
  76.8 1.7 copy-start.9
  76.8 1.7 copy-start.27
  80.3 5.2 %copy-start.14 = (f32[4,128,256]{2,1,0:T(8,128)}, f32[4,128,256]{2,1,0:T(8,128)S(1)}, u32[]{:S(2)}) copy-start(f32[4,128,256]{2,1,0:T(8,128)S(1)} %collective-permute-done.5.upper_ref) | copy-start | bytes 1572868
  85.6 0.8 copy-start.15
  90.2 4.2 %copy-start.6 = (bf16[1,2048,256]{2,1,0:T(8,128)(2,1)S(1)}, bf16[1,2048,256]{2,1,0:T(8,128)(2,1)}, u32[]{:S(2)}) copy-start(bf16[1,2048,256]{2,1,0:T(8,128)(2,1)} %param.7) | copy-start | bytes 3145732
  94.4 1.0 copy-start.7
  95.4 7.1 %copy-start.13 = (f32[1,256,256]{2,1,0:T(8,128)S(1)}, f32[1,256,256]{2,1,0:T(8,128)}, u32[]{:S(2)}) copy-start(f32[1,256,256]{2,1,0:T(8,128)} %convolution_bitcast_fusion.2) | copy-start | bytes 786436
  102.5 4.2 %copy-start = (f32[24,128,256]{2,1,0:T(8,128)S(1)}, f32[24,128,256]{2,1,0:T(8,128)}, u32[]{:S(2)}) copy-start(f32[24,128,256]{2,1,0:T(8,128)} %shard_map.106.slot_ref) | copy-start | bytes 9437188
  102.5 4.5 %copy-start.11 = (bf16[16,128,256]{1,2,0:T(8,128)(2,1)S(1)}, bf16[16,128,256]{1,2,0:T(8,128)(2,1)}, u32[]{:S(2)}) copy-start(bf16[16,128,256]{1,2,0:T(8,128)(2,1)} %copy.51) | copy-start | bytes 3145732
  102.6 4.5 %copy-start.19 = (bf16[4,128,256]{1,2,0:T(8,128)(2,1)S(1)}, bf16[4,128,256]{1,2,0:T(8,128)(2,1)}, u32[]{:S(2)}) copy-start(bf16[4,128,256]{1,2,0:T(8,128)(2,1)} %copy-done.18) | copy-start | bytes 786436
  107.1 1.6 copy-start.24
  143.5 41.7 %all-to-all-start.1 = ((f32[128,1,2048]{2,1,0:T(1,128)}), f32[128,1,2048]{2,1,0:T(1,128)}, u32[]{:S(2)}, u32[]{:S(2)}) async-start(f32[128,1,2048]{2,1,0:T(1,128)} %broadcast_in_dim.8), calls=%async_computation.1 | async-start | bytes 2097152 | tf_op jit(solution)/shard_map/all_to_all | solution.py:126
  149.1 5.9 %copy-start.8 = (bf16[2048,256]{1,0:T(8,128)(2,1)S(1)}, bf16[2048,256]{1,0:T(8,128)(2,1)}, u32[]{:S(2)}) copy-start(bf16[2048,256]{1,0:T(8,128)(2,1)} %copy-done.7) | copy-start | bytes 3145732
  149.1 5.8 %copy-start.28 = (bf16[2,256,256]{2,1,0:T(8,128)(2,1)S(1)}, bf16[2,256,256]{2,1,0:T(8,128)(2,1)}, u32[]{:S(2)}) copy-start(bf16[2,256,256]{2,1,0:T(8,128)(2,1)} %param.12) | copy-start | bytes 786436
  149.2 24.4 %collective-permute-start.7 = (f32[4,128,256]{2,1,0:T(8,128)S(1)}, f32[4,128,256]{2,1,0:T(8,128)S(1)}, u32[]{:S(2)}, u32[]{:S(2)}) collective-permute-start(f32[4,128,256]{2,1,0:T(8,128)S(1)} %get-tuple-element.8), channel_id=1, source_target_pairs={{1,0},{2,1},{3,2},{4,3},{5,4},{6,5},{7,6},{8,7},{9,8},{10,9},{11,1... | collective-permute-start | bytes 1572872 | tf_op jit(solution)/shard_map/ppermute | solution.py:118
  155.0 22.6 %collective-permute-start.6 = (f32[4,128,256]{2,1,0:T(8,128)S(1)}, f32[4,128,256]{2,1,0:T(8,128)S(1)}, u32[]{:S(2)}, u32[]{:S(2)}) collective-permute-start(f32[4,128,256]{2,1,0:T(8,128)S(1)} %get-tuple-element.9), channel_id=1, source_target_pairs={{0,1},{1,2},{2,3},{3,4},{4,5},{5,6},{6,7},{7,8},{8,9},{9,10},{10,1... | collective-permute-start | bytes 1572872 | tf_op jit(solution)/shard_map/ppermute | solution.py:113
  173.6 3.9 %copy-start.16 = (f32[4,128,256]{2,1,0:T(8,128)}, f32[4,128,256]{2,1,0:T(8,128)S(1)}, u32[]{:S(2)}) copy-start(f32[4,128,256]{2,1,0:T(8,128)S(1)} %collective-permute-done.7.upper_ref) | copy-start | bytes 1572868
  177.5 0.8 copy-start.17

commit v4 on v1

--- a/solution.py
+++ b/solution.py
@@ -9,34 +9,47 @@
 GROUP = 8
 
 
-def aggregate_kernel(src_ref, tiles_ref, table_ref, out_ref):
+def layer_kernel(src_ref, tiles_ref, table_ref, hits_ref, weight_ref, pre_ref, out_ref):
     step = pl.program_id(0)
+    listed = tiles_ref.shape[1]
     for i in range(GROUP):
         block = step * GROUP + i
-        acc = None
-        for k in range(tiles_ref.shape[1]):
-            slot = src_ref[block, k]
-            part = jnp.dot(tiles_ref[i, k], table_ref[slot], preferred_element_type=jnp.float32)
-            acc = part if acc is None else acc + part
-        out_ref[i] = acc
-
-
-def block_aggregate(slot_ids, tile_data, table):
+        lhs = jnp.concatenate([tiles_ref[i, k] for k in range(listed)], axis=1)
+        rhs = jnp.concatenate(
+            [table_ref[src_ref[block, k]] for k in range(listed)], axis=0
+        )
+        rows = hits_ref[i]
+        pre = jnp.dot(lhs, rhs, preferred_element_type=jnp.float32) + jnp.dot(
+            rows, weight_ref[...], preferred_element_type=jnp.float32
+        )
+        pre_ref[i] = pre
+        out_ref[i] = (rows.astype(jnp.float32) + pre * jax.nn.sigmoid(pre)).astype(
+            out_ref.dtype
+        )
+
+
+def block_layer(slot_ids, tile_data, table, hit_blocks, weight):
     blocks, listed, rows, _ = tile_data.shape
     width = table.shape[-1]
+    block_spec = pl.BlockSpec((GROUP, rows, width), lambda g, src: (g, 0, 0))
     return pl.pallas_call(
-        aggregate_kernel,
+        layer_kernel,
         grid_spec=pltpu.PrefetchScalarGridSpec(
             num_scalar_prefetch=1,
             grid=(blocks // GROUP,),
             in_specs=[
                 pl.BlockSpec((GROUP, listed, rows, rows), lambda g, src: (g, 0, 0, 0)),
                 pl.BlockSpec(table.shape, lambda g, src: (0, 0, 0)),
+                block_spec,
+                pl.BlockSpec(weight.shape, lambda g, src: (0, 0)),
             ],
-            out_specs=pl.BlockSpec((GROUP, rows, width), lambda g, src: (g, 0, 0)),
+            out_specs=[block_spec, block_spec],
         ),
-        out_shape=jax.ShapeDtypeStruct((blocks, rows, width), jnp.float32),
-    )(slot_ids, tile_data, table)
+        out_shape=[
+            jax.ShapeDtypeStruct((blocks, rows, width), jnp.float32),
+            jax.ShapeDtypeStruct((blocks, rows, width), hit_blocks.dtype),
+        ],
+    )(slot_ids, tile_data, table, hit_blocks, weight)
 
 
 def slot_grad_kernel(src_ref, tiles_ref, dpre_ref, out_ref):
@@ -153,12 +166,12 @@
         from_lower = to_upper(message_blocks[own_lists[0]], "sector")
         from_upper = to_lower(message_blocks[own_lists[1]], "sector")
         table = jnp.concatenate([message_blocks, from_lower, from_upper])
-        aggregate = block_aggregate(slot_ids, tile_data, table)
-        pre = aggregate.reshape(-1, width) + jnp.dot(
-            current, w_self[layer_index], preferred_element_type=jnp.float32
-        )
-        saved.append((current, pre))
-        current = (current.astype(jnp.float32) + jax.nn.silu(pre)).astype(jnp.bfloat16)
+        pre, following = block_layer(
+            slot_ids, tile_data, table, current.reshape(message_blocks.shape),
+            w_self[layer_index],
+        )
+        saved.append((current, pre.reshape(-1, width)))
+        current = following.reshape(-1, width)
     grad = cotangent[0]
     message_steps = [None] * LAYERS
     self_steps = [None] * LAYERS

time: 179 us -> 174 us (0.972)
  matrix products: 25.6 us -> 18.3 us
  other arithmetic: 6.38 us -> 10.5 us
    dot_general x2 -> x0, matrix products: 8.64 us -> none  [per_device(): jnp.dot(current, w_self[layer_index], preferred_element_type=jnp.float32)]
    convert_element_type x0 -> x2, other arithmetic: none -> 4.18 us  [per_device(): dpre = (grad * silu_grad(pre)).astype(jnp.bfloat16)]
  transfers between devices with their start and end apart: 9 -> 9, of which waited for: 7 -> 7; matrix products, arithmetic and copies ran while one was open for 6% -> 7% of each run, Pallas kernels for 0% -> 0%
where the time goes in v4:
time: 174 us
  waiting for transfers between devices  44 us (25%)
  Pallas kernels  33.8 us (19%)
  blocking collectives  27.7 us (16%)
  starting transfers between devices  23.2 us (13%)
  matrix products  18.3 us (11%)
  local copies, waits for them, and re-layouts  15.5 us (9%)
  other arithmetic  10.5 us (6%)
    all_to_all x1, blocking collectives, all_reduce(): mine = lax.all_to_all(pieces, axes, 0, 0, tiled=True).sum(0)  27.7 us
    ppermute x4, waiting for transfers between devices, to_upper(): return lax.ppermute(x, axis, [(i, (i + 1) % count) for i in range(count)])  16.4 us
    ppermute x4, starting transfers between devices, to_lower(): return lax.ppermute(x, axis, [((i + 1) % count, i) for i in range(count)])  15.5 us
    all_to_all x1, waiting for transfers between devices, all_reduce(): return lax.all_to_all(spread, axes, 0, 0, tiled=True).reshape(x.shape)  15.1 us
    pallas_call x2, Pallas kernels, block_slot_grad(): pl.pallas_call(slot_grad_kernel, grid_spec=pltpu.PrefetchScalarGridSpec(n...  13.9 us
    ppermute x4, waiting for transfers between devices, to_lower(): return lax.ppermute(x, axis, [((i + 1) % count, i) for i in range(count)])  12.5 us
    pallas_call x2, Pallas kernels, block_layer(): pl.pallas_call(layer_kernel, grid_spec=pltpu.PrefetchScalarGridSpec(num_s...  12.2 us
    pallas_call x2, Pallas kernels, fold_lent(): pl.pallas_call(fold_kernel, grid_spec=pltpu.PrefetchScalarGridSpec(num_sc...  7.68 us
  transfers between devices with their start and end apart: 9, of which 7 were waited for; matrix products, arithmetic and copies ran while one was open for 7% of the time, Pallas kernels for 0%

profile of v4, /device:TPU:1, one launch (start us, length us, event | category | flops | bytes accessed | tf_op | source)
XLA Modules:
  0.0 173.9 jit_solution(16383578678497583899)
XLA Ops:
  0.7 1.0 dynamic-slice_reduce_fusion.2
  1.6 1.7 convolution_convert_fusion.1
  3.3 0.6 gather_fusion
  3.9 2.5 %collective-permute-start = (bf16[4,128,256]{2,1,0:T(8,128)(2,1)S(1)}, bf16[4,128,256]{2,1,0:T(8,128)(2,1)S(1)}, u32[]{:S(2)}, u32[]{:S(2)}) collective-permute-start(bf16[4,128,256]{2,1,0:T(8,128)(2,1)S(1)} %gather_fusion), channel_id=1, source_target_pairs={{0,1},{1,2},{2,3},{3,4},{4,5},{5,6},{6,7},{7,8},{8,9},{9,10},{10,1... | collective-permute-start | bytes 786440 | tf_op jit(solution)/shard_map/ppermute | solution.py:126
  7.0 4.7 %collective-permute-start.1 = (bf16[4,128,256]{2,1,0:T(8,128)(2,1)S(1)}, bf16[4,128,256]{2,1,0:T(8,128)(2,1)S(1)}, u32[]{:S(2)}, u32[]{:S(2)}) collective-permute-start(bf16[4,128,256]{2,1,0:T(8,128)(2,1)S(1)} %gather_fusion.1), channel_id=1, source_target_pairs={{1,0},{2,1},{3,2},{4,3},{5,4},{6,5},{7,6},{8,7},{9,8},{10,9},{11,1... | collective-permute-start | bytes 786440 | tf_op jit(solution)/shard_map/ppermute | solution.py:131
  11.6 0.7 copy.27.src_ref
  12.3 0.7 slice_bitcast_fusion
  13.0 4.0 %collective-permute-done = bf16[4,128,256]{2,1,0:T(8,128)(2,1)S(1)} collective-permute-done((bf16[4,128,256]{2,1,0:T(8,128)(2,1)S(1)}, bf16[4,128,256]{2,1,0:T(8,128)(2,1)S(1)}, u32[]{:S(2)}, u32[]{:S(2)}) %collective-permute-start) | collective-permute-done | bytes 262176 | tf_op jit(solution)/shard_map/ppermute | solution.py:126
  17.0 1.4 pad_maximum_fusion.table_ref
  18.3 6.1 %shard_map.102 = (f32[16,128,256]{2,1,0:T(8,128)}, bf16[16,128,256]{2,1,0:T(8,128)(2,1)}) custom-call(s32[16,8]{1,0:T(8,128)} %copy.27.src_ref, bf16[16,8,128,128]{3,2,1,0:T(8,128)(2,1)} %bitcast.120, bf16[24,128,256]{2,1,0:T(8,128)(2,1)} %pad_maximum_fusion.table_ref, bf16[16,128,256]{2,1,0:T(8,128)(2,1)} %bitcast.125, ...), custom_call_target="tpu_custom_call" | custom-call | tf_op jit(solution)/shard_map/pallas_call | solution.py:35
  24.4 1.7 convolution_convert_fusion
  27.3 5.2 %collective-permute-start.3 = (bf16[4,128,256]{2,1,0:T(8,128)(2,1)S(1)}, bf16[4,128,256]{2,1,0:T(8,128)(2,1)S(1)}, u32[]{:S(2)}, u32[]{:S(2)}) collective-permute-start(bf16[4,128,256]{2,1,0:T(8,128)(2,1)S(1)} %gather_fusion.3), channel_id=1, source_target_pairs={{1,0},{2,1},{3,2},{4,3},{5,4},{6,5},{7,6},{8,7},{9,8},{10,9},{11,1... | collective-permute-start | bytes 786440 | tf_op jit(solution)/shard_map/ppermute | solution.py:131
  32.6 0.7 dynamic-slice_reduce_fusion.lists_ref
  33.3 4.3 %collective-permute-done.2 = bf16[4,128,256]{2,1,0:T(8,128)(2,1)S(1)} collective-permute-done((bf16[4,128,256]{2,1,0:T(8,128)(2,1)S(1)}, bf16[4,128,256]{2,1,0:T(8,128)(2,1)S(1)}, u32[]{:S(2)}, u32[]{:S(2)}) %collective-permute-start.2) | collective-permute-done | bytes 262176 | tf_op jit(solution)/shard_map/ppermute | solution.py:126
  37.6 1.3 pad_maximum_fusion.1.table_ref
  39.0 6.1 %shard_map.103 = (f32[16,128,256]{2,1,0:T(8,128)}, bf16[16,128,256]{2,1,0:T(8,128)(2,1)}) custom-call(s32[16,8]{1,0:T(8,128)} %copy.27.src_ref, bf16[16,8,128,128]{3,2,1,0:T(8,128)(2,1)} %bitcast.121, bf16[24,128,256]{2,1,0:T(8,128)(2,1)} %pad_maximum_fusion.1.table_ref, bf16[16,128,256]{2,1,0:T(8,128)(2,1)} %get-tuple-element.8.hits_ref, ...), custom_call_target="tpu_custom_call" | custom-call | tf_op jit(solution)/shard_map/pallas_call | solution.py:35
  45.0 2.4 %fusion.14 = bf16[1,2048,256]{2,1,0:T(8,128)(2,1)S(1)} fusion(f32[1,2048,256]{2,1,0:T(8,128)S(1)} %copy-done, f32[1,2048,256]{2,1,0:T(8,128)} %bitcast.129), kind=kLoop, calls=%fused_computation.28 | loop fusion | flops 4718592 | bytes 5242880 | tf_op jit(solution)/shard_map/convert_element_type | solution.py:180
  47.5 1.8 %multiply_convert_fusion.dpre_ref = bf16[16,128,256]{2,1,0:T(8,128)(2,1)} fusion(f32[16,128,256]{2,1,0:T(8,128)S(1)} %bitcast.124, f32[16,128,256]{2,1,0:T(8,128)S(1)} %copy-done.4), kind=kLoop, calls=%fused_computation.29 | loop fusion | flops 4718592 | bytes 5242880 | tf_op jit(solution)/shard_map/convert_element_type | solution.py:180
  49.2 7.0 %shard_map.104.slot_ref = f32[24,128,256]{2,1,0:T(8,128)} custom-call(s32[16,8]{1,0:T(8,128)} %copy.27.src_ref, bf16[16,8,128,128]{3,2,1,0:T(8,128)(2,1)} %bitcast.122, bf16[16,128,256]{2,1,0:T(8,128)(2,1)} %multiply_convert_fusion.dpre_ref), custom_call_target="tpu_custom_call" | custom-call | tf_op jit(solution)/shard_map/pallas_call | solution.py:77
  56.2 1.4 fusion.33
  57.6 4.6 %collective-permute-start.5 = (f32[4,128,256]{2,1,0:T(8,128)S(1)}, f32[4,128,256]{2,1,0:T(8,128)S(1)}, u32[]{:S(2)}, u32[]{:S(2)}) collective-permute-start(f32[4,128,256]{2,1,0:T(8,128)S(1)} %get-tuple-element.18), channel_id=1, source_target_pairs={{1,0},{2,1},{3,2},{4,3},{5,4},{6,5},{7,6},{8,7},{9,8},{10,9},{11,1... | collective-permute-start | bytes 1572872 | tf_op jit(solution)/shard_map/ppermute | solution.py:131
  62.2 1.2 convolution_bitcast_fusion
  63.5 1.8 %convolution_add_fusion.3 = f32[2048,256]{1,0:T(8,128)} fusion(f32[1,2048,256]{2,1,0:T(8,128)S(1)} %copy-done, bf16[1,2048,256]{2,1,0:T(8,128)(2,1)S(1)} %fusion.14, bf16[2,256,256]{2,1,0:T(8,128)(2,1)S(1)} %copy-done.9), kind=kOutput, calls=%fused_computation.8 | convolution fusion | flops 268959744 | bytes 5373952 | tf_op jit(solution)/shard_map/dot_general | solution.py:193
  65.3 5.8 %collective-permute-done.5.upper_ref = f32[4,128,256]{2,1,0:T(8,128)S(1)} collective-permute-done((f32[4,128,256]{2,1,0:T(8,128)S(1)}, f32[4,128,256]{2,1,0:T(8,128)S(1)}, u32[]{:S(2)}, u32[]{:S(2)}) %collective-permute-start.5) | collective-permute-done | bytes 524320 | tf_op jit(solution)/shard_map/ppermute | solution.py:131
  71.1 0.8 copy-done.14
  71.9 4.6 %collective-permute-done.4.lower_ref = f32[4,128,256]{2,1,0:T(8,128)} collective-permute-done((f32[4,128,256]{2,1,0:T(8,128)S(1)}, f32[4,128,256]{2,1,0:T(8,128)}, u32[]{:S(2)}, u32[]{:S(2)}) %collective-permute-start.4) | collective-permute-done | bytes 524320 | tf_op jit(solution)/shard_map/ppermute | solution.py:126
  76.5 3.8 %shard_map.105 = bf16[16,128,256]{2,1,0:T(8,128)(2,1)} custom-call(s32[2,4]{1,0:T(2,128)} %dynamic-slice_reduce_fusion.lists_ref, f32[24,128,256]{2,1,0:T(8,128)} %shard_map.104.slot_ref, f32[4,128,256]{2,1,0:T(8,128)} %collective-permute-done.4.lower_ref, f32[4,128,256]{2,1,0:T(8,128)} %copy-done.14), custom_call_target="tpu_custom_call" | custom-call | tf_op jit(solution)/shard_map/pallas_call | solution.py:107
  80.3 4.5 %fusion.7 = (bf16[2048,256]{1,0:T(8,128)(2,1)}, f32[2048,256]{1,0:T(8,128)}) fusion(f32[16,128,256]{2,1,0:T(8,128)} %get-tuple-element.11, f32[2048,256]{1,0:T(8,128)S(1)} %copy-done.7, bf16[2048,256]{1,0:T(8,128)(2,1)} %bitcast.138, bf16[2,256,256]{2,1,0:T(8,128)(2,1)S(1)} %copy-done.11), kind=kOutput, calls=%fused_computation.19 | convolution fusion | flops 273678336 | bytes 8519680 | tf_op jit(solution)/shard_map/dot_general | solution.py:194
  84.8 7.0 %shard_map.106.slot_ref = f32[24,128,256]{2,1,0:T(8,128)} custom-call(s32[16,8]{1,0:T(8,128)} %copy.27.src_ref, bf16[16,8,128,128]{3,2,1,0:T(8,128)(2,1)} %bitcast.123, bf16[16,128,256]{2,1,0:T(8,128)(2,1)} %bitcast.126), custom_call_target="tpu_custom_call" | custom-call | tf_op jit(solution)/shard_map/pallas_call | solution.py:77
  91.8 1.4 fusion.32
  93.3 1.0 collective-permute-start.7
  95.4 1.2 convolution_bitcast_fusion.2
  96.6 6.7 %collective-permute-done.7.upper_ref = f32[4,128,256]{2,1,0:T(8,128)S(1)} collective-permute-done((f32[4,128,256]{2,1,0:T(8,128)S(1)}, f32[4,128,256]{2,1,0:T(8,128)S(1)}, u32[]{:S(2)}, u32[]{:S(2)}) %collective-permute-start.7) | collective-permute-done | bytes 524320 | tf_op jit(solution)/shard_map/ppermute | solution.py:131
  103.3 0.8 copy-done.13
  104.1 3.6 %collective-permute-done.6.lower_ref = f32[4,128,256]{2,1,0:T(8,128)} collective-permute-done((f32[4,128,256]{2,1,0:T(8,128)S(1)}, f32[4,128,256]{2,1,0:T(8,128)}, u32[]{:S(2)}, u32[]{:S(2)}) %collective-permute-start.6) | collective-permute-done | bytes 524320 | tf_op jit(solution)/shard_map/ppermute | solution.py:126
  107.7 3.8 %shard_map.107 = bf16[16,128,256]{2,1,0:T(8,128)(2,1)} custom-call(s32[2,4]{1,0:T(2,128)} %dynamic-slice_reduce_fusion.lists_ref, f32[24,128,256]{2,1,0:T(8,128)} %shard_map.106.slot_ref, f32[4,128,256]{2,1,0:T(8,128)} %collective-permute-done.6.lower_ref, f32[4,128,256]{2,1,0:T(8,128)} %copy-done.13), custom_call_target="tpu_custom_call" | custom-call | tf_op jit(solution)/shard_map/pallas_call | solution.py:107
  111.5 1.7 convolution_bitcast_fusion.3
  113.7 2.1 %all_to_all.13 = f32[128,1,2048]{2,1,0:T(1,128)} reshape(f32[2,2,256,256]{3,2,1,0:T(8,128)S(1)} %copy.33) | data formatting | bytes 2097152 | tf_op jit(solution)/shard_map/all_to_all | solution.py:137
  115.8 27.7 %all_to_all.16 = f32[128,1,2048]{2,1,0:T(1,128)S(1)} all-to-all(f32[128,1,2048]{2,1,0:T(1,128)} %all_to_all.13), channel_id=1, replica_groups=mesh['dp'=8,'sector'=16] {'dp','sector'}, dimensions={0} | all-to-all | bytes 2097152 | tf_op jit(solution)/shard_map/all_to_all | solution.py:137
  143.5 0.6 reduce_sum.9
  144.1 1.5 broadcast_in_dim.5
  145.7 4.5 %all-to-all-start.1 = ((f32[128,1,2048]{2,1,0:T(1,128)}), f32[128,1,2048]{2,1,0:T(1,128)S(1)}, u32[]{:S(2)}, u32[]{:S(2)}) async-start(f32[128,1,2048]{2,1,0:T(1,128)} %broadcast_in_dim.5), calls=%async_computation.1 | async-start | bytes 2097152 | tf_op jit(solution)/shard_map/all_to_all | solution.py:139
  150.2 2.2 %convolution_add_fusion.1 = f32[2048,256]{1,0:T(8,128)S(1)} fusion(f32[2048,256]{1,0:T(8,128)} %get-tuple-element.23, bf16[2048,256]{1,0:T(8,128)(2,1)S(1)} %copy-done.2, bf16[2,256,256]{2,1,0:T(8,128)(2,1)S(1)} %copy-done.9), kind=kOutput, calls=%fused_computation.6 | convolution fusion | flops 268959744 | bytes 5373952 | tf_op jit(solution)/shard_map/dot_general | solution.py:193
  152.4 1.8 %fusion = f32[1,2048,256]{2,1,0:T(8,128)} fusion(f32[2048,256]{1,0:T(8,128)S(1)} %convolution_add_fusion.1, bf16[2048,256]{1,0:T(8,128)(2,1)S(1)} %bitcast.128, bf16[2,256,256]{2,1,0:T(8,128)(2,1)S(1)} %copy-done.12), kind=kOutput, calls=%fused_computation.5 | convolution fusion | flops 268959744 | bytes 5373952 | tf_op jit(solution)/shard_map/dot_general | solution.py:194
  154.2 15.1 %all-to-all-done.1 = f32[128,1,2048]{2,1,0:T(1,128)S(1)} async-done(((f32[128,1,2048]{2,1,0:T(1,128)}), f32[128,1,2048]{2,1,0:T(1,128)S(1)}, u32[]{:S(2)}, u32[]{:S(2)}) %all-to-all-start.1) | async-done | bytes 1048608 | tf_op jit(solution)/shard_map/all_to_all | solution.py:139
  169.3 2.9 %fusion.20 = (f32[64,2048]{1,0:T(8,128)S(1)}, f32[64,2048]{1,0:T(8,128)S(1)}) fusion(f32[128,1,2048]{2,1,0:T(1,128)S(1)} %all-to-all-done.1), kind=kLoop, calls=%fused_computation.43 | loop fusion | flops 262144 | bytes 2097152 | tf_op jit(solution)/shard_map/mul | solution.py:203
  172.2 0.9 mul.69
  173.0 0.9 mul.67
  (52 shorter events, 3.3 us)
Async XLA Ops:
  0.6 11.0 %copy-start.18 = (s32[1,16,8]{1,2,0:T(8,128)S(1)}, s32[1,16,8]{1,2,0:T(8,128)}, u32[]{:S(2)}) copy-start(s32[1,16,8]{1,2,0:T(8,128)} %param.9) | copy-start | bytes 1540
  0.6 11.7 %copy-start.9 = (bf16[2,256,256]{2,1,0:T(8,128)(2,1)S(1)}, bf16[2,256,256]{2,1,0:T(8,128)(2,1)}, u32[]{:S(2)}) copy-start(bf16[2,256,256]{2,1,0:T(8,128)(2,1)} %param.12) | copy-start | bytes 786436
  3.9 13.1 %collective-permute-start = (bf16[4,128,256]{2,1,0:T(8,128)(2,1)S(1)}, bf16[4,128,256]{2,1,0:T(8,128)(2,1)S(1)}, u32[]{:S(2)}, u32[]{:S(2)}) collective-permute-start(bf16[4,128,256]{2,1,0:T(8,128)(2,1)S(1)} %gather_fusion), channel_id=1, source_target_pairs={{0,1},{1,2},{2,3},{3,4},{4,5},{5,6},{6,7},{7,8},{8,9},{9,10},{10,1... | collective-permute-start | bytes 786440 | tf_op jit(solution)/shard_map/ppermute | solution.py:126
  7.0 10.0 %collective-permute-start.1 = (bf16[4,128,256]{2,1,0:T(8,128)(2,1)S(1)}, bf16[4,128,256]{2,1,0:T(8,128)(2,1)S(1)}, u32[]{:S(2)}, u32[]{:S(2)}) collective-permute-start(bf16[4,128,256]{2,1,0:T(8,128)(2,1)S(1)} %gather_fusion.1), channel_id=1, source_target_pairs={{1,0},{2,1},{3,2},{4,3},{5,4},{6,5},{7,6},{8,7},{9,8},{10,9},{11,1... | collective-permute-start | bytes 786440 | tf_op jit(solution)/shard_map/ppermute | solution.py:131
  18.3 6.1 %copy-start.10 = (bf16[2,256,256]{2,1,0:T(8,128)(2,1)S(1)}, bf16[2,256,256]{2,1,0:T(8,128)(2,1)}, u32[]{:S(2)}) copy-start(bf16[2,256,256]{2,1,0:T(8,128)(2,1)} %param.11) | copy-start | bytes 786436
  24.4 8.1 %copy-start.17 = (s32[1,16,2,4]{1,3,2,0:T(4,128)S(1)}, s32[1,16,2,4]{1,3,2,0:T(4,128)}, u32[]{:S(2)}) copy-start(s32[1,16,2,4]{1,3,2,0:T(4,128)} %param.10) | copy-start | bytes 1540
  27.2 10.4 %collective-permute-start.2 = (bf16[4,128,256]{2,1,0:T(8,128)(2,1)S(1)}, bf16[4,128,256]{2,1,0:T(8,128)(2,1)S(1)}, u32[]{:S(2)}, u32[]{:S(2)}) collective-permute-start(bf16[4,128,256]{2,1,0:T(8,128)(2,1)S(1)} %gather_fusion.2), channel_id=1, source_target_pairs={{0,1},{1,2},{2,3},{3,4},{4,5},{5,6},{6,7},{7,8},{8,9},{9,10},{10,1... | collective-permute-start | bytes 786440 | tf_op jit(solution)/shard_map/ppermute | solution.py:126
  27.3 10.3 %collective-permute-start.3 = (bf16[4,128,256]{2,1,0:T(8,128)(2,1)S(1)}, bf16[4,128,256]{2,1,0:T(8,128)(2,1)S(1)}, u32[]{:S(2)}, u32[]{:S(2)}) collective-permute-start(bf16[4,128,256]{2,1,0:T(8,128)(2,1)S(1)} %gather_fusion.3), channel_id=1, source_target_pairs={{1,0},{2,1},{3,2},{4,3},{5,4},{6,5},{7,6},{8,7},{9,8},{10,9},{11,1... | collective-permute-start | bytes 786440 | tf_op jit(solution)/shard_map/ppermute | solution.py:131
  38.9 6.1 %copy-start = (f32[1,2048,256]{2,1,0:T(8,128)S(1)}, f32[1,2048,256]{2,1,0:T(8,128)}, u32[]{:S(2)}) copy-start(f32[1,2048,256]{2,1,0:T(8,128)} %param.13) | copy-start | bytes 6291460
  45.0 2.4 %copy-start.4 = (f32[16,128,256]{2,1,0:T(8,128)S(1)}, f32[16,128,256]{2,1,0:T(8,128)}, u32[]{:S(2)}) copy-start(f32[16,128,256]{2,1,0:T(8,128)} %get-tuple-element.10) | copy-start | bytes 6291460
  56.2 6.0 %copy-start.5 = (bf16[16,128,256]{2,1,0:T(8,128)(2,1)S(1)}, bf16[16,128,256]{2,1,0:T(8,128)(2,1)}, u32[]{:S(2)}) copy-start(bf16[16,128,256]{2,1,0:T(8,128)(2,1)} %get-tuple-element.8.hits_ref) | copy-start | bytes 3145732
  57.6 13.5 %collective-permute-start.5 = (f32[4,128,256]{2,1,0:T(8,128)S(1)}, f32[4,128,256]{2,1,0:T(8,128)S(1)}, u32[]{:S(2)}, u32[]{:S(2)}) collective-permute-start(f32[4,128,256]{2,1,0:T(8,128)S(1)} %get-tuple-element.18), channel_id=1, source_target_pairs={{1,0},{2,1},{3,2},{4,3},{5,4},{6,5},{7,6},{8,7},{9,8},{10,9},{11,1... | collective-permute-start | bytes 1572872 | tf_op jit(solution)/shard_map/ppermute | solution.py:131
  62.2 14.2 %collective-permute-start.4 = (f32[4,128,256]{2,1,0:T(8,128)S(1)}, f32[4,128,256]{2,1,0:T(8,128)}, u32[]{:S(2)}, u32[]{:S(2)}) collective-permute-start(f32[4,128,256]{2,1,0:T(8,128)S(1)} %get-tuple-element.19), channel_id=1, source_target_pairs={{0,1},{1,2},{2,3},{3,4},{4,5},{5,6},{6,7},{7,8},{8,9},{9,10},{10,1... | collective-permute-start | bytes 1572872 | tf_op jit(solution)/shard_map/ppermute | solution.py:126
  65.3 15.0 %copy-start.7 = (f32[2048,256]{1,0:T(8,128)S(1)}, f32[2048,256]{1,0:T(8,128)}, u32[]{:S(2)}) copy-start(f32[2048,256]{1,0:T(8,128)} %convolution_add_fusion.3) | copy-start | bytes 6291460
  65.3 15.0 %copy-start.11 = (bf16[2,256,256]{2,1,0:T(8,128)(2,1)S(1)}, bf16[2,256,256]{2,1,0:T(8,128)(2,1)}, u32[]{:S(2)}) copy-start(bf16[2,256,256]{2,1,0:T(8,128)(2,1)} %param.11) | copy-start | bytes 786436
  71.1 0.8 copy-start.14
  91.8 3.0 %copy-start.1 = (bf16[1,2048,256]{2,1,0:T(8,128)(2,1)S(1)}, bf16[1,2048,256]{2,1,0:T(8,128)(2,1)}, u32[]{:S(2)}) copy-start(bf16[1,2048,256]{2,1,0:T(8,128)(2,1)} %param.7) | copy-start | bytes 3145732
  91.8 3.0 %copy-start.2 = (bf16[2048,256]{1,0:T(8,128)(2,1)S(1)}, bf16[2048,256]{1,0:T(8,128)(2,1)}, u32[]{:S(2)}) copy-start(bf16[2048,256]{1,0:T(8,128)(2,1)} %get-tuple-element.22) | copy-start | bytes 3145732
  91.8 3.5 %copy-start.15 = (f32[1,256,256]{1,2,0:T(8,128)S(1)}, f32[1,256,256]{1,2,0:T(8,128)}, u32[]{:S(2)}) copy-start(f32[1,256,256]{1,2,0:T(8,128)} %convolution_bitcast_fusion) | copy-start | bytes 786436
  93.2 2.1 %copy-start.6 = (bf16[16,128,256]{2,1,0:T(8,128)(2,1)S(1)}, bf16[16,128,256]{2,1,0:T(8,128)(2,1)}, u32[]{:S(2)}) copy-start(bf16[16,128,256]{2,1,0:T(8,128)(2,1)} %get-tuple-element.8.hits_ref) | copy-start | bytes 3145732
  93.3 2.1 %copy-start.8 = (bf16[16,128,256]{2,1,0:T(8,128)(2,1)S(1)}, bf16[16,128,256]{2,1,0:T(8,128)(2,1)}, u32[]{:S(2)}) copy-start(bf16[16,128,256]{2,1,0:T(8,128)(2,1)} %shard_map.105) | copy-start | bytes 3145732
  93.3 10.0 %collective-permute-start.7 = (f32[4,128,256]{2,1,0:T(8,128)S(1)}, f32[4,128,256]{2,1,0:T(8,128)S(1)}, u32[]{:S(2)}, u32[]{:S(2)}) collective-permute-start(f32[4,128,256]{2,1,0:T(8,128)S(1)} %get-tuple-element.16), channel_id=1, source_target_pairs={{1,0},{2,1},{3,2},{4,3},{5,4},{6,5},{7,6},{8,7},{9,8},{10,9},{11,1... | collective-permute-start | bytes 1572872 | tf_op jit(solution)/shard_map/ppermute | solution.py:131
  94.3 13.3 %collective-permute-start.6 = (f32[4,128,256]{2,1,0:T(8,128)S(1)}, f32[4,128,256]{2,1,0:T(8,128)}, u32[]{:S(2)}, u32[]{:S(2)}) collective-permute-start(f32[4,128,256]{2,1,0:T(8,128)S(1)} %get-tuple-element.17), channel_id=1, source_target_pairs={{0,1},{1,2},{2,3},{3,4},{4,5},{5,6},{6,7},{7,8},{8,9},{9,10},{10,1... | collective-permute-start | bytes 1572872 | tf_op jit(solution)/shard_map/ppermute | solution.py:126
  103.3 0.8 copy-start.13
  111.5 1.7 %copy-start.16 = (f32[1,256,256]{1,2,0:T(8,128)S(1)}, f32[1,256,256]{1,2,0:T(8,128)}, u32[]{:S(2)}) copy-start(f32[1,256,256]{1,2,0:T(8,128)} %convolution_bitcast_fusion.2) | copy-start | bytes 786436
  145.7 23.7 %all-to-all-start.1 = ((f32[128,1,2048]{2,1,0:T(1,128)}), f32[128,1,2048]{2,1,0:T(1,128)S(1)}, u32[]{:S(2)}, u32[]{:S(2)}) async-start(f32[128,1,2048]{2,1,0:T(1,128)} %broadcast_in_dim.5), calls=%async_computation.1 | async-start | bytes 2097152 | tf_op jit(solution)/shard_map/all_to_all | solution.py:139
  150.2 2.2 %copy-start.3 = (bf16[16,128,256]{2,1,0:T(8,128)(2,1)S(1)}, bf16[16,128,256]{2,1,0:T(8,128)(2,1)}, u32[]{:S(2)}) copy-start(bf16[16,128,256]{2,1,0:T(8,128)(2,1)} %shard_map.107) | copy-start | bytes 3145732
  150.2 2.2 %copy-start.12 = (bf16[2,256,256]{2,1,0:T(8,128)(2,1)S(1)}, bf16[2,256,256]{2,1,0:T(8,128)(2,1)}, u32[]{:S(2)}) copy-start(bf16[2,256,256]{2,1,0:T(8,128)(2,1)} %param.11) | copy-start | bytes 786436

commit v5 on v4

--- a/solution.py
+++ b/solution.py
@@ -131,10 +131,11 @@
     return lax.ppermute(x, axis, [((i + 1) % count, i) for i in range(count)])
 
 
-def all_reduce(x, axes):
+def all_reduce(x, axes, scale):
     count = lax.axis_size(axes)
-    pieces = x.reshape(count, -1)
-    mine = lax.all_to_all(pieces, axes, 0, 0, tiled=True).sum(0)
+    width = x.shape[-1]
+    pieces = x.reshape(count, -1, width)
+    mine = lax.all_to_all(pieces, axes, 0, 0, tiled=True).sum(0) * scale
     spread = jnp.broadcast_to(mine[None], (count,) + mine.shape)
     return lax.all_to_all(spread, axes, 0, 0, tiled=True).reshape(x.shape)
 
@@ -196,11 +197,10 @@
         )
     message_total = jnp.stack(message_steps)
     self_total = jnp.stack(self_steps)
-    both = all_reduce(jnp.stack([message_total, self_total]), ("dp", "sector"))
-    message_total, self_total = both[0], both[1]
     total_rows = blocks_here * tile_rows * lax.axis_size(("dp", "sector"))
     scale = 1.0 / jnp.sqrt(jnp.float32(total_rows))
-    return (current[None], grad[None], message_total * scale, self_total * scale)
+    both = all_reduce(jnp.stack([message_total, self_total]), ("dp", "sector"), scale)
+    return (current[None], grad[None], both[0], both[1])
 
 
 def solution(mesh):

time: 174 us -> 168 us (0.966)
  local copies, waits for them, and re-layouts: 15.5 us -> 12 us
    mul x1, other arithmetic: 2.85 us -> 0.01 us  [all_reduce(): mine = lax.all_to_all(pieces, axes, 0, 0, tiled=True).sum(0) * scale]
    all_to_all x1 -> x0, local copies, waits for them, and re-layouts: 2.05 us -> none  [all_reduce(): mine = lax.all_to_all(pieces, axes, 0, 0, tiled=True).sum(0)]
    mul x2 -> x0, local copies, waits for them, and re-layouts: 1.75 us -> none  [the longest x1 0.88 us: per_device(): self_total * scale]
  transfers between devices with their start and end apart: 9 -> 9, of which waited for: 7 -> 7; matrix products, arithmetic and copies ran while one was open for 7% -> 6% of each run, Pallas kernels for 0% -> 0%
where the time goes in v5:
time: 168 us
  waiting for transfers between devices  44.6 us (27%)
  Pallas kernels  33.7 us (20%)
  blocking collectives  27.5 us (16%)
  starting transfers between devices  23.2 us (14%)
  matrix products  16.9 us (10%)
  local copies, waits for them, and re-layouts  12 us (7%)
  other arithmetic  8.97 us (5%)
    all_to_all x1, blocking collectives, all_reduce(): mine = lax.all_to_all(pieces, axes, 0, 0, tiled=True).sum(0) * scale  27.5 us
    ppermute x4, waiting for transfers between devices, to_upper(): return lax.ppermute(x, axis, [(i, (i + 1) % count) for i in range(count)])  16.4 us
    ppermute x4, starting transfers between devices, to_lower(): return lax.ppermute(x, axis, [((i + 1) % count, i) for i in range(count)])  15.6 us
    all_to_all x1, waiting for transfers between devices, all_reduce(): return lax.all_to_all(spread, axes, 0, 0, tiled=True).reshape(x.shape)  15.1 us
    pallas_call x2, Pallas kernels, block_slot_grad(): pl.pallas_call(slot_grad_kernel, grid_spec=pltpu.PrefetchScalarGridSpec(n...  13.9 us
    ppermute x4, waiting for transfers between devices, to_lower(): return lax.ppermute(x, axis, [((i + 1) % count, i) for i in range(count)])  13.1 us
    pallas_call x2, Pallas kernels, block_layer(): pl.pallas_call(layer_kernel, grid_spec=pltpu.PrefetchScalarGridSpec(num_s...  12.2 us
    pallas_call x2, Pallas kernels, fold_lent(): pl.pallas_call(fold_kernel, grid_spec=pltpu.PrefetchScalarGridSpec(num_sc...  7.68 us
  transfers between devices with their start and end apart: 9, of which 7 were waited for; matrix products, arithmetic and copies ran while one was open for 6% of the time, Pallas kernels for 0%

profile of v5, /device:TPU:1, one launch (start us, length us, event | category | flops | bytes accessed | tf_op | source)
XLA Modules:
  0.0 167.9 jit_solution(10133460616474116256)
XLA Ops:
  0.7 1.0 dynamic-slice_reduce_fusion.2
  1.6 1.7 convolution_convert_fusion.1
  3.3 0.6 gather_fusion
  3.9 2.5 %collective-permute-start = (bf16[4,128,256]{2,1,0:T(8,128)(2,1)S(1)}, bf16[4,128,256]{2,1,0:T(8,128)(2,1)S(1)}, u32[]{:S(2)}, u32[]{:S(2)}) collective-permute-start(bf16[4,128,256]{2,1,0:T(8,128)(2,1)S(1)} %gather_fusion), channel_id=1, source_target_pairs={{0,1},{1,2},{2,3},{3,4},{4,5},{5,6},{6,7},{7,8},{8,9},{9,10},{10,1... | collective-permute-start | bytes 786440 | tf_op jit(solution)/shard_map/ppermute | solution.py:126
  6.4 0.6 gather_fusion.1
  7.0 4.7 %collective-permute-start.1 = (bf16[4,128,256]{2,1,0:T(8,128)(2,1)S(1)}, bf16[4,128,256]{2,1,0:T(8,128)(2,1)S(1)}, u32[]{:S(2)}, u32[]{:S(2)}) collective-permute-start(bf16[4,128,256]{2,1,0:T(8,128)(2,1)S(1)} %gather_fusion.1), channel_id=1, source_target_pairs={{1,0},{2,1},{3,2},{4,3},{5,4},{6,5},{7,6},{8,7},{9,8},{10,9},{11,1... | collective-permute-start | bytes 786440 | tf_op jit(solution)/shard_map/ppermute | solution.py:131
  11.6 0.7 copy.17.src_ref
  12.3 0.7 slice_bitcast_fusion
  13.0 3.9 %collective-permute-done = bf16[4,128,256]{2,1,0:T(8,128)(2,1)S(1)} collective-permute-done((bf16[4,128,256]{2,1,0:T(8,128)(2,1)S(1)}, bf16[4,128,256]{2,1,0:T(8,128)(2,1)S(1)}, u32[]{:S(2)}, u32[]{:S(2)}) %collective-permute-start) | collective-permute-done | bytes 262176 | tf_op jit(solution)/shard_map/ppermute | solution.py:126
  17.0 1.4 pad_maximum_fusion.table_ref
  18.3 6.1 %shard_map.102 = (f32[16,128,256]{2,1,0:T(8,128)}, bf16[16,128,256]{2,1,0:T(8,128)(2,1)}) custom-call(s32[16,8]{1,0:T(8,128)} %copy.17.src_ref, bf16[16,8,128,128]{3,2,1,0:T(8,128)(2,1)} %bitcast.121, bf16[24,128,256]{2,1,0:T(8,128)(2,1)} %pad_maximum_fusion.table_ref, bf16[16,128,256]{2,1,0:T(8,128)(2,1)} %bitcast.137, ...), custom_call_target="tpu_custom_call" | custom-call | tf_op jit(solution)/shard_map/pallas_call | solution.py:35
  24.4 1.7 convolution_convert_fusion
  26.1 0.6 gather_fusion.3
  26.7 0.6 gather_fusion.2
  27.3 5.2 %collective-permute-start.3 = (bf16[4,128,256]{2,1,0:T(8,128)(2,1)S(1)}, bf16[4,128,256]{2,1,0:T(8,128)(2,1)S(1)}, u32[]{:S(2)}, u32[]{:S(2)}) collective-permute-start(bf16[4,128,256]{2,1,0:T(8,128)(2,1)S(1)} %gather_fusion.3), channel_id=1, source_target_pairs={{1,0},{2,1},{3,2},{4,3},{5,4},{6,5},{7,6},{8,7},{9,8},{10,9},{11,1... | collective-permute-start | bytes 786440 | tf_op jit(solution)/shard_map/ppermute | solution.py:131
  32.6 0.8 dynamic-slice_reduce_fusion.lists_ref
  33.3 4.3 %collective-permute-done.2 = bf16[4,128,256]{2,1,0:T(8,128)(2,1)S(1)} collective-permute-done((bf16[4,128,256]{2,1,0:T(8,128)(2,1)S(1)}, bf16[4,128,256]{2,1,0:T(8,128)(2,1)S(1)}, u32[]{:S(2)}, u32[]{:S(2)}) %collective-permute-start.2) | collective-permute-done | bytes 262176 | tf_op jit(solution)/shard_map/ppermute | solution.py:126
  37.6 1.3 pad_maximum_fusion.1.table_ref
  39.0 6.1 %shard_map.103 = (f32[16,128,256]{2,1,0:T(8,128)}, bf16[16,128,256]{2,1,0:T(8,128)(2,1)}) custom-call(s32[16,8]{1,0:T(8,128)} %copy.17.src_ref, bf16[16,8,128,128]{3,2,1,0:T(8,128)(2,1)} %bitcast.122, bf16[24,128,256]{2,1,0:T(8,128)(2,1)} %pad_maximum_fusion.1.table_ref, bf16[16,128,256]{2,1,0:T(8,128)(2,1)} %get-tuple-element.8.hits_ref, ...), custom_call_target="tpu_custom_call" | custom-call | tf_op jit(solution)/shard_map/pallas_call | solution.py:35
  45.0 3.4 %fusion.14 = bf16[1,2048,256]{2,1,0:T(8,128)(2,1)} fusion(f32[1,2048,256]{2,1,0:T(8,128)S(1)} %copy-done, f32[1,2048,256]{2,1,0:T(8,128)} %bitcast.128), kind=kLoop, calls=%fused_computation.28 | loop fusion | flops 4718592 | bytes 5242880 | tf_op jit(solution)/shard_map/convert_element_type | solution.py:181
  48.5 1.7 %multiply_convert_fusion.dpre_ref = bf16[16,128,256]{2,1,0:T(8,128)(2,1)} fusion(f32[16,128,256]{2,1,0:T(8,128)S(1)} %bitcast.125, f32[16,128,256]{2,1,0:T(8,128)S(1)} %copy-done.3), kind=kLoop, calls=%fused_computation.29 | loop fusion | flops 4718592 | bytes 5242880 | tf_op jit(solution)/shard_map/convert_element_type | solution.py:181
  50.2 6.9 %shard_map.104.slot_ref = f32[24,128,256]{2,1,0:T(8,128)} custom-call(s32[16,8]{1,0:T(8,128)} %copy.17.src_ref, bf16[16,8,128,128]{3,2,1,0:T(8,128)(2,1)} %bitcast.123, bf16[16,128,256]{2,1,0:T(8,128)(2,1)} %multiply_convert_fusion.dpre_ref), custom_call_target="tpu_custom_call" | custom-call | tf_op jit(solution)/shard_map/pallas_call | solution.py:77
  57.1 1.5 fusion.31
  58.6 4.6 %collective-permute-start.5 = (f32[4,128,256]{2,1,0:T(8,128)S(1)}, f32[4,128,256]{2,1,0:T(8,128)S(1)}, u32[]{:S(2)}, u32[]{:S(2)}) collective-permute-start(f32[4,128,256]{2,1,0:T(8,128)S(1)} %get-tuple-element.16), channel_id=1, source_target_pairs={{1,0},{2,1},{3,2},{4,3},{5,4},{6,5},{7,6},{8,7},{9,8},{10,9},{11,1... | collective-permute-start | bytes 1572872 | tf_op jit(solution)/shard_map/ppermute | solution.py:131
  63.8 1.8 %convolution_add_fusion.3 = f32[2048,256]{1,0:T(8,128)} fusion(f32[1,2048,256]{2,1,0:T(8,128)S(1)} %copy-done, bf16[1,2048,256]{2,1,0:T(8,128)(2,1)S(1)} %copy-done.2, bf16[2,256,256]{2,1,0:T(8,128)(2,1)S(1)} %copy-done.11), kind=kOutput, calls=%fused_computation.8 | convolution fusion | flops 268959744 | bytes 5373952 | tf_op jit(solution)/shard_map/dot_general | solution.py:194
  65.6 6.5 %collective-permute-done.5.upper_ref = f32[4,128,256]{2,1,0:T(8,128)S(1)} collective-permute-done((f32[4,128,256]{2,1,0:T(8,128)S(1)}, f32[4,128,256]{2,1,0:T(8,128)S(1)}, u32[]{:S(2)}, u32[]{:S(2)}) %collective-permute-start.5) | collective-permute-done | bytes 524320 | tf_op jit(solution)/shard_map/ppermute | solution.py:131
  72.1 0.8 copy-done.16
  72.9 4.6 %collective-permute-done.4.lower_ref = f32[4,128,256]{2,1,0:T(8,128)} collective-permute-done((f32[4,128,256]{2,1,0:T(8,128)S(1)}, f32[4,128,256]{2,1,0:T(8,128)}, u32[]{:S(2)}, u32[]{:S(2)}) %collective-permute-start.4) | collective-permute-done | bytes 524320 | tf_op jit(solution)/shard_map/ppermute | solution.py:126
  77.5 3.8 %shard_map.105 = bf16[16,128,256]{2,1,0:T(8,128)(2,1)} custom-call(s32[2,4]{1,0:T(2,128)} %dynamic-slice_reduce_fusion.lists_ref, f32[24,128,256]{2,1,0:T(8,128)} %shard_map.104.slot_ref, f32[4,128,256]{2,1,0:T(8,128)} %collective-permute-done.4.lower_ref, f32[4,128,256]{2,1,0:T(8,128)} %copy-done.16), custom_call_target="tpu_custom_call" | custom-call | tf_op jit(solution)/shard_map/pallas_call | solution.py:107
  81.3 4.5 %fusion.7 = (bf16[2048,256]{1,0:T(8,128)(2,1)}, f32[2048,256]{1,0:T(8,128)}) fusion(f32[16,128,256]{2,1,0:T(8,128)} %get-tuple-element.11, f32[2048,256]{1,0:T(8,128)S(1)} %copy-done.9, bf16[2048,256]{1,0:T(8,128)(2,1)} %bitcast.138, bf16[2,256,256]{2,1,0:T(8,128)(2,1)} %param.11), kind=kOutput, calls=%fused_computation.19 | convolution fusion | flops 273678336 | bytes 8519680 | tf_op jit(solution)/shard_map/dot_general | solution.py:195
  85.9 6.9 %shard_map.106.slot_ref = f32[24,128,256]{2,1,0:T(8,128)} custom-call(s32[16,8]{1,0:T(8,128)} %copy.17.src_ref, bf16[16,8,128,128]{3,2,1,0:T(8,128)(2,1)} %bitcast.124, bf16[16,128,256]{2,1,0:T(8,128)(2,1)} %bitcast.135), custom_call_target="tpu_custom_call" | custom-call | tf_op jit(solution)/shard_map/pallas_call | solution.py:77
  92.8 1.4 fusion.30
  94.2 1.0 collective-permute-start.7
  95.3 0.5 collective-permute-start.6
  95.8 0.5 convolution_bitcast_fusion.1
  96.3 0.8 maximum_bitcast_fusion.1
  97.6 6.6 %collective-permute-done.7.upper_ref = f32[4,128,256]{2,1,0:T(8,128)S(1)} collective-permute-done((f32[4,128,256]{2,1,0:T(8,128)S(1)}, f32[4,128,256]{2,1,0:T(8,128)S(1)}, u32[]{:S(2)}, u32[]{:S(2)}) %collective-permute-start.7) | collective-permute-done | bytes 524320 | tf_op jit(solution)/shard_map/ppermute | solution.py:131
  104.2 0.8 copy-done.15
  105.0 3.6 %collective-permute-done.6.lower_ref = f32[4,128,256]{2,1,0:T(8,128)} collective-permute-done((f32[4,128,256]{2,1,0:T(8,128)S(1)}, f32[4,128,256]{2,1,0:T(8,128)}, u32[]{:S(2)}, u32[]{:S(2)}) %collective-permute-start.6) | collective-permute-done | bytes 524320 | tf_op jit(solution)/shard_map/ppermute | solution.py:126
  108.6 3.8 %shard_map.107 = bf16[16,128,256]{2,1,0:T(8,128)(2,1)} custom-call(s32[2,4]{1,0:T(2,128)} %dynamic-slice_reduce_fusion.lists_ref, f32[24,128,256]{2,1,0:T(8,128)} %shard_map.106.slot_ref, f32[4,128,256]{2,1,0:T(8,128)} %collective-permute-done.6.lower_ref, f32[4,128,256]{2,1,0:T(8,128)} %copy-done.15), custom_call_target="tpu_custom_call" | custom-call | tf_op jit(solution)/shard_map/pallas_call | solution.py:107
  112.4 1.8 %convolution_bitcast_fusion.3 = f32[1,256,256]{2,1,0:T(8,128)S(1)} fusion(bf16[2048,256]{1,0:T(8,128)(2,1)} %bitcast.139, bf16[1,2048,256]{2,1,0:T(8,128)(2,1)S(1)} %copy-done.5), kind=kOutput, calls=%fused_computation.35 | convolution fusion | flops 268435456 | bytes 2359296 | tf_op jit(solution)/shard_map/dot_general | solution.py:191
  114.4 27.5 %all_to_all.10 = f32[128,8,256]{2,1,0:T(8,128)S(1)} all-to-all(f32[128,8,256]{2,1,0:T(8,128)S(1)} %bitcast.136), channel_id=1, replica_groups=mesh['dp'=8,'sector'=16] {'dp','sector'}, dimensions={0} | all-to-all | bytes 2097152 | tf_op jit(solution)/shard_map/all_to_all | solution.py:138
  142.1 1.1 broadcast_in_dim.5
  143.2 4.5 %all-to-all-start.1 = ((f32[128,8,256]{2,1,0:T(8,128)}), f32[128,8,256]{2,1,0:T(8,128)S(1)}, u32[]{:S(2)}, u32[]{:S(2)}) async-start(f32[128,8,256]{2,1,0:T(8,128)} %broadcast_in_dim.5), calls=%async_computation.1 | async-start | bytes 2097152 | tf_op jit(solution)/shard_map/all_to_all | solution.py:140
  147.7 2.2 %convolution_add_fusion.1 = f32[2048,256]{1,0:T(8,128)S(1)} fusion(f32[2048,256]{1,0:T(8,128)} %get-tuple-element.23, bf16[2048,256]{1,0:T(8,128)(2,1)S(1)} %copy-done.4, bf16[2,256,256]{2,1,0:T(8,128)(2,1)S(1)} %copy-done.12), kind=kOutput, calls=%fused_computation.6 | convolution fusion | flops 268959744 | bytes 5373952 | tf_op jit(solution)/shard_map/dot_general | solution.py:194
  149.9 1.8 %fusion = f32[1,2048,256]{2,1,0:T(8,128)} fusion(f32[2048,256]{1,0:T(8,128)S(1)} %convolution_add_fusion.1, bf16[2048,256]{1,0:T(8,128)(2,1)S(1)} %bitcast.140, bf16[2,256,256]{2,1,0:T(8,128)(2,1)S(1)} %copy-done.14), kind=kOutput, calls=%fused_computation.5 | convolution fusion | flops 268959744 | bytes 5373952 | tf_op jit(solution)/shard_map/dot_general | solution.py:195
  151.7 15.1 %all-to-all-done.1 = f32[128,8,256]{2,1,0:T(8,128)S(1)} async-done(((f32[128,8,256]{2,1,0:T(8,128)}), f32[128,8,256]{2,1,0:T(8,128)S(1)}, u32[]{:S(2)}, u32[]{:S(2)}) %all-to-all-start.1) | async-done | bytes 1048608 | tf_op jit(solution)/shard_map/all_to_all | solution.py:140
  166.8 1.0 fusion.32
  (49 shorter events, 1.4 us)
Async XLA Ops:
  0.6 11.0 %copy-start.18 = (s32[1,16,8]{1,2,0:T(8,128)S(1)}, s32[1,16,8]{1,2,0:T(8,128)}, u32[]{:S(2)}) copy-start(s32[1,16,8]{1,2,0:T(8,128)} %param.9) | copy-start | bytes 1540
  0.6 11.7 %copy-start.10 = (bf16[2,256,256]{2,1,0:T(8,128)(2,1)S(1)}, bf16[2,256,256]{2,1,0:T(8,128)(2,1)}, u32[]{:S(2)}) copy-start(bf16[2,256,256]{2,1,0:T(8,128)(2,1)} %param.12) | copy-start | bytes 786436
  3.9 13.1 %collective-permute-start = (bf16[4,128,256]{2,1,0:T(8,128)(2,1)S(1)}, bf16[4,128,256]{2,1,0:T(8,128)(2,1)S(1)}, u32[]{:S(2)}, u32[]{:S(2)}) collective-permute-start(bf16[4,128,256]{2,1,0:T(8,128)(2,1)S(1)} %gather_fusion), channel_id=1, source_target_pairs={{0,1},{1,2},{2,3},{3,4},{4,5},{5,6},{6,7},{7,8},{8,9},{9,10},{10,1... | collective-permute-start | bytes 786440 | tf_op jit(solution)/shard_map/ppermute | solution.py:126
  7.0 10.0 %collective-permute-start.1 = (bf16[4,128,256]{2,1,0:T(8,128)(2,1)S(1)}, bf16[4,128,256]{2,1,0:T(8,128)(2,1)S(1)}, u32[]{:S(2)}, u32[]{:S(2)}) collective-permute-start(bf16[4,128,256]{2,1,0:T(8,128)(2,1)S(1)} %gather_fusion.1), channel_id=1, source_target_pairs={{1,0},{2,1},{3,2},{4,3},{5,4},{6,5},{7,6},{8,7},{9,8},{10,9},{11,1... | collective-permute-start | bytes 786440 | tf_op jit(solution)/shard_map/ppermute | solution.py:131
  18.3 6.1 %copy-start.13 = (bf16[2,256,256]{2,1,0:T(8,128)(2,1)S(1)}, bf16[2,256,256]{2,1,0:T(8,128)(2,1)}, u32[]{:S(2)}) copy-start(bf16[2,256,256]{2,1,0:T(8,128)(2,1)} %param.11) | copy-start | bytes 786436
  24.4 8.1 %copy-start.17 = (s32[1,16,2,4]{1,3,2,0:T(4,128)S(1)}, s32[1,16,2,4]{1,3,2,0:T(4,128)}, u32[]{:S(2)}) copy-start(s32[1,16,2,4]{1,3,2,0:T(4,128)} %param.10) | copy-start | bytes 1540
  27.3 10.4 %collective-permute-start.2 = (bf16[4,128,256]{2,1,0:T(8,128)(2,1)S(1)}, bf16[4,128,256]{2,1,0:T(8,128)(2,1)S(1)}, u32[]{:S(2)}, u32[]{:S(2)}) collective-permute-start(bf16[4,128,256]{2,1,0:T(8,128)(2,1)S(1)} %gather_fusion.2), channel_id=1, source_target_pairs={{0,1},{1,2},{2,3},{3,4},{4,5},{5,6},{6,7},{7,8},{8,9},{9,10},{10,1... | collective-permute-start | bytes 786440 | tf_op jit(solution)/shard_map/ppermute | solution.py:126
  27.3 10.3 %collective-permute-start.3 = (bf16[4,128,256]{2,1,0:T(8,128)(2,1)S(1)}, bf16[4,128,256]{2,1,0:T(8,128)(2,1)S(1)}, u32[]{:S(2)}, u32[]{:S(2)}) collective-permute-start(bf16[4,128,256]{2,1,0:T(8,128)(2,1)S(1)} %gather_fusion.3), channel_id=1, source_target_pairs={{1,0},{2,1},{3,2},{4,3},{5,4},{6,5},{7,6},{8,7},{9,8},{10,9},{11,1... | collective-permute-start | bytes 786440 | tf_op jit(solution)/shard_map/ppermute | solution.py:131
  39.0 6.1 %copy-start = (f32[1,2048,256]{2,1,0:T(8,128)S(1)}, f32[1,2048,256]{2,1,0:T(8,128)}, u32[]{:S(2)}) copy-start(f32[1,2048,256]{2,1,0:T(8,128)} %param.13) | copy-start | bytes 6291460
  45.0 3.4 %copy-start.3 = (f32[16,128,256]{2,1,0:T(8,128)S(1)}, f32[16,128,256]{2,1,0:T(8,128)}, u32[]{:S(2)}) copy-start(f32[16,128,256]{2,1,0:T(8,128)} %get-tuple-element.10) | copy-start | bytes 6291460
  57.1 6.1 %copy-start.1 = (bf16[16,128,256]{2,1,0:T(8,128)(2,1)S(1)}, bf16[16,128,256]{2,1,0:T(8,128)(2,1)}, u32[]{:S(2)}) copy-start(bf16[16,128,256]{2,1,0:T(8,128)(2,1)} %get-tuple-element.8.hits_ref) | copy-start | bytes 3145732
  57.1 6.1 %copy-start.2 = (bf16[1,2048,256]{2,1,0:T(8,128)(2,1)S(1)}, bf16[1,2048,256]{2,1,0:T(8,128)(2,1)}, u32[]{:S(2)}) copy-start(bf16[1,2048,256]{2,1,0:T(8,128)(2,1)} %fusion.14) | copy-start | bytes 3145732
  57.1 6.6 %copy-start.11 = (bf16[2,256,256]{2,1,0:T(8,128)(2,1)S(1)}, bf16[2,256,256]{2,1,0:T(8,128)(2,1)}, u32[]{:S(2)}) copy-start(bf16[2,256,256]{2,1,0:T(8,128)(2,1)} %param.12) | copy-start | bytes 786436
  58.6 13.5 %collective-permute-start.5 = (f32[4,128,256]{2,1,0:T(8,128)S(1)}, f32[4,128,256]{2,1,0:T(8,128)S(1)}, u32[]{:S(2)}, u32[]{:S(2)}) collective-permute-start(f32[4,128,256]{2,1,0:T(8,128)S(1)} %get-tuple-element.16), channel_id=1, source_target_pairs={{1,0},{2,1},{3,2},{4,3},{5,4},{6,5},{7,6},{8,7},{9,8},{10,9},{11,1... | collective-permute-start | bytes 1572872 | tf_op jit(solution)/shard_map/ppermute | solution.py:131
  63.3 14.2 %collective-permute-start.4 = (f32[4,128,256]{2,1,0:T(8,128)S(1)}, f32[4,128,256]{2,1,0:T(8,128)}, u32[]{:S(2)}, u32[]{:S(2)}) collective-permute-start(f32[4,128,256]{2,1,0:T(8,128)S(1)} %get-tuple-element.17), channel_id=1, source_target_pairs={{0,1},{1,2},{2,3},{3,4},{4,5},{5,6},{6,7},{7,8},{8,9},{9,10},{10,1... | collective-permute-start | bytes 1572872 | tf_op jit(solution)/shard_map/ppermute | solution.py:126
  65.6 15.7 %copy-start.9 = (f32[2048,256]{1,0:T(8,128)S(1)}, f32[2048,256]{1,0:T(8,128)}, u32[]{:S(2)}) copy-start(f32[2048,256]{1,0:T(8,128)} %convolution_add_fusion.3) | copy-start | bytes 6291460
  72.1 0.8 copy-start.16
  92.8 3.0 %copy-start.4 = (bf16[2048,256]{1,0:T(8,128)(2,1)S(1)}, bf16[2048,256]{1,0:T(8,128)(2,1)}, u32[]{:S(2)}) copy-start(bf16[2048,256]{1,0:T(8,128)(2,1)} %get-tuple-element.22) | copy-start | bytes 3145732
  92.8 3.0 %copy-start.5 = (bf16[1,2048,256]{2,1,0:T(8,128)(2,1)S(1)}, bf16[1,2048,256]{2,1,0:T(8,128)(2,1)}, u32[]{:S(2)}) copy-start(bf16[1,2048,256]{2,1,0:T(8,128)(2,1)} %param.7) | copy-start | bytes 3145732
  94.2 2.9 %copy-start.6 = (bf16[16,128,256]{2,1,0:T(8,128)(2,1)S(1)}, bf16[16,128,256]{2,1,0:T(8,128)(2,1)}, u32[]{:S(2)}) copy-start(bf16[16,128,256]{2,1,0:T(8,128)(2,1)} %shard_map.105) | copy-start | bytes 3145732
  94.2 10.0 %collective-permute-start.7 = (f32[4,128,256]{2,1,0:T(8,128)S(1)}, f32[4,128,256]{2,1,0:T(8,128)S(1)}, u32[]{:S(2)}, u32[]{:S(2)}) collective-permute-start(f32[4,128,256]{2,1,0:T(8,128)S(1)} %get-tuple-element.14), channel_id=1, source_target_pairs={{1,0},{2,1},{3,2},{4,3},{5,4},{6,5},{7,6},{8,7},{9,8},{10,9},{11,1... | collective-permute-start | bytes 1572872 | tf_op jit(solution)/shard_map/ppermute | solution.py:131
  95.3 13.3 %collective-permute-start.6 = (f32[4,128,256]{2,1,0:T(8,128)S(1)}, f32[4,128,256]{2,1,0:T(8,128)}, u32[]{:S(2)}, u32[]{:S(2)}) collective-permute-start(f32[4,128,256]{2,1,0:T(8,128)S(1)} %get-tuple-element.15), channel_id=1, source_target_pairs={{0,1},{1,2},{2,3},{3,4},{4,5},{5,6},{6,7},{7,8},{8,9},{9,10},{10,1... | collective-permute-start | bytes 1572872 | tf_op jit(solution)/shard_map/ppermute | solution.py:126
  104.2 0.8 copy-start.15
  112.4 1.9 %copy-start.8 = (f32[1,2,256,256]{3,2,1,0:T(8,128)S(1)}, f32[1,2,256,256]{3,2,1,0:T(8,128)}, u32[]{:S(2)}) copy-start(f32[1,2,256,256]{3,2,1,0:T(8,128)} %maximum_bitcast_fusion.1) | copy-start | bytes 1572868
  141.9 5.8 %copy-start.12 = (bf16[2,256,256]{2,1,0:T(8,128)(2,1)S(1)}, bf16[2,256,256]{2,1,0:T(8,128)(2,1)}, u32[]{:S(2)}) copy-start(bf16[2,256,256]{2,1,0:T(8,128)(2,1)} %param.12) | copy-start | bytes 786436
  143.2 23.7 %all-to-all-start.1 = ((f32[128,8,256]{2,1,0:T(8,128)}), f32[128,8,256]{2,1,0:T(8,128)S(1)}, u32[]{:S(2)}, u32[]{:S(2)}) async-start(f32[128,8,256]{2,1,0:T(8,128)} %broadcast_in_dim.5), calls=%async_computation.1 | async-start | bytes 2097152 | tf_op jit(solution)/shard_map/all_to_all | solution.py:140
  147.7 2.2 %copy-start.7 = (bf16[16,128,256]{2,1,0:T(8,128)(2,1)S(1)}, bf16[16,128,256]{2,1,0:T(8,128)(2,1)}, u32[]{:S(2)}) copy-start(bf16[16,128,256]{2,1,0:T(8,128)(2,1)} %shard_map.107) | copy-start | bytes 3145732
  147.7 2.2 %copy-start.14 = (bf16[2,256,256]{2,1,0:T(8,128)(2,1)S(1)}, bf16[2,256,256]{2,1,0:T(8,128)(2,1)}, u32[]{:S(2)}) copy-start(bf16[2,256,256]{2,1,0:T(8,128)(2,1)} %param.11) | copy-start | bytes 786436

commit v6 on v5

--- a/solution.py
+++ b/solution.py
@@ -9,14 +9,23 @@
 GROUP = 8
 
 
-def layer_kernel(src_ref, tiles_ref, table_ref, hits_ref, weight_ref, pre_ref, out_ref):
+def slot_rows(own_ref, lent_ref, slot):
+    own = own_ref.shape[0]
+    return jnp.where(
+        slot < own,
+        own_ref[jnp.minimum(slot, own - 1)],
+        lent_ref[jnp.maximum(slot - own, 0)],
+    )
+
+
+def layer_kernel(src_ref, tiles_ref, own_ref, lent_ref, hits_ref, weight_ref, pre_ref, out_ref):
     step = pl.program_id(0)
     listed = tiles_ref.shape[1]
     for i in range(GROUP):
         block = step * GROUP + i
         lhs = jnp.concatenate([tiles_ref[i, k] for k in range(listed)], axis=1)
         rhs = jnp.concatenate(
-            [table_ref[src_ref[block, k]] for k in range(listed)], axis=0
+            [slot_rows(own_ref, lent_ref, src_ref[block, k]) for k in range(listed)], axis=0
         )
         rows = hits_ref[i]
         pre = jnp.dot(lhs, rhs, preferred_element_type=jnp.float32) + jnp.dot(
@@ -28,9 +37,9 @@
         )
 
 
-def block_layer(slot_ids, tile_data, table, hit_blocks, weight):
+def block_layer(slot_ids, tile_data, own_table, lent_table, hit_blocks, weight):
     blocks, listed, rows, _ = tile_data.shape
-    width = table.shape[-1]
+    width = own_table.shape[-1]
     block_spec = pl.BlockSpec((GROUP, rows, width), lambda g, src: (g, 0, 0))
     return pl.pallas_call(
         layer_kernel,
@@ -39,7 +48,8 @@
             grid=(blocks // GROUP,),
             in_specs=[
                 pl.BlockSpec((GROUP, listed, rows, rows), lambda g, src: (g, 0, 0, 0)),
-                pl.BlockSpec(table.shape, lambda g, src: (0, 0, 0)),
+                pl.BlockSpec(own_table.shape, lambda g, src: (0, 0, 0)),
+                pl.BlockSpec(lent_table.shape, lambda g, src: (0, 0, 0)),
                 block_spec,
                 pl.BlockSpec(weight.shape, lambda g, src: (0, 0)),
             ],
@@ -49,10 +59,10 @@
             jax.ShapeDtypeStruct((blocks, rows, width), jnp.float32),
             jax.ShapeDtypeStruct((blocks, rows, width), hit_blocks.dtype),
         ],
-    )(slot_ids, tile_data, table, hit_blocks, weight)
-
-
-def slot_grad_kernel(src_ref, tiles_ref, dpre_ref, out_ref):
+    )(slot_ids, tile_data, own_table, lent_table, hit_blocks, weight)
+
+
+def slot_grad_kernel(src_ref, tiles_ref, dpre_ref, own_ref, lent_ref, out_ref):
     step = pl.program_id(0)
 
     @pl.when(step == 0)
@@ -69,6 +79,12 @@
                 preferred_element_type=jnp.float32,
             )
             out_ref[slot] += part
+
+    @pl.when(step == pl.num_programs(0) - 1)
+    def _():
+        own = own_ref.shape[0]
+        own_ref[...] = out_ref[:own]
+        lent_ref[...] = out_ref[own:]
 
 
 def block_slot_grad(slot_ids, tile_data, dpre_blocks, slot_count):
@@ -83,9 +99,16 @@
                 pl.BlockSpec((GROUP, listed, rows, rows), lambda g, src: (g, 0, 0, 0)),
                 pl.BlockSpec((GROUP, rows, width), lambda g, src: (g, 0, 0)),
             ],
-            out_specs=pl.BlockSpec((slot_count, rows, width), lambda g, src: (0, 0, 0)),
+            out_specs=[
+                pl.BlockSpec((blocks, rows, width), lambda g, src: (0, 0, 0)),
+                pl.BlockSpec((slot_count - blocks, rows, width), lambda g, src: (0, 0, 0)),
+            ],
+            scratch_shapes=[pltpu.VMEM((slot_count, rows, width), jnp.float32)],
         ),
-        out_shape=jax.ShapeDtypeStruct((slot_count, rows, width), jnp.float32),
+        out_shape=[
+            jax.ShapeDtypeStruct((blocks, rows, width), jnp.float32),
+            jax.ShapeDtypeStruct((slot_count - blocks, rows, width), jnp.float32),
+        ],
         compiler_params=pltpu.CompilerParams(dimension_semantics=("arbitrary",)),
     )(slot_ids, tile_data, dpre_blocks)
 
@@ -166,9 +189,9 @@
         message_blocks = message.reshape(blocks_here, tile_rows, width)
         from_lower = to_upper(message_blocks[own_lists[0]], "sector")
         from_upper = to_lower(message_blocks[own_lists[1]], "sector")
-        table = jnp.concatenate([message_blocks, from_lower, from_upper])
         pre, following = block_layer(
-            slot_ids, tile_data, table, current.reshape(message_blocks.shape),
+            slot_ids, tile_data, message_blocks, jnp.concatenate([from_lower, from_upper]),
+            current.reshape(message_blocks.shape),
             w_self[layer_index],
         )
         saved.append((current, pre.reshape(-1, width)))
@@ -179,13 +202,13 @@
     for layer_index in reversed(range(LAYERS)):
         layer_in, pre = saved[layer_index]
         dpre = (grad * silu_grad(pre)).astype(jnp.bfloat16)
-        slot_grad = block_slot_grad(
+        own_grad, lent_grad = block_slot_grad(
             slot_ids, tile_data, dpre.reshape(blocks_here, tile_rows, width), slot_count
         )
-        lent_down_grad = to_upper(slot_grad[blocks_here + lent :], "sector")
-        lent_up_grad = to_lower(slot_grad[blocks_here : blocks_here + lent], "sector")
+        lent_down_grad = to_upper(lent_grad[lent:], "sector")
+        lent_up_grad = to_lower(lent_grad[:lent], "sector")
         dmessage = fold_lent(
-            own_lists, slot_grad, lent_down_grad, lent_up_grad, blocks_here
+            own_lists, own_grad, lent_down_grad, lent_up_grad, blocks_here
         ).reshape(-1, width)
         self_part = jnp.dot(layer_in.T, dpre, preferred_element_type=jnp.float32)
         message_part = jnp.dot(layer_in.T, dmessage, preferred_element_type=jnp.float32)

time: 168 us -> 169 us (level)
  waiting for transfers between devices: 44.6 us -> 46.3 us
where the time goes in v6:
time: 169 us; the launch traced here: 168 us
  waiting for transfers between devices  46.3 us (27%)
  Pallas kernels  34.6 us (20%)
  blocking collectives  27.1 us (16%)
  starting transfers between devices  23.2 us (14%)
  matrix products  16.8 us (10%)
  local copies, waits for them, and re-layouts  11.2 us (7%)
  other arithmetic  7.94 us (5%)
    all_to_all x1, blocking collectives, all_reduce(): mine = lax.all_to_all(pieces, axes, 0, 0, tiled=True).sum(0) * scale  27.1 us
    ppermute x4, waiting for transfers between devices, to_upper(): return lax.ppermute(x, axis, [(i, (i + 1) % count) for i in range(count)])  17.8 us
    ppermute x4, starting transfers between devices, to_lower(): return lax.ppermute(x, axis, [((i + 1) % count, i) for i in range(count)])  15.6 us
    all_to_all x1, waiting for transfers between devices, all_reduce(): return lax.all_to_all(spread, axes, 0, 0, tiled=True).reshape(x.shape)  15.1 us
    pallas_call x2, Pallas kernels, block_slot_grad(): pl.pallas_call(slot_grad_kernel, grid_spec=pltpu.PrefetchScalarGridSpec(n...  14.3 us
    ppermute x4, waiting for transfers between devices, to_lower(): return lax.ppermute(x, axis, [((i + 1) % count, i) for i in range(count)])  13.4 us
    pallas_call x2, Pallas kernels, block_layer(): pl.pallas_call(layer_kernel, grid_spec=pltpu.PrefetchScalarGridSpec(num_s...  12.5 us
    pallas_call x2, Pallas kernels, fold_lent(): pl.pallas_call(fold_kernel, grid_spec=pltpu.PrefetchScalarGridSpec(num_sc...  7.85 us
  transfers between devices with their start and end apart: 9, of which 7 were waited for; matrix products, arithmetic and copies ran while one was open for 6% of the time, Pallas kernels for 0%

profile of v6, /device:TPU:1, one launch (start us, length us, event | category | flops | bytes accessed | tf_op | source)
XLA Modules:
  0.0 168.1 jit_solution(59275588175935183)
XLA Ops:
  0.7 1.0 dynamic-slice_reduce_fusion.2
  1.6 1.7 convolution_convert_fusion.1
  3.3 0.6 gather_fusion
  3.9 2.5 %collective-permute-start = (bf16[4,128,256]{2,1,0:T(8,128)(2,1)S(1)}, bf16[4,128,256]{2,1,0:T(8,128)(2,1)S(1)}, u32[]{:S(2)}, u32[]{:S(2)}) collective-permute-start(bf16[4,128,256]{2,1,0:T(8,128)(2,1)S(1)} %gather_fusion), channel_id=1, source_target_pairs={{0,1},{1,2},{2,3},{3,4},{4,5},{5,6},{6,7},{7,8},{8,9},{9,10},{10,1... | collective-permute-start | bytes 786440 | tf_op jit(solution)/shard_map/ppermute | solution.py:149
  6.4 0.6 gather_fusion.1
  7.0 4.7 %collective-permute-start.1 = (bf16[4,128,256]{2,1,0:T(8,128)(2,1)S(1)}, bf16[4,128,256]{2,1,0:T(8,128)(2,1)S(1)}, u32[]{:S(2)}, u32[]{:S(2)}) collective-permute-start(bf16[4,128,256]{2,1,0:T(8,128)(2,1)S(1)} %gather_fusion.1), channel_id=1, source_target_pairs={{1,0},{2,1},{3,2},{4,3},{5,4},{6,5},{7,6},{8,7},{9,8},{10,9},{11,1... | collective-permute-start | bytes 786440 | tf_op jit(solution)/shard_map/ppermute | solution.py:154
  11.6 0.7 copy.17.src_ref
  12.3 0.7 slice_bitcast_fusion
  13.0 3.9 %collective-permute-done = bf16[4,128,256]{2,1,0:T(8,128)(2,1)S(1)} collective-permute-done((bf16[4,128,256]{2,1,0:T(8,128)(2,1)S(1)}, bf16[4,128,256]{2,1,0:T(8,128)(2,1)S(1)}, u32[]{:S(2)}, u32[]{:S(2)}) %collective-permute-start) | collective-permute-done | bytes 262176 | tf_op jit(solution)/shard_map/ppermute | solution.py:149
  17.0 0.8 pad_maximum_fusion.1.lent_ref
  17.8 6.3 %shard_map.102 = (f32[16,128,256]{2,1,0:T(8,128)}, bf16[16,128,256]{2,1,0:T(8,128)(2,1)}) custom-call(s32[16,8]{1,0:T(8,128)} %copy.17.src_ref, bf16[16,8,128,128]{3,2,1,0:T(8,128)(2,1)} %bitcast.121, bf16[16,128,256]{2,1,0:T(8,128)(2,1)} %bitcast.131, bf16[8,128,256]{2,1,0:T(8,128)(2,1)} %pad_maximum_fusion.1.lent_ref, bf16[16,128,256]{2,1,0:T(8,128)(2,1)} %bitcast.140, ...), custom_call_target="tpu_custom_call" | custom-call | tf_op jit(solution)/shard_map/pallas_call | solution.py:44
  24.1 1.7 convolution_convert_fusion
  25.8 0.6 gather_fusion.3
  26.3 0.6 gather_fusion.2
  27.0 5.2 %collective-permute-start.3 = (bf16[4,128,256]{2,1,0:T(8,128)(2,1)S(1)}, bf16[4,128,256]{2,1,0:T(8,128)(2,1)S(1)}, u32[]{:S(2)}, u32[]{:S(2)}) collective-permute-start(bf16[4,128,256]{2,1,0:T(8,128)(2,1)S(1)} %gather_fusion.3), channel_id=1, source_target_pairs={{1,0},{2,1},{3,2},{4,3},{5,4},{6,5},{7,6},{8,7},{9,8},{10,9},{11,1... | collective-permute-start | bytes 786440 | tf_op jit(solution)/shard_map/ppermute | solution.py:154
  32.2 0.8 dynamic-slice_reduce_fusion.lists_ref
  33.0 4.2 %collective-permute-done.2 = bf16[4,128,256]{2,1,0:T(8,128)(2,1)S(1)} collective-permute-done((bf16[4,128,256]{2,1,0:T(8,128)(2,1)S(1)}, bf16[4,128,256]{2,1,0:T(8,128)(2,1)S(1)}, u32[]{:S(2)}, u32[]{:S(2)}) %collective-permute-start.2) | collective-permute-done | bytes 262176 | tf_op jit(solution)/shard_map/ppermute | solution.py:149
  37.3 0.8 pad_maximum_fusion.2.lent_ref
  38.1 6.3 %shard_map.103 = (f32[16,128,256]{2,1,0:T(8,128)}, bf16[16,128,256]{2,1,0:T(8,128)(2,1)}) custom-call(s32[16,8]{1,0:T(8,128)} %copy.17.src_ref, bf16[16,8,128,128]{3,2,1,0:T(8,128)(2,1)} %bitcast.122, bf16[16,128,256]{2,1,0:T(8,128)(2,1)} %bitcast.134, bf16[8,128,256]{2,1,0:T(8,128)(2,1)} %pad_maximum_fusion.2.lent_ref, ...), custom_call_target="tpu_custom_call" | custom-call | tf_op jit(solution)/shard_map/pallas_call | solution.py:44
  44.4 3.4 %fusion.14 = bf16[1,2048,256]{2,1,0:T(8,128)(2,1)} fusion(f32[1,2048,256]{2,1,0:T(8,128)S(1)} %copy-done, f32[1,2048,256]{2,1,0:T(8,128)} %bitcast.128), kind=kLoop, calls=%fused_computation.28 | loop fusion | flops 4718592 | bytes 5242880 | tf_op jit(solution)/shard_map/convert_element_type | solution.py:204
  47.8 1.8 %multiply_convert_fusion.dpre_ref = bf16[16,128,256]{2,1,0:T(8,128)(2,1)} fusion(f32[16,128,256]{2,1,0:T(8,128)S(1)} %bitcast.125, f32[16,128,256]{2,1,0:T(8,128)S(1)} %copy-done.3), kind=kLoop, calls=%fused_computation.29 | loop fusion | flops 4718592 | bytes 5242880 | tf_op jit(solution)/shard_map/convert_element_type | solution.py:204
  49.6 7.1 %shard_map.104 = (f32[16,128,256]{2,1,0:T(8,128)}, f32[8,128,256]{2,1,0:T(8,128)}) custom-call(s32[16,8]{1,0:T(8,128)} %copy.17.src_ref, bf16[16,8,128,128]{3,2,1,0:T(8,128)(2,1)} %bitcast.123, bf16[16,128,256]{2,1,0:T(8,128)(2,1)} %multiply_convert_fusion.dpre_ref), custom_call_target="tpu_custom_call" | custom-call | tf_op jit(solution)/shard_map/pallas_call | solution.py:93
  56.7 1.5 fusion.32
  58.2 4.6 %collective-permute-start.5 = (f32[4,128,256]{2,1,0:T(8,128)S(1)}, f32[4,128,256]{2,1,0:T(8,128)S(1)}, u32[]{:S(2)}, u32[]{:S(2)}) collective-permute-start(f32[4,128,256]{2,1,0:T(8,128)S(1)} %get-tuple-element.26), channel_id=1, source_target_pairs={{1,0},{2,1},{3,2},{4,3},{5,4},{6,5},{7,6},{8,7},{9,8},{10,9},{11,1... | collective-permute-start | bytes 1572872 | tf_op jit(solution)/shard_map/ppermute | solution.py:154
  62.8 0.5 convolution_bitcast_fusion
  63.3 1.8 %convolution_add_fusion.3 = f32[2048,256]{1,0:T(8,128)} fusion(f32[1,2048,256]{2,1,0:T(8,128)S(1)} %copy-done, bf16[1,2048,256]{2,1,0:T(8,128)(2,1)S(1)} %copy-done.2, bf16[2,256,256]{2,1,0:T(8,128)(2,1)S(1)} %copy-done.13), kind=kOutput, calls=%fused_computation.8 | convolution fusion | flops 268959744 | bytes 5373952 | tf_op jit(solution)/shard_map/dot_general | solution.py:217
  65.1 6.6 %collective-permute-done.5.upper_ref = f32[4,128,256]{2,1,0:T(8,128)S(1)} collective-permute-done((f32[4,128,256]{2,1,0:T(8,128)S(1)}, f32[4,128,256]{2,1,0:T(8,128)S(1)}, u32[]{:S(2)}, u32[]{:S(2)}) %collective-permute-start.5) | collective-permute-done | bytes 524320 | tf_op jit(solution)/shard_map/ppermute | solution.py:154
  71.7 5.2 %collective-permute-done.4.lower_ref = f32[4,128,256]{2,1,0:T(8,128)S(1)} collective-permute-done((f32[4,128,256]{2,1,0:T(8,128)S(1)}, f32[4,128,256]{2,1,0:T(8,128)S(1)}, u32[]{:S(2)}, u32[]{:S(2)}) %collective-permute-start.4) | collective-permute-done | bytes 524320 | tf_op jit(solution)/shard_map/ppermute | solution.py:149
  76.9 0.8 copy-done.18
  77.7 4.0 %shard_map.105 = bf16[16,128,256]{2,1,0:T(8,128)(2,1)} custom-call(s32[2,4]{1,0:T(2,128)} %dynamic-slice_reduce_fusion.lists_ref, f32[16,128,256]{2,1,0:T(8,128)} %get-tuple-element.15.slot_ref, f32[4,128,256]{2,1,0:T(8,128)} %copy-done.18, f32[4,128,256]{2,1,0:T(8,128)} %copy-done.17), custom_call_target="tpu_custom_call" | custom-call | tf_op jit(solution)/shard_map/pallas_call | solution.py:130
  81.7 4.5 %fusion.7 = (bf16[2048,256]{1,0:T(8,128)(2,1)}, f32[2048,256]{1,0:T(8,128)}) fusion(f32[16,128,256]{2,1,0:T(8,128)} %get-tuple-element.17, f32[2048,256]{1,0:T(8,128)S(1)} %copy-done.11, bf16[2048,256]{1,0:T(8,128)(2,1)} %bitcast.135, bf16[2,256,256]{2,1,0:T(8,128)(2,1)} %param.11), kind=kOutput, calls=%fused_computation.19 | convolution fusion | flops 273678336 | bytes 8519680 | tf_op jit(solution)/shard_map/dot_general | solution.py:218
  86.2 7.1 %shard_map.106 = (f32[16,128,256]{2,1,0:T(8,128)}, f32[8,128,256]{2,1,0:T(8,128)}) custom-call(s32[16,8]{1,0:T(8,128)} %copy.17.src_ref, bf16[16,8,128,128]{3,2,1,0:T(8,128)(2,1)} %bitcast.124, bf16[16,128,256]{2,1,0:T(8,128)(2,1)} %bitcast.136), custom_call_target="tpu_custom_call" | custom-call | tf_op jit(solution)/shard_map/pallas_call | solution.py:93
  93.4 1.4 fusion.31
  94.8 1.1 collective-permute-start.7
  96.3 0.5 convolution_bitcast_fusion.1
  96.9 0.8 maximum_bitcast_fusion.1
  97.7 0.5 convolution_bitcast_fusion.2
  98.2 6.8 %collective-permute-done.7.upper_ref = f32[4,128,256]{2,1,0:T(8,128)} collective-permute-done((f32[4,128,256]{2,1,0:T(8,128)S(1)}, f32[4,128,256]{2,1,0:T(8,128)}, u32[]{:S(2)}, u32[]{:S(2)}) %collective-permute-start.7) | collective-permute-done | bytes 524320 | tf_op jit(solution)/shard_map/ppermute | solution.py:154
  105.0 4.3 %collective-permute-done.6.lower_ref = f32[4,128,256]{2,1,0:T(8,128)} collective-permute-done((f32[4,128,256]{2,1,0:T(8,128)S(1)}, f32[4,128,256]{2,1,0:T(8,128)}, u32[]{:S(2)}, u32[]{:S(2)}) %collective-permute-start.6) | collective-permute-done | bytes 524320 | tf_op jit(solution)/shard_map/ppermute | solution.py:149
  109.3 3.8 %shard_map.107 = bf16[16,128,256]{2,1,0:T(8,128)(2,1)} custom-call(s32[2,4]{1,0:T(2,128)} %dynamic-slice_reduce_fusion.lists_ref, f32[16,128,256]{2,1,0:T(8,128)} %get-tuple-element.18.slot_ref, f32[4,128,256]{2,1,0:T(8,128)} %collective-permute-done.6.lower_ref, f32[4,128,256]{2,1,0:T(8,128)} %collective-permute-done.7.upper_ref), custom_call_target="tpu_custom_call" | custom-call | tf_op jit(solution)/shard_map/pallas_call | solution.py:130
  113.1 1.8 %convolution_bitcast_fusion.3 = f32[1,256,256]{2,1,0:T(8,128)S(1)} fusion(bf16[2048,256]{1,0:T(8,128)(2,1)} %bitcast.137, bf16[1,2048,256]{2,1,0:T(8,128)(2,1)S(1)} %copy-done.9), kind=kOutput, calls=%fused_computation.33 | convolution fusion | flops 268435456 | bytes 2359296 | tf_op jit(solution)/shard_map/dot_general | solution.py:214
  115.1 27.1 %all_to_all.10 = f32[128,8,256]{2,1,0:T(8,128)S(1)} all-to-all(f32[128,8,256]{2,1,0:T(8,128)S(1)} %bitcast.139), channel_id=1, replica_groups=mesh['dp'=8,'sector'=16] {'dp','sector'}, dimensions={0} | all-to-all | bytes 2097152 | tf_op jit(solution)/shard_map/all_to_all | solution.py:161
  142.4 1.0 broadcast_in_dim.5
  143.4 4.5 %all-to-all-start.1 = ((f32[128,8,256]{2,1,0:T(8,128)}), f32[128,8,256]{2,1,0:T(8,128)S(1)}, u32[]{:S(2)}, u32[]{:S(2)}) async-start(f32[128,8,256]{2,1,0:T(8,128)} %broadcast_in_dim.5), calls=%async_computation.1 | async-start | bytes 2097152 | tf_op jit(solution)/shard_map/all_to_all | solution.py:163
  148.0 2.2 %convolution_add_fusion.1 = f32[2048,256]{1,0:T(8,128)S(1)} fusion(f32[2048,256]{1,0:T(8,128)} %get-tuple-element.31, bf16[2048,256]{1,0:T(8,128)(2,1)S(1)} %copy-done.7, bf16[2,256,256]{2,1,0:T(8,128)(2,1)S(1)} %copy-done.14), kind=kOutput, calls=%fused_computation.6 | convolution fusion | flops 268959744 | bytes 5373952 | tf_op jit(solution)/shard_map/dot_general | solution.py:217
  150.2 1.8 %fusion = f32[1,2048,256]{2,1,0:T(8,128)} fusion(f32[2048,256]{1,0:T(8,128)S(1)} %convolution_add_fusion.1, bf16[2048,256]{1,0:T(8,128)(2,1)S(1)} %bitcast.138, bf16[2,256,256]{2,1,0:T(8,128)(2,1)S(1)} %copy-done.16), kind=kOutput, calls=%fused_computation.5 | convolution fusion | flops 268959744 | bytes 5373952 | tf_op jit(solution)/shard_map/dot_general | solution.py:218
  152.0 15.1 %all-to-all-done.1 = f32[128,8,256]{2,1,0:T(8,128)S(1)} async-done(((f32[128,8,256]{2,1,0:T(8,128)}), f32[128,8,256]{2,1,0:T(8,128)S(1)}, u32[]{:S(2)}, u32[]{:S(2)}) %all-to-all-start.1) | async-done | bytes 1048608 | tf_op jit(solution)/shard_map/all_to_all | solution.py:163
  167.1 1.0 fusion.30
  (53 shorter events, 0.9 us)
Async XLA Ops:
  0.6 11.0 %copy-start.20 = (s32[1,16,8]{1,2,0:T(8,128)S(1)}, s32[1,16,8]{1,2,0:T(8,128)}, u32[]{:S(2)}) copy-start(s32[1,16,8]{1,2,0:T(8,128)} %param.9) | copy-start | bytes 1540
  0.6 11.7 %copy-start.12 = (bf16[2,256,256]{2,1,0:T(8,128)(2,1)S(1)}, bf16[2,256,256]{2,1,0:T(8,128)(2,1)}, u32[]{:S(2)}) copy-start(bf16[2,256,256]{2,1,0:T(8,128)(2,1)} %param.12) | copy-start | bytes 786436
  3.3 14.5 %copy-start.4 = (bf16[2048,256]{1,0:T(8,128)(2,1)}, bf16[2048,256]{1,0:T(8,128)(2,1)S(1)}, u32[]{:S(2)}) copy-start(bf16[2048,256]{1,0:T(8,128)(2,1)S(1)} %convolution_convert_fusion.1) | copy-start | bytes 3145732
  3.9 13.1 %collective-permute-start = (bf16[4,128,256]{2,1,0:T(8,128)(2,1)S(1)}, bf16[4,128,256]{2,1,0:T(8,128)(2,1)S(1)}, u32[]{:S(2)}, u32[]{:S(2)}) collective-permute-start(bf16[4,128,256]{2,1,0:T(8,128)(2,1)S(1)} %gather_fusion), channel_id=1, source_target_pairs={{0,1},{1,2},{2,3},{3,4},{4,5},{5,6},{6,7},{7,8},{8,9},{9,10},{10,1... | collective-permute-start | bytes 786440 | tf_op jit(solution)/shard_map/ppermute | solution.py:149
  7.0 10.0 %collective-permute-start.1 = (bf16[4,128,256]{2,1,0:T(8,128)(2,1)S(1)}, bf16[4,128,256]{2,1,0:T(8,128)(2,1)S(1)}, u32[]{:S(2)}, u32[]{:S(2)}) collective-permute-start(bf16[4,128,256]{2,1,0:T(8,128)(2,1)S(1)} %gather_fusion.1), channel_id=1, source_target_pairs={{1,0},{2,1},{3,2},{4,3},{5,4},{6,5},{7,6},{8,7},{9,8},{10,9},{11,1... | collective-permute-start | bytes 786440 | tf_op jit(solution)/shard_map/ppermute | solution.py:154
  17.8 6.3 %copy-start.15 = (bf16[2,256,256]{2,1,0:T(8,128)(2,1)S(1)}, bf16[2,256,256]{2,1,0:T(8,128)(2,1)}, u32[]{:S(2)}) copy-start(bf16[2,256,256]{2,1,0:T(8,128)(2,1)} %param.11) | copy-start | bytes 786436
  24.1 8.1 %copy-start.19 = (s32[1,16,2,4]{1,3,2,0:T(4,128)S(1)}, s32[1,16,2,4]{1,3,2,0:T(4,128)}, u32[]{:S(2)}) copy-start(s32[1,16,2,4]{1,3,2,0:T(4,128)} %param.10) | copy-start | bytes 1540
  25.8 12.4 %copy-start.5 = (bf16[2048,256]{1,0:T(8,128)(2,1)}, bf16[2048,256]{1,0:T(8,128)(2,1)S(1)}, u32[]{:S(2)}) copy-start(bf16[2048,256]{1,0:T(8,128)(2,1)S(1)} %convolution_convert_fusion) | copy-start | bytes 3145732
  26.9 10.4 %collective-permute-start.2 = (bf16[4,128,256]{2,1,0:T(8,128)(2,1)S(1)}, bf16[4,128,256]{2,1,0:T(8,128)(2,1)S(1)}, u32[]{:S(2)}, u32[]{:S(2)}) collective-permute-start(bf16[4,128,256]{2,1,0:T(8,128)(2,1)S(1)} %gather_fusion.2), channel_id=1, source_target_pairs={{0,1},{1,2},{2,3},{3,4},{4,5},{5,6},{6,7},{7,8},{8,9},{9,10},{10,1... | collective-permute-start | bytes 786440 | tf_op jit(solution)/shard_map/ppermute | solution.py:149
  27.0 10.3 %collective-permute-start.3 = (bf16[4,128,256]{2,1,0:T(8,128)(2,1)S(1)}, bf16[4,128,256]{2,1,0:T(8,128)(2,1)S(1)}, u32[]{:S(2)}, u32[]{:S(2)}) collective-permute-start(bf16[4,128,256]{2,1,0:T(8,128)(2,1)S(1)} %gather_fusion.3), channel_id=1, source_target_pairs={{1,0},{2,1},{3,2},{4,3},{5,4},{6,5},{7,6},{8,7},{9,8},{10,9},{11,1... | collective-permute-start | bytes 786440 | tf_op jit(solution)/shard_map/ppermute | solution.py:154
  38.1 6.3 %copy-start = (f32[1,2048,256]{2,1,0:T(8,128)S(1)}, f32[1,2048,256]{2,1,0:T(8,128)}, u32[]{:S(2)}) copy-start(f32[1,2048,256]{2,1,0:T(8,128)} %param.13) | copy-start | bytes 6291460
  44.4 3.4 %copy-start.3 = (f32[16,128,256]{2,1,0:T(8,128)S(1)}, f32[16,128,256]{2,1,0:T(8,128)}, u32[]{:S(2)}) copy-start(f32[16,128,256]{2,1,0:T(8,128)} %get-tuple-element.14) | copy-start | bytes 6291460
  56.7 6.1 %copy-start.1 = (bf16[16,128,256]{2,1,0:T(8,128)(2,1)S(1)}, bf16[16,128,256]{2,1,0:T(8,128)(2,1)}, u32[]{:S(2)}) copy-start(bf16[16,128,256]{2,1,0:T(8,128)(2,1)} %get-tuple-element.12.hits_ref) | copy-start | bytes 3145732
  56.7 6.1 %copy-start.2 = (bf16[1,2048,256]{2,1,0:T(8,128)(2,1)S(1)}, bf16[1,2048,256]{2,1,0:T(8,128)(2,1)}, u32[]{:S(2)}) copy-start(bf16[1,2048,256]{2,1,0:T(8,128)(2,1)} %fusion.14) | copy-start | bytes 3145732
  56.7 6.6 %copy-start.13 = (bf16[2,256,256]{2,1,0:T(8,128)(2,1)S(1)}, bf16[2,256,256]{2,1,0:T(8,128)(2,1)}, u32[]{:S(2)}) copy-start(bf16[2,256,256]{2,1,0:T(8,128)(2,1)} %param.12) | copy-start | bytes 786436
  58.2 13.5 %collective-permute-start.5 = (f32[4,128,256]{2,1,0:T(8,128)S(1)}, f32[4,128,256]{2,1,0:T(8,128)S(1)}, u32[]{:S(2)}, u32[]{:S(2)}) collective-permute-start(f32[4,128,256]{2,1,0:T(8,128)S(1)} %get-tuple-element.26), channel_id=1, source_target_pairs={{1,0},{2,1},{3,2},{4,3},{5,4},{6,5},{7,6},{8,7},{9,8},{10,9},{11,1... | collective-permute-start | bytes 1572872 | tf_op jit(solution)/shard_map/ppermute | solution.py:154
  62.8 14.1 %collective-permute-start.4 = (f32[4,128,256]{2,1,0:T(8,128)S(1)}, f32[4,128,256]{2,1,0:T(8,128)S(1)}, u32[]{:S(2)}, u32[]{:S(2)}) collective-permute-start(f32[4,128,256]{2,1,0:T(8,128)S(1)} %get-tuple-element.27), channel_id=1, source_target_pairs={{0,1},{1,2},{2,3},{3,4},{4,5},{5,6},{6,7},{7,8},{8,9},{9,10},{10,1... | collective-permute-start | bytes 1572872 | tf_op jit(solution)/shard_map/ppermute | solution.py:149
  71.7 5.2 %copy-start.17 = (f32[4,128,256]{2,1,0:T(8,128)}, f32[4,128,256]{2,1,0:T(8,128)S(1)}, u32[]{:S(2)}) copy-start(f32[4,128,256]{2,1,0:T(8,128)S(1)} %collective-permute-done.5.upper_ref) | copy-start | bytes 1572868
  76.9 0.8 copy-start.18
  77.7 4.0 %copy-start.11 = (f32[2048,256]{1,0:T(8,128)S(1)}, f32[2048,256]{1,0:T(8,128)}, u32[]{:S(2)}) copy-start(f32[2048,256]{1,0:T(8,128)} %convolution_add_fusion.3) | copy-start | bytes 6291460
  93.4 3.0 %copy-start.7 = (bf16[2048,256]{1,0:T(8,128)(2,1)S(1)}, bf16[2048,256]{1,0:T(8,128)(2,1)}, u32[]{:S(2)}) copy-start(bf16[2048,256]{1,0:T(8,128)(2,1)} %get-tuple-element.30) | copy-start | bytes 3145732
  93.4 3.0 %copy-start.9 = (bf16[1,2048,256]{2,1,0:T(8,128)(2,1)S(1)}, bf16[1,2048,256]{2,1,0:T(8,128)(2,1)}, u32[]{:S(2)}) copy-start(bf16[1,2048,256]{2,1,0:T(8,128)(2,1)} %param.7) | copy-start | bytes 3145732
  94.8 2.9 %copy-start.6 = (bf16[16,128,256]{2,1,0:T(8,128)(2,1)S(1)}, bf16[16,128,256]{2,1,0:T(8,128)(2,1)}, u32[]{:S(2)}) copy-start(bf16[16,128,256]{2,1,0:T(8,128)(2,1)} %shard_map.105) | copy-start | bytes 3145732
  94.8 10.1 %collective-permute-start.7 = (f32[4,128,256]{2,1,0:T(8,128)S(1)}, f32[4,128,256]{2,1,0:T(8,128)}, u32[]{:S(2)}, u32[]{:S(2)}) collective-permute-start(f32[4,128,256]{2,1,0:T(8,128)S(1)} %get-tuple-element.24), channel_id=1, source_target_pairs={{1,0},{2,1},{3,2},{4,3},{5,4},{6,5},{7,6},{8,7},{9,8},{10,9},{11,1... | collective-permute-start | bytes 1572872 | tf_op jit(solution)/shard_map/ppermute | solution.py:154
  95.9 13.4 %collective-permute-start.6 = (f32[4,128,256]{2,1,0:T(8,128)S(1)}, f32[4,128,256]{2,1,0:T(8,128)}, u32[]{:S(2)}, u32[]{:S(2)}) collective-permute-start(f32[4,128,256]{2,1,0:T(8,128)S(1)} %get-tuple-element.25), channel_id=1, source_target_pairs={{0,1},{1,2},{2,3},{3,4},{4,5},{5,6},{6,7},{7,8},{8,9},{9,10},{10,1... | collective-permute-start | bytes 1572872 | tf_op jit(solution)/shard_map/ppermute | solution.py:149
  113.1 1.9 %copy-start.10 = (f32[1,2,256,256]{3,2,1,0:T(8,128)S(1)}, f32[1,2,256,256]{3,2,1,0:T(8,128)}, u32[]{:S(2)}) copy-start(f32[1,2,256,256]{3,2,1,0:T(8,128)} %maximum_bitcast_fusion.1) | copy-start | bytes 1572868
  142.2 5.7 %copy-start.14 = (bf16[2,256,256]{2,1,0:T(8,128)(2,1)S(1)}, bf16[2,256,256]{2,1,0:T(8,128)(2,1)}, u32[]{:S(2)}) copy-start(bf16[2,256,256]{2,1,0:T(8,128)(2,1)} %param.12) | copy-start | bytes 786436
  143.4 23.7 %all-to-all-start.1 = ((f32[128,8,256]{2,1,0:T(8,128)}), f32[128,8,256]{2,1,0:T(8,128)S(1)}, u32[]{:S(2)}, u32[]{:S(2)}) async-start(f32[128,8,256]{2,1,0:T(8,128)} %broadcast_in_dim.5), calls=%async_computation.1 | async-start | bytes 2097152 | tf_op jit(solution)/shard_map/all_to_all | solution.py:163
  148.0 2.2 %copy-start.8 = (bf16[16,128,256]{2,1,0:T(8,128)(2,1)S(1)}, bf16[16,128,256]{2,1,0:T(8,128)(2,1)}, u32[]{:S(2)}) copy-start(bf16[16,128,256]{2,1,0:T(8,128)(2,1)} %shard_map.107) | copy-start | bytes 3145732
  148.0 2.2 %copy-start.16 = (bf16[2,256,256]{2,1,0:T(8,128)(2,1)S(1)}, bf16[2,256,256]{2,1,0:T(8,128)(2,1)}, u32[]{:S(2)}) copy-start(bf16[2,256,256]{2,1,0:T(8,128)(2,1)} %param.11) | copy-start | bytes 786436

commit v7 on v6

--- a/solution.py
+++ b/solution.py
@@ -62,7 +62,7 @@
     )(slot_ids, tile_data, own_table, lent_table, hit_blocks, weight)
 
 
-def slot_grad_kernel(src_ref, tiles_ref, dpre_ref, own_ref, lent_ref, out_ref):
+def slot_grad_kernel(src_ref, tiles_ref, grad_ref, pre_ref, own_ref, low_ref, high_ref, dpre_ref, out_ref):
     step = pl.program_id(0)
 
     @pl.when(step == 0)
@@ -71,7 +71,10 @@
 
     for i in range(GROUP):
         block = step * GROUP + i
-        grad = dpre_ref[i]
+        pre = pre_ref[i]
+        sig = jax.nn.sigmoid(pre)
+        grad = (grad_ref[i] * (sig * (1.0 + pre * (1.0 - sig)))).astype(dpre_ref.dtype)
+        dpre_ref[i] = grad
         for k in range(tiles_ref.shape[1]):
             slot = src_ref[block, k]
             part = lax.dot_general(
@@ -83,13 +86,18 @@
     @pl.when(step == pl.num_programs(0) - 1)
     def _():
         own = own_ref.shape[0]
+        lent = low_ref.shape[0]
         own_ref[...] = out_ref[:own]
-        lent_ref[...] = out_ref[own:]
-
-
-def block_slot_grad(slot_ids, tile_data, dpre_blocks, slot_count):
+        low_ref[...] = out_ref[own : own + lent]
+        high_ref[...] = out_ref[own + lent :]
+
+
+def block_slot_grad(slot_ids, tile_data, grad_blocks, pre_blocks, slot_count):
     blocks, listed, rows, _ = tile_data.shape
-    width = dpre_blocks.shape[-1]
+    width = grad_blocks.shape[-1]
+    lent = (slot_count - blocks) // 2
+    block_spec = pl.BlockSpec((GROUP, rows, width), lambda g, src: (g, 0, 0))
+    whole = lambda count: pl.BlockSpec((count, rows, width), lambda g, src: (0, 0, 0))
     return pl.pallas_call(
         slot_grad_kernel,
         grid_spec=pltpu.PrefetchScalarGridSpec(
@@ -97,20 +105,20 @@
             grid=(blocks // GROUP,),
             in_specs=[
                 pl.BlockSpec((GROUP, listed, rows, rows), lambda g, src: (g, 0, 0, 0)),
-                pl.BlockSpec((GROUP, rows, width), lambda g, src: (g, 0, 0)),
+                block_spec,
+                block_spec,
             ],
-            out_specs=[
-                pl.BlockSpec((blocks, rows, width), lambda g, src: (0, 0, 0)),
-                pl.BlockSpec((slot_count - blocks, rows, width), lambda g, src: (0, 0, 0)),
-            ],
+            out_specs=[whole(blocks), whole(lent), whole(lent), block_spec],
             scratch_shapes=[pltpu.VMEM((slot_count, rows, width), jnp.float32)],
         ),
         out_shape=[
             jax.ShapeDtypeStruct((blocks, rows, width), jnp.float32),
-            jax.ShapeDtypeStruct((slot_count - blocks, rows, width), jnp.float32),
+            jax.ShapeDtypeStruct((lent, rows, width), jnp.float32),
+            jax.ShapeDtypeStruct((lent, rows, width), jnp.float32),
+            jax.ShapeDtypeStruct((blocks, rows, width), jnp.bfloat16),
         ],
         compiler_params=pltpu.CompilerParams(dimension_semantics=("arbitrary",)),
-    )(slot_ids, tile_data, dpre_blocks)
+    )(slot_ids, tile_data, grad_blocks, pre_blocks)
 
 
 def fold_kernel(lists_ref, slot_ref, lower_ref, upper_ref, out_ref, acc_ref):
@@ -201,12 +209,13 @@
     self_steps = [None] * LAYERS
     for layer_index in reversed(range(LAYERS)):
         layer_in, pre = saved[layer_index]
-        dpre = (grad * silu_grad(pre)).astype(jnp.bfloat16)
-        own_grad, lent_grad = block_slot_grad(
-            slot_ids, tile_data, dpre.reshape(blocks_here, tile_rows, width), slot_count
-        )
-        lent_down_grad = to_upper(lent_grad[lent:], "sector")
-        lent_up_grad = to_lower(lent_grad[:lent], "sector")
+        own_grad, low_grad, high_grad, dpre_blocks = block_slot_grad(
+            slot_ids, tile_data, grad.reshape(blocks_here, tile_rows, width),
+            pre.reshape(blocks_here, tile_rows, width), slot_count,
+        )
+        dpre = dpre_blocks.reshape(-1, width)
+        lent_down_grad = to_upper(high_grad, "sector")
+        lent_up_grad = to_lower(low_grad, "sector")
         dmessage = fold_lent(
             own_lists, own_grad, lent_down_grad, lent_up_grad, blocks_here
         ).reshape(-1, width)

time: 169 us -> 160 us (0.947)
  waiting for transfers between devices: 46.3 us -> 37.4 us
  other arithmetic: 7.94 us -> 1.99 us
  starting transfers between devices: 23.2 us -> 26.7 us
  blocking collectives: 27.1 us -> 30.4 us
  local copies, waits for them, and re-layouts: 11.2 us -> 8.32 us
    ppermute x4, waiting for transfers between devices: 13.4 us -> 0.01 us  [to_lower(): return lax.ppermute(x, axis, [((i + 1) % count, i) for i in range(count)])]
    convert_element_type x2 -> x0, other arithmetic: 5.16 us -> none  [per_device(): dpre = (grad * silu_grad(pre)).astype(jnp.bfloat16)]
    ppermute x4, waiting for transfers between devices: 17.8 us -> 22 us  [to_upper(): return lax.ppermute(x, axis, [(i, (i + 1) % count) for i in range(count)])]
    ppermute x4, starting transfers between devices: 15.6 us -> 19.4 us  [to_lower(): return lax.ppermute(x, axis, [((i + 1) % count, i) for i in range(count)])]
    all_to_all x1, blocking collectives: 27.1 us -> 30.4 us  [all_reduce(): mine = lax.all_to_all(pieces, axes, 0, 0, tiled=True).sum(0) * scale]
    slice x2 -> x0, local copies, waits for them, and re-layouts: 2.87 us -> none  [per_device(): lent_up_grad = to_lower(lent_grad[:lent], 'sector')]
    dot_general x2, matrix products: 0.99 us -> 3.44 us  [per_device(): self_part = jnp.dot(layer_in.T, dpre, preferred_element_type=jnp.float32)]
    pallas_call x2, Pallas kernels: 14.3 us -> 16.1 us  [block_slot_grad(): pl.pallas_call(slot_grad_kernel, grid_spec=pltpu.PrefetchScalarGridSpec(n...]
  transfers between devices with their start and end apart: 9 -> 9, of which waited for: 7 -> 5; matrix products, arithmetic and copies ran while one was open for 6% -> 8% of each run, Pallas kernels for 0% -> 0%
where the time goes in v7:
time: 160 us; the launch traced here: 159 us
  waiting for transfers between devices  37.4 us (23%)
  Pallas kernels  36.2 us (23%)
  blocking collectives  30.4 us (19%)
  starting transfers between devices  26.7 us (17%)
  matrix products  17.3 us (11%)
  local copies, waits for them, and re-layouts  8.32 us (5%)
  other arithmetic  1.99 us (1%)
    all_to_all x1, blocking collectives, all_reduce(): mine = lax.all_to_all(pieces, axes, 0, 0, tiled=True).sum(0) * scale  30.4 us
    ppermute x4, waiting for transfers between devices, to_upper(): return lax.ppermute(x, axis, [(i, (i + 1) % count) for i in range(count)])  22 us
    ppermute x4, starting transfers between devices, to_lower(): return lax.ppermute(x, axis, [((i + 1) % count, i) for i in range(count)])  19.4 us
    pallas_call x2, Pallas kernels, block_slot_grad(): pl.pallas_call(slot_grad_kernel, grid_spec=pltpu.PrefetchScalarGridSpec(n...  16.1 us
    all_to_all x1, waiting for transfers between devices, all_reduce(): return lax.all_to_all(spread, axes, 0, 0, tiled=True).reshape(x.shape)  15.5 us
    pallas_call x2, Pallas kernels, block_layer(): pl.pallas_call(layer_kernel, grid_spec=pltpu.PrefetchScalarGridSpec(num_s...  12.4 us
    pallas_call x2, Pallas kernels, fold_lent(): pl.pallas_call(fold_kernel, grid_spec=pltpu.PrefetchScalarGridSpec(num_sc...  7.69 us
    dot_general x2, matrix products, per_device(): jnp.dot(dmessage, w_message[layer_index].T, preferred_element_type=jnp.fl...  4.81 us
  transfers between devices with their start and end apart: 9, of which 5 were waited for; matrix products, arithmetic and copies ran while one was open for 8% of the time, Pallas kernels for 0%

profile of v7, /device:TPU:1, one launch (start us, length us, event | category | flops | bytes accessed | tf_op | source)
XLA Modules:
  0.0 159.2 jit_solution(14126230923417774408)
XLA Ops:
  0.7 1.0 dynamic-slice_reduce_fusion.2
  1.6 1.7 %convolution_convert_fusion.1 = bf16[2048,256]{1,0:T(8,128)(2,1)S(1)} fusion(bf16[1,2048,256]{2,1,0:T(8,128)(2,1)} %param.7, bf16[2,256,256]{2,1,0:T(8,128)(2,1)} %param.11), kind=kOutput, calls=%fused_computation.10 | convolution fusion | flops 268959744 | bytes 2228224 | tf_op jit(solution)/shard_map/dot_general | solution.py:194
  3.3 0.0 copy-start.4
  3.3 0.6 gather_fusion
  3.9 2.5 %collective-permute-start = (bf16[4,128,256]{2,1,0:T(8,128)(2,1)S(1)}, bf16[4,128,256]{2,1,0:T(8,128)(2,1)S(1)}, u32[]{:S(2)}, u32[]{:S(2)}) collective-permute-start(bf16[4,128,256]{2,1,0:T(8,128)(2,1)S(1)} %gather_fusion), channel_id=1, source_target_pairs={{0,1},{1,2},{2,3},{3,4},{4,5},{5,6},{6,7},{7,8},{8,9},{9,10},{10,1... | collective-permute-start | bytes 786440 | tf_op jit(solution)/shard_map/ppermute | solution.py:157
  6.4 0.6 gather_fusion.1
  7.0 4.7 %collective-permute-start.1 = (bf16[4,128,256]{2,1,0:T(8,128)(2,1)S(1)}, bf16[4,128,256]{2,1,0:T(8,128)(2,1)S(1)}, u32[]{:S(2)}, u32[]{:S(2)}) collective-permute-start(bf16[4,128,256]{2,1,0:T(8,128)(2,1)S(1)} %gather_fusion.1), channel_id=1, source_target_pairs={{1,0},{2,1},{3,2},{4,3},{5,4},{6,5},{7,6},{8,7},{9,8},{10,9},{11,1... | collective-permute-start | bytes 786440 | tf_op jit(solution)/shard_map/ppermute | solution.py:162
  11.6 0.7 copy.18.src_ref
  12.3 0.7 slice_bitcast_fusion
  13.0 3.9 %collective-permute-done = bf16[4,128,256]{2,1,0:T(8,128)(2,1)S(1)} collective-permute-done((bf16[4,128,256]{2,1,0:T(8,128)(2,1)S(1)}, bf16[4,128,256]{2,1,0:T(8,128)(2,1)S(1)}, u32[]{:S(2)}, u32[]{:S(2)}) %collective-permute-start) | collective-permute-done | bytes 262176 | tf_op jit(solution)/shard_map/ppermute | solution.py:157
  17.0 0.8 pad_maximum_fusion.1.lent_ref
  17.8 6.3 %shard_map.102 = (f32[16,128,256]{2,1,0:T(8,128)}, bf16[16,128,256]{2,1,0:T(8,128)(2,1)}) custom-call(s32[16,8]{1,0:T(8,128)} %copy.18.src_ref, bf16[16,8,128,128]{3,2,1,0:T(8,128)(2,1)} %bitcast.80, bf16[16,128,256]{2,1,0:T(8,128)(2,1)} %bitcast.90, bf16[8,128,256]{2,1,0:T(8,128)(2,1)} %pad_maximum_fusion.1.lent_ref, bf16[16,128,256]{2,1,0:T(8,128)(2,1)} %bitcast.97, ...), custom_call_target="tpu_custom_call" | custom-call | tf_op jit(solution)/shard_map/pallas_call | solution.py:44
  24.1 1.7 %convolution_convert_fusion = bf16[2048,256]{1,0:T(8,128)(2,1)S(1)} fusion(bf16[2048,256]{1,0:T(8,128)(2,1)} %bitcast.85, bf16[2,256,256]{2,1,0:T(8,128)(2,1)S(1)} %copy-done.8), kind=kOutput, calls=%fused_computation.9 | convolution fusion | flops 268959744 | bytes 2228224 | tf_op jit(solution)/shard_map/dot_general | solution.py:194
  25.8 0.6 gather_fusion.3
  26.3 0.6 gather_fusion.2
  26.9 0.1 collective-permute-start.2
  27.0 5.2 %collective-permute-start.3 = (bf16[4,128,256]{2,1,0:T(8,128)(2,1)S(1)}, bf16[4,128,256]{2,1,0:T(8,128)(2,1)S(1)}, u32[]{:S(2)}, u32[]{:S(2)}) collective-permute-start(bf16[4,128,256]{2,1,0:T(8,128)(2,1)S(1)} %gather_fusion.3), channel_id=1, source_target_pairs={{1,0},{2,1},{3,2},{4,3},{5,4},{6,5},{7,6},{8,7},{9,8},{10,9},{11,1... | collective-permute-start | bytes 786440 | tf_op jit(solution)/shard_map/ppermute | solution.py:162
  32.2 0.8 dynamic-slice_reduce_fusion.lists_ref
  33.0 4.3 %collective-permute-done.2 = bf16[4,128,256]{2,1,0:T(8,128)(2,1)S(1)} collective-permute-done((bf16[4,128,256]{2,1,0:T(8,128)(2,1)S(1)}, bf16[4,128,256]{2,1,0:T(8,128)(2,1)S(1)}, u32[]{:S(2)}, u32[]{:S(2)}) %collective-permute-start.2) | collective-permute-done | bytes 262176 | tf_op jit(solution)/shard_map/ppermute | solution.py:157
  37.3 0.8 pad_maximum_fusion.2.lent_ref
  38.1 6.1 %shard_map.103 = (f32[16,128,256]{2,1,0:T(8,128)}, bf16[16,128,256]{2,1,0:T(8,128)(2,1)}) custom-call(s32[16,8]{1,0:T(8,128)} %copy.18.src_ref, bf16[16,8,128,128]{3,2,1,0:T(8,128)(2,1)} %bitcast.81, bf16[16,128,256]{2,1,0:T(8,128)(2,1)} %bitcast.93, bf16[8,128,256]{2,1,0:T(8,128)(2,1)} %pad_maximum_fusion.2.lent_ref, ...), custom_call_target="tpu_custom_call" | custom-call | tf_op jit(solution)/shard_map/pallas_call | solution.py:44
  44.3 8.1 %shard_map.104 = (f32[16,128,256]{2,1,0:T(8,128)}, f32[4,128,256]{2,1,0:T(8,128)}, f32[4,128,256]{2,1,0:T(8,128)}, bf16[16,128,256]{2,1,0:T(8,128)(2,1)}) custom-call(s32[16,8]{1,0:T(8,128)} %copy.18.src_ref, bf16[16,8,128,128]{3,2,1,0:T(8,128)(2,1)} %bitcast.82, f32[16,128,256]{2,1,0:T(8,128)} %bitcast.87, f32[16,128,256]{2,1,0:T(8,128)} %get-tuple-element.18.pre_ref), custom_call_target="tpu_custom_call" | custom-call | tf_op jit(solution)/shard_map/pallas_call | solution.py:101
  52.3 0.1 collective-permute-start.4
  52.4 4.8 %collective-permute-start.5 = (f32[4,128,256]{2,1,0:T(8,128)}, f32[4,128,256]{2,1,0:T(8,128)}, u32[]{:S(2)}, u32[]{:S(2)}) collective-permute-start(f32[4,128,256]{2,1,0:T(8,128)} %get-tuple-element.22), channel_id=1, source_target_pairs={{1,0},{2,1},{3,2},{4,3},{5,4},{6,5},{7,6},{8,7},{9,8},{10,9},{11,1... | collective-permute-start | bytes 1572872 | tf_op jit(solution)/shard_map/ppermute | solution.py:162
  57.2 1.7 %convolution_bitcast_fusion = f32[1,256,256]{2,1,0:T(8,128)S(1)} fusion(bf16[16,128,256]{2,1,0:T(8,128)(2,1)S(1)} %copy-done.1, bf16[16,128,256]{2,1,0:T(8,128)(2,1)} %get-tuple-element.19), kind=kOutput, calls=%fused_computation.11 | convolution fusion | flops 268435456 | bytes 2359296 | tf_op jit(solution)/shard_map/dot_general | solution.py:222
  58.9 1.7 %convolution_add_fusion.3 = f32[2048,256]{1,0:T(8,128)S(1)} fusion(bf16[2048,256]{1,0:T(8,128)(2,1)} %bitcast.98, f32[1,2048,256]{2,1,0:T(8,128)S(1)} %copy-done.3, bf16[2,256,256]{2,1,0:T(8,128)(2,1)S(1)} %copy-done.11), kind=kOutput, calls=%fused_computation.8 | convolution fusion | flops 268959744 | bytes 5373952 | tf_op jit(solution)/shard_map/dot_general | solution.py:226
  60.6 6.8 %collective-permute-done.4.lower_ref = f32[4,128,256]{2,1,0:T(8,128)} collective-permute-done((f32[4,128,256]{2,1,0:T(8,128)}, f32[4,128,256]{2,1,0:T(8,128)}, u32[]{:S(2)}, u32[]{:S(2)}) %collective-permute-start.4) | collective-permute-done | bytes 524320 | tf_op jit(solution)/shard_map/ppermute | solution.py:157
  67.4 3.9 %shard_map.105 = bf16[16,128,256]{2,1,0:T(8,128)(2,1)} custom-call(s32[2,4]{1,0:T(2,128)} %dynamic-slice_reduce_fusion.lists_ref, f32[16,128,256]{2,1,0:T(8,128)} %get-tuple-element.20.slot_ref, f32[4,128,256]{2,1,0:T(8,128)} %collective-permute-done.4.lower_ref, f32[4,128,256]{2,1,0:T(8,128)} %collective-permute-done.5.upper_ref), custom_call_target="tpu_custom_call" | custom-call | tf_op jit(solution)/shard_map/pallas_call | solution.py:138
  71.2 3.0 %convolution_add_fusion.2 = f32[2048,256]{1,0:T(8,128)} fusion(f32[2048,256]{1,0:T(8,128)S(1)} %convolution_add_fusion.3, bf16[2048,256]{1,0:T(8,128)(2,1)} %bitcast.86, bf16[2,256,256]{2,1,0:T(8,128)(2,1)} %param.11), kind=kOutput, calls=%fused_computation.7 | convolution fusion | flops 268959744 | bytes 5373952 | tf_op jit(solution)/shard_map/dot_general | solution.py:227
  74.3 8.1 %shard_map.106 = (f32[16,128,256]{2,1,0:T(8,128)}, f32[4,128,256]{2,1,0:T(8,128)}, f32[4,128,256]{2,1,0:T(8,128)}, bf16[16,128,256]{2,1,0:T(8,128)(2,1)}) custom-call(s32[16,8]{1,0:T(8,128)} %copy.18.src_ref, bf16[16,8,128,128]{3,2,1,0:T(8,128)(2,1)} %bitcast.83, f32[16,128,256]{2,1,0:T(8,128)} %bitcast.84, f32[16,128,256]{2,1,0:T(8,128)} %get-tuple-element.23.pre_ref), custom_call_target="tpu_custom_call" | custom-call | tf_op jit(solution)/shard_map/pallas_call | solution.py:101
  82.3 4.8 %collective-permute-start.7 = (f32[4,128,256]{2,1,0:T(8,128)}, f32[4,128,256]{2,1,0:T(8,128)}, u32[]{:S(2)}, u32[]{:S(2)}) collective-permute-start(f32[4,128,256]{2,1,0:T(8,128)} %get-tuple-element.27), channel_id=1, source_target_pairs={{1,0},{2,1},{3,2},{4,3},{5,4},{6,5},{7,6},{8,7},{9,8},{10,9},{11,1... | collective-permute-start | bytes 1572872 | tf_op jit(solution)/shard_map/ppermute | solution.py:162
  87.1 1.7 %convolution_bitcast_fusion.1 = f32[1,256,256]{2,1,0:T(8,128)S(1)} fusion(bf16[2048,256]{1,0:T(8,128)(2,1)} %bitcast.99, bf16[1,2048,256]{2,1,0:T(8,128)(2,1)S(1)} %copy-done.7), kind=kOutput, calls=%fused_computation.12 | convolution fusion | flops 268435456 | bytes 2359296 | tf_op jit(solution)/shard_map/dot_general | solution.py:222
  88.9 0.5 convolution_bitcast_fusion.2
  89.4 7.0 %collective-permute-done.6.lower_ref = f32[4,128,256]{2,1,0:T(8,128)S(1)} collective-permute-done((f32[4,128,256]{2,1,0:T(8,128)}, f32[4,128,256]{2,1,0:T(8,128)S(1)}, u32[]{:S(2)}, u32[]{:S(2)}) %collective-permute-start.6) | collective-permute-done | bytes 524320 | tf_op jit(solution)/shard_map/ppermute | solution.py:157
  96.4 0.8 copy-done.13
  97.1 3.8 %shard_map.107 = bf16[16,128,256]{2,1,0:T(8,128)(2,1)} custom-call(s32[2,4]{1,0:T(2,128)} %dynamic-slice_reduce_fusion.lists_ref, f32[16,128,256]{2,1,0:T(8,128)} %get-tuple-element.25.slot_ref, f32[4,128,256]{2,1,0:T(8,128)} %copy-done.13, f32[4,128,256]{2,1,0:T(8,128)} %collective-permute-done.7.upper_ref), custom_call_target="tpu_custom_call" | custom-call | tf_op jit(solution)/shard_map/pallas_call | solution.py:138
  101.0 1.7 %convolution_bitcast_fusion.3 = f32[1,256,256]{2,1,0:T(8,128)S(1)} fusion(bf16[2048,256]{1,0:T(8,128)(2,1)} %bitcast.94, bf16[1,2048,256]{2,1,0:T(8,128)(2,1)S(1)} %copy-done.7), kind=kOutput, calls=%fused_computation.14 | convolution fusion | flops 268435456 | bytes 2359296 | tf_op jit(solution)/shard_map/dot_general | solution.py:223
  102.8 0.1 pad_maximum_fusion
  102.9 30.4 %all_to_all.10 = f32[128,8,256]{2,1,0:T(8,128)S(1)} all-to-all(f32[128,8,256]{2,1,0:T(8,128)S(1)} %bitcast.96), channel_id=1, replica_groups=mesh['dp'=8,'sector'=16] {'dp','sector'}, dimensions={0} | all-to-all | bytes 2097152 | tf_op jit(solution)/shard_map/all_to_all | solution.py:169
  133.3 0.1 reduce_sum.9
  133.4 1.1 broadcast_in_dim.5
  134.5 4.5 %all-to-all-start.1 = ((f32[128,8,256]{2,1,0:T(8,128)}), f32[128,8,256]{2,1,0:T(8,128)S(1)}, u32[]{:S(2)}, u32[]{:S(2)}) async-start(f32[128,8,256]{2,1,0:T(8,128)} %broadcast_in_dim.5), calls=%async_computation.1 | async-start | bytes 2097152 | tf_op jit(solution)/shard_map/all_to_all | solution.py:171
  139.0 0.0 copy-start.6
  139.0 0.0 copy-start.9
  139.0 1.8 %convolution_add_fusion.1 = f32[2048,256]{1,0:T(8,128)S(1)} fusion(f32[2048,256]{1,0:T(8,128)S(1)} %copy-done, bf16[2048,256]{1,0:T(8,128)(2,1)} %bitcast.100, bf16[2,256,256]{2,1,0:T(8,128)(2,1)S(1)} %copy-done.12), kind=kOutput, calls=%fused_computation.6 | convolution fusion | flops 268959744 | bytes 5373952 | tf_op jit(solution)/shard_map/dot_general | solution.py:226
  140.9 1.8 %fusion = f32[1,2048,256]{2,1,0:T(8,128)} fusion(f32[2048,256]{1,0:T(8,128)S(1)} %convolution_add_fusion.1, bf16[2048,256]{1,0:T(8,128)(2,1)S(1)} %bitcast.95, bf16[2,256,256]{2,1,0:T(8,128)(2,1)S(1)} %copy-done.9), kind=kOutput, calls=%fused_computation.5 | convolution fusion | flops 268959744 | bytes 5373952 | tf_op jit(solution)/shard_map/dot_general | solution.py:227
  142.6 15.5 %all-to-all-done.1 = f32[128,8,256]{2,1,0:T(8,128)S(1)} async-done(((f32[128,8,256]{2,1,0:T(8,128)}), f32[128,8,256]{2,1,0:T(8,128)S(1)}, u32[]{:S(2)}, u32[]{:S(2)}) %all-to-all-start.1) | async-done | bytes 1048608 | tf_op jit(solution)/shard_map/all_to_all | solution.py:171
  158.1 1.0 fusion.14
  (39 shorter events, 0.2 us)
Async XLA Ops:
  0.6 11.0 %copy-start.15 = (s32[1,16,8]{1,2,0:T(8,128)S(1)}, s32[1,16,8]{1,2,0:T(8,128)}, u32[]{:S(2)}) copy-start(s32[1,16,8]{1,2,0:T(8,128)} %param.9) | copy-start | bytes 1540
  0.6 11.7 %copy-start.10 = (bf16[2,256,256]{2,1,0:T(8,128)(2,1)S(1)}, bf16[2,256,256]{2,1,0:T(8,128)(2,1)}, u32[]{:S(2)}) copy-start(bf16[2,256,256]{2,1,0:T(8,128)(2,1)} %param.12) | copy-start | bytes 786436
  3.3 14.5 %copy-start.4 = (bf16[2048,256]{1,0:T(8,128)(2,1)}, bf16[2048,256]{1,0:T(8,128)(2,1)S(1)}, u32[]{:S(2)}) copy-start(bf16[2048,256]{1,0:T(8,128)(2,1)S(1)} %convolution_convert_fusion.1) | copy-start | bytes 3145732
  3.9 13.1 %collective-permute-start = (bf16[4,128,256]{2,1,0:T(8,128)(2,1)S(1)}, bf16[4,128,256]{2,1,0:T(8,128)(2,1)S(1)}, u32[]{:S(2)}, u32[]{:S(2)}) collective-permute-start(bf16[4,128,256]{2,1,0:T(8,128)(2,1)S(1)} %gather_fusion), channel_id=1, source_target_pairs={{0,1},{1,2},{2,3},{3,4},{4,5},{5,6},{6,7},{7,8},{8,9},{9,10},{10,1... | collective-permute-start | bytes 786440 | tf_op jit(solution)/shard_map/ppermute | solution.py:157
  7.0 10.0 %collective-permute-start.1 = (bf16[4,128,256]{2,1,0:T(8,128)(2,1)S(1)}, bf16[4,128,256]{2,1,0:T(8,128)(2,1)S(1)}, u32[]{:S(2)}, u32[]{:S(2)}) collective-permute-start(bf16[4,128,256]{2,1,0:T(8,128)(2,1)S(1)} %gather_fusion.1), channel_id=1, source_target_pairs={{1,0},{2,1},{3,2},{4,3},{5,4},{6,5},{7,6},{8,7},{9,8},{10,9},{11,1... | collective-permute-start | bytes 786440 | tf_op jit(solution)/shard_map/ppermute | solution.py:162
  17.8 6.3 %copy-start.8 = (bf16[2,256,256]{2,1,0:T(8,128)(2,1)S(1)}, bf16[2,256,256]{2,1,0:T(8,128)(2,1)}, u32[]{:S(2)}) copy-start(bf16[2,256,256]{2,1,0:T(8,128)(2,1)} %param.11) | copy-start | bytes 786436
  24.1 8.1 %copy-start.14 = (s32[1,16,2,4]{1,3,2,0:T(4,128)S(1)}, s32[1,16,2,4]{1,3,2,0:T(4,128)}, u32[]{:S(2)}) copy-start(s32[1,16,2,4]{1,3,2,0:T(4,128)} %param.10) | copy-start | bytes 1540
  25.8 12.4 %copy-start.5 = (bf16[2048,256]{1,0:T(8,128)(2,1)}, bf16[2048,256]{1,0:T(8,128)(2,1)S(1)}, u32[]{:S(2)}) copy-start(bf16[2048,256]{1,0:T(8,128)(2,1)S(1)} %convolution_convert_fusion) | copy-start | bytes 3145732
  26.9 10.4 %collective-permute-start.2 = (bf16[4,128,256]{2,1,0:T(8,128)(2,1)S(1)}, bf16[4,128,256]{2,1,0:T(8,128)(2,1)S(1)}, u32[]{:S(2)}, u32[]{:S(2)}) collective-permute-start(bf16[4,128,256]{2,1,0:T(8,128)(2,1)S(1)} %gather_fusion.2), channel_id=1, source_target_pairs={{0,1},{1,2},{2,3},{3,4},{4,5},{5,6},{6,7},{7,8},{8,9},{9,10},{10,1... | collective-permute-start | bytes 786440 | tf_op jit(solution)/shard_map/ppermute | solution.py:157
  27.0 10.3 %collective-permute-start.3 = (bf16[4,128,256]{2,1,0:T(8,128)(2,1)S(1)}, bf16[4,128,256]{2,1,0:T(8,128)(2,1)S(1)}, u32[]{:S(2)}, u32[]{:S(2)}) collective-permute-start(bf16[4,128,256]{2,1,0:T(8,128)(2,1)S(1)} %gather_fusion.3), channel_id=1, source_target_pairs={{1,0},{2,1},{3,2},{4,3},{5,4},{6,5},{7,6},{8,7},{9,8},{10,9},{11,1... | collective-permute-start | bytes 786440 | tf_op jit(solution)/shard_map/ppermute | solution.py:162
  44.3 12.9 %copy-start.1 = (bf16[16,128,256]{2,1,0:T(8,128)(2,1)S(1)}, bf16[16,128,256]{2,1,0:T(8,128)(2,1)}, u32[]{:S(2)}) copy-start(bf16[16,128,256]{2,1,0:T(8,128)(2,1)} %get-tuple-element.16.hits_ref) | copy-start | bytes 3145732
  52.3 6.6 %copy-start.3 = (f32[1,2048,256]{2,1,0:T(8,128)S(1)}, f32[1,2048,256]{2,1,0:T(8,128)}, u32[]{:S(2)}) copy-start(f32[1,2048,256]{2,1,0:T(8,128)} %param.13) | copy-start | bytes 6291460
  52.3 6.6 %copy-start.11 = (bf16[2,256,256]{2,1,0:T(8,128)(2,1)S(1)}, bf16[2,256,256]{2,1,0:T(8,128)(2,1)}, u32[]{:S(2)}) copy-start(bf16[2,256,256]{2,1,0:T(8,128)(2,1)} %param.12) | copy-start | bytes 786436
  52.3 15.1 %collective-permute-start.4 = (f32[4,128,256]{2,1,0:T(8,128)}, f32[4,128,256]{2,1,0:T(8,128)}, u32[]{:S(2)}, u32[]{:S(2)}) collective-permute-start(f32[4,128,256]{2,1,0:T(8,128)} %get-tuple-element.21), channel_id=1, source_target_pairs={{0,1},{1,2},{2,3},{3,4},{4,5},{5,6},{6,7},{7,8},{8,9},{9,10},{10,1... | collective-permute-start | bytes 1572872 | tf_op jit(solution)/shard_map/ppermute | solution.py:157
  52.4 15.0 %collective-permute-start.5 = (f32[4,128,256]{2,1,0:T(8,128)}, f32[4,128,256]{2,1,0:T(8,128)}, u32[]{:S(2)}, u32[]{:S(2)}) collective-permute-start(f32[4,128,256]{2,1,0:T(8,128)} %get-tuple-element.22), channel_id=1, source_target_pairs={{1,0},{2,1},{3,2},{4,3},{5,4},{6,5},{7,6},{8,7},{9,8},{10,9},{11,1... | collective-permute-start | bytes 1572872 | tf_op jit(solution)/shard_map/ppermute | solution.py:162
  74.3 12.8 %copy-start.7 = (bf16[1,2048,256]{2,1,0:T(8,128)(2,1)S(1)}, bf16[1,2048,256]{2,1,0:T(8,128)(2,1)}, u32[]{:S(2)}) copy-start(bf16[1,2048,256]{2,1,0:T(8,128)(2,1)} %param.7) | copy-start | bytes 3145732
  82.3 6.6 %copy-start.2 = (bf16[16,128,256]{2,1,0:T(8,128)(2,1)S(1)}, bf16[16,128,256]{2,1,0:T(8,128)(2,1)}, u32[]{:S(2)}) copy-start(bf16[16,128,256]{2,1,0:T(8,128)(2,1)} %shard_map.105) | copy-start | bytes 3145732
  82.3 14.0 %collective-permute-start.6 = (f32[4,128,256]{2,1,0:T(8,128)}, f32[4,128,256]{2,1,0:T(8,128)S(1)}, u32[]{:S(2)}, u32[]{:S(2)}) collective-permute-start(f32[4,128,256]{2,1,0:T(8,128)} %get-tuple-element.26), channel_id=1, source_target_pairs={{0,1},{1,2},{2,3},{3,4},{4,5},{5,6},{6,7},{7,8},{8,9},{9,10},{10,1... | collective-permute-start | bytes 1572872 | tf_op jit(solution)/shard_map/ppermute | solution.py:157
  82.3 14.0 %collective-permute-start.7 = (f32[4,128,256]{2,1,0:T(8,128)}, f32[4,128,256]{2,1,0:T(8,128)}, u32[]{:S(2)}, u32[]{:S(2)}) collective-permute-start(f32[4,128,256]{2,1,0:T(8,128)} %get-tuple-element.27), channel_id=1, source_target_pairs={{1,0},{2,1},{3,2},{4,3},{5,4},{6,5},{7,6},{8,7},{9,8},{10,9},{11,1... | collective-permute-start | bytes 1572872 | tf_op jit(solution)/shard_map/ppermute | solution.py:162
  96.4 0.8 copy-start.13
  133.2 5.7 %copy-start = (f32[2048,256]{1,0:T(8,128)S(1)}, f32[2048,256]{1,0:T(8,128)}, u32[]{:S(2)}) copy-start(f32[2048,256]{1,0:T(8,128)} %convolution_add_fusion.2) | copy-start | bytes 6291460
  133.3 5.8 %copy-start.12 = (bf16[2,256,256]{2,1,0:T(8,128)(2,1)S(1)}, bf16[2,256,256]{2,1,0:T(8,128)(2,1)}, u32[]{:S(2)}) copy-start(bf16[2,256,256]{2,1,0:T(8,128)(2,1)} %param.12) | copy-start | bytes 786436
  134.5 23.7 %all-to-all-start.1 = ((f32[128,8,256]{2,1,0:T(8,128)}), f32[128,8,256]{2,1,0:T(8,128)S(1)}, u32[]{:S(2)}, u32[]{:S(2)}) async-start(f32[128,8,256]{2,1,0:T(8,128)} %broadcast_in_dim.5), calls=%async_computation.1 | async-start | bytes 2097152 | tf_op jit(solution)/shard_map/all_to_all | solution.py:171
  139.0 1.8 %copy-start.6 = (bf16[16,128,256]{2,1,0:T(8,128)(2,1)S(1)}, bf16[16,128,256]{2,1,0:T(8,128)(2,1)}, u32[]{:S(2)}) copy-start(bf16[16,128,256]{2,1,0:T(8,128)(2,1)} %shard_map.107) | copy-start | bytes 3145732
  139.0 1.8 %copy-start.9 = (bf16[2,256,256]{2,1,0:T(8,128)(2,1)S(1)}, bf16[2,256,256]{2,1,0:T(8,128)(2,1)}, u32[]{:S(2)}) copy-start(bf16[2,256,256]{2,1,0:T(8,128)(2,1)} %param.11) | copy-start | bytes 786436

commit v8 on v7

--- a/solution.py
+++ b/solution.py
@@ -88,8 +88,8 @@
         own = own_ref.shape[0]
         lent = low_ref.shape[0]
         own_ref[...] = out_ref[:own]
-        low_ref[...] = out_ref[own : own + lent]
-        high_ref[...] = out_ref[own + lent :]
+        low_ref[...] = out_ref[own : own + lent].astype(low_ref.dtype)
+        high_ref[...] = out_ref[own + lent :].astype(high_ref.dtype)
 
 
 def block_slot_grad(slot_ids, tile_data, grad_blocks, pre_blocks, slot_count):
@@ -113,8 +113,8 @@
         ),
         out_shape=[
             jax.ShapeDtypeStruct((blocks, rows, width), jnp.float32),
-            jax.ShapeDtypeStruct((lent, rows, width), jnp.float32),
-            jax.ShapeDtypeStruct((lent, rows, width), jnp.float32),
+            jax.ShapeDtypeStruct((lent, rows, width), jnp.bfloat16),
+            jax.ShapeDtypeStruct((lent, rows, width), jnp.bfloat16),
             jax.ShapeDtypeStruct((blocks, rows, width), jnp.bfloat16),
         ],
         compiler_params=pltpu.CompilerParams(dimension_semantics=("arbitrary",)),
@@ -125,10 +125,10 @@
     acc_ref[...] = slot_ref[...]
     for i in range(lower_ref.shape[0]):
         block = lists_ref[1, i]
-        acc_ref[block] += lower_ref[i]
+        acc_ref[block] += lower_ref[i].astype(jnp.float32)
     for i in range(upper_ref.shape[0]):
         block = lists_ref[0, i]
-        acc_ref[block] += upper_ref[i]
+        acc_ref[block] += upper_ref[i].astype(jnp.float32)
     out_ref[...] = acc_ref[...].astype(out_ref.dtype)
 
 

time: 160 us -> 151 us (0.944)
  waiting for transfers between devices: 37.4 us -> 27.8 us
    ppermute x4, waiting for transfers between devices: 22 us -> 12.4 us  [to_upper(): return lax.ppermute(x, axis, [(i, (i + 1) % count) for i in range(count)])]
  transfers between devices with their start and end apart: 9 -> 9, of which waited for: 5 -> 5; matrix products, arithmetic and copies ran while one was open for 8% -> 7% of each run, Pallas kernels for 0% -> 0%
where the time goes in v8:
time: 151 us; the launch traced here: 150 us
  Pallas kernels  35.5 us (24%)
  blocking collectives  31.6 us (21%)
  waiting for transfers between devices  27.8 us (18%)
  starting transfers between devices  26.7 us (18%)
  matrix products  17.6 us (12%)
  local copies, waits for them, and re-layouts  8.34 us (6%)
  other arithmetic  1.99 us (1%)
    all_to_all x1, blocking collectives, all_reduce(): mine = lax.all_to_all(pieces, axes, 0, 0, tiled=True).sum(0) * scale  31.6 us
    ppermute x4, starting transfers between devices, to_lower(): return lax.ppermute(x, axis, [((i + 1) % count, i) for i in range(count)])  19.4 us
    pallas_call x2, Pallas kernels, block_slot_grad(): pl.pallas_call(slot_grad_kernel, grid_spec=pltpu.PrefetchScalarGridSpec(n...  15.7 us
    all_to_all x1, waiting for transfers between devices, all_reduce(): return lax.all_to_all(spread, axes, 0, 0, tiled=True).reshape(x.shape)  15.5 us
    pallas_call x2, Pallas kernels, block_layer(): pl.pallas_call(layer_kernel, grid_spec=pltpu.PrefetchScalarGridSpec(num_s...  12.4 us
    ppermute x4, waiting for transfers between devices, to_upper(): return lax.ppermute(x, axis, [(i, (i + 1) % count) for i in range(count)])  12.4 us
    pallas_call x2, Pallas kernels, fold_lent(): pl.pallas_call(fold_kernel, grid_spec=pltpu.PrefetchScalarGridSpec(num_sc...  7.39 us
    dot_general x2, matrix products, per_device(): jnp.dot(dpre, w_self[layer_index].T, preferred_element_type=jnp.float32)  4.94 us
  transfers between devices with their start and end apart: 9, of which 5 were waited for; matrix products, arithmetic and copies ran while one was open for 7% of the time, Pallas kernels for 0%

profile of v8, /device:TPU:1, one launch (start us, length us, event | category | flops | bytes accessed | tf_op | source)
XLA Modules:
  0.0 150.4 jit_solution(6161208178830434339)
XLA Ops:
  0.7 1.0 dynamic-slice_reduce_fusion.2
  1.6 1.7 %convolution_convert_fusion.1 = bf16[2048,256]{1,0:T(8,128)(2,1)S(1)} fusion(bf16[1,2048,256]{2,1,0:T(8,128)(2,1)} %param.7, bf16[2,256,256]{2,1,0:T(8,128)(2,1)} %param.11), kind=kOutput, calls=%fused_computation.10 | convolution fusion | flops 268959744 | bytes 2228224 | tf_op jit(solution)/shard_map/dot_general | solution.py:194
  3.3 0.0 copy-start.5
  3.3 0.6 gather_fusion
  3.9 2.5 %collective-permute-start = (bf16[4,128,256]{2,1,0:T(8,128)(2,1)S(1)}, bf16[4,128,256]{2,1,0:T(8,128)(2,1)S(1)}, u32[]{:S(2)}, u32[]{:S(2)}) collective-permute-start(bf16[4,128,256]{2,1,0:T(8,128)(2,1)S(1)} %gather_fusion), channel_id=1, source_target_pairs={{0,1},{1,2},{2,3},{3,4},{4,5},{5,6},{6,7},{7,8},{8,9},{9,10},{10,1... | collective-permute-start | bytes 786440 | tf_op jit(solution)/shard_map/ppermute | solution.py:157
  6.4 0.6 gather_fusion.1
  7.0 4.7 %collective-permute-start.1 = (bf16[4,128,256]{2,1,0:T(8,128)(2,1)S(1)}, bf16[4,128,256]{2,1,0:T(8,128)(2,1)S(1)}, u32[]{:S(2)}, u32[]{:S(2)}) collective-permute-start(bf16[4,128,256]{2,1,0:T(8,128)(2,1)S(1)} %gather_fusion.1), channel_id=1, source_target_pairs={{1,0},{2,1},{3,2},{4,3},{5,4},{6,5},{7,6},{8,7},{9,8},{10,9},{11,1... | collective-permute-start | bytes 786440 | tf_op jit(solution)/shard_map/ppermute | solution.py:162
  11.6 0.7 copy.18.src_ref
  12.3 0.7 slice_bitcast_fusion
  13.0 3.9 %collective-permute-done = bf16[4,128,256]{2,1,0:T(8,128)(2,1)S(1)} collective-permute-done((bf16[4,128,256]{2,1,0:T(8,128)(2,1)S(1)}, bf16[4,128,256]{2,1,0:T(8,128)(2,1)S(1)}, u32[]{:S(2)}, u32[]{:S(2)}) %collective-permute-start) | collective-permute-done | bytes 262176 | tf_op jit(solution)/shard_map/ppermute | solution.py:157
  17.0 0.8 pad_maximum_fusion.1.lent_ref
  17.8 6.3 %shard_map.102 = (f32[16,128,256]{2,1,0:T(8,128)}, bf16[16,128,256]{2,1,0:T(8,128)(2,1)}) custom-call(s32[16,8]{1,0:T(8,128)} %copy.18.src_ref, bf16[16,8,128,128]{3,2,1,0:T(8,128)(2,1)} %bitcast.80, bf16[16,128,256]{2,1,0:T(8,128)(2,1)} %bitcast.90, bf16[8,128,256]{2,1,0:T(8,128)(2,1)} %pad_maximum_fusion.1.lent_ref, bf16[16,128,256]{2,1,0:T(8,128)(2,1)} %bitcast.95, ...), custom_call_target="tpu_custom_call" | custom-call | tf_op jit(solution)/shard_map/pallas_call | solution.py:44
  24.1 1.7 %convolution_convert_fusion = bf16[2048,256]{1,0:T(8,128)(2,1)S(1)} fusion(bf16[2048,256]{1,0:T(8,128)(2,1)} %bitcast.85, bf16[2,256,256]{2,1,0:T(8,128)(2,1)S(1)} %copy-done.10), kind=kOutput, calls=%fused_computation.9 | convolution fusion | flops 268959744 | bytes 2228224 | tf_op jit(solution)/shard_map/dot_general | solution.py:194
  25.8 0.6 gather_fusion.3
  26.4 0.6 gather_fusion.2
  26.9 0.1 collective-permute-start.2
  27.0 5.2 %collective-permute-start.3 = (bf16[4,128,256]{2,1,0:T(8,128)(2,1)S(1)}, bf16[4,128,256]{2,1,0:T(8,128)(2,1)S(1)}, u32[]{:S(2)}, u32[]{:S(2)}) collective-permute-start(bf16[4,128,256]{2,1,0:T(8,128)(2,1)S(1)} %gather_fusion.3), channel_id=1, source_target_pairs={{1,0},{2,1},{3,2},{4,3},{5,4},{6,5},{7,6},{8,7},{9,8},{10,9},{11,1... | collective-permute-start | bytes 786440 | tf_op jit(solution)/shard_map/ppermute | solution.py:162
  32.2 0.8 dynamic-slice_reduce_fusion.lists_ref
  33.0 4.3 %collective-permute-done.2 = bf16[4,128,256]{2,1,0:T(8,128)(2,1)S(1)} collective-permute-done((bf16[4,128,256]{2,1,0:T(8,128)(2,1)S(1)}, bf16[4,128,256]{2,1,0:T(8,128)(2,1)S(1)}, u32[]{:S(2)}, u32[]{:S(2)}) %collective-permute-start.2) | collective-permute-done | bytes 262176 | tf_op jit(solution)/shard_map/ppermute | solution.py:157
  37.3 0.8 pad_maximum_fusion.2.lent_ref
  38.1 6.1 %shard_map.103 = (f32[16,128,256]{2,1,0:T(8,128)}, bf16[16,128,256]{2,1,0:T(8,128)(2,1)}) custom-call(s32[16,8]{1,0:T(8,128)} %copy.18.src_ref, bf16[16,8,128,128]{3,2,1,0:T(8,128)(2,1)} %bitcast.81, bf16[16,128,256]{2,1,0:T(8,128)(2,1)} %bitcast.93, bf16[8,128,256]{2,1,0:T(8,128)(2,1)} %pad_maximum_fusion.2.lent_ref, ...), custom_call_target="tpu_custom_call" | custom-call | tf_op jit(solution)/shard_map/pallas_call | solution.py:44
  44.3 7.9 %shard_map.104 = (f32[16,128,256]{2,1,0:T(8,128)}, bf16[4,128,256]{2,1,0:T(8,128)(2,1)}, bf16[4,128,256]{2,1,0:T(8,128)(2,1)}, bf16[16,128,256]{2,1,0:T(8,128)(2,1)}) custom-call(s32[16,8]{1,0:T(8,128)} %copy.18.src_ref, bf16[16,8,128,128]{3,2,1,0:T(8,128)(2,1)} %bitcast.82, f32[16,128,256]{2,1,0:T(8,128)} %bitcast.87, f32[16,128,256]{2,1,0:T(8,128)} %get-tuple-element.18.pre_ref), custom_call_target="tpu_custom_call" | custom-call | tf_op jit(solution)/shard_map/pallas_call | solution.py:101
  52.1 4.8 %collective-permute-start.5 = (bf16[4,128,256]{2,1,0:T(8,128)(2,1)}, bf16[4,128,256]{2,1,0:T(8,128)(2,1)}, u32[]{:S(2)}, u32[]{:S(2)}) collective-permute-start(bf16[4,128,256]{2,1,0:T(8,128)(2,1)} %get-tuple-element.22), channel_id=1, source_target_pairs={{1,0},{2,1},{3,2},{4,3},{5,4},{6,5},{7,6},{8,7},{9,8},{10,9},{11,1... | collective-permute-start | bytes 786440 | tf_op jit(solution)/shard_map/ppermute | solution.py:162
  56.9 3.1 %convolution_add_fusion.3 = f32[2048,256]{1,0:T(8,128)} fusion(bf16[2048,256]{1,0:T(8,128)(2,1)} %bitcast.96, f32[1,2048,256]{2,1,0:T(8,128)S(1)} %copy-done.3, bf16[2,256,256]{2,1,0:T(8,128)(2,1)S(1)} %copy-done.12), kind=kOutput, calls=%fused_computation.8 | convolution fusion | flops 268959744 | bytes 5373952 | tf_op jit(solution)/shard_map/dot_general | solution.py:226
  60.1 0.5 convolution_bitcast_fusion
  60.6 1.0 collective-permute-done.4.lower_ref
  61.5 3.7 %shard_map.105 = bf16[16,128,256]{2,1,0:T(8,128)(2,1)} custom-call(s32[2,4]{1,0:T(2,128)} %dynamic-slice_reduce_fusion.lists_ref, f32[16,128,256]{2,1,0:T(8,128)} %get-tuple-element.20.slot_ref, bf16[4,128,256]{2,1,0:T(8,128)(2,1)} %collective-permute-done.4.lower_ref, bf16[4,128,256]{2,1,0:T(8,128)(2,1)} %collective-permute-done.5.upper_ref), custom_call_target="tpu_custom_call" | custom-call | tf_op jit(solution)/shard_map/pallas_call | solution.py:138
  65.2 3.0 %convolution_add_fusion.2 = f32[2048,256]{1,0:T(8,128)} fusion(f32[2048,256]{1,0:T(8,128)S(1)} %copy-done.4, bf16[2048,256]{1,0:T(8,128)(2,1)} %bitcast.86, bf16[2,256,256]{2,1,0:T(8,128)(2,1)} %param.11), kind=kOutput, calls=%fused_computation.7 | convolution fusion | flops 268959744 | bytes 5373952 | tf_op jit(solution)/shard_map/dot_general | solution.py:227
  68.3 7.9 %shard_map.106 = (f32[16,128,256]{2,1,0:T(8,128)}, bf16[4,128,256]{2,1,0:T(8,128)(2,1)}, bf16[4,128,256]{2,1,0:T(8,128)(2,1)}, bf16[16,128,256]{2,1,0:T(8,128)(2,1)}) custom-call(s32[16,8]{1,0:T(8,128)} %copy.18.src_ref, bf16[16,8,128,128]{3,2,1,0:T(8,128)(2,1)} %bitcast.83, f32[16,128,256]{2,1,0:T(8,128)} %bitcast.84, f32[16,128,256]{2,1,0:T(8,128)} %get-tuple-element.23.pre_ref), custom_call_target="tpu_custom_call" | custom-call | tf_op jit(solution)/shard_map/pallas_call | solution.py:101
  76.1 1.9 %convolution_bitcast_fusion.1 = f32[1,256,256]{2,1,0:T(8,128)S(1)} fusion(bf16[2048,256]{1,0:T(8,128)(2,1)} %bitcast.99, bf16[1,2048,256]{2,1,0:T(8,128)(2,1)S(1)} %copy-done.7), kind=kOutput, calls=%fused_computation.12 | convolution fusion | flops 268435456 | bytes 2359296 | tf_op jit(solution)/shard_map/dot_general | solution.py:222
  78.0 0.1 collective-permute-start.6
  78.1 4.8 %collective-permute-start.7 = (bf16[4,128,256]{2,1,0:T(8,128)(2,1)S(1)}, bf16[4,128,256]{2,1,0:T(8,128)(2,1)S(1)}, u32[]{:S(2)}, u32[]{:S(2)}) collective-permute-start(bf16[4,128,256]{2,1,0:T(8,128)(2,1)S(1)} %copy-done.18), channel_id=1, source_target_pairs={{1,0},{2,1},{3,2},{4,3},{5,4},{6,5},{7,6},{8,7},{9,8},{10,9},{11,1... | collective-permute-start | bytes 786440 | tf_op jit(solution)/shard_map/ppermute | solution.py:162
  82.9 0.5 convolution_bitcast_fusion.2
  83.4 3.2 %collective-permute-done.6.lower_ref = bf16[4,128,256]{2,1,0:T(8,128)(2,1)S(1)} collective-permute-done((bf16[4,128,256]{2,1,0:T(8,128)(2,1)S(1)}, bf16[4,128,256]{2,1,0:T(8,128)(2,1)S(1)}, u32[]{:S(2)}, u32[]{:S(2)}) %collective-permute-start.6) | collective-permute-done | bytes 262176 | tf_op jit(solution)/shard_map/ppermute | solution.py:157
  86.6 0.7 copy-done.14
  87.3 0.1 copy-done.15
  87.4 3.7 %shard_map.107 = bf16[16,128,256]{2,1,0:T(8,128)(2,1)} custom-call(s32[2,4]{1,0:T(2,128)} %dynamic-slice_reduce_fusion.lists_ref, f32[16,128,256]{2,1,0:T(8,128)} %get-tuple-element.25.slot_ref, bf16[4,128,256]{2,1,0:T(8,128)(2,1)} %copy-done.14, bf16[4,128,256]{2,1,0:T(8,128)(2,1)} %copy-done.15), custom_call_target="tpu_custom_call" | custom-call | tf_op jit(solution)/shard_map/pallas_call | solution.py:138
  91.1 1.7 %convolution_bitcast_fusion.3 = f32[1,256,256]{2,1,0:T(8,128)S(1)} fusion(bf16[2048,256]{1,0:T(8,128)(2,1)} %bitcast.97, bf16[1,2048,256]{2,1,0:T(8,128)(2,1)S(1)} %copy-done.7), kind=kOutput, calls=%fused_computation.14 | convolution fusion | flops 268435456 | bytes 2359296 | tf_op jit(solution)/shard_map/dot_general | solution.py:223
  92.9 0.1 pad_maximum_fusion
  93.0 31.6 %all_to_all.10 = f32[128,8,256]{2,1,0:T(8,128)S(1)} all-to-all(f32[128,8,256]{2,1,0:T(8,128)S(1)} %bitcast.94), channel_id=1, replica_groups=mesh['dp'=8,'sector'=16] {'dp','sector'}, dimensions={0} | all-to-all | bytes 2097152 | tf_op jit(solution)/shard_map/all_to_all | solution.py:169
  124.6 0.1 reduce_sum.9
  124.7 1.1 broadcast_in_dim.5
  125.8 4.5 %all-to-all-start.1 = ((f32[128,8,256]{2,1,0:T(8,128)}), f32[128,8,256]{2,1,0:T(8,128)S(1)}, u32[]{:S(2)}, u32[]{:S(2)}) async-start(f32[128,8,256]{2,1,0:T(8,128)} %broadcast_in_dim.5), calls=%async_computation.1 | async-start | bytes 2097152 | tf_op jit(solution)/shard_map/all_to_all | solution.py:171
  130.3 0.0 copy-start.9
  130.3 1.8 %convolution_add_fusion.1 = f32[2048,256]{1,0:T(8,128)S(1)} fusion(f32[2048,256]{1,0:T(8,128)S(1)} %copy-done, bf16[2048,256]{1,0:T(8,128)(2,1)} %bitcast.100, bf16[2,256,256]{2,1,0:T(8,128)(2,1)S(1)} %copy-done.13), kind=kOutput, calls=%fused_computation.6 | convolution fusion | flops 268959744 | bytes 5373952 | tf_op jit(solution)/shard_map/dot_general | solution.py:226
  132.2 1.8 %fusion = f32[1,2048,256]{2,1,0:T(8,128)} fusion(f32[2048,256]{1,0:T(8,128)S(1)} %convolution_add_fusion.1, bf16[2048,256]{1,0:T(8,128)(2,1)S(1)} %bitcast.98, bf16[2,256,256]{2,1,0:T(8,128)(2,1)S(1)} %copy-done.11), kind=kOutput, calls=%fused_computation.5 | convolution fusion | flops 268959744 | bytes 5373952 | tf_op jit(solution)/shard_map/dot_general | solution.py:227
  134.0 15.5 %all-to-all-done.1 = f32[128,8,256]{2,1,0:T(8,128)S(1)} async-done(((f32[128,8,256]{2,1,0:T(8,128)}), f32[128,8,256]{2,1,0:T(8,128)S(1)}, u32[]{:S(2)}, u32[]{:S(2)}) %all-to-all-start.1) | async-done | bytes 1048608 | tf_op jit(solution)/shard_map/all_to_all | solution.py:171
  149.4 1.0 fusion.14
  (47 shorter events, 0.2 us)
Async XLA Ops:
  0.6 11.0 %copy-start.17 = (s32[1,16,8]{1,2,0:T(8,128)S(1)}, s32[1,16,8]{1,2,0:T(8,128)}, u32[]{:S(2)}) copy-start(s32[1,16,8]{1,2,0:T(8,128)} %param.9) | copy-start | bytes 1540
  0.6 11.7 %copy-start.12 = (bf16[2,256,256]{2,1,0:T(8,128)(2,1)S(1)}, bf16[2,256,256]{2,1,0:T(8,128)(2,1)}, u32[]{:S(2)}) copy-start(bf16[2,256,256]{2,1,0:T(8,128)(2,1)} %param.12) | copy-start | bytes 786436
  3.3 14.5 %copy-start.5 = (bf16[2048,256]{1,0:T(8,128)(2,1)}, bf16[2048,256]{1,0:T(8,128)(2,1)S(1)}, u32[]{:S(2)}) copy-start(bf16[2048,256]{1,0:T(8,128)(2,1)S(1)} %convolution_convert_fusion.1) | copy-start | bytes 3145732
  3.9 13.1 %collective-permute-start = (bf16[4,128,256]{2,1,0:T(8,128)(2,1)S(1)}, bf16[4,128,256]{2,1,0:T(8,128)(2,1)S(1)}, u32[]{:S(2)}, u32[]{:S(2)}) collective-permute-start(bf16[4,128,256]{2,1,0:T(8,128)(2,1)S(1)} %gather_fusion), channel_id=1, source_target_pairs={{0,1},{1,2},{2,3},{3,4},{4,5},{5,6},{6,7},{7,8},{8,9},{9,10},{10,1... | collective-permute-start | bytes 786440 | tf_op jit(solution)/shard_map/ppermute | solution.py:157
  7.0 10.0 %collective-permute-start.1 = (bf16[4,128,256]{2,1,0:T(8,128)(2,1)S(1)}, bf16[4,128,256]{2,1,0:T(8,128)(2,1)S(1)}, u32[]{:S(2)}, u32[]{:S(2)}) collective-permute-start(bf16[4,128,256]{2,1,0:T(8,128)(2,1)S(1)} %gather_fusion.1), channel_id=1, source_target_pairs={{1,0},{2,1},{3,2},{4,3},{5,4},{6,5},{7,6},{8,7},{9,8},{10,9},{11,1... | collective-permute-start | bytes 786440 | tf_op jit(solution)/shard_map/ppermute | solution.py:162
  17.8 6.3 %copy-start.10 = (bf16[2,256,256]{2,1,0:T(8,128)(2,1)S(1)}, bf16[2,256,256]{2,1,0:T(8,128)(2,1)}, u32[]{:S(2)}) copy-start(bf16[2,256,256]{2,1,0:T(8,128)(2,1)} %param.11) | copy-start | bytes 786436
  24.1 8.1 %copy-start.16 = (s32[1,16,2,4]{1,3,2,0:T(4,128)S(1)}, s32[1,16,2,4]{1,3,2,0:T(4,128)}, u32[]{:S(2)}) copy-start(s32[1,16,2,4]{1,3,2,0:T(4,128)} %param.10) | copy-start | bytes 1540
  25.8 12.4 %copy-start.6 = (bf16[2048,256]{1,0:T(8,128)(2,1)}, bf16[2048,256]{1,0:T(8,128)(2,1)S(1)}, u32[]{:S(2)}) copy-start(bf16[2048,256]{1,0:T(8,128)(2,1)S(1)} %convolution_convert_fusion) | copy-start | bytes 3145732
  26.9 10.4 %collective-permute-start.2 = (bf16[4,128,256]{2,1,0:T(8,128)(2,1)S(1)}, bf16[4,128,256]{2,1,0:T(8,128)(2,1)S(1)}, u32[]{:S(2)}, u32[]{:S(2)}) collective-permute-start(bf16[4,128,256]{2,1,0:T(8,128)(2,1)S(1)} %gather_fusion.2), channel_id=1, source_target_pairs={{0,1},{1,2},{2,3},{3,4},{4,5},{5,6},{6,7},{7,8},{8,9},{9,10},{10,1... | collective-permute-start | bytes 786440 | tf_op jit(solution)/shard_map/ppermute | solution.py:157
  27.0 10.3 %collective-permute-start.3 = (bf16[4,128,256]{2,1,0:T(8,128)(2,1)S(1)}, bf16[4,128,256]{2,1,0:T(8,128)(2,1)S(1)}, u32[]{:S(2)}, u32[]{:S(2)}) collective-permute-start(bf16[4,128,256]{2,1,0:T(8,128)(2,1)S(1)} %gather_fusion.3), channel_id=1, source_target_pairs={{1,0},{2,1},{3,2},{4,3},{5,4},{6,5},{7,6},{8,7},{9,8},{10,9},{11,1... | collective-permute-start | bytes 786440 | tf_op jit(solution)/shard_map/ppermute | solution.py:162
  44.3 12.7 %copy-start.3 = (f32[1,2048,256]{2,1,0:T(8,128)S(1)}, f32[1,2048,256]{2,1,0:T(8,128)}, u32[]{:S(2)}) copy-start(f32[1,2048,256]{2,1,0:T(8,128)} %param.13) | copy-start | bytes 6291460
  52.1 9.4 %collective-permute-start.4 = (bf16[4,128,256]{2,1,0:T(8,128)(2,1)}, bf16[4,128,256]{2,1,0:T(8,128)(2,1)}, u32[]{:S(2)}, u32[]{:S(2)}) collective-permute-start(bf16[4,128,256]{2,1,0:T(8,128)(2,1)} %get-tuple-element.21), channel_id=1, source_target_pairs={{0,1},{1,2},{2,3},{3,4},{4,5},{5,6},{6,7},{7,8},{8,9},{9,10},{10,1... | collective-permute-start | bytes 786440 | tf_op jit(solution)/shard_map/ppermute | solution.py:157
  52.1 9.4 %collective-permute-start.5 = (bf16[4,128,256]{2,1,0:T(8,128)(2,1)}, bf16[4,128,256]{2,1,0:T(8,128)(2,1)}, u32[]{:S(2)}, u32[]{:S(2)}) collective-permute-start(bf16[4,128,256]{2,1,0:T(8,128)(2,1)} %get-tuple-element.22), channel_id=1, source_target_pairs={{1,0},{2,1},{3,2},{4,3},{5,4},{6,5},{7,6},{8,7},{9,8},{10,9},{11,1... | collective-permute-start | bytes 786440 | tf_op jit(solution)/shard_map/ppermute | solution.py:162
  56.9 3.2 %copy-start.1 = (bf16[16,128,256]{2,1,0:T(8,128)(2,1)S(1)}, bf16[16,128,256]{2,1,0:T(8,128)(2,1)}, u32[]{:S(2)}) copy-start(bf16[16,128,256]{2,1,0:T(8,128)(2,1)} %get-tuple-element.16.hits_ref) | copy-start | bytes 3145732
  56.9 3.2 %copy-start.8 = (bf16[16,128,256]{2,1,0:T(8,128)(2,1)S(1)}, bf16[16,128,256]{2,1,0:T(8,128)(2,1)}, u32[]{:S(2)}) copy-start(bf16[16,128,256]{2,1,0:T(8,128)(2,1)} %get-tuple-element.19) | copy-start | bytes 3145732
  60.6 4.7 %copy-start.4 = (f32[2048,256]{1,0:T(8,128)S(1)}, f32[2048,256]{1,0:T(8,128)}, u32[]{:S(2)}) copy-start(f32[2048,256]{1,0:T(8,128)} %convolution_add_fusion.3) | copy-start | bytes 6291460
  68.3 7.9 %copy-start.7 = (bf16[1,2048,256]{2,1,0:T(8,128)(2,1)S(1)}, bf16[1,2048,256]{2,1,0:T(8,128)(2,1)}, u32[]{:S(2)}) copy-start(bf16[1,2048,256]{2,1,0:T(8,128)(2,1)} %param.7) | copy-start | bytes 3145732
  76.1 1.9 %copy-start.19 = (bf16[4,128,256]{2,1,0:T(8,128)(2,1)S(1)}, bf16[4,128,256]{2,1,0:T(8,128)(2,1)}, u32[]{:S(2)}) copy-start(bf16[4,128,256]{2,1,0:T(8,128)(2,1)} %get-tuple-element.26) | copy-start | bytes 786436
  76.1 2.0 %copy-start.18 = (bf16[4,128,256]{2,1,0:T(8,128)(2,1)S(1)}, bf16[4,128,256]{2,1,0:T(8,128)(2,1)}, u32[]{:S(2)}) copy-start(bf16[4,128,256]{2,1,0:T(8,128)(2,1)} %get-tuple-element.27) | copy-start | bytes 786436
  76.1 6.8 %copy-start.2 = (bf16[16,128,256]{2,1,0:T(8,128)(2,1)S(1)}, bf16[16,128,256]{2,1,0:T(8,128)(2,1)}, u32[]{:S(2)}) copy-start(bf16[16,128,256]{2,1,0:T(8,128)(2,1)} %shard_map.105) | copy-start | bytes 3145732
  78.0 8.6 %collective-permute-start.6 = (bf16[4,128,256]{2,1,0:T(8,128)(2,1)S(1)}, bf16[4,128,256]{2,1,0:T(8,128)(2,1)S(1)}, u32[]{:S(2)}, u32[]{:S(2)}) collective-permute-start(bf16[4,128,256]{2,1,0:T(8,128)(2,1)S(1)} %copy-done.19), channel_id=1, source_target_pairs={{0,1},{1,2},{2,3},{3,4},{4,5},{5,6},{6,7},{7,8},{8,9},{9,10},{10,1... | collective-permute-start | bytes 786440 | tf_op jit(solution)/shard_map/ppermute | solution.py:157
  78.1 8.5 %collective-permute-start.7 = (bf16[4,128,256]{2,1,0:T(8,128)(2,1)S(1)}, bf16[4,128,256]{2,1,0:T(8,128)(2,1)S(1)}, u32[]{:S(2)}, u32[]{:S(2)}) collective-permute-start(bf16[4,128,256]{2,1,0:T(8,128)(2,1)S(1)} %copy-done.18), channel_id=1, source_target_pairs={{1,0},{2,1},{3,2},{4,3},{5,4},{6,5},{7,6},{8,7},{9,8},{10,9},{11,1... | collective-permute-start | bytes 786440 | tf_op jit(solution)/shard_map/ppermute | solution.py:162
  86.6 0.7 copy-start.14
  86.6 0.8 copy-start.15
  124.5 5.7 %copy-start = (f32[2048,256]{1,0:T(8,128)S(1)}, f32[2048,256]{1,0:T(8,128)}, u32[]{:S(2)}) copy-start(f32[2048,256]{1,0:T(8,128)} %convolution_add_fusion.2) | copy-start | bytes 6291460
  124.6 5.8 %copy-start.13 = (bf16[2,256,256]{2,1,0:T(8,128)(2,1)S(1)}, bf16[2,256,256]{2,1,0:T(8,128)(2,1)}, u32[]{:S(2)}) copy-start(bf16[2,256,256]{2,1,0:T(8,128)(2,1)} %param.12) | copy-start | bytes 786436
  125.8 23.7 %all-to-all-start.1 = ((f32[128,8,256]{2,1,0:T(8,128)}), f32[128,8,256]{2,1,0:T(8,128)S(1)}, u32[]{:S(2)}, u32[]{:S(2)}) async-start(f32[128,8,256]{2,1,0:T(8,128)} %broadcast_in_dim.5), calls=%async_computation.1 | async-start | bytes 2097152 | tf_op jit(solution)/shard_map/all_to_all | solution.py:171
  130.3 1.8 %copy-start.9 = (bf16[16,128,256]{2,1,0:T(8,128)(2,1)S(1)}, bf16[16,128,256]{2,1,0:T(8,128)(2,1)}, u32[]{:S(2)}) copy-start(bf16[16,128,256]{2,1,0:T(8,128)(2,1)} %shard_map.107) | copy-start | bytes 3145732
  130.3 1.8 %copy-start.11 = (bf16[2,256,256]{2,1,0:T(8,128)(2,1)S(1)}, bf16[2,256,256]{2,1,0:T(8,128)(2,1)}, u32[]{:S(2)}) copy-start(bf16[2,256,256]{2,1,0:T(8,128)(2,1)} %param.11) | copy-start | bytes 786436

commit v9 on v8

--- a/solution.py
+++ b/solution.py
@@ -121,32 +121,39 @@
     )(slot_ids, tile_data, grad_blocks, pre_blocks)
 
 
-def fold_kernel(lists_ref, slot_ref, lower_ref, upper_ref, out_ref, acc_ref):
-    acc_ref[...] = slot_ref[...]
-    for i in range(lower_ref.shape[0]):
-        block = lists_ref[1, i]
-        acc_ref[block] += lower_ref[i].astype(jnp.float32)
-    for i in range(upper_ref.shape[0]):
-        block = lists_ref[0, i]
-        acc_ref[block] += upper_ref[i].astype(jnp.float32)
+FOLD = 4
+
+
+def fold_kernel(lists_ref, own_ref, lower_ref, upper_ref, out_ref, acc_ref):
+    base = pl.program_id(0) * acc_ref.shape[0]
+    acc_ref[...] = own_ref[...]
+    for list_index, part_ref in ((1, lower_ref), (0, upper_ref)):
+        for i in range(part_ref.shape[0]):
+            local = lists_ref[list_index, i] - base
+
+            @pl.when((local >= 0) & (local < acc_ref.shape[0]))
+            def _():
+                acc_ref[local] += part_ref[i].astype(jnp.float32)
+
     out_ref[...] = acc_ref[...].astype(out_ref.dtype)
 
 
 def fold_lent(own_lists, slot_grad, from_lower, from_upper, blocks):
     _, rows, width = slot_grad.shape
     lent = from_lower.shape[0]
+    step_spec = pl.BlockSpec((FOLD, rows, width), lambda g, lists: (g, 0, 0))
     return pl.pallas_call(
         fold_kernel,
         grid_spec=pltpu.PrefetchScalarGridSpec(
             num_scalar_prefetch=1,
-            grid=(1,),
+            grid=(blocks // FOLD,),
             in_specs=[
-                pl.BlockSpec((blocks, rows, width), lambda g, lists: (0, 0, 0)),
+                step_spec,
                 pl.BlockSpec((lent, rows, width), lambda g, lists: (0, 0, 0)),
                 pl.BlockSpec((lent, rows, width), lambda g, lists: (0, 0, 0)),
             ],
-            out_specs=pl.BlockSpec((blocks, rows, width), lambda g, lists: (0, 0, 0)),
-            scratch_shapes=[pltpu.VMEM((blocks, rows, width), jnp.float32)],
+            out_specs=step_spec,
+            scratch_shapes=[pltpu.VMEM((FOLD, rows, width), jnp.float32)],
         ),
         out_shape=jax.ShapeDtypeStruct((blocks, rows, width), jnp.bfloat16),
     )(own_lists, slot_grad, from_lower, from_upper)

time: 151 us -> 153 us (1.013)
  Pallas kernels: 35.5 us -> 37.5 us
    pallas_call x2, Pallas kernels: 7.39 us -> 9.35 us  [fold_lent(): pl.pallas_call(fold_kernel, grid_spec=pltpu.PrefetchScalarGridSpec(num_sc...]
where the time goes in v9:
time: 153 us; the launch traced here: 152 us
  Pallas kernels  37.5 us (25%)
  blocking collectives  31.6 us (21%)
  waiting for transfers between devices  27.9 us (18%)
  starting transfers between devices  26.7 us (17%)
  matrix products  17.6 us (12%)
  local copies, waits for them, and re-layouts  8.34 us (5%)
  other arithmetic  1.99 us (1%)
    all_to_all x1, blocking collectives, all_reduce(): mine = lax.all_to_all(pieces, axes, 0, 0, tiled=True).sum(0) * scale  31.6 us
    ppermute x4, starting transfers between devices, to_lower(): return lax.ppermute(x, axis, [((i + 1) % count, i) for i in range(count)])  19.4 us
    pallas_call x2, Pallas kernels, block_slot_grad(): pl.pallas_call(slot_grad_kernel, grid_spec=pltpu.PrefetchScalarGridSpec(n...  15.7 us
    all_to_all x1, waiting for transfers between devices, all_reduce(): return lax.all_to_all(spread, axes, 0, 0, tiled=True).reshape(x.shape)  15.5 us
    pallas_call x2, Pallas kernels, block_layer(): pl.pallas_call(layer_kernel, grid_spec=pltpu.PrefetchScalarGridSpec(num_s...  12.4 us
    ppermute x4, waiting for transfers between devices, to_upper(): return lax.ppermute(x, axis, [(i, (i + 1) % count) for i in range(count)])  12.4 us
    pallas_call x2, Pallas kernels, fold_lent(): pl.pallas_call(fold_kernel, grid_spec=pltpu.PrefetchScalarGridSpec(num_sc...  9.35 us
    dot_general x2, matrix products, per_device(): jnp.dot(dpre, w_self[layer_index].T, preferred_element_type=jnp.float32)  4.93 us
  transfers between devices with their start and end apart: 9, of which 5 were waited for; matrix products, arithmetic and copies ran while one was open for 7% of the time, Pallas kernels for 0%

profile of v9, /device:TPU:1, one launch (start us, length us, event | category | flops | bytes accessed | tf_op | source)
XLA Modules:
  0.0 152.4 jit_solution(9397061418277987206)
XLA Ops:
  0.7 1.0 dynamic-slice_reduce_fusion.2
  1.6 1.7 %convolution_convert_fusion.1 = bf16[2048,256]{1,0:T(8,128)(2,1)S(1)} fusion(bf16[1,2048,256]{2,1,0:T(8,128)(2,1)} %param.7, bf16[2,256,256]{2,1,0:T(8,128)(2,1)} %param.11), kind=kOutput, calls=%fused_computation.10 | convolution fusion | flops 268959744 | bytes 2228224 | tf_op jit(solution)/shard_map/dot_general | solution.py:201
  3.3 0.0 copy-start.5
  3.3 0.6 gather_fusion
  3.9 2.5 %collective-permute-start = (bf16[4,128,256]{2,1,0:T(8,128)(2,1)S(1)}, bf16[4,128,256]{2,1,0:T(8,128)(2,1)S(1)}, u32[]{:S(2)}, u32[]{:S(2)}) collective-permute-start(bf16[4,128,256]{2,1,0:T(8,128)(2,1)S(1)} %gather_fusion), channel_id=1, source_target_pairs={{0,1},{1,2},{2,3},{3,4},{4,5},{5,6},{6,7},{7,8},{8,9},{9,10},{10,1... | collective-permute-start | bytes 786440 | tf_op jit(solution)/shard_map/ppermute | solution.py:164
  6.4 0.6 gather_fusion.1
  7.0 4.7 %collective-permute-start.1 = (bf16[4,128,256]{2,1,0:T(8,128)(2,1)S(1)}, bf16[4,128,256]{2,1,0:T(8,128)(2,1)S(1)}, u32[]{:S(2)}, u32[]{:S(2)}) collective-permute-start(bf16[4,128,256]{2,1,0:T(8,128)(2,1)S(1)} %gather_fusion.1), channel_id=1, source_target_pairs={{1,0},{2,1},{3,2},{4,3},{5,4},{6,5},{7,6},{8,7},{9,8},{10,9},{11,1... | collective-permute-start | bytes 786440 | tf_op jit(solution)/shard_map/ppermute | solution.py:169
  11.6 0.7 copy.18.src_ref
  12.3 0.7 slice_bitcast_fusion
  13.0 3.9 %collective-permute-done = bf16[4,128,256]{2,1,0:T(8,128)(2,1)S(1)} collective-permute-done((bf16[4,128,256]{2,1,0:T(8,128)(2,1)S(1)}, bf16[4,128,256]{2,1,0:T(8,128)(2,1)S(1)}, u32[]{:S(2)}, u32[]{:S(2)}) %collective-permute-start) | collective-permute-done | bytes 262176 | tf_op jit(solution)/shard_map/ppermute | solution.py:164
  17.0 0.8 pad_maximum_fusion.1.lent_ref
  17.8 6.3 %shard_map.102 = (f32[16,128,256]{2,1,0:T(8,128)}, bf16[16,128,256]{2,1,0:T(8,128)(2,1)}) custom-call(s32[16,8]{1,0:T(8,128)} %copy.18.src_ref, bf16[16,8,128,128]{3,2,1,0:T(8,128)(2,1)} %bitcast.80, bf16[16,128,256]{2,1,0:T(8,128)(2,1)} %bitcast.90, bf16[8,128,256]{2,1,0:T(8,128)(2,1)} %pad_maximum_fusion.1.lent_ref, bf16[16,128,256]{2,1,0:T(8,128)(2,1)} %bitcast.95, ...), custom_call_target="tpu_custom_call" | custom-call | tf_op jit(solution)/shard_map/pallas_call | solution.py:44
  24.1 1.7 %convolution_convert_fusion = bf16[2048,256]{1,0:T(8,128)(2,1)S(1)} fusion(bf16[2048,256]{1,0:T(8,128)(2,1)} %bitcast.85, bf16[2,256,256]{2,1,0:T(8,128)(2,1)S(1)} %copy-done.10), kind=kOutput, calls=%fused_computation.9 | convolution fusion | flops 268959744 | bytes 2228224 | tf_op jit(solution)/shard_map/dot_general | solution.py:201
  25.8 0.6 gather_fusion.3
  26.4 0.6 gather_fusion.2
  26.9 0.1 collective-permute-start.2
  27.0 5.2 %collective-permute-start.3 = (bf16[4,128,256]{2,1,0:T(8,128)(2,1)S(1)}, bf16[4,128,256]{2,1,0:T(8,128)(2,1)S(1)}, u32[]{:S(2)}, u32[]{:S(2)}) collective-permute-start(bf16[4,128,256]{2,1,0:T(8,128)(2,1)S(1)} %gather_fusion.3), channel_id=1, source_target_pairs={{1,0},{2,1},{3,2},{4,3},{5,4},{6,5},{7,6},{8,7},{9,8},{10,9},{11,1... | collective-permute-start | bytes 786440 | tf_op jit(solution)/shard_map/ppermute | solution.py:169
  32.2 0.8 dynamic-slice_reduce_fusion.lists_ref
  33.0 4.3 %collective-permute-done.2 = bf16[4,128,256]{2,1,0:T(8,128)(2,1)S(1)} collective-permute-done((bf16[4,128,256]{2,1,0:T(8,128)(2,1)S(1)}, bf16[4,128,256]{2,1,0:T(8,128)(2,1)S(1)}, u32[]{:S(2)}, u32[]{:S(2)}) %collective-permute-start.2) | collective-permute-done | bytes 262176 | tf_op jit(solution)/shard_map/ppermute | solution.py:164
  37.3 0.8 pad_maximum_fusion.2.lent_ref
  38.1 6.1 %shard_map.103 = (f32[16,128,256]{2,1,0:T(8,128)}, bf16[16,128,256]{2,1,0:T(8,128)(2,1)}) custom-call(s32[16,8]{1,0:T(8,128)} %copy.18.src_ref, bf16[16,8,128,128]{3,2,1,0:T(8,128)(2,1)} %bitcast.81, bf16[16,128,256]{2,1,0:T(8,128)(2,1)} %bitcast.93, bf16[8,128,256]{2,1,0:T(8,128)(2,1)} %pad_maximum_fusion.2.lent_ref, ...), custom_call_target="tpu_custom_call" | custom-call | tf_op jit(solution)/shard_map/pallas_call | solution.py:44
  44.3 7.9 %shard_map.104 = (f32[16,128,256]{2,1,0:T(8,128)}, bf16[4,128,256]{2,1,0:T(8,128)(2,1)}, bf16[4,128,256]{2,1,0:T(8,128)(2,1)}, bf16[16,128,256]{2,1,0:T(8,128)(2,1)}) custom-call(s32[16,8]{1,0:T(8,128)} %copy.18.src_ref, bf16[16,8,128,128]{3,2,1,0:T(8,128)(2,1)} %bitcast.82, f32[16,128,256]{2,1,0:T(8,128)} %bitcast.87, f32[16,128,256]{2,1,0:T(8,128)} %get-tuple-element.18.pre_ref), custom_call_target="tpu_custom_call" | custom-call | tf_op jit(solution)/shard_map/pallas_call | solution.py:101
  52.1 4.8 %collective-permute-start.5 = (bf16[4,128,256]{2,1,0:T(8,128)(2,1)}, bf16[4,128,256]{2,1,0:T(8,128)(2,1)}, u32[]{:S(2)}, u32[]{:S(2)}) collective-permute-start(bf16[4,128,256]{2,1,0:T(8,128)(2,1)} %get-tuple-element.22), channel_id=1, source_target_pairs={{1,0},{2,1},{3,2},{4,3},{5,4},{6,5},{7,6},{8,7},{9,8},{10,9},{11,1... | collective-permute-start | bytes 786440 | tf_op jit(solution)/shard_map/ppermute | solution.py:169
  56.9 3.1 %convolution_add_fusion.3 = f32[2048,256]{1,0:T(8,128)} fusion(bf16[2048,256]{1,0:T(8,128)(2,1)} %bitcast.96, f32[1,2048,256]{2,1,0:T(8,128)S(1)} %copy-done.3, bf16[2,256,256]{2,1,0:T(8,128)(2,1)S(1)} %copy-done.12), kind=kOutput, calls=%fused_computation.8 | convolution fusion | flops 268959744 | bytes 5373952 | tf_op jit(solution)/shard_map/dot_general | solution.py:233
  60.1 0.5 convolution_bitcast_fusion
  60.6 1.0 collective-permute-done.4.lower_ref
  61.5 4.7 %shard_map.105 = bf16[16,128,256]{2,1,0:T(8,128)(2,1)} custom-call(s32[2,4]{1,0:T(2,128)} %dynamic-slice_reduce_fusion.lists_ref, f32[16,128,256]{2,1,0:T(8,128)} %get-tuple-element.20.own_ref, bf16[4,128,256]{2,1,0:T(8,128)(2,1)} %collective-permute-done.4.lower_ref, bf16[4,128,256]{2,1,0:T(8,128)(2,1)} %collective-permute-done.5.upper_ref), custom_call_target="tpu_custom_call" | custom-call | tf_op jit(solution)/shard_map/pallas_call | solution.py:145
  66.2 3.0 %convolution_add_fusion.2 = f32[2048,256]{1,0:T(8,128)} fusion(f32[2048,256]{1,0:T(8,128)S(1)} %copy-done.4, bf16[2048,256]{1,0:T(8,128)(2,1)} %bitcast.86, bf16[2,256,256]{2,1,0:T(8,128)(2,1)} %param.11), kind=kOutput, calls=%fused_computation.7 | convolution fusion | flops 268959744 | bytes 5373952 | tf_op jit(solution)/shard_map/dot_general | solution.py:234
  69.2 7.9 %shard_map.106 = (f32[16,128,256]{2,1,0:T(8,128)}, bf16[4,128,256]{2,1,0:T(8,128)(2,1)}, bf16[4,128,256]{2,1,0:T(8,128)(2,1)}, bf16[16,128,256]{2,1,0:T(8,128)(2,1)}) custom-call(s32[16,8]{1,0:T(8,128)} %copy.18.src_ref, bf16[16,8,128,128]{3,2,1,0:T(8,128)(2,1)} %bitcast.83, f32[16,128,256]{2,1,0:T(8,128)} %bitcast.84, f32[16,128,256]{2,1,0:T(8,128)} %get-tuple-element.23.pre_ref), custom_call_target="tpu_custom_call" | custom-call | tf_op jit(solution)/shard_map/pallas_call | solution.py:101
  77.1 1.9 %convolution_bitcast_fusion.1 = f32[1,256,256]{2,1,0:T(8,128)S(1)} fusion(bf16[2048,256]{1,0:T(8,128)(2,1)} %bitcast.99, bf16[1,2048,256]{2,1,0:T(8,128)(2,1)S(1)} %copy-done.7), kind=kOutput, calls=%fused_computation.12 | convolution fusion | flops 268435456 | bytes 2359296 | tf_op jit(solution)/shard_map/dot_general | solution.py:229
  79.0 0.1 collective-permute-start.6
  79.1 4.8 %collective-permute-start.7 = (bf16[4,128,256]{2,1,0:T(8,128)(2,1)S(1)}, bf16[4,128,256]{2,1,0:T(8,128)(2,1)S(1)}, u32[]{:S(2)}, u32[]{:S(2)}) collective-permute-start(bf16[4,128,256]{2,1,0:T(8,128)(2,1)S(1)} %copy-done.18), channel_id=1, source_target_pairs={{1,0},{2,1},{3,2},{4,3},{5,4},{6,5},{7,6},{8,7},{9,8},{10,9},{11,1... | collective-permute-start | bytes 786440 | tf_op jit(solution)/shard_map/ppermute | solution.py:169
  83.9 0.5 convolution_bitcast_fusion.2
  84.4 3.2 %collective-permute-done.6.lower_ref = bf16[4,128,256]{2,1,0:T(8,128)(2,1)S(1)} collective-permute-done((bf16[4,128,256]{2,1,0:T(8,128)(2,1)S(1)}, bf16[4,128,256]{2,1,0:T(8,128)(2,1)S(1)}, u32[]{:S(2)}, u32[]{:S(2)}) %collective-permute-start.6) | collective-permute-done | bytes 262176 | tf_op jit(solution)/shard_map/ppermute | solution.py:164
  87.6 0.7 copy-done.14
  88.3 0.1 copy-done.15
  88.4 4.7 %shard_map.107 = bf16[16,128,256]{2,1,0:T(8,128)(2,1)} custom-call(s32[2,4]{1,0:T(2,128)} %dynamic-slice_reduce_fusion.lists_ref, f32[16,128,256]{2,1,0:T(8,128)} %get-tuple-element.25.own_ref, bf16[4,128,256]{2,1,0:T(8,128)(2,1)} %copy-done.14, bf16[4,128,256]{2,1,0:T(8,128)(2,1)} %copy-done.15), custom_call_target="tpu_custom_call" | custom-call | tf_op jit(solution)/shard_map/pallas_call | solution.py:145
  93.1 1.7 %convolution_bitcast_fusion.3 = f32[1,256,256]{2,1,0:T(8,128)S(1)} fusion(bf16[2048,256]{1,0:T(8,128)(2,1)} %bitcast.97, bf16[1,2048,256]{2,1,0:T(8,128)(2,1)S(1)} %copy-done.7), kind=kOutput, calls=%fused_computation.14 | convolution fusion | flops 268435456 | bytes 2359296 | tf_op jit(solution)/shard_map/dot_general | solution.py:230
  94.8 0.1 pad_maximum_fusion
  94.9 31.6 %all_to_all.10 = f32[128,8,256]{2,1,0:T(8,128)S(1)} all-to-all(f32[128,8,256]{2,1,0:T(8,128)S(1)} %bitcast.94), channel_id=1, replica_groups=mesh['dp'=8,'sector'=16] {'dp','sector'}, dimensions={0} | all-to-all | bytes 2097152 | tf_op jit(solution)/shard_map/all_to_all | solution.py:176
  126.5 0.1 reduce_sum.9
  126.7 1.1 broadcast_in_dim.5
  127.7 4.5 %all-to-all-start.1 = ((f32[128,8,256]{2,1,0:T(8,128)}), f32[128,8,256]{2,1,0:T(8,128)S(1)}, u32[]{:S(2)}, u32[]{:S(2)}) async-start(f32[128,8,256]{2,1,0:T(8,128)} %broadcast_in_dim.5), calls=%async_computation.1 | async-start | bytes 2097152 | tf_op jit(solution)/shard_map/all_to_all | solution.py:178
  132.3 0.0 copy-start.9
  132.3 1.8 %convolution_add_fusion.1 = f32[2048,256]{1,0:T(8,128)S(1)} fusion(f32[2048,256]{1,0:T(8,128)S(1)} %copy-done, bf16[2048,256]{1,0:T(8,128)(2,1)} %bitcast.100, bf16[2,256,256]{2,1,0:T(8,128)(2,1)S(1)} %copy-done.13), kind=kOutput, calls=%fused_computation.6 | convolution fusion | flops 268959744 | bytes 5373952 | tf_op jit(solution)/shard_map/dot_general | solution.py:233
  134.1 1.8 %fusion = f32[1,2048,256]{2,1,0:T(8,128)} fusion(f32[2048,256]{1,0:T(8,128)S(1)} %convolution_add_fusion.1, bf16[2048,256]{1,0:T(8,128)(2,1)S(1)} %bitcast.98, bf16[2,256,256]{2,1,0:T(8,128)(2,1)S(1)} %copy-done.11), kind=kOutput, calls=%fused_computation.5 | convolution fusion | flops 268959744 | bytes 5373952 | tf_op jit(solution)/shard_map/dot_general | solution.py:234
  135.9 15.5 %all-to-all-done.1 = f32[128,8,256]{2,1,0:T(8,128)S(1)} async-done(((f32[128,8,256]{2,1,0:T(8,128)}), f32[128,8,256]{2,1,0:T(8,128)S(1)}, u32[]{:S(2)}, u32[]{:S(2)}) %all-to-all-start.1) | async-done | bytes 1048608 | tf_op jit(solution)/shard_map/all_to_all | solution.py:178
  151.4 1.0 fusion.14
  (47 shorter events, 0.2 us)
Async XLA Ops:
  0.6 11.0 %copy-start.17 = (s32[1,16,8]{1,2,0:T(8,128)S(1)}, s32[1,16,8]{1,2,0:T(8,128)}, u32[]{:S(2)}) copy-start(s32[1,16,8]{1,2,0:T(8,128)} %param.9) | copy-start | bytes 1540
  0.6 11.7 %copy-start.12 = (bf16[2,256,256]{2,1,0:T(8,128)(2,1)S(1)}, bf16[2,256,256]{2,1,0:T(8,128)(2,1)}, u32[]{:S(2)}) copy-start(bf16[2,256,256]{2,1,0:T(8,128)(2,1)} %param.12) | copy-start | bytes 786436
  3.3 14.5 %copy-start.5 = (bf16[2048,256]{1,0:T(8,128)(2,1)}, bf16[2048,256]{1,0:T(8,128)(2,1)S(1)}, u32[]{:S(2)}) copy-start(bf16[2048,256]{1,0:T(8,128)(2,1)S(1)} %convolution_convert_fusion.1) | copy-start | bytes 3145732
  3.9 13.1 %collective-permute-start = (bf16[4,128,256]{2,1,0:T(8,128)(2,1)S(1)}, bf16[4,128,256]{2,1,0:T(8,128)(2,1)S(1)}, u32[]{:S(2)}, u32[]{:S(2)}) collective-permute-start(bf16[4,128,256]{2,1,0:T(8,128)(2,1)S(1)} %gather_fusion), channel_id=1, source_target_pairs={{0,1},{1,2},{2,3},{3,4},{4,5},{5,6},{6,7},{7,8},{8,9},{9,10},{10,1... | collective-permute-start | bytes 786440 | tf_op jit(solution)/shard_map/ppermute | solution.py:164
  7.0 10.0 %collective-permute-start.1 = (bf16[4,128,256]{2,1,0:T(8,128)(2,1)S(1)}, bf16[4,128,256]{2,1,0:T(8,128)(2,1)S(1)}, u32[]{:S(2)}, u32[]{:S(2)}) collective-permute-start(bf16[4,128,256]{2,1,0:T(8,128)(2,1)S(1)} %gather_fusion.1), channel_id=1, source_target_pairs={{1,0},{2,1},{3,2},{4,3},{5,4},{6,5},{7,6},{8,7},{9,8},{10,9},{11,1... | collective-permute-start | bytes 786440 | tf_op jit(solution)/shard_map/ppermute | solution.py:169
  17.8 6.3 %copy-start.10 = (bf16[2,256,256]{2,1,0:T(8,128)(2,1)S(1)}, bf16[2,256,256]{2,1,0:T(8,128)(2,1)}, u32[]{:S(2)}) copy-start(bf16[2,256,256]{2,1,0:T(8,128)(2,1)} %param.11) | copy-start | bytes 786436
  24.1 8.1 %copy-start.16 = (s32[1,16,2,4]{1,3,2,0:T(4,128)S(1)}, s32[1,16,2,4]{1,3,2,0:T(4,128)}, u32[]{:S(2)}) copy-start(s32[1,16,2,4]{1,3,2,0:T(4,128)} %param.10) | copy-start | bytes 1540
  25.8 12.4 %copy-start.6 = (bf16[2048,256]{1,0:T(8,128)(2,1)}, bf16[2048,256]{1,0:T(8,128)(2,1)S(1)}, u32[]{:S(2)}) copy-start(bf16[2048,256]{1,0:T(8,128)(2,1)S(1)} %convolution_convert_fusion) | copy-start | bytes 3145732
  26.9 10.4 %collective-permute-start.2 = (bf16[4,128,256]{2,1,0:T(8,128)(2,1)S(1)}, bf16[4,128,256]{2,1,0:T(8,128)(2,1)S(1)}, u32[]{:S(2)}, u32[]{:S(2)}) collective-permute-start(bf16[4,128,256]{2,1,0:T(8,128)(2,1)S(1)} %gather_fusion.2), channel_id=1, source_target_pairs={{0,1},{1,2},{2,3},{3,4},{4,5},{5,6},{6,7},{7,8},{8,9},{9,10},{10,1... | collective-permute-start | bytes 786440 | tf_op jit(solution)/shard_map/ppermute | solution.py:164
  27.0 10.3 %collective-permute-start.3 = (bf16[4,128,256]{2,1,0:T(8,128)(2,1)S(1)}, bf16[4,128,256]{2,1,0:T(8,128)(2,1)S(1)}, u32[]{:S(2)}, u32[]{:S(2)}) collective-permute-start(bf16[4,128,256]{2,1,0:T(8,128)(2,1)S(1)} %gather_fusion.3), channel_id=1, source_target_pairs={{1,0},{2,1},{3,2},{4,3},{5,4},{6,5},{7,6},{8,7},{9,8},{10,9},{11,1... | collective-permute-start | bytes 786440 | tf_op jit(solution)/shard_map/ppermute | solution.py:169
  44.3 12.7 %copy-start.3 = (f32[1,2048,256]{2,1,0:T(8,128)S(1)}, f32[1,2048,256]{2,1,0:T(8,128)}, u32[]{:S(2)}) copy-start(f32[1,2048,256]{2,1,0:T(8,128)} %param.13) | copy-start | bytes 6291460
  52.1 9.4 %collective-permute-start.4 = (bf16[4,128,256]{2,1,0:T(8,128)(2,1)}, bf16[4,128,256]{2,1,0:T(8,128)(2,1)}, u32[]{:S(2)}, u32[]{:S(2)}) collective-permute-start(bf16[4,128,256]{2,1,0:T(8,128)(2,1)} %get-tuple-element.21), channel_id=1, source_target_pairs={{0,1},{1,2},{2,3},{3,4},{4,5},{5,6},{6,7},{7,8},{8,9},{9,10},{10,1... | collective-permute-start | bytes 786440 | tf_op jit(solution)/shard_map/ppermute | solution.py:164
  52.1 9.4 %collective-permute-start.5 = (bf16[4,128,256]{2,1,0:T(8,128)(2,1)}, bf16[4,128,256]{2,1,0:T(8,128)(2,1)}, u32[]{:S(2)}, u32[]{:S(2)}) collective-permute-start(bf16[4,128,256]{2,1,0:T(8,128)(2,1)} %get-tuple-element.22), channel_id=1, source_target_pairs={{1,0},{2,1},{3,2},{4,3},{5,4},{6,5},{7,6},{8,7},{9,8},{10,9},{11,1... | collective-permute-start | bytes 786440 | tf_op jit(solution)/shard_map/ppermute | solution.py:169
  56.9 3.2 %copy-start.1 = (bf16[16,128,256]{2,1,0:T(8,128)(2,1)S(1)}, bf16[16,128,256]{2,1,0:T(8,128)(2,1)}, u32[]{:S(2)}) copy-start(bf16[16,128,256]{2,1,0:T(8,128)(2,1)} %get-tuple-element.16.hits_ref) | copy-start | bytes 3145732
  56.9 3.2 %copy-start.8 = (bf16[16,128,256]{2,1,0:T(8,128)(2,1)S(1)}, bf16[16,128,256]{2,1,0:T(8,128)(2,1)}, u32[]{:S(2)}) copy-start(bf16[16,128,256]{2,1,0:T(8,128)(2,1)} %get-tuple-element.19) | copy-start | bytes 3145732
  60.6 5.7 %copy-start.4 = (f32[2048,256]{1,0:T(8,128)S(1)}, f32[2048,256]{1,0:T(8,128)}, u32[]{:S(2)}) copy-start(f32[2048,256]{1,0:T(8,128)} %convolution_add_fusion.3) | copy-start | bytes 6291460
  69.2 7.9 %copy-start.7 = (bf16[1,2048,256]{2,1,0:T(8,128)(2,1)S(1)}, bf16[1,2048,256]{2,1,0:T(8,128)(2,1)}, u32[]{:S(2)}) copy-start(bf16[1,2048,256]{2,1,0:T(8,128)(2,1)} %param.7) | copy-start | bytes 3145732
  77.1 1.9 %copy-start.19 = (bf16[4,128,256]{2,1,0:T(8,128)(2,1)S(1)}, bf16[4,128,256]{2,1,0:T(8,128)(2,1)}, u32[]{:S(2)}) copy-start(bf16[4,128,256]{2,1,0:T(8,128)(2,1)} %get-tuple-element.26) | copy-start | bytes 786436
  77.1 2.0 %copy-start.18 = (bf16[4,128,256]{2,1,0:T(8,128)(2,1)S(1)}, bf16[4,128,256]{2,1,0:T(8,128)(2,1)}, u32[]{:S(2)}) copy-start(bf16[4,128,256]{2,1,0:T(8,128)(2,1)} %get-tuple-element.27) | copy-start | bytes 786436
  77.1 6.8 %copy-start.2 = (bf16[16,128,256]{2,1,0:T(8,128)(2,1)S(1)}, bf16[16,128,256]{2,1,0:T(8,128)(2,1)}, u32[]{:S(2)}) copy-start(bf16[16,128,256]{2,1,0:T(8,128)(2,1)} %shard_map.105) | copy-start | bytes 3145732
  79.0 8.6 %collective-permute-start.6 = (bf16[4,128,256]{2,1,0:T(8,128)(2,1)S(1)}, bf16[4,128,256]{2,1,0:T(8,128)(2,1)S(1)}, u32[]{:S(2)}, u32[]{:S(2)}) collective-permute-start(bf16[4,128,256]{2,1,0:T(8,128)(2,1)S(1)} %copy-done.19), channel_id=1, source_target_pairs={{0,1},{1,2},{2,3},{3,4},{4,5},{5,6},{6,7},{7,8},{8,9},{9,10},{10,1... | collective-permute-start | bytes 786440 | tf_op jit(solution)/shard_map/ppermute | solution.py:164
  79.1 8.5 %collective-permute-start.7 = (bf16[4,128,256]{2,1,0:T(8,128)(2,1)S(1)}, bf16[4,128,256]{2,1,0:T(8,128)(2,1)S(1)}, u32[]{:S(2)}, u32[]{:S(2)}) collective-permute-start(bf16[4,128,256]{2,1,0:T(8,128)(2,1)S(1)} %copy-done.18), channel_id=1, source_target_pairs={{1,0},{2,1},{3,2},{4,3},{5,4},{6,5},{7,6},{8,7},{9,8},{10,9},{11,1... | collective-permute-start | bytes 786440 | tf_op jit(solution)/shard_map/ppermute | solution.py:169
  87.6 0.7 copy-start.14
  87.6 0.8 copy-start.15
  126.5 5.7 %copy-start = (f32[2048,256]{1,0:T(8,128)S(1)}, f32[2048,256]{1,0:T(8,128)}, u32[]{:S(2)}) copy-start(f32[2048,256]{1,0:T(8,128)} %convolution_add_fusion.2) | copy-start | bytes 6291460
  126.5 5.8 %copy-start.13 = (bf16[2,256,256]{2,1,0:T(8,128)(2,1)S(1)}, bf16[2,256,256]{2,1,0:T(8,128)(2,1)}, u32[]{:S(2)}) copy-start(bf16[2,256,256]{2,1,0:T(8,128)(2,1)} %param.12) | copy-start | bytes 786436
  127.7 23.7 %all-to-all-start.1 = ((f32[128,8,256]{2,1,0:T(8,128)}), f32[128,8,256]{2,1,0:T(8,128)S(1)}, u32[]{:S(2)}, u32[]{:S(2)}) async-start(f32[128,8,256]{2,1,0:T(8,128)} %broadcast_in_dim.5), calls=%async_computation.1 | async-start | bytes 2097152 | tf_op jit(solution)/shard_map/all_to_all | solution.py:178
  132.3 1.8 %copy-start.9 = (bf16[16,128,256]{2,1,0:T(8,128)(2,1)S(1)}, bf16[16,128,256]{2,1,0:T(8,128)(2,1)}, u32[]{:S(2)}) copy-start(bf16[16,128,256]{2,1,0:T(8,128)(2,1)} %shard_map.107) | copy-start | bytes 3145732
  132.3 1.8 %copy-start.11 = (bf16[2,256,256]{2,1,0:T(8,128)(2,1)S(1)}, bf16[2,256,256]{2,1,0:T(8,128)(2,1)}, u32[]{:S(2)}) copy-start(bf16[2,256,256]{2,1,0:T(8,128)(2,1)} %param.11) | copy-start | bytes 786436

commit v10 on v8

--- a/solution.py
+++ b/solution.py
@@ -165,10 +165,12 @@
 def all_reduce(x, axes, scale):
     count = lax.axis_size(axes)
     width = x.shape[-1]
-    pieces = x.reshape(count, -1, width)
-    mine = lax.all_to_all(pieces, axes, 0, 0, tiled=True).sum(0) * scale
+    pieces = x.reshape(count, -1, width).astype(jnp.bfloat16)
+    received = lax.all_to_all(pieces, axes, 0, 0, tiled=True)
+    mine = (received.astype(jnp.float32).sum(0) * scale).astype(jnp.bfloat16)
     spread = jnp.broadcast_to(mine[None], (count,) + mine.shape)
-    return lax.all_to_all(spread, axes, 0, 0, tiled=True).reshape(x.shape)
+    gathered = lax.all_to_all(spread, axes, 0, 0, tiled=True)
+    return gathered.astype(jnp.float32).reshape(x.shape)
 
 
 def silu_grad(pre):

time: 151 us -> 140 us (0.927)
  blocking collectives: 31.6 us -> 26.5 us
  waiting for transfers between devices: 27.8 us -> 22.8 us
    all_to_all x1, blocking collectives: 31.6 us -> 26.5 us  [all_reduce(): received = lax.all_to_all(pieces, axes, 0, 0, tiled=True)]
    all_to_all x1, waiting for transfers between devices: 15.5 us -> 10.4 us  [all_reduce(): gathered = lax.all_to_all(spread, axes, 0, 0, tiled=True)]
where the time goes in v10:
time: 140 us
  Pallas kernels  35.5 us (25%)
  blocking collectives  26.5 us (19%)
  starting transfers between devices  26.3 us (19%)
  waiting for transfers between devices  22.8 us (16%)
  matrix products  17.6 us (13%)
  local copies, waits for them, and re-layouts  8.09 us (6%)
  other arithmetic  1.95 us (1%)
    all_to_all x1, blocking collectives, all_reduce(): received = lax.all_to_all(pieces, axes, 0, 0, tiled=True)  26.5 us
    ppermute x4, starting transfers between devices, to_lower(): return lax.ppermute(x, axis, [((i + 1) % count, i) for i in range(count)])  19.4 us
    pallas_call x2, Pallas kernels, block_slot_grad(): pl.pallas_call(slot_grad_kernel, grid_spec=pltpu.PrefetchScalarGridSpec(n...  15.7 us
    pallas_call x2, Pallas kernels, block_layer(): pl.pallas_call(layer_kernel, grid_spec=pltpu.PrefetchScalarGridSpec(num_s...  12.4 us
    ppermute x4, waiting for transfers between devices, to_upper(): return lax.ppermute(x, axis, [(i, (i + 1) % count) for i in range(count)])  12.4 us
    all_to_all x1, waiting for transfers between devices, all_reduce(): gathered = lax.all_to_all(spread, axes, 0, 0, tiled=True)  10.4 us
    pallas_call x2, Pallas kernels, fold_lent(): pl.pallas_call(fold_kernel, grid_spec=pltpu.PrefetchScalarGridSpec(num_sc...  7.39 us
    dot_general x2, matrix products, per_device(): jnp.dot(dpre, w_self[layer_index].T, preferred_element_type=jnp.float32)  4.93 us
  transfers between devices with their start and end apart: 9, of which 5 were waited for; matrix products, arithmetic and copies ran while one was open for 7% of the time, Pallas kernels for 0%

profile of v10, /device:TPU:1, one launch (start us, length us, event | category | flops | bytes accessed | tf_op | source)
XLA Modules:
  0.0 139.7 jit_solution(10668551591568887005)
XLA Ops:
  0.6 0.0 copy-start.11
  0.7 1.0 dynamic-slice_reduce_fusion.2
  1.6 1.7 %convolution_convert_fusion.1 = bf16[2048,256]{1,0:T(8,128)(2,1)S(1)} fusion(bf16[1,2048,256]{2,1,0:T(8,128)(2,1)} %param.7, bf16[2,256,256]{2,1,0:T(8,128)(2,1)} %param.11), kind=kOutput, calls=%fused_computation.10 | convolution fusion | flops 268959744 | bytes 2228224 | tf_op jit(solution)/shard_map/dot_general | solution.py:196
  3.3 0.6 gather_fusion
  3.9 2.5 %collective-permute-start = (bf16[4,128,256]{2,1,0:T(8,128)(2,1)S(1)}, bf16[4,128,256]{2,1,0:T(8,128)(2,1)S(1)}, u32[]{:S(2)}, u32[]{:S(2)}) collective-permute-start(bf16[4,128,256]{2,1,0:T(8,128)(2,1)S(1)} %gather_fusion), channel_id=1, source_target_pairs={{0,1},{1,2},{2,3},{3,4},{4,5},{5,6},{6,7},{7,8},{8,9},{9,10},{10,1... | collective-permute-start | bytes 786440 | tf_op jit(solution)/shard_map/ppermute | solution.py:157
  6.4 0.6 gather_fusion.1
  7.0 4.7 %collective-permute-start.1 = (bf16[4,128,256]{2,1,0:T(8,128)(2,1)S(1)}, bf16[4,128,256]{2,1,0:T(8,128)(2,1)S(1)}, u32[]{:S(2)}, u32[]{:S(2)}) collective-permute-start(bf16[4,128,256]{2,1,0:T(8,128)(2,1)S(1)} %gather_fusion.1), channel_id=1, source_target_pairs={{1,0},{2,1},{3,2},{4,3},{5,4},{6,5},{7,6},{8,7},{9,8},{10,9},{11,1... | collective-permute-start | bytes 786440 | tf_op jit(solution)/shard_map/ppermute | solution.py:162
  11.6 0.7 copy.18.src_ref
  12.3 0.7 slice_bitcast_fusion
  13.0 4.0 %collective-permute-done = bf16[4,128,256]{2,1,0:T(8,128)(2,1)S(1)} collective-permute-done((bf16[4,128,256]{2,1,0:T(8,128)(2,1)S(1)}, bf16[4,128,256]{2,1,0:T(8,128)(2,1)S(1)}, u32[]{:S(2)}, u32[]{:S(2)}) %collective-permute-start) | collective-permute-done | bytes 262176 | tf_op jit(solution)/shard_map/ppermute | solution.py:157
  17.0 0.8 pad_maximum_fusion.lent_ref
  17.8 6.3 %shard_map.102 = (f32[16,128,256]{2,1,0:T(8,128)}, bf16[16,128,256]{2,1,0:T(8,128)(2,1)}) custom-call(s32[16,8]{1,0:T(8,128)} %copy.18.src_ref, bf16[16,8,128,128]{3,2,1,0:T(8,128)(2,1)} %bitcast.90, bf16[16,128,256]{2,1,0:T(8,128)(2,1)} %bitcast.100, bf16[8,128,256]{2,1,0:T(8,128)(2,1)} %pad_maximum_fusion.lent_ref, bf16[16,128,256]{2,1,0:T(8,128)(2,1)} %bitcast.104, ...), custom_call_target="tpu_custom_call" | custom-call | tf_op jit(solution)/shard_map/pallas_call | solution.py:44
  24.1 1.7 %convolution_convert_fusion = bf16[2048,256]{1,0:T(8,128)(2,1)S(1)} fusion(bf16[2048,256]{1,0:T(8,128)(2,1)} %bitcast.95, bf16[2,256,256]{2,1,0:T(8,128)(2,1)S(1)} %copy-done.10), kind=kOutput, calls=%fused_computation.9 | convolution fusion | flops 268959744 | bytes 2228224 | tf_op jit(solution)/shard_map/dot_general | solution.py:196
  25.8 0.6 gather_fusion.3
  26.4 0.6 gather_fusion.2
  26.9 0.1 collective-permute-start.2
  27.0 5.2 %collective-permute-start.3 = (bf16[4,128,256]{2,1,0:T(8,128)(2,1)S(1)}, bf16[4,128,256]{2,1,0:T(8,128)(2,1)S(1)}, u32[]{:S(2)}, u32[]{:S(2)}) collective-permute-start(bf16[4,128,256]{2,1,0:T(8,128)(2,1)S(1)} %gather_fusion.3), channel_id=1, source_target_pairs={{1,0},{2,1},{3,2},{4,3},{5,4},{6,5},{7,6},{8,7},{9,8},{10,9},{11,1... | collective-permute-start | bytes 786440 | tf_op jit(solution)/shard_map/ppermute | solution.py:162
  32.2 0.8 dynamic-slice_reduce_fusion.lists_ref
  33.0 4.3 %collective-permute-done.2 = bf16[4,128,256]{2,1,0:T(8,128)(2,1)S(1)} collective-permute-done((bf16[4,128,256]{2,1,0:T(8,128)(2,1)S(1)}, bf16[4,128,256]{2,1,0:T(8,128)(2,1)S(1)}, u32[]{:S(2)}, u32[]{:S(2)}) %collective-permute-start.2) | collective-permute-done | bytes 262176 | tf_op jit(solution)/shard_map/ppermute | solution.py:157
  37.3 0.8 pad_maximum_fusion.1.lent_ref
  38.1 6.1 %shard_map.103 = (f32[16,128,256]{2,1,0:T(8,128)}, bf16[16,128,256]{2,1,0:T(8,128)(2,1)}) custom-call(s32[16,8]{1,0:T(8,128)} %copy.18.src_ref, bf16[16,8,128,128]{3,2,1,0:T(8,128)(2,1)} %bitcast.91, bf16[16,128,256]{2,1,0:T(8,128)(2,1)} %bitcast.103, bf16[8,128,256]{2,1,0:T(8,128)(2,1)} %pad_maximum_fusion.1.lent_ref, ...), custom_call_target="tpu_custom_call" | custom-call | tf_op jit(solution)/shard_map/pallas_call | solution.py:44
  44.3 7.9 %shard_map.104 = (f32[16,128,256]{2,1,0:T(8,128)}, bf16[4,128,256]{2,1,0:T(8,128)(2,1)}, bf16[4,128,256]{2,1,0:T(8,128)(2,1)}, bf16[16,128,256]{2,1,0:T(8,128)(2,1)}) custom-call(s32[16,8]{1,0:T(8,128)} %copy.18.src_ref, bf16[16,8,128,128]{3,2,1,0:T(8,128)(2,1)} %bitcast.92, f32[16,128,256]{2,1,0:T(8,128)} %bitcast.97, f32[16,128,256]{2,1,0:T(8,128)} %get-tuple-element.18.pre_ref), custom_call_target="tpu_custom_call" | custom-call | tf_op jit(solution)/shard_map/pallas_call | solution.py:101
  52.1 4.8 %collective-permute-start.5 = (bf16[4,128,256]{2,1,0:T(8,128)(2,1)}, bf16[4,128,256]{2,1,0:T(8,128)(2,1)}, u32[]{:S(2)}, u32[]{:S(2)}) collective-permute-start(bf16[4,128,256]{2,1,0:T(8,128)(2,1)} %get-tuple-element.22), channel_id=1, source_target_pairs={{1,0},{2,1},{3,2},{4,3},{5,4},{6,5},{7,6},{8,7},{9,8},{10,9},{11,1... | collective-permute-start | bytes 786440 | tf_op jit(solution)/shard_map/ppermute | solution.py:162
  56.9 3.2 %convolution_add_fusion.3 = f32[2048,256]{1,0:T(8,128)} fusion(bf16[2048,256]{1,0:T(8,128)(2,1)} %bitcast.105, f32[1,2048,256]{2,1,0:T(8,128)S(1)} %copy-done.3, bf16[2,256,256]{2,1,0:T(8,128)(2,1)} %param.12), kind=kOutput, calls=%fused_computation.8 | convolution fusion | flops 268959744 | bytes 5373952 | tf_op jit(solution)/shard_map/dot_general | solution.py:228
  60.1 0.5 fusion.5
  60.6 0.9 collective-permute-done.4.lower_ref
  61.5 3.7 %shard_map.105 = bf16[16,128,256]{2,1,0:T(8,128)(2,1)} custom-call(s32[2,4]{1,0:T(2,128)} %dynamic-slice_reduce_fusion.lists_ref, f32[16,128,256]{2,1,0:T(8,128)} %get-tuple-element.20.slot_ref, bf16[4,128,256]{2,1,0:T(8,128)(2,1)} %collective-permute-done.4.lower_ref, bf16[4,128,256]{2,1,0:T(8,128)(2,1)} %collective-permute-done.5.upper_ref), custom_call_target="tpu_custom_call" | custom-call | tf_op jit(solution)/shard_map/pallas_call | solution.py:138
  65.2 3.0 %convolution_add_fusion.2 = f32[2048,256]{1,0:T(8,128)} fusion(f32[2048,256]{1,0:T(8,128)S(1)} %copy-done.4, bf16[2048,256]{1,0:T(8,128)(2,1)} %bitcast.96, bf16[2,256,256]{2,1,0:T(8,128)(2,1)S(1)} %copy-done.10), kind=kOutput, calls=%fused_computation.7 | convolution fusion | flops 268959744 | bytes 5373952 | tf_op jit(solution)/shard_map/dot_general | solution.py:229
  68.3 7.9 %shard_map.106 = (f32[16,128,256]{2,1,0:T(8,128)}, bf16[4,128,256]{2,1,0:T(8,128)(2,1)}, bf16[4,128,256]{2,1,0:T(8,128)(2,1)}, bf16[16,128,256]{2,1,0:T(8,128)(2,1)}) custom-call(s32[16,8]{1,0:T(8,128)} %copy.18.src_ref, bf16[16,8,128,128]{3,2,1,0:T(8,128)(2,1)} %bitcast.93, f32[16,128,256]{2,1,0:T(8,128)} %bitcast.94, f32[16,128,256]{2,1,0:T(8,128)} %get-tuple-element.23.pre_ref), custom_call_target="tpu_custom_call" | custom-call | tf_op jit(solution)/shard_map/pallas_call | solution.py:101
  76.1 1.9 %fusion.4 = bf16[1,256,256]{2,1,0:T(8,128)(2,1)S(1)} fusion(bf16[2048,256]{1,0:T(8,128)(2,1)} %bitcast.109, bf16[1,2048,256]{2,1,0:T(8,128)(2,1)S(1)} %copy-done.7), kind=kOutput, calls=%fused_computation.18 | convolution fusion | flops 268500992 | bytes 2228224 | tf_op jit(solution)/shard_map/dot_general | solution.py:224
  78.0 0.1 collective-permute-start.6
  78.1 4.8 %collective-permute-start.7 = (bf16[4,128,256]{2,1,0:T(8,128)(2,1)S(1)}, bf16[4,128,256]{2,1,0:T(8,128)(2,1)S(1)}, u32[]{:S(2)}, u32[]{:S(2)}) collective-permute-start(bf16[4,128,256]{2,1,0:T(8,128)(2,1)S(1)} %copy-done.17), channel_id=1, source_target_pairs={{1,0},{2,1},{3,2},{4,3},{5,4},{6,5},{7,6},{8,7},{9,8},{10,9},{11,1... | collective-permute-start | bytes 786440 | tf_op jit(solution)/shard_map/ppermute | solution.py:162
  82.9 0.5 fusion.6
  83.4 3.2 %collective-permute-done.6.lower_ref = bf16[4,128,256]{2,1,0:T(8,128)(2,1)S(1)} collective-permute-done((bf16[4,128,256]{2,1,0:T(8,128)(2,1)S(1)}, bf16[4,128,256]{2,1,0:T(8,128)(2,1)S(1)}, u32[]{:S(2)}, u32[]{:S(2)}) %collective-permute-start.6) | collective-permute-done | bytes 262176 | tf_op jit(solution)/shard_map/ppermute | solution.py:157
  86.6 0.7 copy-done.13
  87.3 0.1 copy-done.14
  87.4 3.7 %shard_map.107 = bf16[16,128,256]{2,1,0:T(8,128)(2,1)} custom-call(s32[2,4]{1,0:T(2,128)} %dynamic-slice_reduce_fusion.lists_ref, f32[16,128,256]{2,1,0:T(8,128)} %get-tuple-element.25.slot_ref, bf16[4,128,256]{2,1,0:T(8,128)(2,1)} %copy-done.13, bf16[4,128,256]{2,1,0:T(8,128)(2,1)} %copy-done.14), custom_call_target="tpu_custom_call" | custom-call | tf_op jit(solution)/shard_map/pallas_call | solution.py:138
  91.1 1.7 %fusion.3 = bf16[1,256,256]{2,1,0:T(8,128)(2,1)S(1)} fusion(bf16[2048,256]{1,0:T(8,128)(2,1)} %bitcast.106, bf16[1,2048,256]{2,1,0:T(8,128)(2,1)S(1)} %copy-done.7), kind=kOutput, calls=%fused_computation.17 | convolution fusion | flops 268500992 | bytes 2228224 | tf_op jit(solution)/shard_map/dot_general | solution.py:225
  92.9 0.1 pad_maximum_fusion.2
  93.0 26.5 %all_to_all.10 = bf16[128,8,256]{2,1,0:T(8,128)(2,1)S(1)} all-to-all(bf16[128,8,256]{2,1,0:T(8,128)(2,1)S(1)} %bitcast.108), channel_id=1, replica_groups=mesh['dp'=8,'sector'=16] {'dp','sector'}, dimensions={0} | all-to-all | bytes 1048576 | tf_op jit(solution)/shard_map/all_to_all | solution.py:169
  119.4 0.1 convert_reduce_fusion
  119.6 0.8 broadcast_in_dim.5
  120.4 4.2 %all-to-all-start.1 = ((bf16[128,8,256]{2,1,0:T(8,128)(2,1)}), bf16[128,8,256]{2,1,0:T(8,128)(2,1)S(1)}, u32[]{:S(2)}, u32[]{:S(2)}) async-start(bf16[128,8,256]{2,1,0:T(8,128)(2,1)} %broadcast_in_dim.5), calls=%async_computation.1 | async-start | bytes 1048576 | tf_op jit(solution)/shard_map/all_to_all | solution.py:172
  124.6 0.0 copy-start.9
  124.7 1.8 %convolution_add_fusion.1 = f32[2048,256]{1,0:T(8,128)S(1)} fusion(f32[2048,256]{1,0:T(8,128)S(1)} %copy-done, bf16[2048,256]{1,0:T(8,128)(2,1)} %bitcast.110, bf16[2,256,256]{2,1,0:T(8,128)(2,1)S(1)} %copy-done.12), kind=kOutput, calls=%fused_computation.6 | convolution fusion | flops 268959744 | bytes 5373952 | tf_op jit(solution)/shard_map/dot_general | solution.py:228
  126.5 1.8 %fusion = f32[1,2048,256]{2,1,0:T(8,128)} fusion(f32[2048,256]{1,0:T(8,128)S(1)} %convolution_add_fusion.1, bf16[2048,256]{1,0:T(8,128)(2,1)S(1)} %bitcast.107, bf16[2,256,256]{2,1,0:T(8,128)(2,1)S(1)} %copy-done.10), kind=kOutput, calls=%fused_computation.5 | convolution fusion | flops 268959744 | bytes 5373952 | tf_op jit(solution)/shard_map/dot_general | solution.py:229
  128.2 10.4 %all-to-all-done.1 = bf16[128,8,256]{2,1,0:T(8,128)(2,1)S(1)} async-done(((bf16[128,8,256]{2,1,0:T(8,128)(2,1)}), bf16[128,8,256]{2,1,0:T(8,128)(2,1)S(1)}, u32[]{:S(2)}, u32[]{:S(2)}) %all-to-all-start.1) | async-done | bytes 524320 | tf_op jit(solution)/shard_map/all_to_all | solution.py:172
  138.6 1.0 fusion.20
  (45 shorter events, 0.2 us)
Async XLA Ops:
  0.6 11.0 %copy-start.16 = (s32[1,16,8]{1,2,0:T(8,128)S(1)}, s32[1,16,8]{1,2,0:T(8,128)}, u32[]{:S(2)}) copy-start(s32[1,16,8]{1,2,0:T(8,128)} %param.9) | copy-start | bytes 1540
  0.6 11.7 %copy-start.11 = (bf16[2,256,256]{2,1,0:T(8,128)(2,1)S(1)}, bf16[2,256,256]{2,1,0:T(8,128)(2,1)}, u32[]{:S(2)}) copy-start(bf16[2,256,256]{2,1,0:T(8,128)(2,1)} %param.12) | copy-start | bytes 786436
  3.3 14.5 %copy-start.5 = (bf16[2048,256]{1,0:T(8,128)(2,1)}, bf16[2048,256]{1,0:T(8,128)(2,1)S(1)}, u32[]{:S(2)}) copy-start(bf16[2048,256]{1,0:T(8,128)(2,1)S(1)} %convolution_convert_fusion.1) | copy-start | bytes 3145732
  3.9 13.1 %collective-permute-start = (bf16[4,128,256]{2,1,0:T(8,128)(2,1)S(1)}, bf16[4,128,256]{2,1,0:T(8,128)(2,1)S(1)}, u32[]{:S(2)}, u32[]{:S(2)}) collective-permute-start(bf16[4,128,256]{2,1,0:T(8,128)(2,1)S(1)} %gather_fusion), channel_id=1, source_target_pairs={{0,1},{1,2},{2,3},{3,4},{4,5},{5,6},{6,7},{7,8},{8,9},{9,10},{10,1... | collective-permute-start | bytes 786440 | tf_op jit(solution)/shard_map/ppermute | solution.py:157
  7.0 10.0 %collective-permute-start.1 = (bf16[4,128,256]{2,1,0:T(8,128)(2,1)S(1)}, bf16[4,128,256]{2,1,0:T(8,128)(2,1)S(1)}, u32[]{:S(2)}, u32[]{:S(2)}) collective-permute-start(bf16[4,128,256]{2,1,0:T(8,128)(2,1)S(1)} %gather_fusion.1), channel_id=1, source_target_pairs={{1,0},{2,1},{3,2},{4,3},{5,4},{6,5},{7,6},{8,7},{9,8},{10,9},{11,1... | collective-permute-start | bytes 786440 | tf_op jit(solution)/shard_map/ppermute | solution.py:162
  17.8 6.3 %copy-start.10 = (bf16[2,256,256]{2,1,0:T(8,128)(2,1)S(1)}, bf16[2,256,256]{2,1,0:T(8,128)(2,1)}, u32[]{:S(2)}) copy-start(bf16[2,256,256]{2,1,0:T(8,128)(2,1)} %param.11) | copy-start | bytes 786436
  24.1 8.1 %copy-start.15 = (s32[1,16,2,4]{1,3,2,0:T(4,128)S(1)}, s32[1,16,2,4]{1,3,2,0:T(4,128)}, u32[]{:S(2)}) copy-start(s32[1,16,2,4]{1,3,2,0:T(4,128)} %param.10) | copy-start | bytes 1540
  25.8 12.4 %copy-start.6 = (bf16[2048,256]{1,0:T(8,128)(2,1)}, bf16[2048,256]{1,0:T(8,128)(2,1)S(1)}, u32[]{:S(2)}) copy-start(bf16[2048,256]{1,0:T(8,128)(2,1)S(1)} %convolution_convert_fusion) | copy-start | bytes 3145732
  26.9 10.4 %collective-permute-start.2 = (bf16[4,128,256]{2,1,0:T(8,128)(2,1)S(1)}, bf16[4,128,256]{2,1,0:T(8,128)(2,1)S(1)}, u32[]{:S(2)}, u32[]{:S(2)}) collective-permute-start(bf16[4,128,256]{2,1,0:T(8,128)(2,1)S(1)} %gather_fusion.2), channel_id=1, source_target_pairs={{0,1},{1,2},{2,3},{3,4},{4,5},{5,6},{6,7},{7,8},{8,9},{9,10},{10,1... | collective-permute-start | bytes 786440 | tf_op jit(solution)/shard_map/ppermute | solution.py:157
  27.0 10.3 %collective-permute-start.3 = (bf16[4,128,256]{2,1,0:T(8,128)(2,1)S(1)}, bf16[4,128,256]{2,1,0:T(8,128)(2,1)S(1)}, u32[]{:S(2)}, u32[]{:S(2)}) collective-permute-start(bf16[4,128,256]{2,1,0:T(8,128)(2,1)S(1)} %gather_fusion.3), channel_id=1, source_target_pairs={{1,0},{2,1},{3,2},{4,3},{5,4},{6,5},{7,6},{8,7},{9,8},{10,9},{11,1... | collective-permute-start | bytes 786440 | tf_op jit(solution)/shard_map/ppermute | solution.py:162
  44.3 12.7 %copy-start.3 = (f32[1,2048,256]{2,1,0:T(8,128)S(1)}, f32[1,2048,256]{2,1,0:T(8,128)}, u32[]{:S(2)}) copy-start(f32[1,2048,256]{2,1,0:T(8,128)} %param.13) | copy-start | bytes 6291460
  52.1 9.4 %collective-permute-start.4 = (bf16[4,128,256]{2,1,0:T(8,128)(2,1)}, bf16[4,128,256]{2,1,0:T(8,128)(2,1)}, u32[]{:S(2)}, u32[]{:S(2)}) collective-permute-start(bf16[4,128,256]{2,1,0:T(8,128)(2,1)} %get-tuple-element.21), channel_id=1, source_target_pairs={{0,1},{1,2},{2,3},{3,4},{4,5},{5,6},{6,7},{7,8},{8,9},{9,10},{10,1... | collective-permute-start | bytes 786440 | tf_op jit(solution)/shard_map/ppermute | solution.py:157
  52.1 9.4 %collective-permute-start.5 = (bf16[4,128,256]{2,1,0:T(8,128)(2,1)}, bf16[4,128,256]{2,1,0:T(8,128)(2,1)}, u32[]{:S(2)}, u32[]{:S(2)}) collective-permute-start(bf16[4,128,256]{2,1,0:T(8,128)(2,1)} %get-tuple-element.22), channel_id=1, source_target_pairs={{1,0},{2,1},{3,2},{4,3},{5,4},{6,5},{7,6},{8,7},{9,8},{10,9},{11,1... | collective-permute-start | bytes 786440 | tf_op jit(solution)/shard_map/ppermute | solution.py:162
  56.9 3.2 %copy-start.1 = (bf16[16,128,256]{2,1,0:T(8,128)(2,1)S(1)}, bf16[16,128,256]{2,1,0:T(8,128)(2,1)}, u32[]{:S(2)}) copy-start(bf16[16,128,256]{2,1,0:T(8,128)(2,1)} %get-tuple-element.16.hits_ref) | copy-start | bytes 3145732
  56.9 3.2 %copy-start.8 = (bf16[16,128,256]{2,1,0:T(8,128)(2,1)S(1)}, bf16[16,128,256]{2,1,0:T(8,128)(2,1)}, u32[]{:S(2)}) copy-start(bf16[16,128,256]{2,1,0:T(8,128)(2,1)} %get-tuple-element.19) | copy-start | bytes 3145732
  60.6 4.7 %copy-start.4 = (f32[2048,256]{1,0:T(8,128)S(1)}, f32[2048,256]{1,0:T(8,128)}, u32[]{:S(2)}) copy-start(f32[2048,256]{1,0:T(8,128)} %convolution_add_fusion.3) | copy-start | bytes 6291460
  68.3 7.9 %copy-start.7 = (bf16[1,2048,256]{2,1,0:T(8,128)(2,1)S(1)}, bf16[1,2048,256]{2,1,0:T(8,128)(2,1)}, u32[]{:S(2)}) copy-start(bf16[1,2048,256]{2,1,0:T(8,128)(2,1)} %param.7) | copy-start | bytes 3145732
  76.1 1.9 %copy-start.18 = (bf16[4,128,256]{2,1,0:T(8,128)(2,1)S(1)}, bf16[4,128,256]{2,1,0:T(8,128)(2,1)}, u32[]{:S(2)}) copy-start(bf16[4,128,256]{2,1,0:T(8,128)(2,1)} %get-tuple-element.26) | copy-start | bytes 786436
  76.1 2.0 %copy-start.17 = (bf16[4,128,256]{2,1,0:T(8,128)(2,1)S(1)}, bf16[4,128,256]{2,1,0:T(8,128)(2,1)}, u32[]{:S(2)}) copy-start(bf16[4,128,256]{2,1,0:T(8,128)(2,1)} %get-tuple-element.27) | copy-start | bytes 786436
  76.1 6.8 %copy-start.2 = (bf16[16,128,256]{2,1,0:T(8,128)(2,1)S(1)}, bf16[16,128,256]{2,1,0:T(8,128)(2,1)}, u32[]{:S(2)}) copy-start(bf16[16,128,256]{2,1,0:T(8,128)(2,1)} %shard_map.105) | copy-start | bytes 3145732
  78.0 8.6 %collective-permute-start.6 = (bf16[4,128,256]{2,1,0:T(8,128)(2,1)S(1)}, bf16[4,128,256]{2,1,0:T(8,128)(2,1)S(1)}, u32[]{:S(2)}, u32[]{:S(2)}) collective-permute-start(bf16[4,128,256]{2,1,0:T(8,128)(2,1)S(1)} %copy-done.18), channel_id=1, source_target_pairs={{0,1},{1,2},{2,3},{3,4},{4,5},{5,6},{6,7},{7,8},{8,9},{9,10},{10,1... | collective-permute-start | bytes 786440 | tf_op jit(solution)/shard_map/ppermute | solution.py:157
  78.1 8.5 %collective-permute-start.7 = (bf16[4,128,256]{2,1,0:T(8,128)(2,1)S(1)}, bf16[4,128,256]{2,1,0:T(8,128)(2,1)S(1)}, u32[]{:S(2)}, u32[]{:S(2)}) collective-permute-start(bf16[4,128,256]{2,1,0:T(8,128)(2,1)S(1)} %copy-done.17), channel_id=1, source_target_pairs={{1,0},{2,1},{3,2},{4,3},{5,4},{6,5},{7,6},{8,7},{9,8},{10,9},{11,1... | collective-permute-start | bytes 786440 | tf_op jit(solution)/shard_map/ppermute | solution.py:162
  86.6 0.7 copy-start.13
  86.6 0.8 copy-start.14
  92.9 31.7 %copy-start = (f32[2048,256]{1,0:T(8,128)S(1)}, f32[2048,256]{1,0:T(8,128)}, u32[]{:S(2)}) copy-start(f32[2048,256]{1,0:T(8,128)} %convolution_add_fusion.2) | copy-start | bytes 6291460
  92.9 31.7 %copy-start.12 = (bf16[2,256,256]{2,1,0:T(8,128)(2,1)S(1)}, bf16[2,256,256]{2,1,0:T(8,128)(2,1)}, u32[]{:S(2)}) copy-start(bf16[2,256,256]{2,1,0:T(8,128)(2,1)} %param.12) | copy-start | bytes 786436
  120.4 18.2 %all-to-all-start.1 = ((bf16[128,8,256]{2,1,0:T(8,128)(2,1)}), bf16[128,8,256]{2,1,0:T(8,128)(2,1)S(1)}, u32[]{:S(2)}, u32[]{:S(2)}) async-start(bf16[128,8,256]{2,1,0:T(8,128)(2,1)} %broadcast_in_dim.5), calls=%async_computation.1 | async-start | bytes 1048576 | tf_op jit(solution)/shard_map/all_to_all | solution.py:172
  124.6 1.8 %copy-start.9 = (bf16[16,128,256]{2,1,0:T(8,128)(2,1)S(1)}, bf16[16,128,256]{2,1,0:T(8,128)(2,1)}, u32[]{:S(2)}) copy-start(bf16[16,128,256]{2,1,0:T(8,128)(2,1)} %shard_map.107) | copy-start | bytes 3145732

commit v11 on v10

--- a/solution.py
+++ b/solution.py
@@ -7,6 +7,7 @@
 
 LAYERS = 2
 GROUP = 8
+GROUP_BACK = 4
 
 
 def slot_rows(own_ref, lent_ref, slot):
@@ -69,8 +70,9 @@
     def _():
         out_ref[...] = jnp.zeros(out_ref.shape, out_ref.dtype)
 
-    for i in range(GROUP):
-        block = step * GROUP + i
+    group = tiles_ref.shape[0]
+    for i in range(group):
+        block = step * group + i
         pre = pre_ref[i]
         sig = jax.nn.sigmoid(pre)
         grad = (grad_ref[i] * (sig * (1.0 + pre * (1.0 - sig)))).astype(dpre_ref.dtype)
@@ -96,15 +98,15 @@
     blocks, listed, rows, _ = tile_data.shape
     width = grad_blocks.shape[-1]
     lent = (slot_count - blocks) // 2
-    block_spec = pl.BlockSpec((GROUP, rows, width), lambda g, src: (g, 0, 0))
+    block_spec = pl.BlockSpec((GROUP_BACK, rows, width), lambda g, src: (g, 0, 0))
     whole = lambda count: pl.BlockSpec((count, rows, width), lambda g, src: (0, 0, 0))
     return pl.pallas_call(
         slot_grad_kernel,
         grid_spec=pltpu.PrefetchScalarGridSpec(
             num_scalar_prefetch=1,
-            grid=(blocks // GROUP,),
+            grid=(blocks // GROUP_BACK,),
             in_specs=[
-                pl.BlockSpec((GROUP, listed, rows, rows), lambda g, src: (g, 0, 0, 0)),
+                pl.BlockSpec((GROUP_BACK, listed, rows, rows), lambda g, src: (g, 0, 0, 0)),
                 block_spec,
                 block_spec,
             ],

time: 140 us -> 142 us (1.014)
  no operation moved by 1% of the time
where the time goes in v11:
time: 142 us; the launch traced here: 141 us
  Pallas kernels  36.8 us (26%)
  blocking collectives  26.4 us (19%)
  starting transfers between devices  26.3 us (19%)
  waiting for transfers between devices  22.8 us (16%)
  matrix products  17.6 us (12%)
  local copies, waits for them, and re-layouts  8.09 us (6%)
  other arithmetic  1.95 us (1%)
    all_to_all x1, blocking collectives, all_reduce(): received = lax.all_to_all(pieces, axes, 0, 0, tiled=True)  26.4 us
    ppermute x4, starting transfers between devices, to_lower(): return lax.ppermute(x, axis, [((i + 1) % count, i) for i in range(count)])  19.4 us
    pallas_call x2, Pallas kernels, block_slot_grad(): pl.pallas_call(slot_grad_kernel, grid_spec=pltpu.PrefetchScalarGridSpec(n...  17 us
    ppermute x4, waiting for transfers between devices, to_upper(): return lax.ppermute(x, axis, [(i, (i + 1) % count) for i in range(count)])  12.4 us
    pallas_call x2, Pallas kernels, block_layer(): pl.pallas_call(layer_kernel, grid_spec=pltpu.PrefetchScalarGridSpec(num_s...  12.4 us
    all_to_all x1, waiting for transfers between devices, all_reduce(): gathered = lax.all_to_all(spread, axes, 0, 0, tiled=True)  10.4 us
    pallas_call x2, Pallas kernels, fold_lent(): pl.pallas_call(fold_kernel, grid_spec=pltpu.PrefetchScalarGridSpec(num_sc...  7.39 us
    dot_general x2, matrix products, per_device(): jnp.dot(dpre, w_self[layer_index].T, preferred_element_type=jnp.float32)  4.92 us
  transfers between devices with their start and end apart: 9, of which 5 were waited for; matrix products, arithmetic and copies ran while one was open for 7% of the time, Pallas kernels for 0%

profile of v11, /device:TPU:1, one launch (start us, length us, event | category | flops | bytes accessed | tf_op | source)
XLA Modules:
  0.0 140.9 jit_solution(8344419002499795600)
XLA Ops:
  0.6 0.0 copy-start.11
  0.7 1.0 dynamic-slice_reduce_fusion.2
  1.6 1.7 %convolution_convert_fusion.1 = bf16[2048,256]{1,0:T(8,128)(2,1)S(1)} fusion(bf16[1,2048,256]{2,1,0:T(8,128)(2,1)} %param.7, bf16[2,256,256]{2,1,0:T(8,128)(2,1)} %param.11), kind=kOutput, calls=%fused_computation.10 | convolution fusion | flops 268959744 | bytes 2228224 | tf_op jit(solution)/shard_map/dot_general | solution.py:198
  3.3 0.0 copy-start.5
  3.3 0.6 gather_fusion
  3.9 2.5 %collective-permute-start = (bf16[4,128,256]{2,1,0:T(8,128)(2,1)S(1)}, bf16[4,128,256]{2,1,0:T(8,128)(2,1)S(1)}, u32[]{:S(2)}, u32[]{:S(2)}) collective-permute-start(bf16[4,128,256]{2,1,0:T(8,128)(2,1)S(1)} %gather_fusion), channel_id=1, source_target_pairs={{0,1},{1,2},{2,3},{3,4},{4,5},{5,6},{6,7},{7,8},{8,9},{9,10},{10,1... | collective-permute-start | bytes 786440 | tf_op jit(solution)/shard_map/ppermute | solution.py:159
  6.4 0.6 gather_fusion.1
  7.0 4.7 %collective-permute-start.1 = (bf16[4,128,256]{2,1,0:T(8,128)(2,1)S(1)}, bf16[4,128,256]{2,1,0:T(8,128)(2,1)S(1)}, u32[]{:S(2)}, u32[]{:S(2)}) collective-permute-start(bf16[4,128,256]{2,1,0:T(8,128)(2,1)S(1)} %gather_fusion.1), channel_id=1, source_target_pairs={{1,0},{2,1},{3,2},{4,3},{5,4},{6,5},{7,6},{8,7},{9,8},{10,9},{11,1... | collective-permute-start | bytes 786440 | tf_op jit(solution)/shard_map/ppermute | solution.py:164
  11.6 0.7 copy.18.src_ref
  12.3 0.7 slice_bitcast_fusion
  13.0 4.0 %collective-permute-done = bf16[4,128,256]{2,1,0:T(8,128)(2,1)S(1)} collective-permute-done((bf16[4,128,256]{2,1,0:T(8,128)(2,1)S(1)}, bf16[4,128,256]{2,1,0:T(8,128)(2,1)S(1)}, u32[]{:S(2)}, u32[]{:S(2)}) %collective-permute-start) | collective-permute-done | bytes 262176 | tf_op jit(solution)/shard_map/ppermute | solution.py:159
  17.0 0.8 pad_maximum_fusion.lent_ref
  17.8 6.3 %shard_map.102 = (f32[16,128,256]{2,1,0:T(8,128)}, bf16[16,128,256]{2,1,0:T(8,128)(2,1)}) custom-call(s32[16,8]{1,0:T(8,128)} %copy.18.src_ref, bf16[16,8,128,128]{3,2,1,0:T(8,128)(2,1)} %bitcast.90, bf16[16,128,256]{2,1,0:T(8,128)(2,1)} %bitcast.100, bf16[8,128,256]{2,1,0:T(8,128)(2,1)} %pad_maximum_fusion.lent_ref, bf16[16,128,256]{2,1,0:T(8,128)(2,1)} %bitcast.104, ...), custom_call_target="tpu_custom_call" | custom-call | tf_op jit(solution)/shard_map/pallas_call | solution.py:45
  24.1 1.7 %convolution_convert_fusion = bf16[2048,256]{1,0:T(8,128)(2,1)S(1)} fusion(bf16[2048,256]{1,0:T(8,128)(2,1)} %bitcast.95, bf16[2,256,256]{2,1,0:T(8,128)(2,1)S(1)} %copy-done.10), kind=kOutput, calls=%fused_computation.9 | convolution fusion | flops 268959744 | bytes 2228224 | tf_op jit(solution)/shard_map/dot_general | solution.py:198
  25.8 0.6 gather_fusion.3
  26.4 0.6 gather_fusion.2
  26.9 0.1 collective-permute-start.2
  27.0 5.2 %collective-permute-start.3 = (bf16[4,128,256]{2,1,0:T(8,128)(2,1)S(1)}, bf16[4,128,256]{2,1,0:T(8,128)(2,1)S(1)}, u32[]{:S(2)}, u32[]{:S(2)}) collective-permute-start(bf16[4,128,256]{2,1,0:T(8,128)(2,1)S(1)} %gather_fusion.3), channel_id=1, source_target_pairs={{1,0},{2,1},{3,2},{4,3},{5,4},{6,5},{7,6},{8,7},{9,8},{10,9},{11,1... | collective-permute-start | bytes 786440 | tf_op jit(solution)/shard_map/ppermute | solution.py:164
  32.3 0.8 dynamic-slice_reduce_fusion.lists_ref
  33.0 4.3 %collective-permute-done.2 = bf16[4,128,256]{2,1,0:T(8,128)(2,1)S(1)} collective-permute-done((bf16[4,128,256]{2,1,0:T(8,128)(2,1)S(1)}, bf16[4,128,256]{2,1,0:T(8,128)(2,1)S(1)}, u32[]{:S(2)}, u32[]{:S(2)}) %collective-permute-start.2) | collective-permute-done | bytes 262176 | tf_op jit(solution)/shard_map/ppermute | solution.py:159
  37.3 0.8 pad_maximum_fusion.1.lent_ref
  38.2 6.1 %shard_map.103 = (f32[16,128,256]{2,1,0:T(8,128)}, bf16[16,128,256]{2,1,0:T(8,128)(2,1)}) custom-call(s32[16,8]{1,0:T(8,128)} %copy.18.src_ref, bf16[16,8,128,128]{3,2,1,0:T(8,128)(2,1)} %bitcast.91, bf16[16,128,256]{2,1,0:T(8,128)(2,1)} %bitcast.103, bf16[8,128,256]{2,1,0:T(8,128)(2,1)} %pad_maximum_fusion.1.lent_ref, ...), custom_call_target="tpu_custom_call" | custom-call | tf_op jit(solution)/shard_map/pallas_call | solution.py:45
  44.3 8.5 %shard_map.104 = (f32[16,128,256]{2,1,0:T(8,128)}, bf16[4,128,256]{2,1,0:T(8,128)(2,1)}, bf16[4,128,256]{2,1,0:T(8,128)(2,1)}, bf16[16,128,256]{2,1,0:T(8,128)(2,1)}) custom-call(s32[16,8]{1,0:T(8,128)} %copy.18.src_ref, bf16[16,8,128,128]{3,2,1,0:T(8,128)(2,1)} %bitcast.92, f32[16,128,256]{2,1,0:T(8,128)} %bitcast.97, f32[16,128,256]{2,1,0:T(8,128)} %get-tuple-element.18.pre_ref), custom_call_target="tpu_custom_call" | custom-call | tf_op jit(solution)/shard_map/pallas_call | solution.py:103
  52.8 4.8 %collective-permute-start.5 = (bf16[4,128,256]{2,1,0:T(8,128)(2,1)}, bf16[4,128,256]{2,1,0:T(8,128)(2,1)}, u32[]{:S(2)}, u32[]{:S(2)}) collective-permute-start(bf16[4,128,256]{2,1,0:T(8,128)(2,1)} %get-tuple-element.22), channel_id=1, source_target_pairs={{1,0},{2,1},{3,2},{4,3},{5,4},{6,5},{7,6},{8,7},{9,8},{10,9},{11,1... | collective-permute-start | bytes 786440 | tf_op jit(solution)/shard_map/ppermute | solution.py:164
  57.6 3.1 %convolution_add_fusion.3 = f32[2048,256]{1,0:T(8,128)} fusion(bf16[2048,256]{1,0:T(8,128)(2,1)} %bitcast.105, f32[1,2048,256]{2,1,0:T(8,128)S(1)} %copy-done.3, bf16[2,256,256]{2,1,0:T(8,128)(2,1)} %param.12), kind=kOutput, calls=%fused_computation.8 | convolution fusion | flops 268959744 | bytes 5373952 | tf_op jit(solution)/shard_map/dot_general | solution.py:230
  60.8 0.5 fusion.5
  61.3 0.9 collective-permute-done.4.lower_ref
  62.2 3.7 %shard_map.105 = bf16[16,128,256]{2,1,0:T(8,128)(2,1)} custom-call(s32[2,4]{1,0:T(2,128)} %dynamic-slice_reduce_fusion.lists_ref, f32[16,128,256]{2,1,0:T(8,128)} %get-tuple-element.20.slot_ref, bf16[4,128,256]{2,1,0:T(8,128)(2,1)} %collective-permute-done.4.lower_ref, bf16[4,128,256]{2,1,0:T(8,128)(2,1)} %collective-permute-done.5.upper_ref), custom_call_target="tpu_custom_call" | custom-call | tf_op jit(solution)/shard_map/pallas_call | solution.py:140
  65.9 3.0 %convolution_add_fusion.2 = f32[2048,256]{1,0:T(8,128)} fusion(f32[2048,256]{1,0:T(8,128)S(1)} %copy-done.4, bf16[2048,256]{1,0:T(8,128)(2,1)} %bitcast.96, bf16[2,256,256]{2,1,0:T(8,128)(2,1)S(1)} %copy-done.10), kind=kOutput, calls=%fused_computation.7 | convolution fusion | flops 268959744 | bytes 5373952 | tf_op jit(solution)/shard_map/dot_general | solution.py:231
  68.9 8.5 %shard_map.106 = (f32[16,128,256]{2,1,0:T(8,128)}, bf16[4,128,256]{2,1,0:T(8,128)(2,1)}, bf16[4,128,256]{2,1,0:T(8,128)(2,1)}, bf16[16,128,256]{2,1,0:T(8,128)(2,1)}) custom-call(s32[16,8]{1,0:T(8,128)} %copy.18.src_ref, bf16[16,8,128,128]{3,2,1,0:T(8,128)(2,1)} %bitcast.93, f32[16,128,256]{2,1,0:T(8,128)} %bitcast.94, f32[16,128,256]{2,1,0:T(8,128)} %get-tuple-element.23.pre_ref), custom_call_target="tpu_custom_call" | custom-call | tf_op jit(solution)/shard_map/pallas_call | solution.py:103
  77.5 1.9 %fusion.4 = bf16[1,256,256]{2,1,0:T(8,128)(2,1)S(1)} fusion(bf16[2048,256]{1,0:T(8,128)(2,1)} %bitcast.109, bf16[1,2048,256]{2,1,0:T(8,128)(2,1)S(1)} %copy-done.7), kind=kOutput, calls=%fused_computation.18 | convolution fusion | flops 268500992 | bytes 2228224 | tf_op jit(solution)/shard_map/dot_general | solution.py:226
  79.4 0.1 collective-permute-start.6
  79.5 4.8 %collective-permute-start.7 = (bf16[4,128,256]{2,1,0:T(8,128)(2,1)S(1)}, bf16[4,128,256]{2,1,0:T(8,128)(2,1)S(1)}, u32[]{:S(2)}, u32[]{:S(2)}) collective-permute-start(bf16[4,128,256]{2,1,0:T(8,128)(2,1)S(1)} %copy-done.17), channel_id=1, source_target_pairs={{1,0},{2,1},{3,2},{4,3},{5,4},{6,5},{7,6},{8,7},{9,8},{10,9},{11,1... | collective-permute-start | bytes 786440 | tf_op jit(solution)/shard_map/ppermute | solution.py:164
  84.3 0.5 fusion.6
  84.7 3.2 %collective-permute-done.6.lower_ref = bf16[4,128,256]{2,1,0:T(8,128)(2,1)S(1)} collective-permute-done((bf16[4,128,256]{2,1,0:T(8,128)(2,1)S(1)}, bf16[4,128,256]{2,1,0:T(8,128)(2,1)S(1)}, u32[]{:S(2)}, u32[]{:S(2)}) %collective-permute-start.6) | collective-permute-done | bytes 262176 | tf_op jit(solution)/shard_map/ppermute | solution.py:159
  88.0 0.7 copy-done.13
  88.7 0.1 copy-done.14
  88.8 3.7 %shard_map.107 = bf16[16,128,256]{2,1,0:T(8,128)(2,1)} custom-call(s32[2,4]{1,0:T(2,128)} %dynamic-slice_reduce_fusion.lists_ref, f32[16,128,256]{2,1,0:T(8,128)} %get-tuple-element.25.slot_ref, bf16[4,128,256]{2,1,0:T(8,128)(2,1)} %copy-done.13, bf16[4,128,256]{2,1,0:T(8,128)(2,1)} %copy-done.14), custom_call_target="tpu_custom_call" | custom-call | tf_op jit(solution)/shard_map/pallas_call | solution.py:140
  92.4 1.7 %fusion.3 = bf16[1,256,256]{2,1,0:T(8,128)(2,1)S(1)} fusion(bf16[2048,256]{1,0:T(8,128)(2,1)} %bitcast.106, bf16[1,2048,256]{2,1,0:T(8,128)(2,1)S(1)} %copy-done.7), kind=kOutput, calls=%fused_computation.17 | convolution fusion | flops 268500992 | bytes 2228224 | tf_op jit(solution)/shard_map/dot_general | solution.py:227
  94.2 0.1 pad_maximum_fusion.2
  94.3 26.4 %all_to_all.10 = bf16[128,8,256]{2,1,0:T(8,128)(2,1)S(1)} all-to-all(bf16[128,8,256]{2,1,0:T(8,128)(2,1)S(1)} %bitcast.108), channel_id=1, replica_groups=mesh['dp'=8,'sector'=16] {'dp','sector'}, dimensions={0} | all-to-all | bytes 1048576 | tf_op jit(solution)/shard_map/all_to_all | solution.py:171
  120.7 0.1 convert_reduce_fusion
  120.8 0.8 broadcast_in_dim.5
  121.7 4.2 %all-to-all-start.1 = ((bf16[128,8,256]{2,1,0:T(8,128)(2,1)}), bf16[128,8,256]{2,1,0:T(8,128)(2,1)S(1)}, u32[]{:S(2)}, u32[]{:S(2)}) async-start(bf16[128,8,256]{2,1,0:T(8,128)(2,1)} %broadcast_in_dim.5), calls=%async_computation.1 | async-start | bytes 1048576 | tf_op jit(solution)/shard_map/all_to_all | solution.py:174
  125.9 1.8 %convolution_add_fusion.1 = f32[2048,256]{1,0:T(8,128)S(1)} fusion(f32[2048,256]{1,0:T(8,128)S(1)} %copy-done, bf16[2048,256]{1,0:T(8,128)(2,1)} %bitcast.110, bf16[2,256,256]{2,1,0:T(8,128)(2,1)S(1)} %copy-done.12), kind=kOutput, calls=%fused_computation.6 | convolution fusion | flops 268959744 | bytes 5373952 | tf_op jit(solution)/shard_map/dot_general | solution.py:230
  127.7 1.8 %fusion = f32[1,2048,256]{2,1,0:T(8,128)} fusion(f32[2048,256]{1,0:T(8,128)S(1)} %convolution_add_fusion.1, bf16[2048,256]{1,0:T(8,128)(2,1)S(1)} %bitcast.107, bf16[2,256,256]{2,1,0:T(8,128)(2,1)S(1)} %copy-done.10), kind=kOutput, calls=%fused_computation.5 | convolution fusion | flops 268959744 | bytes 5373952 | tf_op jit(solution)/shard_map/dot_general | solution.py:231
  129.5 10.4 %all-to-all-done.1 = bf16[128,8,256]{2,1,0:T(8,128)(2,1)S(1)} async-done(((bf16[128,8,256]{2,1,0:T(8,128)(2,1)}), bf16[128,8,256]{2,1,0:T(8,128)(2,1)S(1)}, u32[]{:S(2)}, u32[]{:S(2)}) %all-to-all-start.1) | async-done | bytes 524320 | tf_op jit(solution)/shard_map/all_to_all | solution.py:174
  139.9 1.0 fusion.20
  (45 shorter events, 0.2 us)
Async XLA Ops:
  0.6 11.0 %copy-start.16 = (s32[1,16,8]{1,2,0:T(8,128)S(1)}, s32[1,16,8]{1,2,0:T(8,128)}, u32[]{:S(2)}) copy-start(s32[1,16,8]{1,2,0:T(8,128)} %param.9) | copy-start | bytes 1540
  0.6 11.7 %copy-start.11 = (bf16[2,256,256]{2,1,0:T(8,128)(2,1)S(1)}, bf16[2,256,256]{2,1,0:T(8,128)(2,1)}, u32[]{:S(2)}) copy-start(bf16[2,256,256]{2,1,0:T(8,128)(2,1)} %param.12) | copy-start | bytes 786436
  3.3 14.5 %copy-start.5 = (bf16[2048,256]{1,0:T(8,128)(2,1)}, bf16[2048,256]{1,0:T(8,128)(2,1)S(1)}, u32[]{:S(2)}) copy-start(bf16[2048,256]{1,0:T(8,128)(2,1)S(1)} %convolution_convert_fusion.1) | copy-start | bytes 3145732
  3.9 13.1 %collective-permute-start = (bf16[4,128,256]{2,1,0:T(8,128)(2,1)S(1)}, bf16[4,128,256]{2,1,0:T(8,128)(2,1)S(1)}, u32[]{:S(2)}, u32[]{:S(2)}) collective-permute-start(bf16[4,128,256]{2,1,0:T(8,128)(2,1)S(1)} %gather_fusion), channel_id=1, source_target_pairs={{0,1},{1,2},{2,3},{3,4},{4,5},{5,6},{6,7},{7,8},{8,9},{9,10},{10,1... | collective-permute-start | bytes 786440 | tf_op jit(solution)/shard_map/ppermute | solution.py:159
  7.0 10.0 %collective-permute-start.1 = (bf16[4,128,256]{2,1,0:T(8,128)(2,1)S(1)}, bf16[4,128,256]{2,1,0:T(8,128)(2,1)S(1)}, u32[]{:S(2)}, u32[]{:S(2)}) collective-permute-start(bf16[4,128,256]{2,1,0:T(8,128)(2,1)S(1)} %gather_fusion.1), channel_id=1, source_target_pairs={{1,0},{2,1},{3,2},{4,3},{5,4},{6,5},{7,6},{8,7},{9,8},{10,9},{11,1... | collective-permute-start | bytes 786440 | tf_op jit(solution)/shard_map/ppermute | solution.py:164
  17.8 6.3 %copy-start.10 = (bf16[2,256,256]{2,1,0:T(8,128)(2,1)S(1)}, bf16[2,256,256]{2,1,0:T(8,128)(2,1)}, u32[]{:S(2)}) copy-start(bf16[2,256,256]{2,1,0:T(8,128)(2,1)} %param.11) | copy-start | bytes 786436
  24.1 8.1 %copy-start.15 = (s32[1,16,2,4]{1,3,2,0:T(4,128)S(1)}, s32[1,16,2,4]{1,3,2,0:T(4,128)}, u32[]{:S(2)}) copy-start(s32[1,16,2,4]{1,3,2,0:T(4,128)} %param.10) | copy-start | bytes 1540
  25.8 12.4 %copy-start.6 = (bf16[2048,256]{1,0:T(8,128)(2,1)}, bf16[2048,256]{1,0:T(8,128)(2,1)S(1)}, u32[]{:S(2)}) copy-start(bf16[2048,256]{1,0:T(8,128)(2,1)S(1)} %convolution_convert_fusion) | copy-start | bytes 3145732
  26.9 10.4 %collective-permute-start.2 = (bf16[4,128,256]{2,1,0:T(8,128)(2,1)S(1)}, bf16[4,128,256]{2,1,0:T(8,128)(2,1)S(1)}, u32[]{:S(2)}, u32[]{:S(2)}) collective-permute-start(bf16[4,128,256]{2,1,0:T(8,128)(2,1)S(1)} %gather_fusion.2), channel_id=1, source_target_pairs={{0,1},{1,2},{2,3},{3,4},{4,5},{5,6},{6,7},{7,8},{8,9},{9,10},{10,1... | collective-permute-start | bytes 786440 | tf_op jit(solution)/shard_map/ppermute | solution.py:159
  27.0 10.3 %collective-permute-start.3 = (bf16[4,128,256]{2,1,0:T(8,128)(2,1)S(1)}, bf16[4,128,256]{2,1,0:T(8,128)(2,1)S(1)}, u32[]{:S(2)}, u32[]{:S(2)}) collective-permute-start(bf16[4,128,256]{2,1,0:T(8,128)(2,1)S(1)} %gather_fusion.3), channel_id=1, source_target_pairs={{1,0},{2,1},{3,2},{4,3},{5,4},{6,5},{7,6},{8,7},{9,8},{10,9},{11,1... | collective-permute-start | bytes 786440 | tf_op jit(solution)/shard_map/ppermute | solution.py:164
  44.3 13.3 %copy-start.3 = (f32[1,2048,256]{2,1,0:T(8,128)S(1)}, f32[1,2048,256]{2,1,0:T(8,128)}, u32[]{:S(2)}) copy-start(f32[1,2048,256]{2,1,0:T(8,128)} %param.13) | copy-start | bytes 6291460
  52.8 9.4 %collective-permute-start.4 = (bf16[4,128,256]{2,1,0:T(8,128)(2,1)}, bf16[4,128,256]{2,1,0:T(8,128)(2,1)}, u32[]{:S(2)}, u32[]{:S(2)}) collective-permute-start(bf16[4,128,256]{2,1,0:T(8,128)(2,1)} %get-tuple-element.21), channel_id=1, source_target_pairs={{0,1},{1,2},{2,3},{3,4},{4,5},{5,6},{6,7},{7,8},{8,9},{9,10},{10,1... | collective-permute-start | bytes 786440 | tf_op jit(solution)/shard_map/ppermute | solution.py:159
  52.8 9.4 %collective-permute-start.5 = (bf16[4,128,256]{2,1,0:T(8,128)(2,1)}, bf16[4,128,256]{2,1,0:T(8,128)(2,1)}, u32[]{:S(2)}, u32[]{:S(2)}) collective-permute-start(bf16[4,128,256]{2,1,0:T(8,128)(2,1)} %get-tuple-element.22), channel_id=1, source_target_pairs={{1,0},{2,1},{3,2},{4,3},{5,4},{6,5},{7,6},{8,7},{9,8},{10,9},{11,1... | collective-permute-start | bytes 786440 | tf_op jit(solution)/shard_map/ppermute | solution.py:164
  57.6 3.1 %copy-start.1 = (bf16[16,128,256]{2,1,0:T(8,128)(2,1)S(1)}, bf16[16,128,256]{2,1,0:T(8,128)(2,1)}, u32[]{:S(2)}) copy-start(bf16[16,128,256]{2,1,0:T(8,128)(2,1)} %get-tuple-element.16.hits_ref) | copy-start | bytes 3145732
  57.6 3.1 %copy-start.8 = (bf16[16,128,256]{2,1,0:T(8,128)(2,1)S(1)}, bf16[16,128,256]{2,1,0:T(8,128)(2,1)}, u32[]{:S(2)}) copy-start(bf16[16,128,256]{2,1,0:T(8,128)(2,1)} %get-tuple-element.19) | copy-start | bytes 3145732
  61.2 4.7 %copy-start.4 = (f32[2048,256]{1,0:T(8,128)S(1)}, f32[2048,256]{1,0:T(8,128)}, u32[]{:S(2)}) copy-start(f32[2048,256]{1,0:T(8,128)} %convolution_add_fusion.3) | copy-start | bytes 6291460
  68.9 8.5 %copy-start.7 = (bf16[1,2048,256]{2,1,0:T(8,128)(2,1)S(1)}, bf16[1,2048,256]{2,1,0:T(8,128)(2,1)}, u32[]{:S(2)}) copy-start(bf16[1,2048,256]{2,1,0:T(8,128)(2,1)} %param.7) | copy-start | bytes 3145732
  77.5 1.9 %copy-start.18 = (bf16[4,128,256]{2,1,0:T(8,128)(2,1)S(1)}, bf16[4,128,256]{2,1,0:T(8,128)(2,1)}, u32[]{:S(2)}) copy-start(bf16[4,128,256]{2,1,0:T(8,128)(2,1)} %get-tuple-element.26) | copy-start | bytes 786436
  77.5 2.0 %copy-start.17 = (bf16[4,128,256]{2,1,0:T(8,128)(2,1)S(1)}, bf16[4,128,256]{2,1,0:T(8,128)(2,1)}, u32[]{:S(2)}) copy-start(bf16[4,128,256]{2,1,0:T(8,128)(2,1)} %get-tuple-element.27) | copy-start | bytes 786436
  77.5 6.8 %copy-start.2 = (bf16[16,128,256]{2,1,0:T(8,128)(2,1)S(1)}, bf16[16,128,256]{2,1,0:T(8,128)(2,1)}, u32[]{:S(2)}) copy-start(bf16[16,128,256]{2,1,0:T(8,128)(2,1)} %shard_map.105) | copy-start | bytes 3145732
  79.4 8.6 %collective-permute-start.6 = (bf16[4,128,256]{2,1,0:T(8,128)(2,1)S(1)}, bf16[4,128,256]{2,1,0:T(8,128)(2,1)S(1)}, u32[]{:S(2)}, u32[]{:S(2)}) collective-permute-start(bf16[4,128,256]{2,1,0:T(8,128)(2,1)S(1)} %copy-done.18), channel_id=1, source_target_pairs={{0,1},{1,2},{2,3},{3,4},{4,5},{5,6},{6,7},{7,8},{8,9},{9,10},{10,1... | collective-permute-start | bytes 786440 | tf_op jit(solution)/shard_map/ppermute | solution.py:159
  79.5 8.5 %collective-permute-start.7 = (bf16[4,128,256]{2,1,0:T(8,128)(2,1)S(1)}, bf16[4,128,256]{2,1,0:T(8,128)(2,1)S(1)}, u32[]{:S(2)}, u32[]{:S(2)}) collective-permute-start(bf16[4,128,256]{2,1,0:T(8,128)(2,1)S(1)} %copy-done.17), channel_id=1, source_target_pairs={{1,0},{2,1},{3,2},{4,3},{5,4},{6,5},{7,6},{8,7},{9,8},{10,9},{11,1... | collective-permute-start | bytes 786440 | tf_op jit(solution)/shard_map/ppermute | solution.py:164
  88.0 0.7 copy-start.13
  88.0 0.8 copy-start.14
  94.2 31.7 %copy-start = (f32[2048,256]{1,0:T(8,128)S(1)}, f32[2048,256]{1,0:T(8,128)}, u32[]{:S(2)}) copy-start(f32[2048,256]{1,0:T(8,128)} %convolution_add_fusion.2) | copy-start | bytes 6291460
  94.2 31.7 %copy-start.12 = (bf16[2,256,256]{2,1,0:T(8,128)(2,1)S(1)}, bf16[2,256,256]{2,1,0:T(8,128)(2,1)}, u32[]{:S(2)}) copy-start(bf16[2,256,256]{2,1,0:T(8,128)(2,1)} %param.12) | copy-start | bytes 786436
  121.7 18.2 %all-to-all-start.1 = ((bf16[128,8,256]{2,1,0:T(8,128)(2,1)}), bf16[128,8,256]{2,1,0:T(8,128)(2,1)S(1)}, u32[]{:S(2)}, u32[]{:S(2)}) async-start(bf16[128,8,256]{2,1,0:T(8,128)(2,1)} %broadcast_in_dim.5), calls=%async_computation.1 | async-start | bytes 1048576 | tf_op jit(solution)/shard_map/all_to_all | solution.py:174
  125.9 1.8 %copy-start.9 = (bf16[16,128,256]{2,1,0:T(8,128)(2,1)S(1)}, bf16[16,128,256]{2,1,0:T(8,128)(2,1)}, u32[]{:S(2)}) copy-start(bf16[16,128,256]{2,1,0:T(8,128)(2,1)} %shard_map.107) | copy-start | bytes 3145732

commit v12 on v10

--- a/solution.py
+++ b/solution.py
@@ -121,7 +121,7 @@
     )(slot_ids, tile_data, grad_blocks, pre_blocks)
 
 
-def fold_kernel(lists_ref, slot_ref, lower_ref, upper_ref, out_ref, acc_ref):
+def fold_kernel(lists_ref, slot_ref, lower_ref, upper_ref, rows_ref, out_ref, step_ref, acc_ref):
     acc_ref[...] = slot_ref[...]
     for i in range(lower_ref.shape[0]):
         block = lists_ref[1, i]
@@ -129,27 +129,39 @@
     for i in range(upper_ref.shape[0]):
         block = lists_ref[0, i]
         acc_ref[block] += upper_ref[i].astype(jnp.float32)
-    out_ref[...] = acc_ref[...].astype(out_ref.dtype)
-
-
-def fold_lent(own_lists, slot_grad, from_lower, from_upper, blocks):
-    _, rows, width = slot_grad.shape
+    total = None
+    for block in range(acc_ref.shape[0]):
+        grad = acc_ref[block].astype(out_ref.dtype)
+        out_ref[block] = grad
+        part = lax.dot_general(
+            rows_ref[block], grad, (((0,), (0,)), ((), ())),
+            preferred_element_type=jnp.float32,
+        )
+        total = part if total is None else total + part
+    step_ref[...] = total
+
+
+def fold_lent(own_lists, slot_grad, from_lower, from_upper, row_blocks):
+    blocks, rows, width = slot_grad.shape
     lent = from_lower.shape[0]
+    whole = lambda count: pl.BlockSpec((count, rows, width), lambda g, lists: (0, 0, 0))
     return pl.pallas_call(
         fold_kernel,
         grid_spec=pltpu.PrefetchScalarGridSpec(
             num_scalar_prefetch=1,
             grid=(1,),
-            in_specs=[
-                pl.BlockSpec((blocks, rows, width), lambda g, lists: (0, 0, 0)),
-                pl.BlockSpec((lent, rows, width), lambda g, lists: (0, 0, 0)),
-                pl.BlockSpec((lent, rows, width), lambda g, lists: (0, 0, 0)),
+            in_specs=[whole(blocks), whole(lent), whole(lent), whole(blocks)],
+            out_specs=[
+                whole(blocks),
+                pl.BlockSpec((width, width), lambda g, lists: (0, 0)),
             ],
-            out_specs=pl.BlockSpec((blocks, rows, width), lambda g, lists: (0, 0, 0)),
             scratch_shapes=[pltpu.VMEM((blocks, rows, width), jnp.float32)],
         ),
-        out_shape=jax.ShapeDtypeStruct((blocks, rows, width), jnp.bfloat16),
-    )(own_lists, slot_grad, from_lower, from_upper)
+        out_shape=[
+            jax.ShapeDtypeStruct((blocks, rows, width), jnp.bfloat16),
+            jax.ShapeDtypeStruct((width, width), jnp.float32),
+        ],
+    )(own_lists, slot_grad, from_lower, from_upper, row_blocks)
 
 
 def to_upper(x, axis):
@@ -218,11 +230,12 @@
         dpre = dpre_blocks.reshape(-1, width)
         lent_down_grad = to_upper(high_grad, "sector")
         lent_up_grad = to_lower(low_grad, "sector")
-        dmessage = fold_lent(
-            own_lists, own_grad, lent_down_grad, lent_up_grad, blocks_here
-        ).reshape(-1, width)
+        dmessage, message_part = fold_lent(
+            own_lists, own_grad, lent_down_grad, lent_up_grad,
+            layer_in.reshape(blocks_here, tile_rows, width),
+        )
+        dmessage = dmessage.reshape(-1, width)
         self_part = jnp.dot(layer_in.T, dpre, preferred_element_type=jnp.float32)
-        message_part = jnp.dot(layer_in.T, dmessage, preferred_element_type=jnp.float32)
         message_steps[layer_index] = message_part
         self_steps[layer_index] = self_part
         grad = grad + jnp.dot(dpre, w_self[layer_index].T, preferred_element_type=jnp.float32)

time: 140 us -> 142 us (1.014)
  matrix products: 17.6 us -> 15.4 us
  Pallas kernels: 35.5 us -> 37 us
    dot_general x2 -> x0, matrix products: 2.22 us -> none  [per_device(): jnp.dot(layer_in.T, dmessage, preferred_element_type=jnp.float32)]
    pallas_call x2, Pallas kernels: 7.39 us -> 8.9 us  [fold_lent(): pl.pallas_call(fold_kernel, grid_spec=pltpu.PrefetchScalarGridSpec(num_sc...]
where the time goes in v12:
time: 142 us; the launch traced here: 141 us
  Pallas kernels  37 us (26%)
  blocking collectives  26.4 us (19%)
  starting transfers between devices  26.3 us (19%)
  waiting for transfers between devices  23.1 us (16%)
  matrix products  15.4 us (11%)
  local copies, waits for them, and re-layouts  8.9 us (6%)
  other arithmetic  2.93 us (2%)
    all_to_all x1, blocking collectives, all_reduce(): received = lax.all_to_all(pieces, axes, 0, 0, tiled=True)  26.4 us
    ppermute x4, starting transfers between devices, to_lower(): return lax.ppermute(x, axis, [((i + 1) % count, i) for i in range(count)])  19.4 us
    pallas_call x2, Pallas kernels, block_slot_grad(): pl.pallas_call(slot_grad_kernel, grid_spec=pltpu.PrefetchScalarGridSpec(n...  15.7 us
    ppermute x4, waiting for transfers between devices, to_upper(): return lax.ppermute(x, axis, [(i, (i + 1) % count) for i in range(count)])  12.7 us
    pallas_call x2, Pallas kernels, block_layer(): pl.pallas_call(layer_kernel, grid_spec=pltpu.PrefetchScalarGridSpec(num_s...  12.4 us
    all_to_all x1, waiting for transfers between devices, all_reduce(): gathered = lax.all_to_all(spread, axes, 0, 0, tiled=True)  10.4 us
    pallas_call x2, Pallas kernels, fold_lent(): pl.pallas_call(fold_kernel, grid_spec=pltpu.PrefetchScalarGridSpec(num_sc...  8.9 us
    dot_general x2, matrix products, per_device(): jnp.dot(dpre, w_self[layer_index].T, preferred_element_type=jnp.float32)  4.92 us
  transfers between devices with their start and end apart: 9, of which 5 were waited for; matrix products, arithmetic and copies ran while one was open for 7% of the time, Pallas kernels for 0%

profile of v12, /device:TPU:1, one launch (start us, length us, event | category | flops | bytes accessed | tf_op | source)
XLA Modules:
  0.0 141.0 jit_solution(4983034613720175666)
XLA Ops:
  0.7 1.0 dynamic-slice_reduce_fusion.2
  1.6 1.7 %convolution_convert_fusion.1 = bf16[2048,256]{1,0:T(8,128)(2,1)S(1)} fusion(bf16[1,2048,256]{2,1,0:T(8,128)(2,1)} %param.7, bf16[2,256,256]{2,1,0:T(8,128)(2,1)} %param.11), kind=kOutput, calls=%fused_computation.10 | convolution fusion | flops 268959744 | bytes 2228224 | tf_op jit(solution)/shard_map/dot_general | solution.py:208
  3.3 0.6 gather_fusion
  3.9 2.5 %collective-permute-start = (bf16[4,128,256]{2,1,0:T(8,128)(2,1)S(1)}, bf16[4,128,256]{2,1,0:T(8,128)(2,1)S(1)}, u32[]{:S(2)}, u32[]{:S(2)}) collective-permute-start(bf16[4,128,256]{2,1,0:T(8,128)(2,1)S(1)} %gather_fusion), channel_id=1, source_target_pairs={{0,1},{1,2},{2,3},{3,4},{4,5},{5,6},{6,7},{7,8},{8,9},{9,10},{10,1... | collective-permute-start | bytes 786440 | tf_op jit(solution)/shard_map/ppermute | solution.py:169
  6.4 0.6 gather_fusion.1
  7.0 4.7 %collective-permute-start.1 = (bf16[4,128,256]{2,1,0:T(8,128)(2,1)S(1)}, bf16[4,128,256]{2,1,0:T(8,128)(2,1)S(1)}, u32[]{:S(2)}, u32[]{:S(2)}) collective-permute-start(bf16[4,128,256]{2,1,0:T(8,128)(2,1)S(1)} %gather_fusion.1), channel_id=1, source_target_pairs={{1,0},{2,1},{3,2},{4,3},{5,4},{6,5},{7,6},{8,7},{9,8},{10,9},{11,1... | collective-permute-start | bytes 786440 | tf_op jit(solution)/shard_map/ppermute | solution.py:174
  11.6 0.7 copy.17.src_ref
  12.3 0.7 slice_bitcast_fusion
  13.0 3.9 %collective-permute-done = bf16[4,128,256]{2,1,0:T(8,128)(2,1)S(1)} collective-permute-done((bf16[4,128,256]{2,1,0:T(8,128)(2,1)S(1)}, bf16[4,128,256]{2,1,0:T(8,128)(2,1)S(1)}, u32[]{:S(2)}, u32[]{:S(2)}) %collective-permute-start) | collective-permute-done | bytes 262176 | tf_op jit(solution)/shard_map/ppermute | solution.py:169
  17.0 0.8 pad_maximum_fusion.lent_ref
  17.8 6.3 %shard_map.102 = (f32[16,128,256]{2,1,0:T(8,128)}, bf16[16,128,256]{2,1,0:T(8,128)(2,1)}) custom-call(s32[16,8]{1,0:T(8,128)} %copy.17.src_ref, bf16[16,8,128,128]{3,2,1,0:T(8,128)(2,1)} %bitcast.77, bf16[16,128,256]{2,1,0:T(8,128)(2,1)} %bitcast.88, bf16[8,128,256]{2,1,0:T(8,128)(2,1)} %pad_maximum_fusion.lent_ref, bf16[16,128,256]{2,1,0:T(8,128)(2,1)} %bitcast.83, ...), custom_call_target="tpu_custom_call" | custom-call | tf_op jit(solution)/shard_map/pallas_call | solution.py:44
  24.1 1.7 %convolution_convert_fusion = bf16[2048,256]{1,0:T(8,128)(2,1)S(1)} fusion(bf16[2048,256]{1,0:T(8,128)(2,1)} %bitcast.82, bf16[2,256,256]{2,1,0:T(8,128)(2,1)S(1)} %copy-done.9), kind=kOutput, calls=%fused_computation.9 | convolution fusion | flops 268959744 | bytes 2228224 | tf_op jit(solution)/shard_map/dot_general | solution.py:208
  25.8 0.6 gather_fusion.3
  26.3 0.6 gather_fusion.2
  26.9 0.1 collective-permute-start.2
  27.0 5.2 %collective-permute-start.3 = (bf16[4,128,256]{2,1,0:T(8,128)(2,1)S(1)}, bf16[4,128,256]{2,1,0:T(8,128)(2,1)S(1)}, u32[]{:S(2)}, u32[]{:S(2)}) collective-permute-start(bf16[4,128,256]{2,1,0:T(8,128)(2,1)S(1)} %gather_fusion.3), channel_id=1, source_target_pairs={{1,0},{2,1},{3,2},{4,3},{5,4},{6,5},{7,6},{8,7},{9,8},{10,9},{11,1... | collective-permute-start | bytes 786440 | tf_op jit(solution)/shard_map/ppermute | solution.py:174
  32.2 0.8 dynamic-slice_reduce_fusion.lists_ref
  33.0 4.3 %collective-permute-done.2 = bf16[4,128,256]{2,1,0:T(8,128)(2,1)S(1)} collective-permute-done((bf16[4,128,256]{2,1,0:T(8,128)(2,1)S(1)}, bf16[4,128,256]{2,1,0:T(8,128)(2,1)S(1)}, u32[]{:S(2)}, u32[]{:S(2)}) %collective-permute-start.2) | collective-permute-done | bytes 262176 | tf_op jit(solution)/shard_map/ppermute | solution.py:169
  37.3 0.8 pad_maximum_fusion.1.lent_ref
  38.1 6.1 %shard_map.103 = (f32[16,128,256]{2,1,0:T(8,128)}, bf16[16,128,256]{2,1,0:T(8,128)(2,1)}) custom-call(s32[16,8]{1,0:T(8,128)} %copy.17.src_ref, bf16[16,8,128,128]{3,2,1,0:T(8,128)(2,1)} %bitcast.78, bf16[16,128,256]{2,1,0:T(8,128)(2,1)} %bitcast.91, bf16[8,128,256]{2,1,0:T(8,128)(2,1)} %pad_maximum_fusion.1.lent_ref, ...), custom_call_target="tpu_custom_call" | custom-call | tf_op jit(solution)/shard_map/pallas_call | solution.py:44
  44.3 7.9 %shard_map.104 = (f32[16,128,256]{2,1,0:T(8,128)}, bf16[4,128,256]{2,1,0:T(8,128)(2,1)}, bf16[4,128,256]{2,1,0:T(8,128)(2,1)}, bf16[16,128,256]{2,1,0:T(8,128)(2,1)}) custom-call(s32[16,8]{1,0:T(8,128)} %copy.17.src_ref, bf16[16,8,128,128]{3,2,1,0:T(8,128)(2,1)} %bitcast.79, f32[16,128,256]{2,1,0:T(8,128)} %bitcast.85, f32[16,128,256]{2,1,0:T(8,128)} %get-tuple-element.22.pre_ref), custom_call_target="tpu_custom_call" | custom-call | tf_op jit(solution)/shard_map/pallas_call | solution.py:101
  52.1 4.8 %collective-permute-start.5 = (bf16[4,128,256]{2,1,0:T(8,128)(2,1)}, bf16[4,128,256]{2,1,0:T(8,128)(2,1)S(1)}, u32[]{:S(2)}, u32[]{:S(2)}) collective-permute-start(bf16[4,128,256]{2,1,0:T(8,128)(2,1)} %get-tuple-element.26), channel_id=1, source_target_pairs={{1,0},{2,1},{3,2},{4,3},{5,4},{6,5},{7,6},{8,7},{9,8},{10,9},{11,1... | collective-permute-start | bytes 786440 | tf_op jit(solution)/shard_map/ppermute | solution.py:174
  56.9 3.1 %convolution_add_fusion.3 = f32[2048,256]{1,0:T(8,128)} fusion(bf16[2048,256]{1,0:T(8,128)(2,1)} %bitcast.92, f32[1,2048,256]{2,1,0:T(8,128)S(1)} %copy-done.3, bf16[2,256,256]{2,1,0:T(8,128)(2,1)S(1)} %copy-done.10), kind=kOutput, calls=%fused_computation.8 | convolution fusion | flops 268959744 | bytes 5373952 | tf_op jit(solution)/shard_map/dot_general | solution.py:241
  60.1 0.5 fusion.3
  60.6 0.8 collective-permute-done.4.lower_ref
  61.4 0.7 copy-done.13
  62.1 0.1 copy-done.15
  62.2 4.5 %shard_map.105 = (bf16[16,128,256]{2,1,0:T(8,128)(2,1)}, f32[256,256]{1,0:T(8,128)}) custom-call(s32[2,4]{1,0:T(2,128)} %dynamic-slice_reduce_fusion.lists_ref, f32[16,128,256]{2,1,0:T(8,128)} %get-tuple-element.24.slot_ref, bf16[4,128,256]{2,1,0:T(8,128)(2,1)} %copy-done.13, bf16[4,128,256]{2,1,0:T(8,128)(2,1)} %copy-done.15, ...), custom_call_target="tpu_custom_call" | custom-call | tf_op jit(solution)/shard_map/pallas_call | solution.py:148
  66.7 3.0 %convolution_add_fusion.2 = f32[2048,256]{1,0:T(8,128)} fusion(f32[2048,256]{1,0:T(8,128)S(1)} %copy-done.4, bf16[2048,256]{1,0:T(8,128)(2,1)} %bitcast.97, bf16[2,256,256]{2,1,0:T(8,128)(2,1)S(1)} %copy-done.9), kind=kOutput, calls=%fused_computation.7 | convolution fusion | flops 268959744 | bytes 5373952 | tf_op jit(solution)/shard_map/dot_general | solution.py:242
  69.7 7.9 %shard_map.106 = (f32[16,128,256]{2,1,0:T(8,128)}, bf16[4,128,256]{2,1,0:T(8,128)(2,1)}, bf16[4,128,256]{2,1,0:T(8,128)(2,1)}, bf16[16,128,256]{2,1,0:T(8,128)(2,1)}) custom-call(s32[16,8]{1,0:T(8,128)} %copy.17.src_ref, bf16[16,8,128,128]{3,2,1,0:T(8,128)(2,1)} %bitcast.80, f32[16,128,256]{2,1,0:T(8,128)} %bitcast.81, f32[16,128,256]{2,1,0:T(8,128)} %get-tuple-element.28.pre_ref), custom_call_target="tpu_custom_call" | custom-call | tf_op jit(solution)/shard_map/pallas_call | solution.py:101
  77.6 1.8 %fusion.2 = bf16[1,256,256]{2,1,0:T(8,128)(2,1)S(1)} fusion(bf16[2048,256]{1,0:T(8,128)(2,1)} %bitcast.94, bf16[1,2048,256]{2,1,0:T(8,128)(2,1)S(1)} %copy-done.2), kind=kOutput, calls=%fused_computation.14 | convolution fusion | flops 268500992 | bytes 2228224 | tf_op jit(solution)/shard_map/dot_general | solution.py:238
  79.4 0.1 collective-permute-start.6
  79.5 4.8 %collective-permute-start.7 = (bf16[4,128,256]{2,1,0:T(8,128)(2,1)S(1)}, bf16[4,128,256]{2,1,0:T(8,128)(2,1)S(1)}, u32[]{:S(2)}, u32[]{:S(2)}) collective-permute-start(bf16[4,128,256]{2,1,0:T(8,128)(2,1)S(1)} %copy-done.18), channel_id=1, source_target_pairs={{1,0},{2,1},{3,2},{4,3},{5,4},{6,5},{7,6},{8,7},{9,8},{10,9},{11,1... | collective-permute-start | bytes 786440 | tf_op jit(solution)/shard_map/ppermute | solution.py:174
  84.3 3.7 %collective-permute-done.6.lower_ref = bf16[4,128,256]{2,1,0:T(8,128)(2,1)S(1)} collective-permute-done((bf16[4,128,256]{2,1,0:T(8,128)(2,1)S(1)}, bf16[4,128,256]{2,1,0:T(8,128)(2,1)S(1)}, u32[]{:S(2)}, u32[]{:S(2)}) %collective-permute-start.6) | collective-permute-done | bytes 262176 | tf_op jit(solution)/shard_map/ppermute | solution.py:169
  88.0 0.7 copy-done.12
  88.7 0.1 copy-done.14
  88.8 4.4 %shard_map.107 = (bf16[16,128,256]{2,1,0:T(8,128)(2,1)}, f32[256,256]{1,0:T(8,128)}) custom-call(s32[2,4]{1,0:T(2,128)} %dynamic-slice_reduce_fusion.lists_ref, f32[16,128,256]{2,1,0:T(8,128)} %get-tuple-element.30.slot_ref, bf16[4,128,256]{2,1,0:T(8,128)(2,1)} %copy-done.12, bf16[4,128,256]{2,1,0:T(8,128)(2,1)} %copy-done.14, bf16[16,128,256]{2,1,0:T(8,128)(2,1)} %bitcast.84), custom_call_target="tpu_custom_call" | custom-call | tf_op jit(solution)/shard_map/pallas_call | solution.py:148
  93.3 1.0 convert_bitcast_fusion.1
  94.3 0.1 pad_maximum_fusion.2
  94.3 26.4 %all_to_all.10 = bf16[128,8,256]{2,1,0:T(8,128)(2,1)S(1)} all-to-all(bf16[128,8,256]{2,1,0:T(8,128)(2,1)S(1)} %bitcast.93), channel_id=1, replica_groups=mesh['dp'=8,'sector'=16] {'dp','sector'}, dimensions={0} | all-to-all | bytes 1048576 | tf_op jit(solution)/shard_map/all_to_all | solution.py:181
  120.8 0.1 convert_reduce_fusion
  120.9 0.8 broadcast_in_dim.5
  121.7 4.2 %all-to-all-start.1 = ((bf16[128,8,256]{2,1,0:T(8,128)(2,1)}), bf16[128,8,256]{2,1,0:T(8,128)(2,1)S(1)}, u32[]{:S(2)}, u32[]{:S(2)}) async-start(bf16[128,8,256]{2,1,0:T(8,128)(2,1)} %broadcast_in_dim.5), calls=%async_computation.1 | async-start | bytes 1048576 | tf_op jit(solution)/shard_map/all_to_all | solution.py:184
  126.0 0.0 copy-start.8
  126.0 1.8 %convolution_add_fusion.1 = f32[2048,256]{1,0:T(8,128)S(1)} fusion(f32[2048,256]{1,0:T(8,128)S(1)} %copy-done, bf16[2048,256]{1,0:T(8,128)(2,1)} %bitcast.95, bf16[2,256,256]{2,1,0:T(8,128)(2,1)S(1)} %copy-done.10), kind=kOutput, calls=%fused_computation.6 | convolution fusion | flops 268959744 | bytes 5373952 | tf_op jit(solution)/shard_map/dot_general | solution.py:241
  127.8 1.8 %fusion = f32[1,2048,256]{2,1,0:T(8,128)} fusion(f32[2048,256]{1,0:T(8,128)S(1)} %convolution_add_fusion.1, bf16[2048,256]{1,0:T(8,128)(2,1)S(1)} %bitcast.96, bf16[2,256,256]{2,1,0:T(8,128)(2,1)S(1)} %copy-done.9), kind=kOutput, calls=%fused_computation.5 | convolution fusion | flops 268959744 | bytes 5373952 | tf_op jit(solution)/shard_map/dot_general | solution.py:242
  129.6 10.4 %all-to-all-done.1 = bf16[128,8,256]{2,1,0:T(8,128)(2,1)S(1)} async-done(((bf16[128,8,256]{2,1,0:T(8,128)(2,1)}), bf16[128,8,256]{2,1,0:T(8,128)(2,1)S(1)}, u32[]{:S(2)}, u32[]{:S(2)}) %all-to-all-start.1) | async-done | bytes 524320 | tf_op jit(solution)/shard_map/all_to_all | solution.py:184
  139.9 1.0 fusion.16
  (47 shorter events, 0.2 us)
Async XLA Ops:
  0.6 11.0 %copy-start.17 = (s32[1,16,8]{1,2,0:T(8,128)S(1)}, s32[1,16,8]{1,2,0:T(8,128)}, u32[]{:S(2)}) copy-start(s32[1,16,8]{1,2,0:T(8,128)} %param.9) | copy-start | bytes 1540
  0.6 11.7 %copy-start.10 = (bf16[2,256,256]{2,1,0:T(8,128)(2,1)S(1)}, bf16[2,256,256]{2,1,0:T(8,128)(2,1)}, u32[]{:S(2)}) copy-start(bf16[2,256,256]{2,1,0:T(8,128)(2,1)} %param.12) | copy-start | bytes 786436
  3.3 14.5 %copy-start.5 = (bf16[2048,256]{1,0:T(8,128)(2,1)}, bf16[2048,256]{1,0:T(8,128)(2,1)S(1)}, u32[]{:S(2)}) copy-start(bf16[2048,256]{1,0:T(8,128)(2,1)S(1)} %convolution_convert_fusion.1) | copy-start | bytes 3145732
  3.9 13.1 %collective-permute-start = (bf16[4,128,256]{2,1,0:T(8,128)(2,1)S(1)}, bf16[4,128,256]{2,1,0:T(8,128)(2,1)S(1)}, u32[]{:S(2)}, u32[]{:S(2)}) collective-permute-start(bf16[4,128,256]{2,1,0:T(8,128)(2,1)S(1)} %gather_fusion), channel_id=1, source_target_pairs={{0,1},{1,2},{2,3},{3,4},{4,5},{5,6},{6,7},{7,8},{8,9},{9,10},{10,1... | collective-permute-start | bytes 786440 | tf_op jit(solution)/shard_map/ppermute | solution.py:169
  7.0 10.0 %collective-permute-start.1 = (bf16[4,128,256]{2,1,0:T(8,128)(2,1)S(1)}, bf16[4,128,256]{2,1,0:T(8,128)(2,1)S(1)}, u32[]{:S(2)}, u32[]{:S(2)}) collective-permute-start(bf16[4,128,256]{2,1,0:T(8,128)(2,1)S(1)} %gather_fusion.1), channel_id=1, source_target_pairs={{1,0},{2,1},{3,2},{4,3},{5,4},{6,5},{7,6},{8,7},{9,8},{10,9},{11,1... | collective-permute-start | bytes 786440 | tf_op jit(solution)/shard_map/ppermute | solution.py:174
  17.8 6.3 %copy-start.9 = (bf16[2,256,256]{2,1,0:T(8,128)(2,1)S(1)}, bf16[2,256,256]{2,1,0:T(8,128)(2,1)}, u32[]{:S(2)}) copy-start(bf16[2,256,256]{2,1,0:T(8,128)(2,1)} %param.11) | copy-start | bytes 786436
  24.1 8.1 %copy-start.16 = (s32[1,16,2,4]{1,3,2,0:T(4,128)S(1)}, s32[1,16,2,4]{1,3,2,0:T(4,128)}, u32[]{:S(2)}) copy-start(s32[1,16,2,4]{1,3,2,0:T(4,128)} %param.10) | copy-start | bytes 1540
  25.8 12.4 %copy-start.6 = (bf16[2048,256]{1,0:T(8,128)(2,1)}, bf16[2048,256]{1,0:T(8,128)(2,1)S(1)}, u32[]{:S(2)}) copy-start(bf16[2048,256]{1,0:T(8,128)(2,1)S(1)} %convolution_convert_fusion) | copy-start | bytes 3145732
  26.9 10.4 %collective-permute-start.2 = (bf16[4,128,256]{2,1,0:T(8,128)(2,1)S(1)}, bf16[4,128,256]{2,1,0:T(8,128)(2,1)S(1)}, u32[]{:S(2)}, u32[]{:S(2)}) collective-permute-start(bf16[4,128,256]{2,1,0:T(8,128)(2,1)S(1)} %gather_fusion.2), channel_id=1, source_target_pairs={{0,1},{1,2},{2,3},{3,4},{4,5},{5,6},{6,7},{7,8},{8,9},{9,10},{10,1... | collective-permute-start | bytes 786440 | tf_op jit(solution)/shard_map/ppermute | solution.py:169
  27.0 10.3 %collective-permute-start.3 = (bf16[4,128,256]{2,1,0:T(8,128)(2,1)S(1)}, bf16[4,128,256]{2,1,0:T(8,128)(2,1)S(1)}, u32[]{:S(2)}, u32[]{:S(2)}) collective-permute-start(bf16[4,128,256]{2,1,0:T(8,128)(2,1)S(1)} %gather_fusion.3), channel_id=1, source_target_pairs={{1,0},{2,1},{3,2},{4,3},{5,4},{6,5},{7,6},{8,7},{9,8},{10,9},{11,1... | collective-permute-start | bytes 786440 | tf_op jit(solution)/shard_map/ppermute | solution.py:174
  44.3 12.7 %copy-start.3 = (f32[1,2048,256]{2,1,0:T(8,128)S(1)}, f32[1,2048,256]{2,1,0:T(8,128)}, u32[]{:S(2)}) copy-start(f32[1,2048,256]{2,1,0:T(8,128)} %param.13) | copy-start | bytes 6291460
  52.1 9.3 %collective-permute-start.4 = (bf16[4,128,256]{2,1,0:T(8,128)(2,1)}, bf16[4,128,256]{2,1,0:T(8,128)(2,1)S(1)}, u32[]{:S(2)}, u32[]{:S(2)}) collective-permute-start(bf16[4,128,256]{2,1,0:T(8,128)(2,1)} %get-tuple-element.25), channel_id=1, source_target_pairs={{0,1},{1,2},{2,3},{3,4},{4,5},{5,6},{6,7},{7,8},{8,9},{9,10},{10,1... | collective-permute-start | bytes 786440 | tf_op jit(solution)/shard_map/ppermute | solution.py:169
  52.1 9.3 %collective-permute-start.5 = (bf16[4,128,256]{2,1,0:T(8,128)(2,1)}, bf16[4,128,256]{2,1,0:T(8,128)(2,1)S(1)}, u32[]{:S(2)}, u32[]{:S(2)}) collective-permute-start(bf16[4,128,256]{2,1,0:T(8,128)(2,1)} %get-tuple-element.26), channel_id=1, source_target_pairs={{1,0},{2,1},{3,2},{4,3},{5,4},{6,5},{7,6},{8,7},{9,8},{10,9},{11,1... | collective-permute-start | bytes 786440 | tf_op jit(solution)/shard_map/ppermute | solution.py:174
  56.9 3.2 %copy-start.1 = (bf16[16,128,256]{2,1,0:T(8,128)(2,1)S(1)}, bf16[16,128,256]{2,1,0:T(8,128)(2,1)}, u32[]{:S(2)}) copy-start(bf16[16,128,256]{2,1,0:T(8,128)(2,1)} %get-tuple-element.20.hits_ref.rows_ref) | copy-start | bytes 3145732
  56.9 3.2 %copy-start.7 = (bf16[16,128,256]{2,1,0:T(8,128)(2,1)S(1)}, bf16[16,128,256]{2,1,0:T(8,128)(2,1)}, u32[]{:S(2)}) copy-start(bf16[16,128,256]{2,1,0:T(8,128)(2,1)} %get-tuple-element.23) | copy-start | bytes 3145732
  60.6 6.1 %copy-start.4 = (f32[2048,256]{1,0:T(8,128)S(1)}, f32[2048,256]{1,0:T(8,128)}, u32[]{:S(2)}) copy-start(f32[2048,256]{1,0:T(8,128)} %convolution_add_fusion.3) | copy-start | bytes 6291460
  61.4 0.7 copy-start.13
  61.4 0.8 copy-start.15
  69.7 7.9 %copy-start.2 = (bf16[1,2048,256]{2,1,0:T(8,128)(2,1)S(1)}, bf16[1,2048,256]{2,1,0:T(8,128)(2,1)}, u32[]{:S(2)}) copy-start(bf16[1,2048,256]{2,1,0:T(8,128)(2,1)} %param.7) | copy-start | bytes 3145732
  77.6 1.8 %copy-start.19 = (bf16[4,128,256]{2,1,0:T(8,128)(2,1)S(1)}, bf16[4,128,256]{2,1,0:T(8,128)(2,1)}, u32[]{:S(2)}) copy-start(bf16[4,128,256]{2,1,0:T(8,128)(2,1)} %get-tuple-element.31) | copy-start | bytes 786436
  77.6 1.9 %copy-start.18 = (bf16[4,128,256]{2,1,0:T(8,128)(2,1)S(1)}, bf16[4,128,256]{2,1,0:T(8,128)(2,1)}, u32[]{:S(2)}) copy-start(bf16[4,128,256]{2,1,0:T(8,128)(2,1)} %get-tuple-element.32) | copy-start | bytes 786436
  77.6 6.7 %copy-start.11 = (f32[256,256]{1,0:T(8,128)S(1)}, f32[256,256]{1,0:T(8,128)}, u32[]{:S(2)}) copy-start(f32[256,256]{1,0:T(8,128)} %get-tuple-element.35) | copy-start | bytes 786436
  79.4 8.6 %collective-permute-start.6 = (bf16[4,128,256]{2,1,0:T(8,128)(2,1)S(1)}, bf16[4,128,256]{2,1,0:T(8,128)(2,1)S(1)}, u32[]{:S(2)}, u32[]{:S(2)}) collective-permute-start(bf16[4,128,256]{2,1,0:T(8,128)(2,1)S(1)} %copy-done.19), channel_id=1, source_target_pairs={{0,1},{1,2},{2,3},{3,4},{4,5},{5,6},{6,7},{7,8},{8,9},{9,10},{10,1... | collective-permute-start | bytes 786440 | tf_op jit(solution)/shard_map/ppermute | solution.py:169
  79.5 8.5 %collective-permute-start.7 = (bf16[4,128,256]{2,1,0:T(8,128)(2,1)S(1)}, bf16[4,128,256]{2,1,0:T(8,128)(2,1)S(1)}, u32[]{:S(2)}, u32[]{:S(2)}) collective-permute-start(bf16[4,128,256]{2,1,0:T(8,128)(2,1)S(1)} %copy-done.18), channel_id=1, source_target_pairs={{1,0},{2,1},{3,2},{4,3},{5,4},{6,5},{7,6},{8,7},{9,8},{10,9},{11,1... | collective-permute-start | bytes 786440 | tf_op jit(solution)/shard_map/ppermute | solution.py:174
  88.0 0.7 copy-start.12
  88.0 0.8 copy-start.14
  94.3 31.7 %copy-start = (f32[2048,256]{1,0:T(8,128)S(1)}, f32[2048,256]{1,0:T(8,128)}, u32[]{:S(2)}) copy-start(f32[2048,256]{1,0:T(8,128)} %convolution_add_fusion.2) | copy-start | bytes 6291460
  121.7 18.2 %all-to-all-start.1 = ((bf16[128,8,256]{2,1,0:T(8,128)(2,1)}), bf16[128,8,256]{2,1,0:T(8,128)(2,1)S(1)}, u32[]{:S(2)}, u32[]{:S(2)}) async-start(bf16[128,8,256]{2,1,0:T(8,128)(2,1)} %broadcast_in_dim.5), calls=%async_computation.1 | async-start | bytes 1048576 | tf_op jit(solution)/shard_map/all_to_all | solution.py:184
  126.0 1.8 %copy-start.8 = (bf16[16,128,256]{2,1,0:T(8,128)(2,1)S(1)}, bf16[16,128,256]{2,1,0:T(8,128)(2,1)}, u32[]{:S(2)}) copy-start(bf16[16,128,256]{2,1,0:T(8,128)(2,1)} %get-tuple-element.33) | copy-start | bytes 3145732

commit v13 on v10

--- a/solution.py
+++ b/solution.py
@@ -197,8 +197,16 @@
             current, w_message[layer_index], preferred_element_type=jnp.float32
         ).astype(jnp.bfloat16)
         message_blocks = message.reshape(blocks_here, tile_rows, width)
-        from_lower = to_upper(message_blocks[own_lists[0]], "sector")
-        from_upper = to_lower(message_blocks[own_lists[1]], "sector")
+        current_blocks = current.reshape(blocks_here, tile_rows, width)
+
+        def lent_message(indices):
+            return jnp.dot(
+                current_blocks[indices].reshape(-1, width), w_message[layer_index],
+                preferred_element_type=jnp.float32,
+            ).astype(jnp.bfloat16).reshape(lent, tile_rows, width)
+
+        from_lower = to_upper(lent_message(own_lists[0]), "sector")
+        from_upper = to_lower(lent_message(own_lists[1]), "sector")
         pre, following = block_layer(
             slot_ids, tile_data, message_blocks, jnp.concatenate([from_lower, from_upper]),
             current.reshape(message_blocks.shape),

time: 140 us -> 147 us (1.050)
  local copies, waits for them, and re-layouts: 8.09 us -> 13.2 us
  matrix products: 17.6 us -> 19.7 us
    gather x4, local copies, waits for them, and re-layouts: 2.25 us -> 7.24 us  [lent_message(): current_blocks[indices].reshape(-1, width)]
    dot_general x0 -> x4, matrix products: none -> 2.7 us  [lent_message(): jnp.dot(current_blocks[indices].reshape(-1, width), w_message[layer_index...]
    ppermute x4, starting transfers between devices: 2.69 us -> 0.16 us  [to_upper(): return lax.ppermute(x, axis, [(i, (i + 1) % count) for i in range(count)])]
    ppermute x4, starting transfers between devices: 19.4 us -> 21.6 us  [to_lower(): return lax.ppermute(x, axis, [((i + 1) % count, i) for i in range(count)])]
  transfers between devices with their start and end apart: 9 -> 9, of which waited for: 5 -> 5; matrix products, arithmetic and copies ran while one was open for 7% -> 12% of each run, Pallas kernels for 0% -> 0%
where the time goes in v13:
time: 147 us
  Pallas kernels  35.5 us (24%)
  blocking collectives  27.3 us (19%)
  starting transfers between devices  25.9 us (18%)
  waiting for transfers between devices  22.2 us (15%)
  matrix products  19.7 us (13%)
  local copies, waits for them, and re-layouts  13.2 us (9%)
  other arithmetic  1.95 us (1%)
    all_to_all x1, blocking collectives, all_reduce(): received = lax.all_to_all(pieces, axes, 0, 0, tiled=True)  27.3 us
    ppermute x4, starting transfers between devices, to_lower(): return lax.ppermute(x, axis, [((i + 1) % count, i) for i in range(count)])  21.6 us
    pallas_call x2, Pallas kernels, block_slot_grad(): pl.pallas_call(slot_grad_kernel, grid_spec=pltpu.PrefetchScalarGridSpec(n...  15.8 us
    pallas_call x2, Pallas kernels, block_layer(): pl.pallas_call(layer_kernel, grid_spec=pltpu.PrefetchScalarGridSpec(num_s...  12.2 us
    ppermute x4, waiting for transfers between devices, to_upper(): return lax.ppermute(x, axis, [(i, (i + 1) % count) for i in range(count)])  11.8 us
    all_to_all x1, waiting for transfers between devices, all_reduce(): gathered = lax.all_to_all(spread, axes, 0, 0, tiled=True)  10.4 us
    pallas_call x2, Pallas kernels, fold_lent(): pl.pallas_call(fold_kernel, grid_spec=pltpu.PrefetchScalarGridSpec(num_sc...  7.5 us
    gather x4, local copies, waits for them, and re-layouts, lent_message(): current_blocks[indices].reshape(-1, width)  7.24 us
  transfers between devices with their start and end apart: 9, of which 5 were waited for; matrix products, arithmetic and copies ran while one was open for 12% of the time, Pallas kernels for 0%

profile of v13, /device:TPU:1, one launch (start us, length us, event | category | flops | bytes accessed | tf_op | source)
XLA Modules:
  0.0 146.7 jit_solution(9045975383561810346)
XLA Ops:
  0.7 1.0 dynamic-slice_reduce_fusion.2
  1.7 1.8 %gather_fusion.1 = bf16[4,128,256]{2,1,0:T(8,128)(2,1)S(1)} fusion(bf16[16,128,256]{2,1,0:T(8,128)(2,1)} %bitcast.118, s32[1024]{0:T(1024)S(1)} %pad_clamp_fusion), kind=kCustom, calls=%fused_computation.1 | custom fusion | bytes 524304 | tf_op jit(solution)/shard_map/gather | solution.py:204
  3.5 1.1 convolution_convert_fusion.4
  4.7 7.1 %collective-permute-start.1 = (bf16[4,128,256]{2,1,0:T(8,128)(2,1)S(1)}, bf16[4,128,256]{2,1,0:T(8,128)(2,1)S(1)}, u32[]{:S(2)}, u32[]{:S(2)}) collective-permute-start(bf16[4,128,256]{2,1,0:T(8,128)(2,1)S(1)} %bitcast.135), channel_id=1, source_target_pairs={{1,0},{2,1},{3,2},{4,3},{5,4},{6,5},{7,6},{8,7},{9,8},{10,9},{11,1... | collective-permute-start | bytes 786440 | tf_op jit(solution)/shard_map/ppermute | solution.py:162
  11.8 1.8 %gather_fusion = bf16[4,128,256]{2,1,0:T(8,128)(2,1)S(1)} fusion(bf16[16,128,256]{2,1,0:T(8,128)(2,1)} %bitcast.119, s32[1024]{0:T(1024)S(1)} %pad_clamp_fusion.1), kind=kCustom, calls=%fused_computation | custom fusion | bytes 524304 | tf_op jit(solution)/shard_map/gather | solution.py:204
  13.6 1.1 convolution_convert_fusion.5
  14.7 0.1 collective-permute-start
  14.8 0.8 dynamic-slice_reduce_fusion.lists_ref
  15.6 0.7 copy.18.src_ref
  16.3 0.7 slice_bitcast_fusion
  17.0 1.4 convolution_convert_fusion.1
  18.4 6.6 %collective-permute-done = bf16[4,128,256]{2,1,0:T(8,128)(2,1)S(1)} collective-permute-done((bf16[4,128,256]{2,1,0:T(8,128)(2,1)S(1)}, bf16[4,128,256]{2,1,0:T(8,128)(2,1)S(1)}, u32[]{:S(2)}, u32[]{:S(2)}) %collective-permute-start) | collective-permute-done | bytes 262176 | tf_op jit(solution)/shard_map/ppermute | solution.py:157
  25.0 0.8 pad_maximum_fusion.lent_ref
  25.8 6.1 %shard_map.102 = (f32[16,128,256]{2,1,0:T(8,128)}, bf16[16,128,256]{2,1,0:T(8,128)(2,1)}) custom-call(s32[16,8]{1,0:T(8,128)} %copy.18.src_ref, bf16[16,8,128,128]{3,2,1,0:T(8,128)(2,1)} %bitcast.110, bf16[16,128,256]{2,1,0:T(8,128)(2,1)} %bitcast.122, bf16[8,128,256]{2,1,0:T(8,128)(2,1)} %pad_maximum_fusion.lent_ref, bf16[16,128,256]{2,1,0:T(8,128)(2,1)} %bitcast.120, ...), custom_call_target="tpu_custom_call" | custom-call | tf_op jit(solution)/shard_map/pallas_call | solution.py:44
  32.0 1.9 %gather_fusion.3 = bf16[4,128,256]{2,1,0:T(8,128)(2,1)S(1)} fusion(bf16[16,128,256]{2,1,0:T(8,128)(2,1)} %get-tuple-element.16.hits_ref, s32[1024]{0:T(1024)S(1)} %pad_clamp_fusion), kind=kCustom, calls=%fused_computation.3 | custom fusion | bytes 524304 | tf_op jit(solution)/shard_map/gather | solution.py:204
  33.8 1.8 %gather_fusion.2 = bf16[4,128,256]{2,1,0:T(8,128)(2,1)S(1)} fusion(bf16[16,128,256]{2,1,0:T(8,128)(2,1)} %get-tuple-element.16.hits_ref, s32[1024]{0:T(1024)S(1)} %pad_clamp_fusion.1), kind=kCustom, calls=%fused_computation.2 | custom fusion | bytes 524304 | tf_op jit(solution)/shard_map/gather | solution.py:204
  35.6 0.2 convolution_convert_fusion.2
  35.9 0.2 convolution_convert_fusion.3
  36.1 0.1 collective-permute-start.2
  36.2 4.8 %collective-permute-start.3 = (bf16[4,128,256]{2,1,0:T(8,128)(2,1)S(1)}, bf16[4,128,256]{2,1,0:T(8,128)(2,1)S(1)}, u32[]{:S(2)}, u32[]{:S(2)}) collective-permute-start(bf16[4,128,256]{2,1,0:T(8,128)(2,1)S(1)} %bitcast.137), channel_id=1, source_target_pairs={{1,0},{2,1},{3,2},{4,3},{5,4},{6,5},{7,6},{8,7},{9,8},{10,9},{11,1... | collective-permute-start | bytes 786440 | tf_op jit(solution)/shard_map/ppermute | solution.py:162
  41.0 1.4 convolution_convert_fusion
  42.4 3.1 %collective-permute-done.2 = bf16[4,128,256]{2,1,0:T(8,128)(2,1)S(1)} collective-permute-done((bf16[4,128,256]{2,1,0:T(8,128)(2,1)S(1)}, bf16[4,128,256]{2,1,0:T(8,128)(2,1)S(1)}, u32[]{:S(2)}, u32[]{:S(2)}) %collective-permute-start.2) | collective-permute-done | bytes 262176 | tf_op jit(solution)/shard_map/ppermute | solution.py:157
  45.6 0.8 pad_maximum_fusion.1.lent_ref
  46.4 6.1 %shard_map.103 = (f32[16,128,256]{2,1,0:T(8,128)}, bf16[16,128,256]{2,1,0:T(8,128)(2,1)}) custom-call(s32[16,8]{1,0:T(8,128)} %copy.18.src_ref, bf16[16,8,128,128]{3,2,1,0:T(8,128)(2,1)} %bitcast.111, bf16[16,128,256]{2,1,0:T(8,128)(2,1)} %bitcast.121, bf16[8,128,256]{2,1,0:T(8,128)(2,1)} %pad_maximum_fusion.1.lent_ref, ...), custom_call_target="tpu_custom_call" | custom-call | tf_op jit(solution)/shard_map/pallas_call | solution.py:44
  52.5 7.9 %shard_map.104 = (f32[16,128,256]{2,1,0:T(8,128)}, bf16[4,128,256]{2,1,0:T(8,128)(2,1)}, bf16[4,128,256]{2,1,0:T(8,128)(2,1)}, bf16[16,128,256]{2,1,0:T(8,128)(2,1)}) custom-call(s32[16,8]{1,0:T(8,128)} %copy.18.src_ref, bf16[16,8,128,128]{3,2,1,0:T(8,128)(2,1)} %bitcast.112, f32[16,128,256]{2,1,0:T(8,128)} %bitcast.117, ...), custom_call_target="tpu_custom_call" | custom-call | tf_op jit(solution)/shard_map/pallas_call | solution.py:101
  60.4 4.8 %collective-permute-start.5 = (bf16[4,128,256]{2,1,0:T(8,128)(2,1)}, bf16[4,128,256]{2,1,0:T(8,128)(2,1)}, u32[]{:S(2)}, u32[]{:S(2)}) collective-permute-start(bf16[4,128,256]{2,1,0:T(8,128)(2,1)} %get-tuple-element.22), channel_id=1, source_target_pairs={{1,0},{2,1},{3,2},{4,3},{5,4},{6,5},{7,6},{8,7},{9,8},{10,9},{11,1... | collective-permute-start | bytes 786440 | tf_op jit(solution)/shard_map/ppermute | solution.py:162
  65.2 3.1 %convolution_add_fusion.3 = f32[2048,256]{1,0:T(8,128)} fusion(bf16[2048,256]{1,0:T(8,128)(2,1)} %bitcast.123, f32[1,2048,256]{2,1,0:T(8,128)S(1)} %copy-done.4, bf16[2,256,256]{2,1,0:T(8,128)(2,1)} %param.12), kind=kOutput, calls=%fused_computation.8 | convolution fusion | flops 268959744 | bytes 5373952 | tf_op jit(solution)/shard_map/dot_general | solution.py:236
  68.3 0.5 fusion.5
  68.8 0.4 collective-permute-done.4.lower_ref
  69.3 3.8 %shard_map.105 = bf16[16,128,256]{2,1,0:T(8,128)(2,1)} custom-call(s32[2,4]{1,0:T(2,128)} %dynamic-slice_reduce_fusion.lists_ref, f32[16,128,256]{2,1,0:T(8,128)} %get-tuple-element.20.slot_ref, bf16[4,128,256]{2,1,0:T(8,128)(2,1)} %collective-permute-done.4.lower_ref, bf16[4,128,256]{2,1,0:T(8,128)(2,1)} %collective-permute-done.5.upper_ref), custom_call_target="tpu_custom_call" | custom-call | tf_op jit(solution)/shard_map/pallas_call | solution.py:138
  73.1 3.0 %convolution_add_fusion.2 = f32[2048,256]{1,0:T(8,128)} fusion(f32[2048,256]{1,0:T(8,128)S(1)} %copy-done.5, bf16[2048,256]{1,0:T(8,128)(2,1)} %bitcast.116, bf16[2,256,256]{2,1,0:T(8,128)(2,1)S(1)} %copy-done.10), kind=kOutput, calls=%fused_computation.7 | convolution fusion | flops 268959744 | bytes 5373952 | tf_op jit(solution)/shard_map/dot_general | solution.py:237
  76.1 7.9 %shard_map.106 = (f32[16,128,256]{2,1,0:T(8,128)}, bf16[4,128,256]{2,1,0:T(8,128)(2,1)}, bf16[4,128,256]{2,1,0:T(8,128)(2,1)}, bf16[16,128,256]{2,1,0:T(8,128)(2,1)}) custom-call(s32[16,8]{1,0:T(8,128)} %copy.18.src_ref, bf16[16,8,128,128]{3,2,1,0:T(8,128)(2,1)} %bitcast.113, f32[16,128,256]{2,1,0:T(8,128)} %bitcast.115, ...), custom_call_target="tpu_custom_call" | custom-call | tf_op jit(solution)/shard_map/pallas_call | solution.py:101
  84.0 4.9 %collective-permute-start.7 = (bf16[4,128,256]{2,1,0:T(8,128)(2,1)}, bf16[4,128,256]{2,1,0:T(8,128)(2,1)S(1)}, u32[]{:S(2)}, u32[]{:S(2)}) collective-permute-start(bf16[4,128,256]{2,1,0:T(8,128)(2,1)} %get-tuple-element.27), channel_id=1, source_target_pairs={{1,0},{2,1},{3,2},{4,3},{5,4},{6,5},{7,6},{8,7},{9,8},{10,9},{11,1... | collective-permute-start | bytes 786440 | tf_op jit(solution)/shard_map/ppermute | solution.py:162
  88.9 1.7 %fusion.4 = bf16[1,256,256]{2,1,0:T(8,128)(2,1)S(1)} fusion(bf16[2048,256]{1,0:T(8,128)(2,1)} %bitcast.131, bf16[1,2048,256]{2,1,0:T(8,128)(2,1)S(1)} %copy-done.7), kind=kOutput, calls=%fused_computation.22 | convolution fusion | flops 268500992 | bytes 2228224 | tf_op jit(solution)/shard_map/dot_general | solution.py:232
  90.7 0.5 fusion.6
  91.2 1.6 %collective-permute-done.6.lower_ref = bf16[4,128,256]{2,1,0:T(8,128)(2,1)S(1)} collective-permute-done((bf16[4,128,256]{2,1,0:T(8,128)(2,1)}, bf16[4,128,256]{2,1,0:T(8,128)(2,1)S(1)}, u32[]{:S(2)}, u32[]{:S(2)}) %collective-permute-start.6) | collective-permute-done | bytes 262176 | tf_op jit(solution)/shard_map/ppermute | solution.py:157
  92.8 0.7 copy-done.13
  93.5 0.1 copy-done.14
  93.5 3.7 %shard_map.107 = bf16[16,128,256]{2,1,0:T(8,128)(2,1)} custom-call(s32[2,4]{1,0:T(2,128)} %dynamic-slice_reduce_fusion.lists_ref, f32[16,128,256]{2,1,0:T(8,128)} %get-tuple-element.25.slot_ref, bf16[4,128,256]{2,1,0:T(8,128)(2,1)} %copy-done.13, bf16[4,128,256]{2,1,0:T(8,128)(2,1)} %copy-done.14), custom_call_target="tpu_custom_call" | custom-call | tf_op jit(solution)/shard_map/pallas_call | solution.py:138
  97.2 1.7 %fusion.3 = bf16[1,256,256]{2,1,0:T(8,128)(2,1)S(1)} fusion(bf16[2048,256]{1,0:T(8,128)(2,1)} %bitcast.124, bf16[1,2048,256]{2,1,0:T(8,128)(2,1)S(1)} %copy-done.7), kind=kOutput, calls=%fused_computation.21 | convolution fusion | flops 268500992 | bytes 2228224 | tf_op jit(solution)/shard_map/dot_general | solution.py:233
  99.1 27.3 %all_to_all.10 = bf16[128,8,256]{2,1,0:T(8,128)(2,1)S(1)} all-to-all(bf16[128,8,256]{2,1,0:T(8,128)(2,1)S(1)} %bitcast.126), channel_id=1, replica_groups=mesh['dp'=8,'sector'=16] {'dp','sector'}, dimensions={0} | all-to-all | bytes 1048576 | tf_op jit(solution)/shard_map/all_to_all | solution.py:169
  126.4 0.1 convert_reduce_fusion
  126.6 0.8 broadcast_in_dim.5
  127.4 4.2 %all-to-all-start.1 = ((bf16[128,8,256]{2,1,0:T(8,128)(2,1)}), bf16[128,8,256]{2,1,0:T(8,128)(2,1)S(1)}, u32[]{:S(2)}, u32[]{:S(2)}) async-start(bf16[128,8,256]{2,1,0:T(8,128)(2,1)} %broadcast_in_dim.5), calls=%async_computation.1 | async-start | bytes 1048576 | tf_op jit(solution)/shard_map/all_to_all | solution.py:172
  131.7 1.8 %convolution_add_fusion.1 = f32[2048,256]{1,0:T(8,128)S(1)} fusion(f32[2048,256]{1,0:T(8,128)S(1)} %copy-done.2, bf16[2048,256]{1,0:T(8,128)(2,1)} %bitcast.132, bf16[2,256,256]{2,1,0:T(8,128)(2,1)S(1)} %copy-done.12), kind=kOutput, calls=%fused_computation.6 | convolution fusion | flops 268959744 | bytes 5373952 | tf_op jit(solution)/shard_map/dot_general | solution.py:236
  133.5 1.8 %fusion = f32[1,2048,256]{2,1,0:T(8,128)} fusion(f32[2048,256]{1,0:T(8,128)S(1)} %convolution_add_fusion.1, bf16[2048,256]{1,0:T(8,128)(2,1)S(1)} %bitcast.125, bf16[2,256,256]{2,1,0:T(8,128)(2,1)S(1)} %copy-done.10), kind=kOutput, calls=%fused_computation.5 | convolution fusion | flops 268959744 | bytes 5373952 | tf_op jit(solution)/shard_map/dot_general | solution.py:237
  135.3 10.4 %all-to-all-done.1 = bf16[128,8,256]{2,1,0:T(8,128)(2,1)S(1)} async-done(((bf16[128,8,256]{2,1,0:T(8,128)(2,1)}), bf16[128,8,256]{2,1,0:T(8,128)(2,1)S(1)}, u32[]{:S(2)}, u32[]{:S(2)}) %all-to-all-start.1) | async-done | bytes 524320 | tf_op jit(solution)/shard_map/all_to_all | solution.py:172
  145.6 1.0 fusion.28
  (45 shorter events, 0.2 us)
Async XLA Ops:
  0.6 14.2 %copy-start.15 = (s32[1,16,2,4]{1,3,2,0:T(4,128)S(1)}, s32[1,16,2,4]{1,3,2,0:T(4,128)}, u32[]{:S(2)}) copy-start(s32[1,16,2,4]{1,3,2,0:T(4,128)} %param.10) | copy-start | bytes 1540
  0.6 16.3 %copy-start.6 = (bf16[1,2048,256]{2,1,0:T(8,128)(2,1)S(1)}, bf16[1,2048,256]{2,1,0:T(8,128)(2,1)}, u32[]{:S(2)}) copy-start(bf16[1,2048,256]{2,1,0:T(8,128)(2,1)} %param.7) | copy-start | bytes 3145732
  0.7 16.3 %copy-start.10 = (bf16[2,256,256]{2,1,0:T(8,128)(2,1)S(1)}, bf16[2,256,256]{2,1,0:T(8,128)(2,1)}, u32[]{:S(2)}) copy-start(bf16[2,256,256]{2,1,0:T(8,128)(2,1)} %param.11) | copy-start | bytes 786436
  0.7 14.9 %copy-start.16 = (s32[1,16,8]{1,2,0:T(8,128)S(1)}, s32[1,16,8]{1,2,0:T(8,128)}, u32[]{:S(2)}) copy-start(s32[1,16,8]{1,2,0:T(8,128)} %param.9) | copy-start | bytes 1540
  0.7 15.6 %copy-start.11 = (bf16[2,256,256]{2,1,0:T(8,128)(2,1)S(1)}, bf16[2,256,256]{2,1,0:T(8,128)(2,1)}, u32[]{:S(2)}) copy-start(bf16[2,256,256]{2,1,0:T(8,128)(2,1)} %param.12) | copy-start | bytes 786436
  4.7 13.7 %collective-permute-start.1 = (bf16[4,128,256]{2,1,0:T(8,128)(2,1)S(1)}, bf16[4,128,256]{2,1,0:T(8,128)(2,1)S(1)}, u32[]{:S(2)}, u32[]{:S(2)}) collective-permute-start(bf16[4,128,256]{2,1,0:T(8,128)(2,1)S(1)} %bitcast.135), channel_id=1, source_target_pairs={{1,0},{2,1},{3,2},{4,3},{5,4},{6,5},{7,6},{8,7},{9,8},{10,9},{11,1... | collective-permute-start | bytes 786440 | tf_op jit(solution)/shard_map/ppermute | solution.py:162
  14.7 10.3 %collective-permute-start = (bf16[4,128,256]{2,1,0:T(8,128)(2,1)S(1)}, bf16[4,128,256]{2,1,0:T(8,128)(2,1)S(1)}, u32[]{:S(2)}, u32[]{:S(2)}) collective-permute-start(bf16[4,128,256]{2,1,0:T(8,128)(2,1)S(1)} %bitcast.136), channel_id=1, source_target_pairs={{0,1},{1,2},{2,3},{3,4},{4,5},{5,6},{6,7},{7,8},{8,9},{9,10},{10,1... | collective-permute-start | bytes 786440 | tf_op jit(solution)/shard_map/ppermute | solution.py:157
  32.0 9.0 %copy-start = (bf16[16,128,256]{2,1,0:T(8,128)(2,1)S(1)}, bf16[16,128,256]{2,1,0:T(8,128)(2,1)}, u32[]{:S(2)}) copy-start(bf16[16,128,256]{2,1,0:T(8,128)(2,1)} %get-tuple-element.16.hits_ref) | copy-start | bytes 3145732
  36.1 9.4 %collective-permute-start.2 = (bf16[4,128,256]{2,1,0:T(8,128)(2,1)S(1)}, bf16[4,128,256]{2,1,0:T(8,128)(2,1)S(1)}, u32[]{:S(2)}, u32[]{:S(2)}) collective-permute-start(bf16[4,128,256]{2,1,0:T(8,128)(2,1)S(1)} %bitcast.138), channel_id=1, source_target_pairs={{0,1},{1,2},{2,3},{3,4},{4,5},{5,6},{6,7},{7,8},{8,9},{9,10},{10,1... | collective-permute-start | bytes 786440 | tf_op jit(solution)/shard_map/ppermute | solution.py:157
  36.2 9.4 %collective-permute-start.3 = (bf16[4,128,256]{2,1,0:T(8,128)(2,1)S(1)}, bf16[4,128,256]{2,1,0:T(8,128)(2,1)S(1)}, u32[]{:S(2)}, u32[]{:S(2)}) collective-permute-start(bf16[4,128,256]{2,1,0:T(8,128)(2,1)S(1)} %bitcast.137), channel_id=1, source_target_pairs={{1,0},{2,1},{3,2},{4,3},{5,4},{6,5},{7,6},{8,7},{9,8},{10,9},{11,1... | collective-permute-start | bytes 786440 | tf_op jit(solution)/shard_map/ppermute | solution.py:162
  52.5 12.7 %copy-start.4 = (f32[1,2048,256]{2,1,0:T(8,128)S(1)}, f32[1,2048,256]{2,1,0:T(8,128)}, u32[]{:S(2)}) copy-start(f32[1,2048,256]{2,1,0:T(8,128)} %param.13) | copy-start | bytes 6291460
  60.4 8.9 %collective-permute-start.4 = (bf16[4,128,256]{2,1,0:T(8,128)(2,1)}, bf16[4,128,256]{2,1,0:T(8,128)(2,1)}, u32[]{:S(2)}, u32[]{:S(2)}) collective-permute-start(bf16[4,128,256]{2,1,0:T(8,128)(2,1)} %get-tuple-element.21), channel_id=1, source_target_pairs={{0,1},{1,2},{2,3},{3,4},{4,5},{5,6},{6,7},{7,8},{8,9},{9,10},{10,1... | collective-permute-start | bytes 786440 | tf_op jit(solution)/shard_map/ppermute | solution.py:157
  60.4 8.9 %collective-permute-start.5 = (bf16[4,128,256]{2,1,0:T(8,128)(2,1)}, bf16[4,128,256]{2,1,0:T(8,128)(2,1)}, u32[]{:S(2)}, u32[]{:S(2)}) collective-permute-start(bf16[4,128,256]{2,1,0:T(8,128)(2,1)} %get-tuple-element.22), channel_id=1, source_target_pairs={{1,0},{2,1},{3,2},{4,3},{5,4},{6,5},{7,6},{8,7},{9,8},{10,9},{11,1... | collective-permute-start | bytes 786440 | tf_op jit(solution)/shard_map/ppermute | solution.py:162
  65.2 3.1 %copy-start.1 = (bf16[16,128,256]{2,1,0:T(8,128)(2,1)S(1)}, bf16[16,128,256]{2,1,0:T(8,128)(2,1)}, u32[]{:S(2)}) copy-start(bf16[16,128,256]{2,1,0:T(8,128)(2,1)} %get-tuple-element.16.hits_ref) | copy-start | bytes 3145732
  65.2 3.2 %copy-start.8 = (bf16[16,128,256]{2,1,0:T(8,128)(2,1)S(1)}, bf16[16,128,256]{2,1,0:T(8,128)(2,1)}, u32[]{:S(2)}) copy-start(bf16[16,128,256]{2,1,0:T(8,128)(2,1)} %get-tuple-element.19) | copy-start | bytes 3145732
  68.8 4.3 %copy-start.5 = (f32[2048,256]{1,0:T(8,128)S(1)}, f32[2048,256]{1,0:T(8,128)}, u32[]{:S(2)}) copy-start(f32[2048,256]{1,0:T(8,128)} %convolution_add_fusion.3) | copy-start | bytes 6291460
  76.1 12.8 %copy-start.7 = (bf16[1,2048,256]{2,1,0:T(8,128)(2,1)S(1)}, bf16[1,2048,256]{2,1,0:T(8,128)(2,1)}, u32[]{:S(2)}) copy-start(bf16[1,2048,256]{2,1,0:T(8,128)(2,1)} %param.7) | copy-start | bytes 3145732
  84.0 6.7 %copy-start.3 = (bf16[16,128,256]{2,1,0:T(8,128)(2,1)S(1)}, bf16[16,128,256]{2,1,0:T(8,128)(2,1)}, u32[]{:S(2)}) copy-start(bf16[16,128,256]{2,1,0:T(8,128)(2,1)} %shard_map.105) | copy-start | bytes 3145732
  84.0 8.8 %collective-permute-start.6 = (bf16[4,128,256]{2,1,0:T(8,128)(2,1)}, bf16[4,128,256]{2,1,0:T(8,128)(2,1)S(1)}, u32[]{:S(2)}, u32[]{:S(2)}) collective-permute-start(bf16[4,128,256]{2,1,0:T(8,128)(2,1)} %get-tuple-element.26), channel_id=1, source_target_pairs={{0,1},{1,2},{2,3},{3,4},{4,5},{5,6},{6,7},{7,8},{8,9},{9,10},{10,1... | collective-permute-start | bytes 786440 | tf_op jit(solution)/shard_map/ppermute | solution.py:157
  84.0 8.8 %collective-permute-start.7 = (bf16[4,128,256]{2,1,0:T(8,128)(2,1)}, bf16[4,128,256]{2,1,0:T(8,128)(2,1)S(1)}, u32[]{:S(2)}, u32[]{:S(2)}) collective-permute-start(bf16[4,128,256]{2,1,0:T(8,128)(2,1)} %get-tuple-element.27), channel_id=1, source_target_pairs={{1,0},{2,1},{3,2},{4,3},{5,4},{6,5},{7,6},{8,7},{9,8},{10,9},{11,1... | collective-permute-start | bytes 786440 | tf_op jit(solution)/shard_map/ppermute | solution.py:162
  92.8 0.7 copy-start.13
  92.8 0.8 copy-start.14
  99.0 32.6 %copy-start.2 = (f32[2048,256]{1,0:T(8,128)S(1)}, f32[2048,256]{1,0:T(8,128)}, u32[]{:S(2)}) copy-start(f32[2048,256]{1,0:T(8,128)} %convolution_add_fusion.2) | copy-start | bytes 6291460
  99.0 32.6 %copy-start.12 = (bf16[2,256,256]{2,1,0:T(8,128)(2,1)S(1)}, bf16[2,256,256]{2,1,0:T(8,128)(2,1)}, u32[]{:S(2)}) copy-start(bf16[2,256,256]{2,1,0:T(8,128)(2,1)} %param.12) | copy-start | bytes 786436
  127.4 18.2 %all-to-all-start.1 = ((bf16[128,8,256]{2,1,0:T(8,128)(2,1)}), bf16[128,8,256]{2,1,0:T(8,128)(2,1)S(1)}, u32[]{:S(2)}, u32[]{:S(2)}) async-start(bf16[128,8,256]{2,1,0:T(8,128)(2,1)} %broadcast_in_dim.5), calls=%async_computation.1 | async-start | bytes 1048576 | tf_op jit(solution)/shard_map/all_to_all | solution.py:172
  131.7 1.8 %copy-start.9 = (bf16[16,128,256]{2,1,0:T(8,128)(2,1)S(1)}, bf16[16,128,256]{2,1,0:T(8,128)(2,1)}, u32[]{:S(2)}) copy-start(bf16[16,128,256]{2,1,0:T(8,128)(2,1)} %shard_map.107) | copy-start | bytes 3145732

commit v14 on v10

--- a/solution.py
+++ b/solution.py
@@ -9,23 +9,28 @@
 GROUP = 8
 
 
-def slot_rows(own_ref, lent_ref, slot):
+def slot_rows(own_ref, lower_ref, upper_ref, slot):
     own = own_ref.shape[0]
+    lent = lower_ref.shape[0]
     return jnp.where(
         slot < own,
         own_ref[jnp.minimum(slot, own - 1)],
-        lent_ref[jnp.maximum(slot - own, 0)],
+        jnp.where(
+            slot < own + lent,
+            lower_ref[jnp.clip(slot - own, 0, lent - 1)],
+            upper_ref[jnp.clip(slot - own - lent, 0, lent - 1)],
+        ),
     )
 
 
-def layer_kernel(src_ref, tiles_ref, own_ref, lent_ref, hits_ref, weight_ref, pre_ref, out_ref):
+def layer_kernel(src_ref, tiles_ref, own_ref, lower_ref, upper_ref, hits_ref, weight_ref, pre_ref, out_ref):
     step = pl.program_id(0)
     listed = tiles_ref.shape[1]
     for i in range(GROUP):
         block = step * GROUP + i
         lhs = jnp.concatenate([tiles_ref[i, k] for k in range(listed)], axis=1)
         rhs = jnp.concatenate(
-            [slot_rows(own_ref, lent_ref, src_ref[block, k]) for k in range(listed)], axis=0
+            [slot_rows(own_ref, lower_ref, upper_ref, src_ref[block, k]) for k in range(listed)], axis=0
         )
         rows = hits_ref[i]
         pre = jnp.dot(lhs, rhs, preferred_element_type=jnp.float32) + jnp.dot(
@@ -37,7 +42,7 @@
         )
 
 
-def block_layer(slot_ids, tile_data, own_table, lent_table, hit_blocks, weight):
+def block_layer(slot_ids, tile_data, own_table, lower_table, upper_table, hit_blocks, weight):
     blocks, listed, rows, _ = tile_data.shape
     width = own_table.shape[-1]
     block_spec = pl.BlockSpec((GROUP, rows, width), lambda g, src: (g, 0, 0))
@@ -49,7 +54,8 @@
             in_specs=[
                 pl.BlockSpec((GROUP, listed, rows, rows), lambda g, src: (g, 0, 0, 0)),
                 pl.BlockSpec(own_table.shape, lambda g, src: (0, 0, 0)),
-                pl.BlockSpec(lent_table.shape, lambda g, src: (0, 0, 0)),
+                pl.BlockSpec(lower_table.shape, lambda g, src: (0, 0, 0)),
+                pl.BlockSpec(upper_table.shape, lambda g, src: (0, 0, 0)),
                 block_spec,
                 pl.BlockSpec(weight.shape, lambda g, src: (0, 0)),
             ],
@@ -59,7 +65,7 @@
             jax.ShapeDtypeStruct((blocks, rows, width), jnp.float32),
             jax.ShapeDtypeStruct((blocks, rows, width), hit_blocks.dtype),
         ],
-    )(slot_ids, tile_data, own_table, lent_table, hit_blocks, weight)
+    )(slot_ids, tile_data, own_table, lower_table, upper_table, hit_blocks, weight)
 
 
 def slot_grad_kernel(src_ref, tiles_ref, grad_ref, pre_ref, own_ref, low_ref, high_ref, dpre_ref, out_ref):
@@ -200,7 +206,7 @@
         from_lower = to_upper(message_blocks[own_lists[0]], "sector")
         from_upper = to_lower(message_blocks[own_lists[1]], "sector")
         pre, following = block_layer(
-            slot_ids, tile_data, message_blocks, jnp.concatenate([from_lower, from_upper]),
+            slot_ids, tile_data, message_blocks, from_lower, from_upper,
             current.reshape(message_blocks.shape),
             w_self[layer_index],
         )

time: 140 us -> 140 us (level)
  other arithmetic: 1.95 us -> 0.27 us
  local copies, waits for them, and re-layouts: 8.09 us -> 9.62 us
    concatenate x2 -> x0, other arithmetic: 1.68 us -> none  [per_device(): jnp.concatenate([from_lower, from_upper])]
    unnamed x38 -> x46, local copies, waits for them, and re-layouts: 0.86 us -> 2.41 us
where the time goes in v14:
time: 140 us
  Pallas kernels  35.8 us (26%)
  blocking collectives  26.4 us (19%)
  starting transfers between devices  26.3 us (19%)
  waiting for transfers between devices  22.8 us (16%)
  matrix products  17.6 us (13%)
  local copies, waits for them, and re-layouts  9.62 us (7%)
    all_to_all x1, blocking collectives, all_reduce(): received = lax.all_to_all(pieces, axes, 0, 0, tiled=True)  26.4 us
    ppermute x4, starting transfers between devices, to_lower(): return lax.ppermute(x, axis, [((i + 1) % count, i) for i in range(count)])  19.4 us
    pallas_call x2, Pallas kernels, block_slot_grad(): pl.pallas_call(slot_grad_kernel, grid_spec=pltpu.PrefetchScalarGridSpec(n...  15.7 us
    pallas_call x2, Pallas kernels, block_layer(): pl.pallas_call(layer_kernel, grid_spec=pltpu.PrefetchScalarGridSpec(num_s...  12.7 us
    ppermute x4, waiting for transfers between devices, to_upper(): return lax.ppermute(x, axis, [(i, (i + 1) % count) for i in range(count)])  12.4 us
    all_to_all x1, waiting for transfers between devices, all_reduce(): gathered = lax.all_to_all(spread, axes, 0, 0, tiled=True)  10.4 us
    pallas_call x2, Pallas kernels, fold_lent(): pl.pallas_call(fold_kernel, grid_spec=pltpu.PrefetchScalarGridSpec(num_sc...  7.4 us
    dot_general x2, matrix products, per_device(): jnp.dot(dpre, w_self[layer_index].T, preferred_element_type=jnp.float32)  4.92 us
  transfers between devices with their start and end apart: 9, of which 5 were waited for; matrix products, arithmetic and copies ran while one was open for 7% of the time, Pallas kernels for 0%

profile of v14, /device:TPU:1, one launch (start us, length us, event | category | flops | bytes accessed | tf_op | source)
XLA Modules:
  0.0 139.7 jit_solution(2314483020507099532)
XLA Ops:
  0.7 1.0 dynamic-slice_reduce_fusion.1
  1.6 1.7 %convolution_convert_fusion.1 = bf16[2048,256]{1,0:T(8,128)(2,1)S(1)} fusion(bf16[1,2048,256]{2,1,0:T(8,128)(2,1)} %param.7, bf16[2,256,256]{2,1,0:T(8,128)(2,1)} %param.11), kind=kOutput, calls=%fused_computation.10 | convolution fusion | flops 268959744 | bytes 2228224 | tf_op jit(solution)/shard_map/dot_general | solution.py:202
  3.3 0.6 gather_fusion
  3.9 2.5 %collective-permute-start = (bf16[4,128,256]{2,1,0:T(8,128)(2,1)S(1)}, bf16[4,128,256]{2,1,0:T(8,128)(2,1)S(1)}, u32[]{:S(2)}, u32[]{:S(2)}) collective-permute-start(bf16[4,128,256]{2,1,0:T(8,128)(2,1)S(1)} %gather_fusion), channel_id=1, source_target_pairs={{0,1},{1,2},{2,3},{3,4},{4,5},{5,6},{6,7},{7,8},{8,9},{9,10},{10,1... | collective-permute-start | bytes 786440 | tf_op jit(solution)/shard_map/ppermute | solution.py:163
  6.4 0.6 gather_fusion.1
  7.0 4.7 %collective-permute-start.1 = (bf16[4,128,256]{2,1,0:T(8,128)(2,1)S(1)}, bf16[4,128,256]{2,1,0:T(8,128)(2,1)S(1)}, u32[]{:S(2)}, u32[]{:S(2)}) collective-permute-start(bf16[4,128,256]{2,1,0:T(8,128)(2,1)S(1)} %gather_fusion.1), channel_id=1, source_target_pairs={{1,0},{2,1},{3,2},{4,3},{5,4},{6,5},{7,6},{8,7},{9,8},{10,9},{11,1... | collective-permute-start | bytes 786440 | tf_op jit(solution)/shard_map/ppermute | solution.py:168
  11.6 0.7 copy.18.src_ref
  12.3 0.7 slice_bitcast_fusion
  13.0 3.9 %collective-permute-done.lower_ref = bf16[4,128,256]{2,1,0:T(8,128)(2,1)S(1)} collective-permute-done((bf16[4,128,256]{2,1,0:T(8,128)(2,1)S(1)}, bf16[4,128,256]{2,1,0:T(8,128)(2,1)S(1)}, u32[]{:S(2)}, u32[]{:S(2)}) %collective-permute-start) | collective-permute-done | bytes 262176 | tf_op jit(solution)/shard_map/ppermute | solution.py:163
  17.0 0.7 copy-done.15
  17.7 0.1 copy-done.17
  17.8 6.4 %shard_map.102 = (f32[16,128,256]{2,1,0:T(8,128)}, bf16[16,128,256]{2,1,0:T(8,128)(2,1)}) custom-call(s32[16,8]{1,0:T(8,128)} %copy.18.src_ref, bf16[16,8,128,128]{3,2,1,0:T(8,128)(2,1)} %bitcast.90, bf16[16,128,256]{2,1,0:T(8,128)(2,1)} %bitcast.100, bf16[4,128,256]{2,1,0:T(8,128)(2,1)} %copy-done.15, bf16[4,128,256]{2,1,0:T(8,128)(2,1)} %copy-done.17, ...), custom_call_target="tpu_custom_call" | custom-call | tf_op jit(solution)/shard_map/pallas_call | solution.py:49
  24.2 1.7 %convolution_convert_fusion = bf16[2048,256]{1,0:T(8,128)(2,1)S(1)} fusion(bf16[2048,256]{1,0:T(8,128)(2,1)} %bitcast.95, bf16[2,256,256]{2,1,0:T(8,128)(2,1)S(1)} %copy-done.10), kind=kOutput, calls=%fused_computation.9 | convolution fusion | flops 268959744 | bytes 2228224 | tf_op jit(solution)/shard_map/dot_general | solution.py:202
  25.9 0.6 gather_fusion.3
  26.4 0.6 gather_fusion.2
  27.0 0.1 collective-permute-start.2
  27.1 5.2 %collective-permute-start.3 = (bf16[4,128,256]{2,1,0:T(8,128)(2,1)S(1)}, bf16[4,128,256]{2,1,0:T(8,128)(2,1)S(1)}, u32[]{:S(2)}, u32[]{:S(2)}) collective-permute-start(bf16[4,128,256]{2,1,0:T(8,128)(2,1)S(1)} %gather_fusion.3), channel_id=1, source_target_pairs={{1,0},{2,1},{3,2},{4,3},{5,4},{6,5},{7,6},{8,7},{9,8},{10,9},{11,1... | collective-permute-start | bytes 786440 | tf_op jit(solution)/shard_map/ppermute | solution.py:168
  32.2 0.7 dynamic-slice_reduce_fusion.lists_ref
  33.0 4.3 %collective-permute-done.2.lower_ref = bf16[4,128,256]{2,1,0:T(8,128)(2,1)S(1)} collective-permute-done((bf16[4,128,256]{2,1,0:T(8,128)(2,1)S(1)}, bf16[4,128,256]{2,1,0:T(8,128)(2,1)S(1)}, u32[]{:S(2)}, u32[]{:S(2)}) %collective-permute-start.2) | collective-permute-done | bytes 262176 | tf_op jit(solution)/shard_map/ppermute | solution.py:163
  37.3 0.7 copy-done.16
  38.0 0.1 copy-done.18
  38.1 6.3 %shard_map.103 = (f32[16,128,256]{2,1,0:T(8,128)}, bf16[16,128,256]{2,1,0:T(8,128)(2,1)}) custom-call(s32[16,8]{1,0:T(8,128)} %copy.18.src_ref, bf16[16,8,128,128]{3,2,1,0:T(8,128)(2,1)} %bitcast.91, bf16[16,128,256]{2,1,0:T(8,128)(2,1)} %bitcast.103, bf16[4,128,256]{2,1,0:T(8,128)(2,1)} %copy-done.16, bf16[4,128,256]{2,1,0:T(8,128)(2,1)} %copy-done.18, ...), custom_call_target="tpu_custom_call" | custom-call | tf_op jit(solution)/shard_map/pallas_call | solution.py:49
  44.4 7.9 %shard_map.104 = (f32[16,128,256]{2,1,0:T(8,128)}, bf16[4,128,256]{2,1,0:T(8,128)(2,1)}, bf16[4,128,256]{2,1,0:T(8,128)(2,1)}, bf16[16,128,256]{2,1,0:T(8,128)(2,1)}) custom-call(s32[16,8]{1,0:T(8,128)} %copy.18.src_ref, bf16[16,8,128,128]{3,2,1,0:T(8,128)(2,1)} %bitcast.92, f32[16,128,256]{2,1,0:T(8,128)} %bitcast.97, f32[16,128,256]{2,1,0:T(8,128)} %get-tuple-element.18.pre_ref), custom_call_target="tpu_custom_call" | custom-call | tf_op jit(solution)/shard_map/pallas_call | solution.py:107
  52.2 4.8 %collective-permute-start.5 = (bf16[4,128,256]{2,1,0:T(8,128)(2,1)}, bf16[4,128,256]{2,1,0:T(8,128)(2,1)}, u32[]{:S(2)}, u32[]{:S(2)}) collective-permute-start(bf16[4,128,256]{2,1,0:T(8,128)(2,1)} %get-tuple-element.22), channel_id=1, source_target_pairs={{1,0},{2,1},{3,2},{4,3},{5,4},{6,5},{7,6},{8,7},{9,8},{10,9},{11,1... | collective-permute-start | bytes 786440 | tf_op jit(solution)/shard_map/ppermute | solution.py:168
  57.0 3.1 %convolution_add_fusion.3 = f32[2048,256]{1,0:T(8,128)} fusion(bf16[2048,256]{1,0:T(8,128)(2,1)} %bitcast.105, f32[1,2048,256]{2,1,0:T(8,128)S(1)} %copy-done.3, bf16[2,256,256]{2,1,0:T(8,128)(2,1)} %param.12), kind=kOutput, calls=%fused_computation.8 | convolution fusion | flops 268959744 | bytes 5373952 | tf_op jit(solution)/shard_map/dot_general | solution.py:234
  60.2 0.5 fusion.5
  60.7 0.9 collective-permute-done.4.lower_ref
  61.6 3.7 %shard_map.105 = bf16[16,128,256]{2,1,0:T(8,128)(2,1)} custom-call(s32[2,4]{1,0:T(2,128)} %dynamic-slice_reduce_fusion.lists_ref, f32[16,128,256]{2,1,0:T(8,128)} %get-tuple-element.20.slot_ref, bf16[4,128,256]{2,1,0:T(8,128)(2,1)} %collective-permute-done.4.lower_ref, bf16[4,128,256]{2,1,0:T(8,128)(2,1)} %collective-permute-done.5.upper_ref), custom_call_target="tpu_custom_call" | custom-call | tf_op jit(solution)/shard_map/pallas_call | solution.py:144
  65.3 3.0 %convolution_add_fusion.2 = f32[2048,256]{1,0:T(8,128)} fusion(f32[2048,256]{1,0:T(8,128)S(1)} %copy-done.4, bf16[2048,256]{1,0:T(8,128)(2,1)} %bitcast.96, bf16[2,256,256]{2,1,0:T(8,128)(2,1)S(1)} %copy-done.10), kind=kOutput, calls=%fused_computation.7 | convolution fusion | flops 268959744 | bytes 5373952 | tf_op jit(solution)/shard_map/dot_general | solution.py:235
  68.4 7.9 %shard_map.106 = (f32[16,128,256]{2,1,0:T(8,128)}, bf16[4,128,256]{2,1,0:T(8,128)(2,1)}, bf16[4,128,256]{2,1,0:T(8,128)(2,1)}, bf16[16,128,256]{2,1,0:T(8,128)(2,1)}) custom-call(s32[16,8]{1,0:T(8,128)} %copy.18.src_ref, bf16[16,8,128,128]{3,2,1,0:T(8,128)(2,1)} %bitcast.93, f32[16,128,256]{2,1,0:T(8,128)} %bitcast.94, f32[16,128,256]{2,1,0:T(8,128)} %get-tuple-element.23.pre_ref), custom_call_target="tpu_custom_call" | custom-call | tf_op jit(solution)/shard_map/pallas_call | solution.py:107
  76.3 1.9 %fusion.4 = bf16[1,256,256]{2,1,0:T(8,128)(2,1)S(1)} fusion(bf16[2048,256]{1,0:T(8,128)(2,1)} %bitcast.109, bf16[1,2048,256]{2,1,0:T(8,128)(2,1)S(1)} %copy-done.7), kind=kOutput, calls=%fused_computation.18 | convolution fusion | flops 268500992 | bytes 2228224 | tf_op jit(solution)/shard_map/dot_general | solution.py:230
  78.1 0.1 collective-permute-start.6
  78.2 4.8 %collective-permute-start.7 = (bf16[4,128,256]{2,1,0:T(8,128)(2,1)S(1)}, bf16[4,128,256]{2,1,0:T(8,128)(2,1)S(1)}, u32[]{:S(2)}, u32[]{:S(2)}) collective-permute-start(bf16[4,128,256]{2,1,0:T(8,128)(2,1)S(1)} %copy-done.21), channel_id=1, source_target_pairs={{1,0},{2,1},{3,2},{4,3},{5,4},{6,5},{7,6},{8,7},{9,8},{10,9},{11,1... | collective-permute-start | bytes 786440 | tf_op jit(solution)/shard_map/ppermute | solution.py:168
  83.0 0.5 fusion.6
  83.5 3.2 %collective-permute-done.6.lower_ref = bf16[4,128,256]{2,1,0:T(8,128)(2,1)S(1)} collective-permute-done((bf16[4,128,256]{2,1,0:T(8,128)(2,1)S(1)}, bf16[4,128,256]{2,1,0:T(8,128)(2,1)S(1)}, u32[]{:S(2)}, u32[]{:S(2)}) %collective-permute-start.6) | collective-permute-done | bytes 262176 | tf_op jit(solution)/shard_map/ppermute | solution.py:163
  86.7 0.7 copy-done.13
  87.4 0.1 copy-done.14
  87.5 3.7 %shard_map.107 = bf16[16,128,256]{2,1,0:T(8,128)(2,1)} custom-call(s32[2,4]{1,0:T(2,128)} %dynamic-slice_reduce_fusion.lists_ref, f32[16,128,256]{2,1,0:T(8,128)} %get-tuple-element.25.slot_ref, bf16[4,128,256]{2,1,0:T(8,128)(2,1)} %copy-done.13, bf16[4,128,256]{2,1,0:T(8,128)(2,1)} %copy-done.14), custom_call_target="tpu_custom_call" | custom-call | tf_op jit(solution)/shard_map/pallas_call | solution.py:144
  91.2 1.7 %fusion.3 = bf16[1,256,256]{2,1,0:T(8,128)(2,1)S(1)} fusion(bf16[2048,256]{1,0:T(8,128)(2,1)} %bitcast.106, bf16[1,2048,256]{2,1,0:T(8,128)(2,1)S(1)} %copy-done.7), kind=kOutput, calls=%fused_computation.17 | convolution fusion | flops 268500992 | bytes 2228224 | tf_op jit(solution)/shard_map/dot_general | solution.py:231
  93.0 0.1 pad_maximum_fusion
  93.1 26.4 %all_to_all.10 = bf16[128,8,256]{2,1,0:T(8,128)(2,1)S(1)} all-to-all(bf16[128,8,256]{2,1,0:T(8,128)(2,1)S(1)} %bitcast.108), channel_id=1, replica_groups=mesh['dp'=8,'sector'=16] {'dp','sector'}, dimensions={0} | all-to-all | bytes 1048576 | tf_op jit(solution)/shard_map/all_to_all | solution.py:175
  119.5 0.1 convert_reduce_fusion
  119.6 0.8 broadcast_in_dim.5
  120.5 4.2 %all-to-all-start.1 = ((bf16[128,8,256]{2,1,0:T(8,128)(2,1)}), bf16[128,8,256]{2,1,0:T(8,128)(2,1)S(1)}, u32[]{:S(2)}, u32[]{:S(2)}) async-start(bf16[128,8,256]{2,1,0:T(8,128)(2,1)} %broadcast_in_dim.5), calls=%async_computation.1 | async-start | bytes 1048576 | tf_op jit(solution)/shard_map/all_to_all | solution.py:178
  124.7 1.8 %convolution_add_fusion.1 = f32[2048,256]{1,0:T(8,128)S(1)} fusion(f32[2048,256]{1,0:T(8,128)S(1)} %copy-done, bf16[2048,256]{1,0:T(8,128)(2,1)} %bitcast.110, bf16[2,256,256]{2,1,0:T(8,128)(2,1)S(1)} %copy-done.12), kind=kOutput, calls=%fused_computation.6 | convolution fusion | flops 268959744 | bytes 5373952 | tf_op jit(solution)/shard_map/dot_general | solution.py:234
  126.5 1.8 %fusion = f32[1,2048,256]{2,1,0:T(8,128)} fusion(f32[2048,256]{1,0:T(8,128)S(1)} %convolution_add_fusion.1, bf16[2048,256]{1,0:T(8,128)(2,1)S(1)} %bitcast.107, bf16[2,256,256]{2,1,0:T(8,128)(2,1)S(1)} %copy-done.10), kind=kOutput, calls=%fused_computation.5 | convolution fusion | flops 268959744 | bytes 5373952 | tf_op jit(solution)/shard_map/dot_general | solution.py:235
  128.3 10.4 %all-to-all-done.1 = bf16[128,8,256]{2,1,0:T(8,128)(2,1)S(1)} async-done(((bf16[128,8,256]{2,1,0:T(8,128)(2,1)}), bf16[128,8,256]{2,1,0:T(8,128)(2,1)S(1)}, u32[]{:S(2)}, u32[]{:S(2)}) %all-to-all-start.1) | async-done | bytes 524320 | tf_op jit(solution)/shard_map/all_to_all | solution.py:178
  138.7 1.0 fusion.20
  (51 shorter events, 0.2 us)
Async XLA Ops:
  0.6 11.0 %copy-start.20 = (s32[1,16,8]{1,2,0:T(8,128)S(1)}, s32[1,16,8]{1,2,0:T(8,128)}, u32[]{:S(2)}) copy-start(s32[1,16,8]{1,2,0:T(8,128)} %param.9) | copy-start | bytes 1540
  0.6 11.7 %copy-start.11 = (bf16[2,256,256]{2,1,0:T(8,128)(2,1)S(1)}, bf16[2,256,256]{2,1,0:T(8,128)(2,1)}, u32[]{:S(2)}) copy-start(bf16[2,256,256]{2,1,0:T(8,128)(2,1)} %param.12) | copy-start | bytes 786436
  3.3 13.7 %copy-start.5 = (bf16[2048,256]{1,0:T(8,128)(2,1)}, bf16[2048,256]{1,0:T(8,128)(2,1)S(1)}, u32[]{:S(2)}) copy-start(bf16[2048,256]{1,0:T(8,128)(2,1)S(1)} %convolution_convert_fusion.1) | copy-start | bytes 3145732
  3.9 13.1 %collective-permute-start = (bf16[4,128,256]{2,1,0:T(8,128)(2,1)S(1)}, bf16[4,128,256]{2,1,0:T(8,128)(2,1)S(1)}, u32[]{:S(2)}, u32[]{:S(2)}) collective-permute-start(bf16[4,128,256]{2,1,0:T(8,128)(2,1)S(1)} %gather_fusion), channel_id=1, source_target_pairs={{0,1},{1,2},{2,3},{3,4},{4,5},{5,6},{6,7},{7,8},{8,9},{9,10},{10,1... | collective-permute-start | bytes 786440 | tf_op jit(solution)/shard_map/ppermute | solution.py:163
  7.0 10.0 %collective-permute-start.1 = (bf16[4,128,256]{2,1,0:T(8,128)(2,1)S(1)}, bf16[4,128,256]{2,1,0:T(8,128)(2,1)S(1)}, u32[]{:S(2)}, u32[]{:S(2)}) collective-permute-start(bf16[4,128,256]{2,1,0:T(8,128)(2,1)S(1)} %gather_fusion.1), channel_id=1, source_target_pairs={{1,0},{2,1},{3,2},{4,3},{5,4},{6,5},{7,6},{8,7},{9,8},{10,9},{11,1... | collective-permute-start | bytes 786440 | tf_op jit(solution)/shard_map/ppermute | solution.py:168
  17.0 0.7 copy-start.15
  17.0 0.8 copy-start.17
  17.8 6.4 %copy-start.10 = (bf16[2,256,256]{2,1,0:T(8,128)(2,1)S(1)}, bf16[2,256,256]{2,1,0:T(8,128)(2,1)}, u32[]{:S(2)}) copy-start(bf16[2,256,256]{2,1,0:T(8,128)(2,1)} %param.11) | copy-start | bytes 786436
  24.2 8.1 %copy-start.19 = (s32[1,16,2,4]{1,3,2,0:T(4,128)S(1)}, s32[1,16,2,4]{1,3,2,0:T(4,128)}, u32[]{:S(2)}) copy-start(s32[1,16,2,4]{1,3,2,0:T(4,128)} %param.10) | copy-start | bytes 1540
  25.8 11.5 %copy-start.6 = (bf16[2048,256]{1,0:T(8,128)(2,1)}, bf16[2048,256]{1,0:T(8,128)(2,1)S(1)}, u32[]{:S(2)}) copy-start(bf16[2048,256]{1,0:T(8,128)(2,1)S(1)} %convolution_convert_fusion) | copy-start | bytes 3145732
  27.0 10.3 %collective-permute-start.2 = (bf16[4,128,256]{2,1,0:T(8,128)(2,1)S(1)}, bf16[4,128,256]{2,1,0:T(8,128)(2,1)S(1)}, u32[]{:S(2)}, u32[]{:S(2)}) collective-permute-start(bf16[4,128,256]{2,1,0:T(8,128)(2,1)S(1)} %gather_fusion.2), channel_id=1, source_target_pairs={{0,1},{1,2},{2,3},{3,4},{4,5},{5,6},{6,7},{7,8},{8,9},{9,10},{10,1... | collective-permute-start | bytes 786440 | tf_op jit(solution)/shard_map/ppermute | solution.py:163
  27.1 10.2 %collective-permute-start.3 = (bf16[4,128,256]{2,1,0:T(8,128)(2,1)S(1)}, bf16[4,128,256]{2,1,0:T(8,128)(2,1)S(1)}, u32[]{:S(2)}, u32[]{:S(2)}) collective-permute-start(bf16[4,128,256]{2,1,0:T(8,128)(2,1)S(1)} %gather_fusion.3), channel_id=1, source_target_pairs={{1,0},{2,1},{3,2},{4,3},{5,4},{6,5},{7,6},{8,7},{9,8},{10,9},{11,1... | collective-permute-start | bytes 786440 | tf_op jit(solution)/shard_map/ppermute | solution.py:168
  37.3 0.7 copy-start.16
  37.3 0.8 copy-start.18
  44.3 12.7 %copy-start.3 = (f32[1,2048,256]{2,1,0:T(8,128)S(1)}, f32[1,2048,256]{2,1,0:T(8,128)}, u32[]{:S(2)}) copy-start(f32[1,2048,256]{2,1,0:T(8,128)} %param.13) | copy-start | bytes 6291460
  52.2 9.4 %collective-permute-start.4 = (bf16[4,128,256]{2,1,0:T(8,128)(2,1)}, bf16[4,128,256]{2,1,0:T(8,128)(2,1)}, u32[]{:S(2)}, u32[]{:S(2)}) collective-permute-start(bf16[4,128,256]{2,1,0:T(8,128)(2,1)} %get-tuple-element.21), channel_id=1, source_target_pairs={{0,1},{1,2},{2,3},{3,4},{4,5},{5,6},{6,7},{7,8},{8,9},{9,10},{10,1... | collective-permute-start | bytes 786440 | tf_op jit(solution)/shard_map/ppermute | solution.py:163
  52.2 9.4 %collective-permute-start.5 = (bf16[4,128,256]{2,1,0:T(8,128)(2,1)}, bf16[4,128,256]{2,1,0:T(8,128)(2,1)}, u32[]{:S(2)}, u32[]{:S(2)}) collective-permute-start(bf16[4,128,256]{2,1,0:T(8,128)(2,1)} %get-tuple-element.22), channel_id=1, source_target_pairs={{1,0},{2,1},{3,2},{4,3},{5,4},{6,5},{7,6},{8,7},{9,8},{10,9},{11,1... | collective-permute-start | bytes 786440 | tf_op jit(solution)/shard_map/ppermute | solution.py:168
  57.0 3.1 %copy-start.1 = (bf16[16,128,256]{2,1,0:T(8,128)(2,1)S(1)}, bf16[16,128,256]{2,1,0:T(8,128)(2,1)}, u32[]{:S(2)}) copy-start(bf16[16,128,256]{2,1,0:T(8,128)(2,1)} %get-tuple-element.16.hits_ref) | copy-start | bytes 3145732
  57.0 3.1 %copy-start.8 = (bf16[16,128,256]{2,1,0:T(8,128)(2,1)S(1)}, bf16[16,128,256]{2,1,0:T(8,128)(2,1)}, u32[]{:S(2)}) copy-start(bf16[16,128,256]{2,1,0:T(8,128)(2,1)} %get-tuple-element.19) | copy-start | bytes 3145732
  60.6 4.7 %copy-start.4 = (f32[2048,256]{1,0:T(8,128)S(1)}, f32[2048,256]{1,0:T(8,128)}, u32[]{:S(2)}) copy-start(f32[2048,256]{1,0:T(8,128)} %convolution_add_fusion.3) | copy-start | bytes 6291460
  68.4 7.9 %copy-start.7 = (bf16[1,2048,256]{2,1,0:T(8,128)(2,1)S(1)}, bf16[1,2048,256]{2,1,0:T(8,128)(2,1)}, u32[]{:S(2)}) copy-start(bf16[1,2048,256]{2,1,0:T(8,128)(2,1)} %param.7) | copy-start | bytes 3145732
  76.2 1.9 %copy-start.22 = (bf16[4,128,256]{2,1,0:T(8,128)(2,1)S(1)}, bf16[4,128,256]{2,1,0:T(8,128)(2,1)}, u32[]{:S(2)}) copy-start(bf16[4,128,256]{2,1,0:T(8,128)(2,1)} %get-tuple-element.26) | copy-start | bytes 786436
  76.2 2.0 %copy-start.21 = (bf16[4,128,256]{2,1,0:T(8,128)(2,1)S(1)}, bf16[4,128,256]{2,1,0:T(8,128)(2,1)}, u32[]{:S(2)}) copy-start(bf16[4,128,256]{2,1,0:T(8,128)(2,1)} %get-tuple-element.27) | copy-start | bytes 786436
  76.2 6.8 %copy-start.2 = (bf16[16,128,256]{2,1,0:T(8,128)(2,1)S(1)}, bf16[16,128,256]{2,1,0:T(8,128)(2,1)}, u32[]{:S(2)}) copy-start(bf16[16,128,256]{2,1,0:T(8,128)(2,1)} %shard_map.105) | copy-start | bytes 3145732
  78.1 8.6 %collective-permute-start.6 = (bf16[4,128,256]{2,1,0:T(8,128)(2,1)S(1)}, bf16[4,128,256]{2,1,0:T(8,128)(2,1)S(1)}, u32[]{:S(2)}, u32[]{:S(2)}) collective-permute-start(bf16[4,128,256]{2,1,0:T(8,128)(2,1)S(1)} %copy-done.22), channel_id=1, source_target_pairs={{0,1},{1,2},{2,3},{3,4},{4,5},{5,6},{6,7},{7,8},{8,9},{9,10},{10,1... | collective-permute-start | bytes 786440 | tf_op jit(solution)/shard_map/ppermute | solution.py:163
  78.2 8.5 %collective-permute-start.7 = (bf16[4,128,256]{2,1,0:T(8,128)(2,1)S(1)}, bf16[4,128,256]{2,1,0:T(8,128)(2,1)S(1)}, u32[]{:S(2)}, u32[]{:S(2)}) collective-permute-start(bf16[4,128,256]{2,1,0:T(8,128)(2,1)S(1)} %copy-done.21), channel_id=1, source_target_pairs={{1,0},{2,1},{3,2},{4,3},{5,4},{6,5},{7,6},{8,7},{9,8},{10,9},{11,1... | collective-permute-start | bytes 786440 | tf_op jit(solution)/shard_map/ppermute | solution.py:168
  86.7 0.7 copy-start.13
  86.7 0.8 copy-start.14
  93.0 31.7 %copy-start = (f32[2048,256]{1,0:T(8,128)S(1)}, f32[2048,256]{1,0:T(8,128)}, u32[]{:S(2)}) copy-start(f32[2048,256]{1,0:T(8,128)} %convolution_add_fusion.2) | copy-start | bytes 6291460
  93.0 31.7 %copy-start.12 = (bf16[2,256,256]{2,1,0:T(8,128)(2,1)S(1)}, bf16[2,256,256]{2,1,0:T(8,128)(2,1)}, u32[]{:S(2)}) copy-start(bf16[2,256,256]{2,1,0:T(8,128)(2,1)} %param.12) | copy-start | bytes 786436
  120.5 18.2 %all-to-all-start.1 = ((bf16[128,8,256]{2,1,0:T(8,128)(2,1)}), bf16[128,8,256]{2,1,0:T(8,128)(2,1)S(1)}, u32[]{:S(2)}, u32[]{:S(2)}) async-start(bf16[128,8,256]{2,1,0:T(8,128)(2,1)} %broadcast_in_dim.5), calls=%async_computation.1 | async-start | bytes 1048576 | tf_op jit(solution)/shard_map/all_to_all | solution.py:178
  124.7 1.8 %copy-start.9 = (bf16[16,128,256]{2,1,0:T(8,128)(2,1)S(1)}, bf16[16,128,256]{2,1,0:T(8,128)(2,1)}, u32[]{:S(2)}) copy-start(bf16[16,128,256]{2,1,0:T(8,128)(2,1)} %shard_map.107) | copy-start | bytes 3145732
